TPU v7x, 32 devices: a whole 2x2x4 slice. The times are simulated.
32 devices in a mesh: illum: 8 (over z, y), tile: 4 (over x, core).
Axes of the slice: x: 2, y: 2, z: 4, core: 2. Of those that a mesh axis runs over, the one named last changes fastest.
Arguments:
- tilts: int32 [8, 2], P('illum'), may hold values from -64 to 64
- taps: float32 [2, 33], replicated, may hold values from -0.75 to 0.75
- stored_planes: float32 [2, 128, 4096], P(None, 'tile', 'illum'), may hold values from -3.140625 to 3.140625
- owner: int32 [2, 8], replicated, may hold values from 0 to 7, each once within a row
Outputs:
- exit_field: float32 [2, 8, 128, 4096], P(None, 'illum', 'tile')
Inputs may be any that keep to these rules, and one draw needn't show every extreme that they name: Each row of owner is a permutation of the 8 stored column blocks.
All inputs are finite; a program needn't handle non-finite values.
Results may differ from a plain program's by a relative error of at most 0.0003.
Values sent between devices are 32-bit elements; how exact they have to be, the bound alone decides.
No kernel may reach another device: no remote copies, remote signals or barrier semaphores. Data moves between devices by JAX's collectives and lax.ppermute only.
A program may use at most 64 MiB of HBM per device.

v0:
```python
import jax
import jax.numpy as jnp
from jax import lax
from jax.sharding import PartitionSpec as P

NY = 4096
PLANES = 2
HALF = 16


two_pi = 6.283185307179586


def extended(cells, sides, width):
    for axis, dim in sides:
        count = lax.axis_size(axis)
        ends = count - 1
        head = lax.slice_in_dim(cells, 0, width, axis=dim)
        tail = lax.slice_in_dim(cells, cells.shape[dim] - width, cells.shape[dim], axis=dim)
        cells = jnp.concatenate(
            [
                lax.ppermute(tail, axis, [(i, (i + 1) % count) for i in range(ends)]),
                cells,
                lax.ppermute(head, axis, [((i + 1) % count, i) for i in range(ends)]),
            ],
            axis=dim,
        )
    return cells


def toeplitz(tap_row, block):
    rows = jnp.arange(block + 2 * HALF)[:, None]
    cols = jnp.arange(block)[None, :]
    offset = rows - cols
    steps = jnp.arange(2 * HALF + 1)
    return jnp.sum(jnp.where(offset[:, :, None] == steps, tap_row, 0.0), axis=2)


def band_matrix(tap_row, count):
    rows = jnp.arange(count)[:, None]
    cols = jnp.arange(count + 2 * HALF)[None, :]
    offset = cols - rows
    steps = jnp.arange(2 * HALF + 1)
    return jnp.sum(jnp.where(offset[:, :, None] == steps, tap_row, 0.0), axis=2)


def windows(field, block):
    length = field.shape[-1]
    count = length // block
    widths = [(0, 0)] * (field.ndim - 1) + [(HALF, block - HALF)]
    padded = jnp.pad(field, widths)
    lead = field.shape[:-1]
    main = padded[..., :length].reshape(lead + (count, block))
    after = padded[..., block : length + block].reshape(lead + (count, block))[..., : 2 * HALF]
    return jnp.concatenate([main, after], axis=-1)


def along_pass(real, imag, taps):
    block = min(128, real.shape[-1])
    win_real = windows(real, block)
    win_imag = windows(imag, block)
    kern_real = toeplitz(taps[0], block)
    kern_imag = toeplitz(taps[1], block)

    def apply(win, kern):
        out = jnp.einsum("...nj,jc->...nc", win, kern, precision=lax.Precision.HIGHEST)
        return out.reshape(real.shape)

    return (
        apply(win_real, kern_real) - apply(win_imag, kern_imag),
        apply(win_real, kern_imag) + apply(win_imag, kern_real),
    )


def cross_pass(real, imag, taps):
    count = real.shape[1] - 2 * HALF
    band_real = band_matrix(taps[0], count)
    band_imag = band_matrix(taps[1], count)

    def apply(band, field):
        return jnp.einsum("ij,ajy->aiy", band, field, precision=lax.Precision.HIGHEST)

    return (
        apply(band_real, real) - apply(band_imag, imag),
        apply(band_real, imag) + apply(band_imag, real),
    )


def transmit(real, imag, screen):
    cosine = jnp.cos(screen)
    sine = jnp.sin(screen)
    return (real * cosine - imag * sine, real * sine + imag * cosine)


def reorder(gathered, owner):
    count = gathered.shape[1]
    blocks = owner.shape[1]
    width = gathered.shape[2] // blocks
    planes = [
        gathered[p].reshape(count, blocks, width)[:, owner[p], :].reshape(count, blocks * width)
        for p in range(gathered.shape[0])
    ]
    return jnp.stack(planes)


def body(tilts, taps, stored_planes, owner):
    local_rows = stored_planes.shape[1]
    total_rows = local_rows * lax.axis_size("tile")
    total_cols = NY
    first_row = lax.axis_index("tile") * local_rows
    gathered = lax.all_gather(stored_planes, "illum", axis=2, tiled=True)
    screens = reorder(gathered, owner)
    extra = 0
    span = local_rows + 2 * extra
    global_rows = first_row - extra + jnp.arange(span, dtype=jnp.int32)
    inside = (global_rows >= 0) & (global_rows < total_rows)
    cols = jnp.arange(total_cols, dtype=jnp.int32)
    across = (
        jnp.mod(tilts[:, 0:1] * global_rows[None, :], total_rows).astype(jnp.float32) / total_rows
    )
    along = jnp.mod(tilts[:, 1:2] * cols[None, :], total_cols).astype(jnp.float32) / total_cols
    theta = two_pi * (across[:, :, None] + along[:, None, :])
    real = jnp.where(inside[None, :, None], jnp.cos(theta), 0.0)
    imag = jnp.where(inside[None, :, None], jnp.sin(theta), 0.0)
    for plane in range(PLANES):
        real, imag = transmit(real, imag, screens[plane])
        packed = extended(jnp.stack([real, imag]), (("tile", 2),), HALF)
        real, imag = cross_pass(packed[0], packed[1], taps)
        real, imag = along_pass(real, imag, taps)
    return jnp.stack([real, imag])


def solution(mesh):
    in_specs = (P("illum", None), P(), P(None, "tile", "illum"), P())
    out_specs = P(None, "illum", "tile", None)
    return jax.shard_map(body, mesh=mesh, in_specs=in_specs, out_specs=out_specs, check_vma=False)
```

profile of v0, /device:TPU:1, one launch (start us, length us, event | category | flops | bytes accessed | tf_op | source)
XLA Modules:
  0.0 116.0 jit_solution(4339684245039347680)
XLA Ops:
  6.5 0.7 all-gather.2.cloned.1.call-update
  7.3 1.4 %fusion.42 = (s32[1,1]{1,0:T(1,128)}, s32[1,1]{1,0:T(1,128)}) fusion(s32[1,2]{1,0:T(1,128)} %param.4), kind=kLoop, calls=%fused_computation.110 | loop fusion | bytes 16 | tf_op jit(solution)/shard_map/slice | solution.py:119
  9.3 0.8 fusion.32
  10.1 0.7 fusion.24
  10.8 0.8 slice_bitcast_fusion.20
  11.8 39.1 %all-gather.2.cloned.1.call-done = f32[2,32,4096]{2,1,0:T(8,128)} async-done(((f32[2,32,512]{2,1,0:T(8,128)}), f32[2,32,4096]{2,1,0:T(8,128)}) %all-gather.2.cloned.1.call-update) | async-done | bytes 1048592 | tf_op jit(solution)/shard_map/all_gather | solution.py:111
  50.9 1.3 %fusion.41 = (f32[1,32,4096]{2,1,0:T(8,128)S(1)}, f32[1,32,4096]{2,1,0:T(8,128)S(1)}) fusion(f32[2,32,4096]{2,1,0:T(8,128)} %all-gather.2.cloned.1.call-done), kind=kLoop, calls=%fused_computation.109 | loop fusion | bytes 2097152 | tf_op jit(solution)/shard_map/slice | solution.py:100
  53.4 1.9 %sine_bitcast_fusion.1 = (f32[32,8,512]{2,0,1:T(8,128)S(1)}, f32[32,8,512]{2,0,1:T(8,128)S(1)}) fusion(f32[8,32,512]{2,1,0:T(8,128)S(1)} %gather_fusion), kind=kLoop, calls=%fused_computation.49 | loop fusion | bytes 1572864 | tf_op jit(solution)/shard_map/sin | solution.py:91
  56.1 2.2 %multiply_subtract_fusion.1 = (f32[1,1,32,4096]{3,2,1,0:T(8,128)S(1)}, f32[1,1,32,4096]{3,2,1,0:T(8,128)S(1)}) fusion(f32[1,1,32,4096]{3,2,1,0:T(8,128)S(1)} %sin.57, f32[1,1,32,4096]{3,2,1,0:T(8,128)S(1)} %cos.57, f32[4096]{0:T(1024)S(1)} %fusion.24, f32[32]{0:T(128)S(1)} %fusion.29, pred[32]{0:T(512)(128)(4,1)S(1)} %compare_and_fusion), kind=kLoop, calls=%fused_computation.62 | loop fusion | flops 1310720 | bytes 2113696 | tf_op jit(solution)/shard_map/sub | solution.py:92
  58.2 0.9 fusion.13
  59.1 4.6 %collective-permute-start = (f32[2,1,16,4096]{3,2,1,0:T(8,128)}, f32[2,1,16,4096]{3,2,1,0:T(8,128)}, u32[]{:S(2)}, u32[]{:S(2)}) collective-permute-start(f32[2,1,16,4096]{3,2,1,0:T(8,128)} %get-tuple-element.17), channel_id=1, source_target_pairs={{0,1},{1,2},{2,3},{4,5},{5,6},{6,7},{8,9},{9,10},{10,11},{12,13},{... | collective-permute-start | bytes 1572872 | tf_op jit(solution)/shard_map/ppermute | solution.py:22
  63.8 2.1 %collective-permute-start.1 = (f32[2,1,16,4096]{3,2,1,0:T(8,128)S(1)}, f32[2,1,16,4096]{3,2,1,0:T(8,128)}, u32[]{:S(2)}, u32[]{:S(2)}) collective-permute-start(f32[2,1,16,4096]{3,2,1,0:T(8,128)S(1)} %get-tuple-element.18), channel_id=1, source_target_pairs={{1,0},{2,1},{3,2},{5,4},{6,5},{7,6},{9,8},{10,9},{11,10},{13,12},{... | collective-permute-start | bytes 1572872 | tf_op jit(solution)/shard_map/ppermute | solution.py:24
  67.7 1.9 %sine_bitcast_fusion = (f32[32,8,512]{2,0,1:T(8,128)S(1)}, f32[32,8,512]{2,0,1:T(8,128)S(1)}) fusion(f32[8,32,512]{2,1,0:T(8,128)S(1)} %gather_fusion.1), kind=kLoop, calls=%fused_computation.47 | loop fusion | bytes 1572864 | tf_op jit(solution)/shard_map/sin | solution.py:91
  70.4 4.0 %collective-permute-done.1 = f32[2,1,16,4096]{3,2,1,0:T(8,128)} collective-permute-done((f32[2,1,16,4096]{3,2,1,0:T(8,128)S(1)}, f32[2,1,16,4096]{3,2,1,0:T(8,128)}, u32[]{:S(2)}, u32[]{:S(2)}) %collective-permute-start.1) | collective-permute-done | bytes 524320 | tf_op jit(solution)/shard_map/ppermute | solution.py:24
  74.4 1.3 %pad_maximum_fusion = f32[2,1,64,4096]{3,2,1,0:T(8,128)S(1)} fusion(f32[2,1,16,4096]{3,2,1,0:T(8,128)} %collective-permute-done.1, f32[1,1,32,4096]{3,2,1,0:T(8,128)S(1)} %get-tuple-element.12, f32[1,1,32,4096]{3,2,1,0:T(8,128)S(1)} %get-tuple-element.11, f32[2,1,16,4096]{3,2,1,0:T(8,128)} %collective-permute-done), kind=kLoop, calls=%fused_computation.13 | loop fusion | flops 1572864 | bytes 4194304 | tf_op jit(solution)/shard_map/concatenate | solution.py:20
  77.1 0.7 fusion
  78.3 0.7 fusion.1
  79.6 1.0 fusion.11
  80.5 1.0 fusion.10
  81.5 1.8 %convolution_subtract_fusion.3 = f32[32,32,128]{2,1,0:T(8,128)} fusion(f32[32,32,128]{2,1,0:T(8,128)S(1)} %fusion.11, f32[1,32,32,32]{3,2,1,0:T(8,128)S(1)} %bitcast.154, f32[1,32,32,128]{3,2,1,0:T(8,128)S(1)} %bitcast.156, f32[160,128]{1,0:T(8,128)S(1)} %get-tuple-element.6), kind=kOutput, calls=%fused_computation.18 | convolution fusion | flops 251953152 | bytes 1785856 | tf_op jit(solution)/shard_map/...nj,jc->...nc/dot_general | solution.py:66
  83.3 1.1 sub.176
  84.4 1.8 %convolution_add_fusion.3 = f32[32,32,128]{2,1,0:T(8,128)} fusion(f32[32,32,128]{2,1,0:T(8,128)S(1)} %fusion.10, f32[1,32,32,32]{3,2,1,0:T(8,128)S(1)} %bitcast.155, f32[1,32,32,128]{3,2,1,0:T(8,128)S(1)} %bitcast.157, f32[160,128]{1,0:T(8,128)S(1)} %get-tuple-element.5), kind=kOutput, calls=%fused_computation.17 | convolution fusion | flops 251953152 | bytes 1785856 | tf_op jit(solution)/shard_map/...nj,jc->...nc/dot_general | solution.py:66
  86.2 1.1 add.184
  87.5 1.9 %collective-permute-start.2 = (f32[2,1,16,4096]{3,2,1,0:T(8,128)S(1)}, f32[2,1,16,4096]{3,2,1,0:T(8,128)S(1)}, u32[]{:S(2)}, u32[]{:S(2)}) collective-permute-start(f32[2,1,16,4096]{3,2,1,0:T(8,128)S(1)} %get-tuple-element.13), channel_id=1, source_target_pairs={{0,1},{1,2},{2,3},{4,5},{5,6},{6,7},{8,9},{9,10},{10,11},{12,13},{... | collective-permute-start | bytes 1572872 | tf_op jit(solution)/shard_map/ppermute | solution.py:22
  89.5 2.7 %collective-permute-start.3 = (f32[2,1,16,4096]{3,2,1,0:T(8,128)S(1)}, f32[2,1,16,4096]{3,2,1,0:T(8,128)S(1)}, u32[]{:S(2)}, u32[]{:S(2)}) collective-permute-start(f32[2,1,16,4096]{3,2,1,0:T(8,128)S(1)} %get-tuple-element.14), channel_id=1, source_target_pairs={{1,0},{2,1},{3,2},{5,4},{6,5},{7,6},{9,8},{10,9},{11,10},{13,12},{... | collective-permute-start | bytes 1572872 | tf_op jit(solution)/shard_map/ppermute | solution.py:24
  92.1 3.4 %collective-permute-done.2 = f32[2,1,16,4096]{3,2,1,0:T(8,128)S(1)} collective-permute-done((f32[2,1,16,4096]{3,2,1,0:T(8,128)S(1)}, f32[2,1,16,4096]{3,2,1,0:T(8,128)S(1)}, u32[]{:S(2)}, u32[]{:S(2)}) %collective-permute-start.2) | collective-permute-done | bytes 524320 | tf_op jit(solution)/shard_map/ppermute | solution.py:22
  95.6 4.4 %collective-permute-done.3 = f32[2,1,16,4096]{3,2,1,0:T(8,128)S(1)} collective-permute-done((f32[2,1,16,4096]{3,2,1,0:T(8,128)S(1)}, f32[2,1,16,4096]{3,2,1,0:T(8,128)S(1)}, u32[]{:S(2)}, u32[]{:S(2)}) %collective-permute-start.3) | collective-permute-done | bytes 524320 | tf_op jit(solution)/shard_map/ppermute | solution.py:24
  102.8 1.0 fusion.9
  103.7 1.0 fusion.8
  105.9 1.0 convolution_subtract_fusion.2
  107.0 1.0 convolution_add_fusion.2
  108.1 1.0 pad_maximum_fusion.2
  (46 shorter events, 12.2 us)
Async XLA Ops:
  6.5 44.3 %all-gather.2.cloned.1.call-start = ((), (), s32[]{:S(2)}) async-start(), calls=%async_computation | async-start | bytes 1179648 | tf_op jit(solution)/shard_map/all_gather | solution.py:111
  59.1 11.3 %collective-permute-start = (f32[2,1,16,4096]{3,2,1,0:T(8,128)}, f32[2,1,16,4096]{3,2,1,0:T(8,128)}, u32[]{:S(2)}, u32[]{:S(2)}) collective-permute-start(f32[2,1,16,4096]{3,2,1,0:T(8,128)} %get-tuple-element.17), channel_id=1, source_target_pairs={{0,1},{1,2},{2,3},{4,5},{5,6},{6,7},{8,9},{9,10},{10,11},{12,13},{... | collective-permute-start | bytes 1572872 | tf_op jit(solution)/shard_map/ppermute | solution.py:22
  63.8 10.6 %collective-permute-start.1 = (f32[2,1,16,4096]{3,2,1,0:T(8,128)S(1)}, f32[2,1,16,4096]{3,2,1,0:T(8,128)}, u32[]{:S(2)}, u32[]{:S(2)}) collective-permute-start(f32[2,1,16,4096]{3,2,1,0:T(8,128)S(1)} %get-tuple-element.18), channel_id=1, source_target_pairs={{1,0},{2,1},{3,2},{5,4},{6,5},{7,6},{9,8},{10,9},{11,10},{13,12},{... | collective-permute-start | bytes 1572872 | tf_op jit(solution)/shard_map/ppermute | solution.py:24
  87.5 8.0 %collective-permute-start.2 = (f32[2,1,16,4096]{3,2,1,0:T(8,128)S(1)}, f32[2,1,16,4096]{3,2,1,0:T(8,128)S(1)}, u32[]{:S(2)}, u32[]{:S(2)}) collective-permute-start(f32[2,1,16,4096]{3,2,1,0:T(8,128)S(1)} %get-tuple-element.13), channel_id=1, source_target_pairs={{0,1},{1,2},{2,3},{4,5},{5,6},{6,7},{8,9},{9,10},{10,11},{12,13},{... | collective-permute-start | bytes 1572872 | tf_op jit(solution)/shard_map/ppermute | solution.py:22
  89.5 10.5 %collective-permute-start.3 = (f32[2,1,16,4096]{3,2,1,0:T(8,128)S(1)}, f32[2,1,16,4096]{3,2,1,0:T(8,128)S(1)}, u32[]{:S(2)}, u32[]{:S(2)}) collective-permute-start(f32[2,1,16,4096]{3,2,1,0:T(8,128)S(1)} %get-tuple-element.14), channel_id=1, source_target_pairs={{1,0},{2,1},{3,2},{5,4},{6,5},{7,6},{9,8},{10,9},{11,10},{13,12},{... | collective-permute-start | bytes 1572872 | tf_op jit(solution)/shard_map/ppermute | solution.py:24
Sparse Core Ops, SparseCore 0:
  9.5 41.2 all-gather.1
where the time goes:
time: 116 us
  waiting for transfers between devices  51.6 us (44%)
  local copies, waits for them, and re-layouts  15.7 us (14%)
  matrix products  14.8 us (13%)
  between operations  13.8 us (12%)
  starting transfers between devices  11.3 us (10%)
  other arithmetic  8.69 us (7%)
    all_gather x1, waiting for transfers between devices, body(): gathered = lax.all_gather(stored_planes, 'illum', axis=2, tiled=True)  39.1 us
    dot_general x8, matrix products, apply(): jnp.einsum('...nj,jc->...nc', win, kern, precision=lax.Precision.HIGHEST)  9.36 us
    ppermute x2, waiting for transfers between devices, extended(): lax.ppermute(head, axis, [((i + 1) % count, i) for i in range(ends)])  8.37 us
    ppermute x2, starting transfers between devices, extended(): lax.ppermute(tail, axis, [(i, (i + 1) % count) for i in range(ends)])  6.56 us
    dot_general x8, matrix products, apply(): jnp.einsum('ij,ajy->aiy', band, field, precision=lax.Precision.HIGHEST)  5.44 us
    ppermute x2, starting transfers between devices, extended(): lax.ppermute(head, axis, [((i + 1) % count, i) for i in range(ends)])  4.76 us
    sin x6, local copies, waits for them, and re-layouts, transmit(): sine = jnp.sin(screen)  4.53 us
    ppermute x2, waiting for transfers between devices, extended(): lax.ppermute(tail, axis, [(i, (i + 1) % count) for i in range(ends)])  3.44 us
  transfers between devices with their start and end apart: 5, of which 4 were waited for; matrix products, arithmetic and copies ran while one was open for 8% of the time, Pallas kernels for 0%

commit v1 on v0

--- a/solution.py
+++ b/solution.py
@@ -103,13 +103,28 @@
     return jnp.stack(planes)
 
 
+def gather_screens(stored_planes, owner, axis):
+    count = lax.axis_size(axis)
+    me = lax.axis_index(axis)
+    parts = [stored_planes]
+    for shift in range(1, count):
+        parts.append(lax.ppermute(stored_planes, axis, [(i, (i + shift) % count) for i in range(count)]))
+    stacked = jnp.stack(parts, axis=1)
+    rows = stored_planes.shape[1]
+    width = stored_planes.shape[2]
+    planes = []
+    for p in range(stored_planes.shape[0]):
+        picked = stacked[p][jnp.mod(me - owner[p], count)]
+        planes.append(jnp.transpose(picked, (1, 0, 2)).reshape(rows, count * width))
+    return jnp.stack(planes)
+
+
 def body(tilts, taps, stored_planes, owner):
     local_rows = stored_planes.shape[1]
     total_rows = local_rows * lax.axis_size("tile")
     total_cols = NY
     first_row = lax.axis_index("tile") * local_rows
-    gathered = lax.all_gather(stored_planes, "illum", axis=2, tiled=True)
-    screens = reorder(gathered, owner)
+    screens = gather_screens(stored_planes, owner, "illum")
     extra = 0
     span = local_rows + 2 * extra
     global_rows = first_row - extra + jnp.arange(span, dtype=jnp.int32)

time: 116 us -> 83.1 us (0.72)
  the two profiles are of different devices: /device:TPU:1 before, /device:TPU:6 now
where the time goes in v1:
time: 83.1 us; the launch traced here: 82.7 us
  starting transfers between devices  23.3 us (28%)
  waiting for transfers between devices  21.2 us (26%)
  matrix products  14.8 us (18%)
  local copies, waits for them, and re-layouts  14.3 us (17%)
  other arithmetic  8.64 us (10%)
    ppermute x7, starting transfers between devices, gather_screens(): lax.ppermute(stored_planes, axis, [(i, (i + shift) % count) for i in rang...  11.5 us
    ppermute x7, waiting for transfers between devices, gather_screens(): lax.ppermute(stored_planes, axis, [(i, (i + shift) % count) for i in rang...  10.3 us
    dot_general x8, matrix products, apply(): jnp.einsum('...nj,jc->...nc', win, kern, precision=lax.Precision.HIGHEST)  9.36 us
    ppermute x2, starting transfers between devices, extended(): lax.ppermute(head, axis, [((i + 1) % count, i) for i in range(ends)])  7.75 us
    ppermute x2, waiting for transfers between devices, extended(): lax.ppermute(head, axis, [((i + 1) % count, i) for i in range(ends)])  5.97 us
    dot_general x8, matrix products, apply(): jnp.einsum('ij,ajy->aiy', band, field, precision=lax.Precision.HIGHEST)  5.44 us
    ppermute x2, waiting for transfers between devices, extended(): lax.ppermute(tail, axis, [(i, (i + 1) % count) for i in range(ends)])  4.99 us
    sin x6, local copies, waits for them, and re-layouts, transmit(): sine = jnp.sin(screen)  4.53 us
  transfers between devices with their start and end apart: 11, of which 8 were waited for; matrix products, arithmetic and copies ran while one was open for 11% of the time, Pallas kernels for 0%

profile of v1, /device:TPU:6, one launch (start us, length us, event | category | flops | bytes accessed | tf_op | source)
XLA Modules:
  0.0 82.7 jit_solution(11082856075410242652)
XLA Ops:
  0.0 1.5 %collective-permute-start = (f32[2,32,512]{2,1,0:T(8,128)}, f32[2,32,512]{2,1,0:T(8,128)S(1)}, u32[]{:S(2)}, u32[]{:S(2)}) collective-permute-start(f32[2,32,512]{2,1,0:T(8,128)} %param.6), channel_id=1, source_target_pairs={{0,4},{4,8},{8,12},{12,16},{16,20},{20,24},{24,28},{28,0},{1,5},{5... | collective-permute-start | bytes 393224 | tf_op jit(solution)/shard_map/ppermute | solution.py:111
  1.5 1.6 %collective-permute-start.1 = (f32[2,32,512]{2,1,0:T(8,128)}, f32[2,32,512]{2,1,0:T(8,128)S(1)}, u32[]{:S(2)}, u32[]{:S(2)}) collective-permute-start(f32[2,32,512]{2,1,0:T(8,128)} %param.6), channel_id=1, source_target_pairs={{0,8},{4,12},{8,16},{12,20},{16,24},{20,28},{24,0},{28,4},{1,9},{5... | collective-permute-start | bytes 393224 | tf_op jit(solution)/shard_map/ppermute | solution.py:111
  3.1 2.5 %collective-permute-start.2 = (f32[2,32,512]{2,1,0:T(8,128)}, f32[2,32,512]{2,1,0:T(8,128)S(1)}, u32[]{:S(2)}, u32[]{:S(2)}) collective-permute-start(f32[2,32,512]{2,1,0:T(8,128)} %param.6), channel_id=1, source_target_pairs={{0,12},{4,16},{8,20},{12,24},{16,28},{20,0},{24,4},{28,8},{1,13},{... | collective-permute-start | bytes 393224 | tf_op jit(solution)/shard_map/ppermute | solution.py:111
  6.0 2.2 %collective-permute-start.4 = (f32[2,32,512]{2,1,0:T(8,128)}, f32[2,32,512]{2,1,0:T(8,128)S(1)}, u32[]{:S(2)}, u32[]{:S(2)}) collective-permute-start(f32[2,32,512]{2,1,0:T(8,128)} %param.6), channel_id=1, source_target_pairs={{0,20},{4,24},{8,28},{12,0},{16,4},{20,8},{24,12},{28,16},{1,21},{... | collective-permute-start | bytes 393224 | tf_op jit(solution)/shard_map/ppermute | solution.py:111
  9.1 1.3 %fusion.43 = (s32[1,1]{1,0:T(1,128)}, s32[1,1]{1,0:T(1,128)}) fusion(s32[1,2]{1,0:T(1,128)} %param.4), kind=kLoop, calls=%fused_computation.127 | loop fusion | bytes 16 | tf_op jit(solution)/shard_map/slice | solution.py:134
  13.5 1.9 %collective-permute-start.5 = (f32[2,32,512]{2,1,0:T(8,128)}, f32[2,32,512]{2,1,0:T(8,128)S(1)}, u32[]{:S(2)}, u32[]{:S(2)}) collective-permute-start(f32[2,32,512]{2,1,0:T(8,128)} %param.6), channel_id=1, source_target_pairs={{0,24},{4,28},{8,0},{12,4},{16,8},{20,12},{24,16},{28,20},{1,25},{... | collective-permute-start | bytes 393224 | tf_op jit(solution)/shard_map/ppermute | solution.py:111
  15.4 1.5 %collective-permute-start.6 = (f32[2,32,512]{2,1,0:T(8,128)}, f32[2,32,512]{2,1,0:T(8,128)S(1)}, u32[]{:S(2)}, u32[]{:S(2)}) collective-permute-start(f32[2,32,512]{2,1,0:T(8,128)} %param.6), channel_id=1, source_target_pairs={{0,28},{4,0},{8,4},{12,8},{16,12},{20,16},{24,20},{28,24},{1,29},{... | collective-permute-start | bytes 393224 | tf_op jit(solution)/shard_map/ppermute | solution.py:111
  16.9 4.6 %collective-permute-done.3 = f32[2,32,512]{2,1,0:T(8,128)S(1)} collective-permute-done((f32[2,32,512]{2,1,0:T(8,128)}, f32[2,32,512]{2,1,0:T(8,128)S(1)}, u32[]{:S(2)}, u32[]{:S(2)}) %collective-permute-start.3) | collective-permute-done | bytes 131104 | tf_op jit(solution)/shard_map/ppermute | solution.py:111
  21.5 1.2 %collective-permute-done.4 = f32[2,32,512]{2,1,0:T(8,128)S(1)} collective-permute-done((f32[2,32,512]{2,1,0:T(8,128)}, f32[2,32,512]{2,1,0:T(8,128)S(1)}, u32[]{:S(2)}, u32[]{:S(2)}) %collective-permute-start.4) | collective-permute-done | bytes 131104 | tf_op jit(solution)/shard_map/ppermute | solution.py:111
  23.2 4.0 %collective-permute-done.6 = f32[2,32,512]{2,1,0:T(8,128)S(1)} collective-permute-done((f32[2,32,512]{2,1,0:T(8,128)}, f32[2,32,512]{2,1,0:T(8,128)S(1)}, u32[]{:S(2)}, u32[]{:S(2)}) %collective-permute-start.6) | collective-permute-done | bytes 131104 | tf_op jit(solution)/shard_map/ppermute | solution.py:111
  27.9 1.9 %sine_bitcast_fusion.1 = (f32[32,8,512]{2,0,1:T(8,128)S(1)}, f32[32,8,512]{2,0,1:T(8,128)S(1)}) fusion(f32[8,32,512]{2,1,0:T(8,128)S(1)} %gather_fusion), kind=kLoop, calls=%fused_computation.63 | loop fusion | bytes 1572864 | tf_op jit(solution)/shard_map/sin | solution.py:91
  30.6 2.2 %multiply_subtract_fusion.1 = (f32[1,1,32,4096]{3,2,1,0:T(8,128)S(1)}, f32[1,1,32,4096]{3,2,1,0:T(8,128)S(1)}) fusion(f32[1,1,32,4096]{3,2,1,0:T(8,128)S(1)} %sin.64, f32[1,1,32,4096]{3,2,1,0:T(8,128)S(1)} %cos.64, f32[4096]{0:T(1024)S(1)} %fusion.24, f32[32]{0:T(128)S(1)} %fusion.29, pred[32]{0:T(512)(128)(4,1)S(1)} %compare_and_fusion), kind=kLoop, calls=%fused_computation.62 | loop fusion | flops 1310720 | bytes 2113696 | tf_op jit(solution)/shard_map/sub | solution.py:92
  33.7 1.9 %collective-permute-start.7 = (f32[2,1,16,4096]{3,2,1,0:T(8,128)}, f32[2,1,16,4096]{3,2,1,0:T(8,128)}, u32[]{:S(2)}, u32[]{:S(2)}) collective-permute-start(f32[2,1,16,4096]{3,2,1,0:T(8,128)} %get-tuple-element.17), channel_id=1, source_target_pairs={{0,1},{1,2},{2,3},{4,5},{5,6},{6,7},{8,9},{9,10},{10,11},{12,13},{... | collective-permute-start | bytes 1572872 | tf_op jit(solution)/shard_map/ppermute | solution.py:22
  35.6 3.8 %collective-permute-start.8 = (f32[2,1,16,4096]{3,2,1,0:T(8,128)S(1)}, f32[2,1,16,4096]{3,2,1,0:T(8,128)}, u32[]{:S(2)}, u32[]{:S(2)}) collective-permute-start(f32[2,1,16,4096]{3,2,1,0:T(8,128)S(1)} %get-tuple-element.18), channel_id=1, source_target_pairs={{1,0},{2,1},{3,2},{5,4},{6,5},{7,6},{9,8},{10,9},{11,10},{13,12},{... | collective-permute-start | bytes 1572872 | tf_op jit(solution)/shard_map/ppermute | solution.py:24
  40.6 1.9 %sine_bitcast_fusion = (f32[32,8,512]{2,0,1:T(8,128)S(1)}, f32[32,8,512]{2,0,1:T(8,128)S(1)}) fusion(f32[8,32,512]{2,1,0:T(8,128)S(1)} %gather_fusion.1), kind=kLoop, calls=%fused_computation.55 | loop fusion | bytes 1572864 | tf_op jit(solution)/shard_map/sin | solution.py:91
  43.3 1.2 %collective-permute-done.7 = f32[2,1,16,4096]{3,2,1,0:T(8,128)} collective-permute-done((f32[2,1,16,4096]{3,2,1,0:T(8,128)}, f32[2,1,16,4096]{3,2,1,0:T(8,128)}, u32[]{:S(2)}, u32[]{:S(2)}) %collective-permute-start.7) | collective-permute-done | bytes 524320 | tf_op jit(solution)/shard_map/ppermute | solution.py:22
  44.5 1.4 %collective-permute-done.8 = f32[2,1,16,4096]{3,2,1,0:T(8,128)} collective-permute-done((f32[2,1,16,4096]{3,2,1,0:T(8,128)S(1)}, f32[2,1,16,4096]{3,2,1,0:T(8,128)}, u32[]{:S(2)}, u32[]{:S(2)}) %collective-permute-start.8) | collective-permute-done | bytes 524320 | tf_op jit(solution)/shard_map/ppermute | solution.py:24
  45.9 1.3 %pad_maximum_fusion = f32[2,1,64,4096]{3,2,1,0:T(8,128)S(1)} fusion(f32[2,1,16,4096]{3,2,1,0:T(8,128)} %collective-permute-done.8, f32[1,1,32,4096]{3,2,1,0:T(8,128)S(1)} %get-tuple-element.12, f32[1,1,32,4096]{3,2,1,0:T(8,128)S(1)} %get-tuple-element.11, f32[2,1,16,4096]{3,2,1,0:T(8,128)} %collective-permute-done.7), kind=kLoop, calls=%fused_computation.13 | loop fusion | flops 1572864 | bytes 4194304 | tf_op jit(solution)/shard_map/concatenate | solution.py:20
  52.1 1.0 %fusion.10 = f32[32,32,128]{2,1,0:T(8,128)S(1)} fusion(f32[1,32,32,32]{3,2,1,0:T(8,128)S(1)} %bitcast.161, f32[1,32,32,128]{3,2,1,0:T(8,128)S(1)} %bitcast.163, f32[160,128]{1,0:T(8,128)S(1)} %get-tuple-element.6), kind=kOutput, calls=%fused_computation.38 | convolution fusion | flops 251822080 | bytes 1261568 | tf_op jit(solution)/shard_map/...nj,jc->...nc/dot_general | solution.py:66
  53.1 1.8 %convolution_subtract_fusion.3 = f32[32,32,128]{2,1,0:T(8,128)} fusion(f32[32,32,128]{2,1,0:T(8,128)S(1)} %fusion.11, f32[1,32,32,32]{3,2,1,0:T(8,128)S(1)} %bitcast.168, f32[1,32,32,128]{3,2,1,0:T(8,128)S(1)} %bitcast.170, f32[160,128]{1,0:T(8,128)S(1)} %get-tuple-element.6), kind=kOutput, calls=%fused_computation.18 | convolution fusion | flops 251953152 | bytes 1785856 | tf_op jit(solution)/shard_map/...nj,jc->...nc/dot_general | solution.py:66
  54.8 1.1 %sub.209 = f32[1,1,32,4096]{3,2,1,0:T(8,128)S(1)} reshape(f32[32,32,128]{2,1,0:T(8,128)} %convolution_subtract_fusion.3) | data formatting | bytes 1048576 | tf_op jit(solution)/shard_map/sub | solution.py:70
  56.0 1.8 %convolution_add_fusion.3 = f32[32,32,128]{2,1,0:T(8,128)} fusion(f32[32,32,128]{2,1,0:T(8,128)S(1)} %fusion.10, f32[1,32,32,32]{3,2,1,0:T(8,128)S(1)} %bitcast.169, f32[1,32,32,128]{3,2,1,0:T(8,128)S(1)} %bitcast.171, f32[160,128]{1,0:T(8,128)S(1)} %get-tuple-element.5), kind=kOutput, calls=%fused_computation.17 | convolution fusion | flops 251953152 | bytes 1785856 | tf_op jit(solution)/shard_map/...nj,jc->...nc/dot_general | solution.py:66
  57.8 1.1 %add.210 = f32[1,1,32,4096]{3,2,1,0:T(8,128)S(1)} reshape(f32[32,32,128]{2,1,0:T(8,128)} %convolution_add_fusion.3) | data formatting | bytes 1048576 | tf_op jit(solution)/shard_map/add | solution.py:71
  59.1 3.9 %collective-permute-start.10 = (f32[2,1,16,4096]{3,2,1,0:T(8,128)S(1)}, f32[2,1,16,4096]{3,2,1,0:T(8,128)S(1)}, u32[]{:S(2)}, u32[]{:S(2)}) collective-permute-start(f32[2,1,16,4096]{3,2,1,0:T(8,128)S(1)} %get-tuple-element.14), channel_id=1, source_target_pairs={{1,0},{2,1},{3,2},{5,4},{6,5},{7,6},{9,8},{10,9},{11,10},{13,12},{... | collective-permute-start | bytes 1572872 | tf_op jit(solution)/shard_map/ppermute | solution.py:24
  63.0 2.1 %collective-permute-start.9 = (f32[2,1,16,4096]{3,2,1,0:T(8,128)S(1)}, f32[2,1,16,4096]{3,2,1,0:T(8,128)S(1)}, u32[]{:S(2)}, u32[]{:S(2)}) collective-permute-start(f32[2,1,16,4096]{3,2,1,0:T(8,128)S(1)} %get-tuple-element.13), channel_id=1, source_target_pairs={{0,1},{1,2},{2,3},{4,5},{5,6},{6,7},{8,9},{9,10},{10,11},{12,13},{... | collective-permute-start | bytes 1572872 | tf_op jit(solution)/shard_map/ppermute | solution.py:22
  65.2 4.5 %collective-permute-done.10 = f32[2,1,16,4096]{3,2,1,0:T(8,128)S(1)} collective-permute-done((f32[2,1,16,4096]{3,2,1,0:T(8,128)S(1)}, f32[2,1,16,4096]{3,2,1,0:T(8,128)S(1)}, u32[]{:S(2)}, u32[]{:S(2)}) %collective-permute-start.10) | collective-permute-done | bytes 524320 | tf_op jit(solution)/shard_map/ppermute | solution.py:24
  69.7 3.8 %collective-permute-done.9 = f32[2,1,16,4096]{3,2,1,0:T(8,128)S(1)} collective-permute-done((f32[2,1,16,4096]{3,2,1,0:T(8,128)S(1)}, f32[2,1,16,4096]{3,2,1,0:T(8,128)S(1)}, u32[]{:S(2)}, u32[]{:S(2)}) %collective-permute-start.9) | collective-permute-done | bytes 524320 | tf_op jit(solution)/shard_map/ppermute | solution.py:22
  76.3 1.0 %fusion.9 = f32[32,32,128]{2,1,0:T(8,128)S(1)} fusion(f32[1,32,32,32]{3,2,1,0:T(8,128)S(1)} %bitcast.164, f32[1,32,32,128]{3,2,1,0:T(8,128)S(1)} %bitcast.166, f32[160,128]{1,0:T(8,128)S(1)} %get-tuple-element.5), kind=kOutput, calls=%fused_computation.37 | convolution fusion | flops 251822080 | bytes 1261568 | tf_op jit(solution)/shard_map/...nj,jc->...nc/dot_general | solution.py:66
  77.3 1.0 %fusion.8 = f32[32,32,128]{2,1,0:T(8,128)S(1)} fusion(f32[1,32,32,32]{3,2,1,0:T(8,128)S(1)} %bitcast.165, f32[1,32,32,128]{3,2,1,0:T(8,128)S(1)} %bitcast.167, f32[160,128]{1,0:T(8,128)S(1)} %get-tuple-element.6), kind=kOutput, calls=%fused_computation.36 | convolution fusion | flops 251822080 | bytes 1261568 | tf_op jit(solution)/shard_map/...nj,jc->...nc/dot_general | solution.py:66
  79.5 1.0 %convolution_subtract_fusion.2 = f32[32,32,128]{2,1,0:T(8,128)S(1)} fusion(f32[32,32,128]{2,1,0:T(8,128)S(1)} %fusion.9, f32[1,32,32,32]{3,2,1,0:T(8,128)S(1)} %bitcast.172, f32[1,32,32,128]{3,2,1,0:T(8,128)S(1)} %bitcast.174, f32[160,128]{1,0:T(8,128)S(1)} %get-tuple-element.6), kind=kOutput, calls=%fused_computation.16 | convolution fusion | flops 251953152 | bytes 1785856 | tf_op jit(solution)/shard_map/...nj,jc->...nc/dot_general | solution.py:66
  80.6 1.0 %convolution_add_fusion.2 = f32[32,32,128]{2,1,0:T(8,128)S(1)} fusion(f32[32,32,128]{2,1,0:T(8,128)S(1)} %fusion.8, f32[1,32,32,32]{3,2,1,0:T(8,128)S(1)} %bitcast.173, f32[1,32,32,128]{3,2,1,0:T(8,128)S(1)} %bitcast.175, f32[160,128]{1,0:T(8,128)S(1)} %get-tuple-element.5), kind=kOutput, calls=%fused_computation.15 | convolution fusion | flops 251953152 | bytes 1785856 | tf_op jit(solution)/shard_map/...nj,jc->...nc/dot_general | solution.py:66
  81.7 1.0 %pad_maximum_fusion.2 = f32[2,1,32,4096]{3,2,1,0:T(8,128)} fusion(f32[1,1,32,4096]{3,2,1,0:T(8,128)S(1)} %add.216, f32[1,1,32,4096]{3,2,1,0:T(8,128)S(1)} %sub.217), kind=kLoop, calls=%fused_computation.31 | loop fusion | flops 262144 | bytes 2097152 | tf_op jit(solution)/shard_map/stack | solution.py:145
  (61 shorter events, 18.3 us)
Async XLA Ops:
  0.0 13.5 %collective-permute-start = (f32[2,32,512]{2,1,0:T(8,128)}, f32[2,32,512]{2,1,0:T(8,128)S(1)}, u32[]{:S(2)}, u32[]{:S(2)}) collective-permute-start(f32[2,32,512]{2,1,0:T(8,128)} %param.6), channel_id=1, source_target_pairs={{0,4},{4,8},{8,12},{12,16},{16,20},{20,24},{24,28},{28,0},{1,5},{5... | collective-permute-start | bytes 393224 | tf_op jit(solution)/shard_map/ppermute | solution.py:111
  1.5 13.9 %collective-permute-start.1 = (f32[2,32,512]{2,1,0:T(8,128)}, f32[2,32,512]{2,1,0:T(8,128)S(1)}, u32[]{:S(2)}, u32[]{:S(2)}) collective-permute-start(f32[2,32,512]{2,1,0:T(8,128)} %param.6), channel_id=1, source_target_pairs={{0,8},{4,12},{8,16},{12,20},{16,24},{20,28},{24,0},{28,4},{1,9},{5... | collective-permute-start | bytes 393224 | tf_op jit(solution)/shard_map/ppermute | solution.py:111
  3.1 13.8 %collective-permute-start.2 = (f32[2,32,512]{2,1,0:T(8,128)}, f32[2,32,512]{2,1,0:T(8,128)S(1)}, u32[]{:S(2)}, u32[]{:S(2)}) collective-permute-start(f32[2,32,512]{2,1,0:T(8,128)} %param.6), channel_id=1, source_target_pairs={{0,12},{4,16},{8,20},{12,24},{16,28},{20,0},{24,4},{28,8},{1,13},{... | collective-permute-start | bytes 393224 | tf_op jit(solution)/shard_map/ppermute | solution.py:111
  5.6 15.9 %collective-permute-start.3 = (f32[2,32,512]{2,1,0:T(8,128)}, f32[2,32,512]{2,1,0:T(8,128)S(1)}, u32[]{:S(2)}, u32[]{:S(2)}) collective-permute-start(f32[2,32,512]{2,1,0:T(8,128)} %param.6), channel_id=1, source_target_pairs={{0,16},{4,20},{8,24},{12,28},{16,0},{20,4},{24,8},{28,12},{1,17},{... | collective-permute-start | bytes 393224 | tf_op jit(solution)/shard_map/ppermute | solution.py:111
  6.0 16.7 %collective-permute-start.4 = (f32[2,32,512]{2,1,0:T(8,128)}, f32[2,32,512]{2,1,0:T(8,128)S(1)}, u32[]{:S(2)}, u32[]{:S(2)}) collective-permute-start(f32[2,32,512]{2,1,0:T(8,128)} %param.6), channel_id=1, source_target_pairs={{0,20},{4,24},{8,28},{12,0},{16,4},{20,8},{24,12},{28,16},{1,21},{... | collective-permute-start | bytes 393224 | tf_op jit(solution)/shard_map/ppermute | solution.py:111
  13.5 9.7 %collective-permute-start.5 = (f32[2,32,512]{2,1,0:T(8,128)}, f32[2,32,512]{2,1,0:T(8,128)S(1)}, u32[]{:S(2)}, u32[]{:S(2)}) collective-permute-start(f32[2,32,512]{2,1,0:T(8,128)} %param.6), channel_id=1, source_target_pairs={{0,24},{4,28},{8,0},{12,4},{16,8},{20,12},{24,16},{28,20},{1,25},{... | collective-permute-start | bytes 393224 | tf_op jit(solution)/shard_map/ppermute | solution.py:111
  15.4 11.8 %collective-permute-start.6 = (f32[2,32,512]{2,1,0:T(8,128)}, f32[2,32,512]{2,1,0:T(8,128)S(1)}, u32[]{:S(2)}, u32[]{:S(2)}) collective-permute-start(f32[2,32,512]{2,1,0:T(8,128)} %param.6), channel_id=1, source_target_pairs={{0,28},{4,0},{8,4},{12,8},{16,12},{20,16},{24,20},{28,24},{1,29},{... | collective-permute-start | bytes 393224 | tf_op jit(solution)/shard_map/ppermute | solution.py:111
  33.7 10.8 %collective-permute-start.7 = (f32[2,1,16,4096]{3,2,1,0:T(8,128)}, f32[2,1,16,4096]{3,2,1,0:T(8,128)}, u32[]{:S(2)}, u32[]{:S(2)}) collective-permute-start(f32[2,1,16,4096]{3,2,1,0:T(8,128)} %get-tuple-element.17), channel_id=1, source_target_pairs={{0,1},{1,2},{2,3},{4,5},{5,6},{6,7},{8,9},{9,10},{10,11},{12,13},{... | collective-permute-start | bytes 1572872 | tf_op jit(solution)/shard_map/ppermute | solution.py:22
  35.6 10.3 %collective-permute-start.8 = (f32[2,1,16,4096]{3,2,1,0:T(8,128)S(1)}, f32[2,1,16,4096]{3,2,1,0:T(8,128)}, u32[]{:S(2)}, u32[]{:S(2)}) collective-permute-start(f32[2,1,16,4096]{3,2,1,0:T(8,128)S(1)} %get-tuple-element.18), channel_id=1, source_target_pairs={{1,0},{2,1},{3,2},{5,4},{6,5},{7,6},{9,8},{10,9},{11,10},{13,12},{... | collective-permute-start | bytes 1572872 | tf_op jit(solution)/shard_map/ppermute | solution.py:24
  59.1 10.6 %collective-permute-start.10 = (f32[2,1,16,4096]{3,2,1,0:T(8,128)S(1)}, f32[2,1,16,4096]{3,2,1,0:T(8,128)S(1)}, u32[]{:S(2)}, u32[]{:S(2)}) collective-permute-start(f32[2,1,16,4096]{3,2,1,0:T(8,128)S(1)} %get-tuple-element.14), channel_id=1, source_target_pairs={{1,0},{2,1},{3,2},{5,4},{6,5},{7,6},{9,8},{10,9},{11,10},{13,12},{... | collective-permute-start | bytes 1572872 | tf_op jit(solution)/shard_map/ppermute | solution.py:24
  63.0 10.5 %collective-permute-start.9 = (f32[2,1,16,4096]{3,2,1,0:T(8,128)S(1)}, f32[2,1,16,4096]{3,2,1,0:T(8,128)S(1)}, u32[]{:S(2)}, u32[]{:S(2)}) collective-permute-start(f32[2,1,16,4096]{3,2,1,0:T(8,128)S(1)} %get-tuple-element.13), channel_id=1, source_target_pairs={{0,1},{1,2},{2,3},{4,5},{5,6},{6,7},{8,9},{9,10},{10,11},{12,13},{... | collective-permute-start | bytes 1572872 | tf_op jit(solution)/shard_map/ppermute | solution.py:22

commit v2 on v1

--- a/solution.py
+++ b/solution.py
@@ -55,35 +55,26 @@
     return jnp.concatenate([main, after], axis=-1)
 
 
+def complex_stack(real_part, imag_part):
+    top = jnp.concatenate([real_part, -imag_part], axis=1)
+    bottom = jnp.concatenate([imag_part, real_part], axis=1)
+    return jnp.concatenate([top, bottom], axis=0)
+
+
 def along_pass(real, imag, taps):
     block = min(128, real.shape[-1])
-    win_real = windows(real, block)
-    win_imag = windows(imag, block)
-    kern_real = toeplitz(taps[0], block)
-    kern_imag = toeplitz(taps[1], block)
-
-    def apply(win, kern):
-        out = jnp.einsum("...nj,jc->...nc", win, kern, precision=lax.Precision.HIGHEST)
-        return out.reshape(real.shape)
-
-    return (
-        apply(win_real, kern_real) - apply(win_imag, kern_imag),
-        apply(win_real, kern_imag) + apply(win_imag, kern_real),
-    )
+    win = jnp.concatenate([windows(real, block), windows(imag, block)], axis=-1)
+    kern = complex_stack(toeplitz(taps[0], block), -toeplitz(taps[1], block))
+    out = jnp.einsum("...nj,jc->...nc", win, kern, precision=lax.Precision.HIGH)
+    return out[..., :block].reshape(real.shape), out[..., block:].reshape(real.shape)
 
 
 def cross_pass(real, imag, taps):
     count = real.shape[1] - 2 * HALF
-    band_real = band_matrix(taps[0], count)
-    band_imag = band_matrix(taps[1], count)
-
-    def apply(band, field):
-        return jnp.einsum("ij,ajy->aiy", band, field, precision=lax.Precision.HIGHEST)
-
-    return (
-        apply(band_real, real) - apply(band_imag, imag),
-        apply(band_real, imag) + apply(band_imag, real),
-    )
+    band = complex_stack(band_matrix(taps[0], count), band_matrix(taps[1], count))
+    field = jnp.concatenate([real, imag], axis=1)
+    out = jnp.einsum("ij,ajy->aiy", band, field, precision=lax.Precision.HIGH)
+    return out[:, :count], out[:, count:]
 
 
 def transmit(real, imag, screen):

time: 83.1 us -> 70.5 us (0.85)
  matrix products: 14.8 us -> 3.65 us
  local copies, waits for them, and re-layouts: 14.3 us -> 13 us
    dot_general x16 -> x4, matrix products: 14.8 us -> 3.65 us  [the longest x2 2.27 us: along_pass(): out = jnp.einsum('...nj,jc->...nc', win, kern, precision=lax.Precision.HIGH)]
    add x2 -> x0, local copies, waits for them, and re-layouts: 1.24 us -> none  [along_pass(): apply(win_real, kern_imag) + apply(win_imag, kern_real)]
    sub x2 -> x0, local copies, waits for them, and re-layouts: 1.24 us -> none  [along_pass(): apply(win_real, kern_real) - apply(win_imag, kern_imag)]
  transfers between devices with their start and end apart: 11 -> 11, of which waited for: 8 -> 8; matrix products, arithmetic and copies ran while one was open for 11% -> 13% of each run, Pallas kernels for 0% -> 0%
where the time goes in v2:
time: 70.5 us; the launch traced here: 70.2 us
  starting transfers between devices  23 us (33%)
  waiting for transfers between devices  21.4 us (30%)
  local copies, waits for them, and re-layouts  13 us (18%)
  other arithmetic  8.65 us (12%)
  matrix products  3.65 us (5%)
    ppermute x7, starting transfers between devices, gather_screens(): lax.ppermute(stored_planes, axis, [(i, (i + shift) % count) for i in rang...  11.5 us
    ppermute x7, waiting for transfers between devices, gather_screens(): lax.ppermute(stored_planes, axis, [(i, (i + shift) % count) for i in rang...  10.3 us
    ppermute x2, starting transfers between devices, extended(): lax.ppermute(head, axis, [((i + 1) % count, i) for i in range(ends)])  7.56 us
    ppermute x2, waiting for transfers between devices, extended(): lax.ppermute(head, axis, [((i + 1) % count, i) for i in range(ends)])  6.01 us
    ppermute x2, waiting for transfers between devices, extended(): lax.ppermute(tail, axis, [(i, (i + 1) % count) for i in range(ends)])  5.15 us
    sin x6, local copies, waits for them, and re-layouts, transmit(): sine = jnp.sin(screen)  4.53 us
    ppermute x2, starting transfers between devices, extended(): lax.ppermute(tail, axis, [(i, (i + 1) % count) for i in range(ends)])  4.01 us
    unnamed x19, local copies, waits for them, and re-layouts  3.11 us
  transfers between devices with their start and end apart: 11, of which 8 were waited for; matrix products, arithmetic and copies ran while one was open for 13% of the time, Pallas kernels for 0%

profile of v2, /device:TPU:6, one launch (start us, length us, event | category | flops | bytes accessed | tf_op | source)
XLA Modules:
  0.0 70.2 jit_solution(15801954306755902259)
XLA Ops:
  0.0 1.5 %collective-permute-start = (f32[2,32,512]{2,1,0:T(8,128)}, f32[2,32,512]{2,1,0:T(8,128)S(1)}, u32[]{:S(2)}, u32[]{:S(2)}) collective-permute-start(f32[2,32,512]{2,1,0:T(8,128)} %param.6), channel_id=1, source_target_pairs={{0,4},{4,8},{8,12},{12,16},{16,20},{20,24},{24,28},{28,0},{1,5},{5... | collective-permute-start | bytes 393224 | tf_op jit(solution)/shard_map/ppermute | solution.py:102
  1.5 1.6 %collective-permute-start.1 = (f32[2,32,512]{2,1,0:T(8,128)}, f32[2,32,512]{2,1,0:T(8,128)S(1)}, u32[]{:S(2)}, u32[]{:S(2)}) collective-permute-start(f32[2,32,512]{2,1,0:T(8,128)} %param.6), channel_id=1, source_target_pairs={{0,8},{4,12},{8,16},{12,20},{16,24},{20,28},{24,0},{28,4},{1,9},{5... | collective-permute-start | bytes 393224 | tf_op jit(solution)/shard_map/ppermute | solution.py:102
  3.1 2.5 %collective-permute-start.2 = (f32[2,32,512]{2,1,0:T(8,128)}, f32[2,32,512]{2,1,0:T(8,128)S(1)}, u32[]{:S(2)}, u32[]{:S(2)}) collective-permute-start(f32[2,32,512]{2,1,0:T(8,128)} %param.6), channel_id=1, source_target_pairs={{0,12},{4,16},{8,20},{12,24},{16,28},{20,0},{24,4},{28,8},{1,13},{... | collective-permute-start | bytes 393224 | tf_op jit(solution)/shard_map/ppermute | solution.py:102
  6.0 2.2 %collective-permute-start.4 = (f32[2,32,512]{2,1,0:T(8,128)}, f32[2,32,512]{2,1,0:T(8,128)S(1)}, u32[]{:S(2)}, u32[]{:S(2)}) collective-permute-start(f32[2,32,512]{2,1,0:T(8,128)} %param.6), channel_id=1, source_target_pairs={{0,20},{4,24},{8,28},{12,0},{16,4},{20,8},{24,12},{28,16},{1,21},{... | collective-permute-start | bytes 393224 | tf_op jit(solution)/shard_map/ppermute | solution.py:102
  8.2 0.9 %bitcast_dynamic-update-slice_fusion.7 = f32[2,8,32,512]{3,2,0,1:T(8,128)S(1)} fusion(f32[2,32,512]{2,1,0:T(8,128)} %param.6), kind=kLoop, calls=%fused_computation.78 | loop fusion | bytes 262144
  9.1 1.3 %fusion.43 = (s32[1,1]{1,0:T(1,128)}, s32[1,1]{1,0:T(1,128)}) fusion(s32[1,2]{1,0:T(1,128)} %param.4), kind=kLoop, calls=%fused_computation.123 | loop fusion | bytes 16 | tf_op jit(solution)/shard_map/slice | solution.py:125
  10.5 0.7 fusion.29
  11.8 0.8 %slice_bitcast_fusion.15 = (f32[33]{0:T(128)S(1)}, f32[33]{0:T(128)S(1)}) fusion(f32[2,33]{1,0:T(2,128)} %param.5), kind=kLoop, calls=%fused_computation.113 | loop fusion | bytes 528 | tf_op jit(solution)/shard_map/squeeze | solution.py:74
  12.5 0.8 %fusion.34 = (s32[8]{0:T(128)S(1)}, s32[8]{0:T(128)S(1)}) fusion(s32[2,8]{1,0:T(2,128)} %param.7, s32[]{:T(128)S(6)} %axis_index.25), kind=kLoop, calls=%fused_computation.111 | loop fusion | flops 240 | bytes 132 | tf_op jit(solution)/shard_map/select_n | solution.py:108
  13.5 1.9 %collective-permute-start.5 = (f32[2,32,512]{2,1,0:T(8,128)}, f32[2,32,512]{2,1,0:T(8,128)S(1)}, u32[]{:S(2)}, u32[]{:S(2)}) collective-permute-start(f32[2,32,512]{2,1,0:T(8,128)} %param.6), channel_id=1, source_target_pairs={{0,24},{4,28},{8,0},{12,4},{16,8},{20,12},{24,16},{28,20},{1,25},{... | collective-permute-start | bytes 393224 | tf_op jit(solution)/shard_map/ppermute | solution.py:102
  15.4 1.5 %collective-permute-start.6 = (f32[2,32,512]{2,1,0:T(8,128)}, f32[2,32,512]{2,1,0:T(8,128)S(1)}, u32[]{:S(2)}, u32[]{:S(2)}) collective-permute-start(f32[2,32,512]{2,1,0:T(8,128)} %param.6), channel_id=1, source_target_pairs={{0,28},{4,0},{8,4},{12,8},{16,12},{20,16},{24,20},{28,24},{1,29},{... | collective-permute-start | bytes 393224 | tf_op jit(solution)/shard_map/ppermute | solution.py:102
  16.9 4.6 %collective-permute-done.3 = f32[2,32,512]{2,1,0:T(8,128)S(1)} collective-permute-done((f32[2,32,512]{2,1,0:T(8,128)}, f32[2,32,512]{2,1,0:T(8,128)S(1)}, u32[]{:S(2)}, u32[]{:S(2)}) %collective-permute-start.3) | collective-permute-done | bytes 131104 | tf_op jit(solution)/shard_map/ppermute | solution.py:102
  21.5 1.2 %collective-permute-done.4 = f32[2,32,512]{2,1,0:T(8,128)S(1)} collective-permute-done((f32[2,32,512]{2,1,0:T(8,128)}, f32[2,32,512]{2,1,0:T(8,128)S(1)}, u32[]{:S(2)}, u32[]{:S(2)}) %collective-permute-start.4) | collective-permute-done | bytes 131104 | tf_op jit(solution)/shard_map/ppermute | solution.py:102
  23.2 4.0 %collective-permute-done.6 = f32[2,32,512]{2,1,0:T(8,128)S(1)} collective-permute-done((f32[2,32,512]{2,1,0:T(8,128)}, f32[2,32,512]{2,1,0:T(8,128)S(1)}, u32[]{:S(2)}, u32[]{:S(2)}) %collective-permute-start.6) | collective-permute-done | bytes 131104 | tf_op jit(solution)/shard_map/ppermute | solution.py:102
  27.9 1.9 %sine_bitcast_fusion.1 = (f32[32,8,512]{2,0,1:T(8,128)S(1)}, f32[32,8,512]{2,0,1:T(8,128)S(1)}) fusion(f32[8,32,512]{2,1,0:T(8,128)S(1)} %gather_fusion), kind=kLoop, calls=%fused_computation.65 | loop fusion | bytes 1572864 | tf_op jit(solution)/shard_map/sin | solution.py:82
  30.6 2.2 %multiply_subtract_fusion.1 = (f32[1,1,32,4096]{3,2,1,0:T(8,128)S(1)}, f32[1,1,32,4096]{3,2,1,0:T(8,128)S(1)}) fusion(f32[1,1,32,4096]{3,2,1,0:T(8,128)S(1)} %sin.64, f32[1,1,32,4096]{3,2,1,0:T(8,128)S(1)} %cos.64, f32[4096]{0:T(1024)S(1)} %fusion.24, f32[32]{0:T(128)S(1)} %fusion.29, pred[32]{0:T(512)(128)(4,1)S(1)} %compare_and_fusion), kind=kLoop, calls=%fused_computation.64 | loop fusion | flops 1310720 | bytes 2113696 | tf_op jit(solution)/shard_map/sub | solution.py:83
  32.8 0.9 %fusion.21 = (f32[2,1,16,4096]{3,2,1,0:T(8,128)}, f32[2,1,16,4096]{3,2,1,0:T(8,128)S(1)}) fusion(f32[1,1,32,4096]{3,2,1,0:T(8,128)S(1)} %get-tuple-element.15, f32[1,1,32,4096]{3,2,1,0:T(8,128)S(1)} %get-tuple-element.16), kind=kLoop, calls=%fused_computation.46 | loop fusion | flops 262144 | bytes 2097152 | tf_op jit(solution)/shard_map/stack | solution.py:133
  33.7 1.9 %collective-permute-start.7 = (f32[2,1,16,4096]{3,2,1,0:T(8,128)}, f32[2,1,16,4096]{3,2,1,0:T(8,128)}, u32[]{:S(2)}, u32[]{:S(2)}) collective-permute-start(f32[2,1,16,4096]{3,2,1,0:T(8,128)} %get-tuple-element.29), channel_id=1, source_target_pairs={{0,1},{1,2},{2,3},{4,5},{5,6},{6,7},{8,9},{9,10},{10,11},{12,13},{... | collective-permute-start | bytes 1572872 | tf_op jit(solution)/shard_map/ppermute | solution.py:22
  35.6 3.6 %collective-permute-start.8 = (f32[2,1,16,4096]{3,2,1,0:T(8,128)S(1)}, f32[2,1,16,4096]{3,2,1,0:T(8,128)}, u32[]{:S(2)}, u32[]{:S(2)}) collective-permute-start(f32[2,1,16,4096]{3,2,1,0:T(8,128)S(1)} %get-tuple-element.30), channel_id=1, source_target_pairs={{1,0},{2,1},{3,2},{5,4},{6,5},{7,6},{9,8},{10,9},{11,10},{13,12},{... | collective-permute-start | bytes 1572872 | tf_op jit(solution)/shard_map/ppermute | solution.py:24
  40.5 1.9 %sine_bitcast_fusion = (f32[32,8,512]{2,0,1:T(8,128)S(1)}, f32[32,8,512]{2,0,1:T(8,128)S(1)}) fusion(f32[8,32,512]{2,1,0:T(8,128)S(1)} %gather_fusion.1), kind=kLoop, calls=%fused_computation.57 | loop fusion | bytes 1572864 | tf_op jit(solution)/shard_map/sin | solution.py:82
  43.2 1.3 %collective-permute-done.7 = f32[2,1,16,4096]{3,2,1,0:T(8,128)} collective-permute-done((f32[2,1,16,4096]{3,2,1,0:T(8,128)}, f32[2,1,16,4096]{3,2,1,0:T(8,128)}, u32[]{:S(2)}, u32[]{:S(2)}) %collective-permute-start.7) | collective-permute-done | bytes 524320 | tf_op jit(solution)/shard_map/ppermute | solution.py:22
  44.5 1.4 %collective-permute-done.8 = f32[2,1,16,4096]{3,2,1,0:T(8,128)} collective-permute-done((f32[2,1,16,4096]{3,2,1,0:T(8,128)S(1)}, f32[2,1,16,4096]{3,2,1,0:T(8,128)}, u32[]{:S(2)}, u32[]{:S(2)}) %collective-permute-start.8) | collective-permute-done | bytes 524320 | tf_op jit(solution)/shard_map/ppermute | solution.py:24
  45.9 1.3 %pad_maximum_fusion = f32[2,1,64,4096]{3,2,1,0:T(8,128)S(1)} fusion(f32[2,1,16,4096]{3,2,1,0:T(8,128)} %collective-permute-done.8, f32[1,1,32,4096]{3,2,1,0:T(8,128)S(1)} %get-tuple-element.16, f32[1,1,32,4096]{3,2,1,0:T(8,128)S(1)} %get-tuple-element.15, f32[2,1,16,4096]{3,2,1,0:T(8,128)} %collective-permute-done.7), kind=kLoop, calls=%fused_computation.7 | loop fusion | flops 1572864 | bytes 4194304 | tf_op jit(solution)/shard_map/concatenate | solution.py:20
  47.5 0.7 convolution_bitcast_fusion.1
  49.3 1.1 %fusion.19 = f32[1,32,32,256]{3,2,1,0:T(8,128)S(1)} fusion(f32[1,32,32,32]{3,2,1,0:T(8,128)S(1)} %bitcast.135, f32[1,32,32,128]{3,2,1,0:T(8,128)S(1)} %bitcast.141, f32[1,32,32,32]{3,2,1,0:T(8,128)S(1)} %bitcast.137, f32[1,32,32,128]{3,2,1,0:T(8,128)S(1)} %bitcast.139, f32[160,128]{1,0:T(8,128)S(1)} %get-tuple-element.6, f32[160,128]{1,0:T(8,128)S(1)} %neg.5, ...), kind=kOutput, calls=%fused_computation.32 | convolution fusion | flops 504545280 | bytes 2605056 | tf_op jit(solution)/shard_map/...nj,jc->...nc/dot_general | solution.py:68
  51.0 3.9 %collective-permute-start.10 = (f32[2,1,16,4096]{3,2,1,0:T(8,128)S(1)}, f32[2,1,16,4096]{3,2,1,0:T(8,128)S(1)}, u32[]{:S(2)}, u32[]{:S(2)}) collective-permute-start(f32[2,1,16,4096]{3,2,1,0:T(8,128)S(1)} %get-tuple-element.22), channel_id=1, source_target_pairs={{1,0},{2,1},{3,2},{5,4},{6,5},{7,6},{9,8},{10,9},{11,10},{13,12},{... | collective-permute-start | bytes 1572872 | tf_op jit(solution)/shard_map/ppermute | solution.py:24
  55.0 2.1 %collective-permute-start.9 = (f32[2,1,16,4096]{3,2,1,0:T(8,128)S(1)}, f32[2,1,16,4096]{3,2,1,0:T(8,128)S(1)}, u32[]{:S(2)}, u32[]{:S(2)}) collective-permute-start(f32[2,1,16,4096]{3,2,1,0:T(8,128)S(1)} %get-tuple-element.21), channel_id=1, source_target_pairs={{0,1},{1,2},{2,3},{4,5},{5,6},{6,7},{8,9},{9,10},{10,11},{12,13},{... | collective-permute-start | bytes 1572872 | tf_op jit(solution)/shard_map/ppermute | solution.py:22
  57.1 4.6 %collective-permute-done.10 = f32[2,1,16,4096]{3,2,1,0:T(8,128)S(1)} collective-permute-done((f32[2,1,16,4096]{3,2,1,0:T(8,128)S(1)}, f32[2,1,16,4096]{3,2,1,0:T(8,128)S(1)}, u32[]{:S(2)}, u32[]{:S(2)}) %collective-permute-start.10) | collective-permute-done | bytes 524320 | tf_op jit(solution)/shard_map/ppermute | solution.py:24
  61.6 3.8 %collective-permute-done.9 = f32[2,1,16,4096]{3,2,1,0:T(8,128)S(1)} collective-permute-done((f32[2,1,16,4096]{3,2,1,0:T(8,128)S(1)}, f32[2,1,16,4096]{3,2,1,0:T(8,128)S(1)}, u32[]{:S(2)}, u32[]{:S(2)}) %collective-permute-start.9) | collective-permute-done | bytes 524320 | tf_op jit(solution)/shard_map/ppermute | solution.py:22
  65.8 0.7 convolution_bitcast_fusion
  67.7 1.1 %fusion.18 = f32[1,32,32,256]{3,2,1,0:T(8,128)S(1)} fusion(f32[1,32,32,32]{3,2,1,0:T(8,128)S(1)} %bitcast.134, f32[1,32,32,128]{3,2,1,0:T(8,128)S(1)} %bitcast.140, f32[1,32,32,32]{3,2,1,0:T(8,128)S(1)} %bitcast.136, f32[1,32,32,128]{3,2,1,0:T(8,128)S(1)} %bitcast.138, f32[160,128]{1,0:T(8,128)S(1)} %get-tuple-element.6, f32[160,128]{1,0:T(8,128)S(1)} %neg.5, ...), kind=kOutput, calls=%fused_computation.31 | convolution fusion | flops 504545280 | bytes 2605056 | tf_op jit(solution)/shard_map/...nj,jc->...nc/dot_general | solution.py:68
  69.2 1.0 %pad_maximum_fusion.2 = f32[2,1,32,4096]{3,2,1,0:T(8,128)} fusion(f32[1,1,32,4096]{3,2,1,0:T(8,128)S(1)} %stack_reshape.7, f32[1,1,32,4096]{3,2,1,0:T(8,128)S(1)} %stack_reshape.6), kind=kLoop, calls=%fused_computation.41 | loop fusion | flops 262144 | bytes 2097152 | tf_op jit(solution)/shard_map/stack | solution.py:136
  (57 shorter events, 8.9 us)
Async XLA Ops:
  0.0 13.5 %collective-permute-start = (f32[2,32,512]{2,1,0:T(8,128)}, f32[2,32,512]{2,1,0:T(8,128)S(1)}, u32[]{:S(2)}, u32[]{:S(2)}) collective-permute-start(f32[2,32,512]{2,1,0:T(8,128)} %param.6), channel_id=1, source_target_pairs={{0,4},{4,8},{8,12},{12,16},{16,20},{20,24},{24,28},{28,0},{1,5},{5... | collective-permute-start | bytes 393224 | tf_op jit(solution)/shard_map/ppermute | solution.py:102
  1.5 13.9 %collective-permute-start.1 = (f32[2,32,512]{2,1,0:T(8,128)}, f32[2,32,512]{2,1,0:T(8,128)S(1)}, u32[]{:S(2)}, u32[]{:S(2)}) collective-permute-start(f32[2,32,512]{2,1,0:T(8,128)} %param.6), channel_id=1, source_target_pairs={{0,8},{4,12},{8,16},{12,20},{16,24},{20,28},{24,0},{28,4},{1,9},{5... | collective-permute-start | bytes 393224 | tf_op jit(solution)/shard_map/ppermute | solution.py:102
  3.1 13.8 %collective-permute-start.2 = (f32[2,32,512]{2,1,0:T(8,128)}, f32[2,32,512]{2,1,0:T(8,128)S(1)}, u32[]{:S(2)}, u32[]{:S(2)}) collective-permute-start(f32[2,32,512]{2,1,0:T(8,128)} %param.6), channel_id=1, source_target_pairs={{0,12},{4,16},{8,20},{12,24},{16,28},{20,0},{24,4},{28,8},{1,13},{... | collective-permute-start | bytes 393224 | tf_op jit(solution)/shard_map/ppermute | solution.py:102
  5.6 15.9 %collective-permute-start.3 = (f32[2,32,512]{2,1,0:T(8,128)}, f32[2,32,512]{2,1,0:T(8,128)S(1)}, u32[]{:S(2)}, u32[]{:S(2)}) collective-permute-start(f32[2,32,512]{2,1,0:T(8,128)} %param.6), channel_id=1, source_target_pairs={{0,16},{4,20},{8,24},{12,28},{16,0},{20,4},{24,8},{28,12},{1,17},{... | collective-permute-start | bytes 393224 | tf_op jit(solution)/shard_map/ppermute | solution.py:102
  6.0 16.7 %collective-permute-start.4 = (f32[2,32,512]{2,1,0:T(8,128)}, f32[2,32,512]{2,1,0:T(8,128)S(1)}, u32[]{:S(2)}, u32[]{:S(2)}) collective-permute-start(f32[2,32,512]{2,1,0:T(8,128)} %param.6), channel_id=1, source_target_pairs={{0,20},{4,24},{8,28},{12,0},{16,4},{20,8},{24,12},{28,16},{1,21},{... | collective-permute-start | bytes 393224 | tf_op jit(solution)/shard_map/ppermute | solution.py:102
  13.5 9.7 %collective-permute-start.5 = (f32[2,32,512]{2,1,0:T(8,128)}, f32[2,32,512]{2,1,0:T(8,128)S(1)}, u32[]{:S(2)}, u32[]{:S(2)}) collective-permute-start(f32[2,32,512]{2,1,0:T(8,128)} %param.6), channel_id=1, source_target_pairs={{0,24},{4,28},{8,0},{12,4},{16,8},{20,12},{24,16},{28,20},{1,25},{... | collective-permute-start | bytes 393224 | tf_op jit(solution)/shard_map/ppermute | solution.py:102
  15.4 11.8 %collective-permute-start.6 = (f32[2,32,512]{2,1,0:T(8,128)}, f32[2,32,512]{2,1,0:T(8,128)S(1)}, u32[]{:S(2)}, u32[]{:S(2)}) collective-permute-start(f32[2,32,512]{2,1,0:T(8,128)} %param.6), channel_id=1, source_target_pairs={{0,28},{4,0},{8,4},{12,8},{16,12},{20,16},{24,20},{28,24},{1,29},{... | collective-permute-start | bytes 393224 | tf_op jit(solution)/shard_map/ppermute | solution.py:102
  33.7 10.8 %collective-permute-start.7 = (f32[2,1,16,4096]{3,2,1,0:T(8,128)}, f32[2,1,16,4096]{3,2,1,0:T(8,128)}, u32[]{:S(2)}, u32[]{:S(2)}) collective-permute-start(f32[2,1,16,4096]{3,2,1,0:T(8,128)} %get-tuple-element.29), channel_id=1, source_target_pairs={{0,1},{1,2},{2,3},{4,5},{5,6},{6,7},{8,9},{9,10},{10,11},{12,13},{... | collective-permute-start | bytes 1572872 | tf_op jit(solution)/shard_map/ppermute | solution.py:22
  35.6 10.3 %collective-permute-start.8 = (f32[2,1,16,4096]{3,2,1,0:T(8,128)S(1)}, f32[2,1,16,4096]{3,2,1,0:T(8,128)}, u32[]{:S(2)}, u32[]{:S(2)}) collective-permute-start(f32[2,1,16,4096]{3,2,1,0:T(8,128)S(1)} %get-tuple-element.30), channel_id=1, source_target_pairs={{1,0},{2,1},{3,2},{5,4},{6,5},{7,6},{9,8},{10,9},{11,10},{13,12},{... | collective-permute-start | bytes 1572872 | tf_op jit(solution)/shard_map/ppermute | solution.py:24
  51.0 10.6 %collective-permute-start.10 = (f32[2,1,16,4096]{3,2,1,0:T(8,128)S(1)}, f32[2,1,16,4096]{3,2,1,0:T(8,128)S(1)}, u32[]{:S(2)}, u32[]{:S(2)}) collective-permute-start(f32[2,1,16,4096]{3,2,1,0:T(8,128)S(1)} %get-tuple-element.22), channel_id=1, source_target_pairs={{1,0},{2,1},{3,2},{5,4},{6,5},{7,6},{9,8},{10,9},{11,10},{13,12},{... | collective-permute-start | bytes 1572872 | tf_op jit(solution)/shard_map/ppermute | solution.py:24
  55.0 10.5 %collective-permute-start.9 = (f32[2,1,16,4096]{3,2,1,0:T(8,128)S(1)}, f32[2,1,16,4096]{3,2,1,0:T(8,128)S(1)}, u32[]{:S(2)}, u32[]{:S(2)}) collective-permute-start(f32[2,1,16,4096]{3,2,1,0:T(8,128)S(1)} %get-tuple-element.21), channel_id=1, source_target_pairs={{0,1},{1,2},{2,3},{4,5},{5,6},{6,7},{8,9},{9,10},{10,11},{12,13},{... | collective-permute-start | bytes 1572872 | tf_op jit(solution)/shard_map/ppermute | solution.py:22

commit v3 on v2

--- a/solution.py
+++ b/solution.py
@@ -97,15 +97,21 @@
 def gather_screens(stored_planes, owner, axis):
     count = lax.axis_size(axis)
     me = lax.axis_index(axis)
+    paired = count & (count - 1) == 0
+
+    def partner(i, k):
+        return i ^ k if paired else (i + k) % count
+
     parts = [stored_planes]
-    for shift in range(1, count):
-        parts.append(lax.ppermute(stored_planes, axis, [(i, (i + shift) % count) for i in range(count)]))
+    for k in range(1, count):
+        parts.append(lax.ppermute(stored_planes, axis, [(i, partner(i, k)) for i in range(count)]))
     stacked = jnp.stack(parts, axis=1)
     rows = stored_planes.shape[1]
     width = stored_planes.shape[2]
     planes = []
     for p in range(stored_planes.shape[0]):
-        picked = stacked[p][jnp.mod(me - owner[p], count)]
+        source = jnp.bitwise_xor(me, owner[p]) if paired else jnp.mod(me - owner[p], count)
+        picked = stacked[p][source]
         planes.append(jnp.transpose(picked, (1, 0, 2)).reshape(rows, count * width))
     return jnp.stack(planes)
 
@@ -125,9 +131,12 @@
         jnp.mod(tilts[:, 0:1] * global_rows[None, :], total_rows).astype(jnp.float32) / total_rows
     )
     along = jnp.mod(tilts[:, 1:2] * cols[None, :], total_cols).astype(jnp.float32) / total_cols
-    theta = two_pi * (across[:, :, None] + along[:, None, :])
-    real = jnp.where(inside[None, :, None], jnp.cos(theta), 0.0)
-    imag = jnp.where(inside[None, :, None], jnp.sin(theta), 0.0)
+    across_cos = jnp.where(inside[None, :], jnp.cos(two_pi * across), 0.0)[:, :, None]
+    across_sin = jnp.where(inside[None, :], jnp.sin(two_pi * across), 0.0)[:, :, None]
+    along_cos = jnp.cos(two_pi * along)[:, None, :]
+    along_sin = jnp.sin(two_pi * along)[:, None, :]
+    real = across_cos * along_cos - across_sin * along_sin
+    imag = across_sin * along_cos + across_cos * along_sin
     for plane in range(PLANES):
         real, imag = transmit(real, imag, screens[plane])
         packed = extended(jnp.stack([real, imag]), (("tile", 2),), HALF)

time: 70.5 us -> 71.1 us (level)
  the two profiles are of different devices: /device:TPU:6 before, /device:TPU:18 now
where the time goes in v3:
time: 71.1 us; the launch traced here: 70.9 us
  waiting for transfers between devices  25.9 us (36%)
  starting transfers between devices  21 us (30%)
  local copies, waits for them, and re-layouts  13 us (18%)
  other arithmetic  6.86 us (10%)
  matrix products  3.65 us (5%)
    ppermute x7, waiting for transfers between devices, gather_screens(): lax.ppermute(stored_planes, axis, [(i, partner(i, k)) for i in range(coun...  14.7 us
    ppermute x7, starting transfers between devices, gather_screens(): lax.ppermute(stored_planes, axis, [(i, partner(i, k)) for i in range(coun...  9.47 us
    ppermute x2, starting transfers between devices, extended(): lax.ppermute(head, axis, [((i + 1) % count, i) for i in range(ends)])  7.56 us
    ppermute x2, waiting for transfers between devices, extended(): lax.ppermute(head, axis, [((i + 1) % count, i) for i in range(ends)])  6.01 us
    ppermute x2, waiting for transfers between devices, extended(): lax.ppermute(tail, axis, [(i, (i + 1) % count) for i in range(ends)])  5.15 us
    sin x6, local copies, waits for them, and re-layouts, transmit(): sine = jnp.sin(screen)  4.53 us
    ppermute x2, starting transfers between devices, extended(): lax.ppermute(tail, axis, [(i, (i + 1) % count) for i in range(ends)])  4.01 us
    unnamed x19, local copies, waits for them, and re-layouts  3.11 us
  transfers between devices with their start and end apart: 11, of which 7 were waited for; matrix products, arithmetic and copies ran while one was open for 13% of the time, Pallas kernels for 0%

profile of v3, /device:TPU:18, one launch (start us, length us, event | category | flops | bytes accessed | tf_op | source)
XLA Modules:
  0.0 70.9 jit_solution(8229025101684846154)
XLA Ops:
  0.0 1.5 %collective-permute-start = (f32[2,32,512]{2,1,0:T(8,128)}, f32[2,32,512]{2,1,0:T(8,128)S(1)}, u32[]{:S(2)}, u32[]{:S(2)}) collective-permute-start(f32[2,32,512]{2,1,0:T(8,128)} %param.6), channel_id=1, source_target_pairs={{0,4},{4,0},{8,12},{12,8},{16,20},{20,16},{24,28},{28,24},{1,5},{5... | collective-permute-start | bytes 393224 | tf_op jit(solution)/shard_map/ppermute | solution.py:107
  1.5 1.6 %collective-permute-start.1 = (f32[2,32,512]{2,1,0:T(8,128)}, f32[2,32,512]{2,1,0:T(8,128)S(1)}, u32[]{:S(2)}, u32[]{:S(2)}) collective-permute-start(f32[2,32,512]{2,1,0:T(8,128)} %param.6), channel_id=1, source_target_pairs={{0,8},{4,12},{8,0},{12,4},{16,24},{20,28},{24,16},{28,20},{1,9},{5... | collective-permute-start | bytes 393224 | tf_op jit(solution)/shard_map/ppermute | solution.py:107
  3.8 3.5 %collective-permute-start.4 = (f32[2,32,512]{2,1,0:T(8,128)}, f32[2,32,512]{2,1,0:T(8,128)S(1)}, u32[]{:S(2)}, u32[]{:S(2)}) collective-permute-start(f32[2,32,512]{2,1,0:T(8,128)} %param.6), channel_id=1, source_target_pairs={{0,20},{4,16},{8,28},{12,24},{16,4},{20,0},{24,12},{28,8},{1,21},{... | collective-permute-start | bytes 393224 | tf_op jit(solution)/shard_map/ppermute | solution.py:107
  7.4 0.9 %bitcast_dynamic-update-slice_fusion.7 = f32[2,8,32,512]{3,2,0,1:T(8,128)S(1)} fusion(f32[2,32,512]{2,1,0:T(8,128)} %param.6), kind=kLoop, calls=%fused_computation.77 | loop fusion | bytes 262144
  8.3 1.3 %fusion.43 = (s32[1,1]{1,0:T(1,128)}, s32[1,1]{1,0:T(1,128)}) fusion(s32[1,2]{1,0:T(1,128)} %param.4), kind=kLoop, calls=%fused_computation.118 | loop fusion | bytes 16 | tf_op jit(solution)/shard_map/slice | solution.py:131
  9.7 0.7 fusion.28
  10.4 0.8 %slice_bitcast_fusion.15 = (f32[33]{0:T(128)S(1)}, f32[33]{0:T(128)S(1)}) fusion(f32[2,33]{1,0:T(2,128)} %param.5), kind=kLoop, calls=%fused_computation.106 | loop fusion | bytes 528 | tf_op jit(solution)/shard_map/squeeze | solution.py:74
  11.1 0.8 %fusion.34 = (s32[8]{0:T(128)S(1)}, s32[8]{0:T(128)S(1)}) fusion(s32[2,8]{1,0:T(2,128)} %param.7, s32[]{:T(128)S(6)} %axis_index.25), kind=kLoop, calls=%fused_computation.104 | loop fusion | flops 64 | bytes 132 | tf_op jit(solution)/shard_map/select_n | solution.py:114
  11.9 0.7 sine_select_fusion
  13.4 1.6 %collective-permute-start.6 = (f32[2,32,512]{2,1,0:T(8,128)}, f32[2,32,512]{2,1,0:T(8,128)S(1)}, u32[]{:S(2)}, u32[]{:S(2)}) collective-permute-start(f32[2,32,512]{2,1,0:T(8,128)} %param.6), channel_id=1, source_target_pairs={{0,28},{4,24},{8,20},{12,16},{16,12},{20,8},{24,4},{28,0},{1,29},{... | collective-permute-start | bytes 393224 | tf_op jit(solution)/shard_map/ppermute | solution.py:107
  15.0 6.4 %collective-permute-done.4 = f32[2,32,512]{2,1,0:T(8,128)S(1)} collective-permute-done((f32[2,32,512]{2,1,0:T(8,128)}, f32[2,32,512]{2,1,0:T(8,128)S(1)}, u32[]{:S(2)}, u32[]{:S(2)}) %collective-permute-start.4) | collective-permute-done | bytes 131104 | tf_op jit(solution)/shard_map/ppermute | solution.py:107
  21.5 6.0 %collective-permute-done.5 = f32[2,32,512]{2,1,0:T(8,128)S(1)} collective-permute-done((f32[2,32,512]{2,1,0:T(8,128)}, f32[2,32,512]{2,1,0:T(8,128)S(1)}, u32[]{:S(2)}, u32[]{:S(2)}) %collective-permute-start.5) | collective-permute-done | bytes 131104 | tf_op jit(solution)/shard_map/ppermute | solution.py:107
  27.4 2.3 %collective-permute-done.6 = f32[2,32,512]{2,1,0:T(8,128)S(1)} collective-permute-done((f32[2,32,512]{2,1,0:T(8,128)}, f32[2,32,512]{2,1,0:T(8,128)S(1)}, u32[]{:S(2)}, u32[]{:S(2)}) %collective-permute-start.6) | collective-permute-done | bytes 131104 | tf_op jit(solution)/shard_map/ppermute | solution.py:107
  29.8 0.6 gather_fusion
  30.4 1.9 %sine_bitcast_fusion.1 = (f32[32,8,512]{2,0,1:T(8,128)S(1)}, f32[32,8,512]{2,0,1:T(8,128)S(1)}) fusion(f32[8,32,512]{2,1,0:T(8,128)S(1)} %gather_fusion), kind=kLoop, calls=%fused_computation.65 | loop fusion | bytes 1572864 | tf_op jit(solution)/shard_map/sin | solution.py:82
  33.4 0.9 %fusion.21 = (f32[2,1,16,4096]{3,2,1,0:T(8,128)}, f32[2,1,16,4096]{3,2,1,0:T(8,128)S(1)}) fusion(f32[1,1,32,4096]{3,2,1,0:T(8,128)S(1)} %get-tuple-element.15, f32[1,1,32,4096]{3,2,1,0:T(8,128)S(1)} %get-tuple-element.16), kind=kLoop, calls=%fused_computation.46 | loop fusion | flops 262144 | bytes 2097152 | tf_op jit(solution)/shard_map/stack | solution.py:142
  34.3 1.9 %collective-permute-start.7 = (f32[2,1,16,4096]{3,2,1,0:T(8,128)}, f32[2,1,16,4096]{3,2,1,0:T(8,128)}, u32[]{:S(2)}, u32[]{:S(2)}) collective-permute-start(f32[2,1,16,4096]{3,2,1,0:T(8,128)} %get-tuple-element.29), channel_id=1, source_target_pairs={{0,1},{1,2},{2,3},{4,5},{5,6},{6,7},{8,9},{9,10},{10,11},{12,13},{... | collective-permute-start | bytes 1572872 | tf_op jit(solution)/shard_map/ppermute | solution.py:22
  36.2 3.6 %collective-permute-start.8 = (f32[2,1,16,4096]{3,2,1,0:T(8,128)S(1)}, f32[2,1,16,4096]{3,2,1,0:T(8,128)}, u32[]{:S(2)}, u32[]{:S(2)}) collective-permute-start(f32[2,1,16,4096]{3,2,1,0:T(8,128)S(1)} %get-tuple-element.30), channel_id=1, source_target_pairs={{1,0},{2,1},{3,2},{5,4},{6,5},{7,6},{9,8},{10,9},{11,10},{13,12},{... | collective-permute-start | bytes 1572872 | tf_op jit(solution)/shard_map/ppermute | solution.py:24
  40.5 0.6 gather_fusion.1
  41.1 1.9 %sine_bitcast_fusion = (f32[32,8,512]{2,0,1:T(8,128)S(1)}, f32[32,8,512]{2,0,1:T(8,128)S(1)}) fusion(f32[8,32,512]{2,1,0:T(8,128)S(1)} %gather_fusion.1), kind=kLoop, calls=%fused_computation.57 | loop fusion | bytes 1572864 | tf_op jit(solution)/shard_map/sin | solution.py:82
  43.8 1.3 %collective-permute-done.7 = f32[2,1,16,4096]{3,2,1,0:T(8,128)} collective-permute-done((f32[2,1,16,4096]{3,2,1,0:T(8,128)}, f32[2,1,16,4096]{3,2,1,0:T(8,128)}, u32[]{:S(2)}, u32[]{:S(2)}) %collective-permute-start.7) | collective-permute-done | bytes 524320 | tf_op jit(solution)/shard_map/ppermute | solution.py:22
  45.1 1.4 %collective-permute-done.8 = f32[2,1,16,4096]{3,2,1,0:T(8,128)} collective-permute-done((f32[2,1,16,4096]{3,2,1,0:T(8,128)S(1)}, f32[2,1,16,4096]{3,2,1,0:T(8,128)}, u32[]{:S(2)}, u32[]{:S(2)}) %collective-permute-start.8) | collective-permute-done | bytes 524320 | tf_op jit(solution)/shard_map/ppermute | solution.py:24
  46.5 1.3 %pad_maximum_fusion = f32[2,1,64,4096]{3,2,1,0:T(8,128)S(1)} fusion(f32[2,1,16,4096]{3,2,1,0:T(8,128)} %collective-permute-done.8, f32[1,1,32,4096]{3,2,1,0:T(8,128)S(1)} %get-tuple-element.16, f32[1,1,32,4096]{3,2,1,0:T(8,128)S(1)} %get-tuple-element.15, f32[2,1,16,4096]{3,2,1,0:T(8,128)} %collective-permute-done.7), kind=kLoop, calls=%fused_computation.7 | loop fusion | flops 1572864 | bytes 4194304 | tf_op jit(solution)/shard_map/concatenate | solution.py:20
  48.1 0.7 convolution_bitcast_fusion.1
  49.9 1.1 %fusion.19 = f32[1,32,32,256]{3,2,1,0:T(8,128)S(1)} fusion(f32[1,32,32,32]{3,2,1,0:T(8,128)S(1)} %bitcast.135, f32[1,32,32,128]{3,2,1,0:T(8,128)S(1)} %bitcast.141, f32[1,32,32,32]{3,2,1,0:T(8,128)S(1)} %bitcast.137, f32[1,32,32,128]{3,2,1,0:T(8,128)S(1)} %bitcast.139, f32[160,128]{1,0:T(8,128)S(1)} %get-tuple-element.6, f32[160,128]{1,0:T(8,128)S(1)} %neg.5, ...), kind=kOutput, calls=%fused_computation.32 | convolution fusion | flops 504545280 | bytes 2605056 | tf_op jit(solution)/shard_map/...nj,jc->...nc/dot_general | solution.py:68
  51.6 3.9 %collective-permute-start.10 = (f32[2,1,16,4096]{3,2,1,0:T(8,128)S(1)}, f32[2,1,16,4096]{3,2,1,0:T(8,128)S(1)}, u32[]{:S(2)}, u32[]{:S(2)}) collective-permute-start(f32[2,1,16,4096]{3,2,1,0:T(8,128)S(1)} %get-tuple-element.22), channel_id=1, source_target_pairs={{1,0},{2,1},{3,2},{5,4},{6,5},{7,6},{9,8},{10,9},{11,10},{13,12},{... | collective-permute-start | bytes 1572872 | tf_op jit(solution)/shard_map/ppermute | solution.py:24
  55.6 2.1 %collective-permute-start.9 = (f32[2,1,16,4096]{3,2,1,0:T(8,128)S(1)}, f32[2,1,16,4096]{3,2,1,0:T(8,128)S(1)}, u32[]{:S(2)}, u32[]{:S(2)}) collective-permute-start(f32[2,1,16,4096]{3,2,1,0:T(8,128)S(1)} %get-tuple-element.21), channel_id=1, source_target_pairs={{0,1},{1,2},{2,3},{4,5},{5,6},{6,7},{8,9},{9,10},{10,11},{12,13},{... | collective-permute-start | bytes 1572872 | tf_op jit(solution)/shard_map/ppermute | solution.py:22
  57.7 4.6 %collective-permute-done.10 = f32[2,1,16,4096]{3,2,1,0:T(8,128)S(1)} collective-permute-done((f32[2,1,16,4096]{3,2,1,0:T(8,128)S(1)}, f32[2,1,16,4096]{3,2,1,0:T(8,128)S(1)}, u32[]{:S(2)}, u32[]{:S(2)}) %collective-permute-start.10) | collective-permute-done | bytes 524320 | tf_op jit(solution)/shard_map/ppermute | solution.py:24
  62.3 3.8 %collective-permute-done.9 = f32[2,1,16,4096]{3,2,1,0:T(8,128)S(1)} collective-permute-done((f32[2,1,16,4096]{3,2,1,0:T(8,128)S(1)}, f32[2,1,16,4096]{3,2,1,0:T(8,128)S(1)}, u32[]{:S(2)}, u32[]{:S(2)}) %collective-permute-start.9) | collective-permute-done | bytes 524320 | tf_op jit(solution)/shard_map/ppermute | solution.py:22
  66.5 0.7 convolution_bitcast_fusion
  68.3 1.1 %fusion.18 = f32[1,32,32,256]{3,2,1,0:T(8,128)S(1)} fusion(f32[1,32,32,32]{3,2,1,0:T(8,128)S(1)} %bitcast.134, f32[1,32,32,128]{3,2,1,0:T(8,128)S(1)} %bitcast.140, f32[1,32,32,32]{3,2,1,0:T(8,128)S(1)} %bitcast.136, f32[1,32,32,128]{3,2,1,0:T(8,128)S(1)} %bitcast.138, f32[160,128]{1,0:T(8,128)S(1)} %get-tuple-element.6, f32[160,128]{1,0:T(8,128)S(1)} %neg.5, ...), kind=kOutput, calls=%fused_computation.31 | convolution fusion | flops 504545280 | bytes 2605056 | tf_op jit(solution)/shard_map/...nj,jc->...nc/dot_general | solution.py:68
  69.8 1.0 %pad_maximum_fusion.2 = f32[2,1,32,4096]{3,2,1,0:T(8,128)} fusion(f32[1,1,32,4096]{3,2,1,0:T(8,128)S(1)} %stack_reshape.7, f32[1,1,32,4096]{3,2,1,0:T(8,128)S(1)} %stack_reshape.6), kind=kLoop, calls=%fused_computation.41 | loop fusion | flops 262144 | bytes 2097152 | tf_op jit(solution)/shard_map/stack | solution.py:145
  (56 shorter events, 7.8 us)
Async XLA Ops:
  0.0 12.8 %collective-permute-start = (f32[2,32,512]{2,1,0:T(8,128)}, f32[2,32,512]{2,1,0:T(8,128)S(1)}, u32[]{:S(2)}, u32[]{:S(2)}) collective-permute-start(f32[2,32,512]{2,1,0:T(8,128)} %param.6), channel_id=1, source_target_pairs={{0,4},{4,0},{8,12},{12,8},{16,20},{20,16},{24,28},{28,24},{1,5},{5... | collective-permute-start | bytes 393224 | tf_op jit(solution)/shard_map/ppermute | solution.py:107
  1.5 11.8 %collective-permute-start.1 = (f32[2,32,512]{2,1,0:T(8,128)}, f32[2,32,512]{2,1,0:T(8,128)S(1)}, u32[]{:S(2)}, u32[]{:S(2)}) collective-permute-start(f32[2,32,512]{2,1,0:T(8,128)} %param.6), channel_id=1, source_target_pairs={{0,8},{4,12},{8,0},{12,4},{16,24},{20,28},{24,16},{28,20},{1,9},{5... | collective-permute-start | bytes 393224 | tf_op jit(solution)/shard_map/ppermute | solution.py:107
  3.1 11.9 %collective-permute-start.2 = (f32[2,32,512]{2,1,0:T(8,128)}, f32[2,32,512]{2,1,0:T(8,128)S(1)}, u32[]{:S(2)}, u32[]{:S(2)}) collective-permute-start(f32[2,32,512]{2,1,0:T(8,128)} %param.6), channel_id=1, source_target_pairs={{0,12},{4,8},{8,4},{12,0},{16,28},{20,24},{24,20},{28,16},{1,13},{... | collective-permute-start | bytes 393224 | tf_op jit(solution)/shard_map/ppermute | solution.py:107
  3.5 11.5 %collective-permute-start.3 = (f32[2,32,512]{2,1,0:T(8,128)}, f32[2,32,512]{2,1,0:T(8,128)S(1)}, u32[]{:S(2)}, u32[]{:S(2)}) collective-permute-start(f32[2,32,512]{2,1,0:T(8,128)} %param.6), channel_id=1, source_target_pairs={{0,16},{4,20},{8,24},{12,28},{16,0},{20,4},{24,8},{28,12},{1,17},{... | collective-permute-start | bytes 393224 | tf_op jit(solution)/shard_map/ppermute | solution.py:107
  3.8 17.6 %collective-permute-start.4 = (f32[2,32,512]{2,1,0:T(8,128)}, f32[2,32,512]{2,1,0:T(8,128)S(1)}, u32[]{:S(2)}, u32[]{:S(2)}) collective-permute-start(f32[2,32,512]{2,1,0:T(8,128)} %param.6), channel_id=1, source_target_pairs={{0,20},{4,16},{8,28},{12,24},{16,4},{20,0},{24,12},{28,8},{1,21},{... | collective-permute-start | bytes 393224 | tf_op jit(solution)/shard_map/ppermute | solution.py:107
  12.8 14.6 %collective-permute-start.5 = (f32[2,32,512]{2,1,0:T(8,128)}, f32[2,32,512]{2,1,0:T(8,128)S(1)}, u32[]{:S(2)}, u32[]{:S(2)}) collective-permute-start(f32[2,32,512]{2,1,0:T(8,128)} %param.6), channel_id=1, source_target_pairs={{0,24},{4,28},{8,16},{12,20},{16,8},{20,12},{24,0},{28,4},{1,25},{... | collective-permute-start | bytes 393224 | tf_op jit(solution)/shard_map/ppermute | solution.py:107
  13.4 16.4 %collective-permute-start.6 = (f32[2,32,512]{2,1,0:T(8,128)}, f32[2,32,512]{2,1,0:T(8,128)S(1)}, u32[]{:S(2)}, u32[]{:S(2)}) collective-permute-start(f32[2,32,512]{2,1,0:T(8,128)} %param.6), channel_id=1, source_target_pairs={{0,28},{4,24},{8,20},{12,16},{16,12},{20,8},{24,4},{28,0},{1,29},{... | collective-permute-start | bytes 393224 | tf_op jit(solution)/shard_map/ppermute | solution.py:107
  34.3 10.8 %collective-permute-start.7 = (f32[2,1,16,4096]{3,2,1,0:T(8,128)}, f32[2,1,16,4096]{3,2,1,0:T(8,128)}, u32[]{:S(2)}, u32[]{:S(2)}) collective-permute-start(f32[2,1,16,4096]{3,2,1,0:T(8,128)} %get-tuple-element.29), channel_id=1, source_target_pairs={{0,1},{1,2},{2,3},{4,5},{5,6},{6,7},{8,9},{9,10},{10,11},{12,13},{... | collective-permute-start | bytes 1572872 | tf_op jit(solution)/shard_map/ppermute | solution.py:22
  36.2 10.3 %collective-permute-start.8 = (f32[2,1,16,4096]{3,2,1,0:T(8,128)S(1)}, f32[2,1,16,4096]{3,2,1,0:T(8,128)}, u32[]{:S(2)}, u32[]{:S(2)}) collective-permute-start(f32[2,1,16,4096]{3,2,1,0:T(8,128)S(1)} %get-tuple-element.30), channel_id=1, source_target_pairs={{1,0},{2,1},{3,2},{5,4},{6,5},{7,6},{9,8},{10,9},{11,10},{13,12},{... | collective-permute-start | bytes 1572872 | tf_op jit(solution)/shard_map/ppermute | solution.py:24
  51.6 10.6 %collective-permute-start.10 = (f32[2,1,16,4096]{3,2,1,0:T(8,128)S(1)}, f32[2,1,16,4096]{3,2,1,0:T(8,128)S(1)}, u32[]{:S(2)}, u32[]{:S(2)}) collective-permute-start(f32[2,1,16,4096]{3,2,1,0:T(8,128)S(1)} %get-tuple-element.22), channel_id=1, source_target_pairs={{1,0},{2,1},{3,2},{5,4},{6,5},{7,6},{9,8},{10,9},{11,10},{13,12},{... | collective-permute-start | bytes 1572872 | tf_op jit(solution)/shard_map/ppermute | solution.py:24
  55.6 10.5 %collective-permute-start.9 = (f32[2,1,16,4096]{3,2,1,0:T(8,128)S(1)}, f32[2,1,16,4096]{3,2,1,0:T(8,128)S(1)}, u32[]{:S(2)}, u32[]{:S(2)}) collective-permute-start(f32[2,1,16,4096]{3,2,1,0:T(8,128)S(1)} %get-tuple-element.21), channel_id=1, source_target_pairs={{0,1},{1,2},{2,3},{4,5},{5,6},{6,7},{8,9},{9,10},{10,11},{12,13},{... | collective-permute-start | bytes 1572872 | tf_op jit(solution)/shard_map/ppermute | solution.py:22

commit v4 on v3

--- a/solution.py
+++ b/solution.py
@@ -122,7 +122,7 @@
     total_cols = NY
     first_row = lax.axis_index("tile") * local_rows
     screens = gather_screens(stored_planes, owner, "illum")
-    extra = 0
+    extra = HALF
     span = local_rows + 2 * extra
     global_rows = first_row - extra + jnp.arange(span, dtype=jnp.int32)
     inside = (global_rows >= 0) & (global_rows < total_rows)
@@ -137,7 +137,20 @@
     along_sin = jnp.sin(two_pi * along)[:, None, :]
     real = across_cos * along_cos - across_sin * along_sin
     imag = across_sin * along_cos + across_cos * along_sin
-    for plane in range(PLANES):
+    halo = extended(screens[0], (("tile", 0),), HALF)
+    pieces = [
+        transmit(real[:, rows], imag[:, rows], screen)
+        for rows, screen in (
+            (slice(0, HALF), halo[:HALF]),
+            (slice(HALF, HALF + local_rows), screens[0]),
+            (slice(HALF + local_rows, span), halo[HALF + local_rows :]),
+        )
+    ]
+    real = jnp.concatenate([piece[0] for piece in pieces], axis=1)
+    imag = jnp.concatenate([piece[1] for piece in pieces], axis=1)
+    real, imag = cross_pass(real, imag, taps)
+    real, imag = along_pass(real, imag, taps)
+    for plane in range(1, PLANES):
         real, imag = transmit(real, imag, screens[plane])
         packed = extended(jnp.stack([real, imag]), (("tile", 2),), HALF)
         real, imag = cross_pass(packed[0], packed[1], taps)

time: 71.1 us -> 85.4 us (1.20)
  local copies, waits for them, and re-layouts: 13 us -> 39 us
  waiting for transfers between devices: 25.9 us -> 15.9 us
  starting transfers between devices: 21 us -> 19.5 us
    cos x4 -> x7, local copies, waits for them, and re-layouts: 0.81 us -> 9.99 us  [transmit(): cosine = jnp.cos(screen)]
    ppermute x7, waiting for transfers between devices: 14.7 us -> 8.02 us  [gather_screens(): lax.ppermute(stored_planes, axis, [(i, partner(i, k)) for i in range(coun...]
    unnamed x19 -> x30, local copies, waits for them, and re-layouts: 3.11 us -> 8.84 us
    sin x6 -> x5, local copies, waits for them, and re-layouts: 4.53 us -> 9.81 us  [transmit(): sine = jnp.sin(screen)]
    squeeze x1, local copies, waits for them, and re-layouts: 0.09 us -> 2.12 us  [gather_screens(): picked = stacked[p][source]]
    ppermute x2, starting transfers between devices: 7.56 us -> 5.55 us  [extended(): lax.ppermute(head, axis, [((i + 1) % count, i) for i in range(ends)])]
    ppermute x2, waiting for transfers between devices: 6.01 us -> 4.06 us  [extended(): lax.ppermute(head, axis, [((i + 1) % count, i) for i in range(ends)])]
    gather x2, local copies, waits for them, and re-layouts: 1.16 us -> 2.99 us  [gather_screens(): picked = stacked[p][source]]
  transfers between devices with their start and end apart: 11 -> 11, of which waited for: 7 -> 4; matrix products, arithmetic and copies ran while one was open for 13% -> 38% of each run, Pallas kernels for 0% -> 0%
where the time goes in v4:
time: 85.4 us; the launch traced here: 84.7 us
  local copies, waits for them, and re-layouts  39 us (46%)
  starting transfers between devices  19.5 us (23%)
  waiting for transfers between devices  15.9 us (19%)
  other arithmetic  6.28 us (7%)
  matrix products  3.63 us (4%)
    cos x7, local copies, waits for them, and re-layouts, transmit(): cosine = jnp.cos(screen)  9.99 us
    sin x5, local copies, waits for them, and re-layouts, transmit(): sine = jnp.sin(screen)  9.81 us
    ppermute x7, starting transfers between devices, gather_screens(): lax.ppermute(stored_planes, axis, [(i, partner(i, k)) for i in range(coun...  9.4 us
    unnamed x30, local copies, waits for them, and re-layouts  8.84 us
    ppermute x7, waiting for transfers between devices, gather_screens(): lax.ppermute(stored_planes, axis, [(i, partner(i, k)) for i in range(coun...  8.02 us
    ppermute x2, starting transfers between devices, extended(): lax.ppermute(head, axis, [((i + 1) % count, i) for i in range(ends)])  5.55 us
    ppermute x2, starting transfers between devices, extended(): lax.ppermute(tail, axis, [(i, (i + 1) % count) for i in range(ends)])  4.52 us
    ppermute x2, waiting for transfers between devices, extended(): lax.ppermute(head, axis, [((i + 1) % count, i) for i in range(ends)])  4.06 us
  transfers between devices with their start and end apart: 11, of which 4 were waited for; matrix products, arithmetic and copies ran while one was open for 38% of the time, Pallas kernels for 0%

profile of v4, /device:TPU:18, one launch (start us, length us, event | category | flops | bytes accessed | tf_op | source)
XLA Modules:
  0.0 84.7 jit_solution(10817521688912713095)
XLA Ops:
  0.0 1.5 %collective-permute-start = (f32[2,32,512]{2,1,0:T(8,128)}, f32[2,32,512]{2,1,0:T(8,128)S(1)}, u32[]{:S(2)}, u32[]{:S(2)}) collective-permute-start(f32[2,32,512]{2,1,0:T(8,128)} %param.6), channel_id=1, source_target_pairs={{0,4},{4,0},{8,12},{12,8},{16,20},{20,16},{24,28},{28,24},{1,5},{5... | collective-permute-start | bytes 393224 | tf_op jit(solution)/shard_map/ppermute | solution.py:107
  1.5 1.6 %collective-permute-start.1 = (f32[2,32,512]{2,1,0:T(8,128)}, f32[2,32,512]{2,1,0:T(8,128)S(1)}, u32[]{:S(2)}, u32[]{:S(2)}) collective-permute-start(f32[2,32,512]{2,1,0:T(8,128)} %param.6), channel_id=1, source_target_pairs={{0,8},{4,12},{8,0},{12,4},{16,24},{20,28},{24,16},{28,20},{1,9},{5... | collective-permute-start | bytes 393224 | tf_op jit(solution)/shard_map/ppermute | solution.py:107
  3.8 3.5 %collective-permute-start.4 = (f32[2,32,512]{2,1,0:T(8,128)}, f32[2,32,512]{2,1,0:T(8,128)S(1)}, u32[]{:S(2)}, u32[]{:S(2)}) collective-permute-start(f32[2,32,512]{2,1,0:T(8,128)} %param.6), channel_id=1, source_target_pairs={{0,20},{4,16},{8,28},{12,24},{16,4},{20,0},{24,12},{28,8},{1,21},{... | collective-permute-start | bytes 393224 | tf_op jit(solution)/shard_map/ppermute | solution.py:107
  7.4 1.6 %bitcast_dynamic-update-slice_fusion.7 = f32[2,8,32,512]{3,2,0,1:T(8,128)} fusion(f32[2,32,512]{2,1,0:T(8,128)} %param.6), kind=kLoop, calls=%fused_computation.84 | loop fusion | bytes 262144
  9.0 1.4 %fusion.51 = (s32[1,1]{1,0:T(1,128)}, s32[1,1]{1,0:T(1,128)}) fusion(s32[1,2]{1,0:T(1,128)} %param.4), kind=kLoop, calls=%fused_computation.129 | loop fusion | bytes 16 | tf_op jit(solution)/shard_map/slice | solution.py:131
  13.4 1.1 %select_reduce_fusion = (f32[160,128]{1,0:T(8,128)S(1)}, f32[160,128]{1,0:T(8,128)}) fusion(f32[33]{0:T(128)S(1)} %get-tuple-element.48, s32[160,128]{1,0:T(8,128)S(1)} %iota_subtract_fusion, f32[33]{0:T(128)S(1)} %get-tuple-element.47), kind=kLoop, calls=%fused_computation.4 | loop fusion | flops 3338240 | bytes 246024 | tf_op jit(solution)/shard_map/reduce_sum | solution.py:36
  16.9 1.5 %collective-permute-start.6 = (f32[2,32,512]{2,1,0:T(8,128)S(1)}, f32[2,32,512]{2,1,0:T(8,128)S(1)}, u32[]{:S(2)}, u32[]{:S(2)}) collective-permute-start(f32[2,32,512]{2,1,0:T(8,128)S(1)} %copy-done.2), channel_id=1, source_target_pairs={{0,28},{4,24},{8,20},{12,16},{16,12},{20,8},{24,4},{28,0},{1,29},{... | collective-permute-start | bytes 393224 | tf_op jit(solution)/shard_map/ppermute | solution.py:107
  21.1 6.2 %collective-permute-done.5 = f32[2,32,512]{2,1,0:T(8,128)S(1)} collective-permute-done((f32[2,32,512]{2,1,0:T(8,128)S(1)}, f32[2,32,512]{2,1,0:T(8,128)S(1)}, u32[]{:S(2)}, u32[]{:S(2)}) %collective-permute-start.5) | collective-permute-done | bytes 131104 | tf_op jit(solution)/shard_map/ppermute | solution.py:107
  27.9 1.8 %collective-permute-done.6 = f32[2,32,512]{2,1,0:T(8,128)S(1)} collective-permute-done((f32[2,32,512]{2,1,0:T(8,128)S(1)}, f32[2,32,512]{2,1,0:T(8,128)S(1)}, u32[]{:S(2)}, u32[]{:S(2)}) %collective-permute-start.6) | collective-permute-done | bytes 131104 | tf_op jit(solution)/shard_map/ppermute | solution.py:107
  30.4 2.1 %slice_bitcast_fusion.2 = (f32[8,32,512]{2,1,0:T(8,128)}, f32[8,32,512]{2,1,0:T(8,128)S(1)}) fusion(f32[2,8,32,512]{3,2,0,1:T(8,128)} %bitcast_dynamic-update-slice_fusion), kind=kLoop, calls=%fused_computation.42 | loop fusion | bytes 2097152 | tf_op jit(solution)/shard_map/squeeze | solution.py:114
  33.1 1.9 %bitcast_cosine_fusion = (f32[32,8,512]{2,0,1:T(8,128)S(1)}, f32[32,8,512]{2,0,1:T(8,128)S(1)}) fusion(f32[8,32,512]{2,1,0:T(8,128)S(1)} %gather_fusion), kind=kLoop, calls=%fused_computation.122 | loop fusion | bytes 1572864 | tf_op jit(solution)/shard_map/cos | solution.py:81
  35.8 1.9 %collective-permute-start.7 = (f32[16,4096]{1,0:T(8,128)}, f32[16,4096]{1,0:T(8,128)}, u32[]{:S(2)}, u32[]{:S(2)}) collective-permute-start(f32[16,4096]{1,0:T(8,128)} %bitcast.41), channel_id=1, source_target_pairs={{0,1},{1,2},{2,3},{4,5},{5,6},{6,7},{8,9},{9,10},{10,11},{12,13},{... | collective-permute-start | bytes 786440 | tf_op jit(solution)/shard_map/ppermute | solution.py:22
  37.7 1.1 %copy.12 = f32[32,8,512]{2,1,0:T(8,128)} copy(f32[32,8,512]{2,0,1:T(8,128)S(1)} %get-tuple-element.37) | data formatting | bytes 1048576 | tf_op jit(solution)/shard_map/cos | solution.py:81
  38.8 1.1 %cos.63 = f32[1,32,4096]{2,1,0:T(8,128)S(1)} reshape(f32[32,8,512]{2,1,0:T(8,128)} %copy.12) | data formatting | bytes 1048576 | tf_op jit(solution)/shard_map/cos | solution.py:81
  39.9 1.1 %copy.13 = f32[32,8,512]{2,1,0:T(8,128)} copy(f32[32,8,512]{2,0,1:T(8,128)S(1)} %get-tuple-element.38) | data formatting | bytes 1048576 | tf_op jit(solution)/shard_map/sin | solution.py:82
  41.0 1.1 %sin.63 = f32[1,32,4096]{2,1,0:T(8,128)S(1)} reshape(f32[32,8,512]{2,1,0:T(8,128)} %copy.13) | data formatting | bytes 1048576 | tf_op jit(solution)/shard_map/sin | solution.py:82
  42.9 3.6 %collective-permute-start.8 = (f32[16,4096]{1,0:T(8,128)}, f32[16,4096]{1,0:T(8,128)S(1)}, u32[]{:S(2)}, u32[]{:S(2)}) collective-permute-start(f32[16,4096]{1,0:T(8,128)} %bitcast.43), channel_id=1, source_target_pairs={{1,0},{2,1},{3,2},{5,4},{6,5},{7,6},{9,8},{10,9},{11,10},{13,12},{... | collective-permute-start | bytes 786440 | tf_op jit(solution)/shard_map/ppermute | solution.py:24
  46.5 2.4 %gather_fusion.1 = f32[8,32,512]{2,1,0:T(8,128)} fusion(f32[8,32,512]{2,1,0:T(8,128)} %get-tuple-element.21, s32[1024]{0:T(1024)S(1)} %get-tuple-element.51), kind=kCustom, calls=%fused_computation.1 | custom fusion | bytes 1048608 | tf_op jit(solution)/shard_map/gather | solution.py:114
  49.0 3.5 %sine_bitcast_fusion = (f32[32,8,512]{2,0,1:T(8,128)}, f32[32,8,512]{2,0,1:T(8,128)S(1)}) fusion(f32[8,32,512]{2,1,0:T(8,128)} %gather_fusion.1), kind=kLoop, calls=%fused_computation.50 | loop fusion | bytes 1572864 | tf_op jit(solution)/shard_map/sin | solution.py:82
  52.4 1.1 %copy.15 = f32[32,8,512]{2,1,0:T(8,128)} copy(f32[32,8,512]{2,0,1:T(8,128)S(1)} %get-tuple-element.30) | data formatting | bytes 1048576 | tf_op jit(solution)/shard_map/cos | solution.py:81
  53.5 2.0 %cos.67 = f32[1,1,32,4096]{3,2,1,0:T(8,128)} reshape(f32[32,8,512]{2,1,0:T(8,128)} %copy.15) | data formatting | bytes 1048576 | tf_op jit(solution)/shard_map/cos | solution.py:81
  55.5 2.2 %copy.16 = f32[32,8,512]{2,1,0:T(8,128)} copy(f32[32,8,512]{2,0,1:T(8,128)} %get-tuple-element.29) | data formatting | bytes 1048576 | tf_op jit(solution)/shard_map/sin | solution.py:82
  57.7 1.9 %sin.67 = f32[1,1,32,4096]{3,2,1,0:T(8,128)} reshape(f32[32,8,512]{2,1,0:T(8,128)} %copy.16) | data formatting | bytes 1048576 | tf_op jit(solution)/shard_map/sin | solution.py:82
  59.6 1.9 %fusion.50 = (f32[16,4096]{1,0:T(8,128)S(1)}, f32[16,4096]{1,0:T(8,128)S(1)}) fusion(f32[16,4096]{1,0:T(8,128)} %collective-permute-done.7), kind=kLoop, calls=%fused_computation.128 | loop fusion | bytes 786432 | tf_op jit(solution)/shard_map/cos | solution.py:81
  61.6 1.0 %fusion.49 = (f32[16,4096]{1,0:T(8,128)S(1)}, f32[16,4096]{1,0:T(8,128)S(1)}) fusion(f32[16,4096]{1,0:T(8,128)S(1)} %collective-permute-done.8), kind=kLoop, calls=%fused_computation.127 | loop fusion | bytes 786432 | tf_op jit(solution)/shard_map/cos | solution.py:81
  65.0 1.1 %fusion.18 = f32[1,32,32,256]{3,2,1,0:T(8,128)S(1)} fusion(f32[1,32,32,32]{3,2,1,0:T(8,128)S(1)} %bitcast.173, f32[1,32,32,128]{3,2,1,0:T(8,128)S(1)} %bitcast.179, f32[1,32,32,32]{3,2,1,0:T(8,128)S(1)} %bitcast.175, f32[1,32,32,128]{3,2,1,0:T(8,128)S(1)} %bitcast.177, f32[160,128]{1,0:T(8,128)S(1)} %copy-done.4, f32[160,128]{1,0:T(8,128)S(1)} %copy-done.3, ...), kind=kOutput, calls=%fused_computation.29 | convolution fusion | flops 504545280 | bytes 2605056 | tf_op jit(solution)/shard_map/...nj,jc->...nc/dot_general | solution.py:68
  67.6 1.9 %collective-permute-start.10 = (f32[2,1,16,4096]{3,2,1,0:T(8,128)S(1)}, f32[2,1,16,4096]{3,2,1,0:T(8,128)S(1)}, u32[]{:S(2)}, u32[]{:S(2)}) collective-permute-start(f32[2,1,16,4096]{3,2,1,0:T(8,128)S(1)} %get-tuple-element.18), channel_id=1, source_target_pairs={{1,0},{2,1},{3,2},{5,4},{6,5},{7,6},{9,8},{10,9},{11,10},{13,12},{... | collective-permute-start | bytes 1572872 | tf_op jit(solution)/shard_map/ppermute | solution.py:24
  69.5 2.6 %collective-permute-start.9 = (f32[2,1,16,4096]{3,2,1,0:T(8,128)S(1)}, f32[2,1,16,4096]{3,2,1,0:T(8,128)S(1)}, u32[]{:S(2)}, u32[]{:S(2)}) collective-permute-start(f32[2,1,16,4096]{3,2,1,0:T(8,128)S(1)} %get-tuple-element.17), channel_id=1, source_target_pairs={{0,1},{1,2},{2,3},{4,5},{5,6},{6,7},{8,9},{9,10},{10,11},{12,13},{... | collective-permute-start | bytes 1572872 | tf_op jit(solution)/shard_map/ppermute | solution.py:22
  72.1 4.1 %collective-permute-done.10 = f32[2,1,16,4096]{3,2,1,0:T(8,128)S(1)} collective-permute-done((f32[2,1,16,4096]{3,2,1,0:T(8,128)S(1)}, f32[2,1,16,4096]{3,2,1,0:T(8,128)S(1)}, u32[]{:S(2)}, u32[]{:S(2)}) %collective-permute-start.10) | collective-permute-done | bytes 524320 | tf_op jit(solution)/shard_map/ppermute | solution.py:24
  76.2 3.8 %collective-permute-done.9 = f32[2,1,16,4096]{3,2,1,0:T(8,128)S(1)} collective-permute-done((f32[2,1,16,4096]{3,2,1,0:T(8,128)S(1)}, f32[2,1,16,4096]{3,2,1,0:T(8,128)S(1)}, u32[]{:S(2)}, u32[]{:S(2)}) %collective-permute-start.9) | collective-permute-done | bytes 524320 | tf_op jit(solution)/shard_map/ppermute | solution.py:22
  82.2 1.1 %fusion.17 = f32[1,32,32,256]{3,2,1,0:T(8,128)S(1)} fusion(f32[1,32,32,32]{3,2,1,0:T(8,128)S(1)} %bitcast.172, f32[1,32,32,128]{3,2,1,0:T(8,128)S(1)} %bitcast.178, f32[1,32,32,32]{3,2,1,0:T(8,128)S(1)} %bitcast.174, f32[1,32,32,128]{3,2,1,0:T(8,128)S(1)} %bitcast.176, f32[160,128]{1,0:T(8,128)S(1)} %copy-done.4, f32[160,128]{1,0:T(8,128)S(1)} %copy-done.3, ...), kind=kOutput, calls=%fused_computation.28 | convolution fusion | flops 504545280 | bytes 2605056 | tf_op jit(solution)/shard_map/...nj,jc->...nc/dot_general | solution.py:68
  83.6 1.0 %pad_maximum_fusion.1 = f32[2,1,32,4096]{3,2,1,0:T(8,128)} fusion(f32[1,1,32,4096]{3,2,1,0:T(8,128)S(1)} %stack_reshape.7, f32[1,1,32,4096]{3,2,1,0:T(8,128)S(1)} %stack_reshape.6), kind=kLoop, calls=%fused_computation.34 | loop fusion | flops 262144 | bytes 2097152 | tf_op jit(solution)/shard_map/stack | solution.py:158
  (74 shorter events, 18.4 us)
Async XLA Ops:
  0.0 15.7 %copy-start.2 = (f32[2,32,512]{2,1,0:T(8,128)S(1)}, f32[2,32,512]{2,1,0:T(8,128)}, u32[]{:S(2)}) copy-start(f32[2,32,512]{2,1,0:T(8,128)} %param.6) | copy-start | bytes 393220
  0.0 15.7 %collective-permute-start = (f32[2,32,512]{2,1,0:T(8,128)}, f32[2,32,512]{2,1,0:T(8,128)S(1)}, u32[]{:S(2)}, u32[]{:S(2)}) collective-permute-start(f32[2,32,512]{2,1,0:T(8,128)} %param.6), channel_id=1, source_target_pairs={{0,4},{4,0},{8,12},{12,8},{16,20},{20,16},{24,28},{28,24},{1,5},{5... | collective-permute-start | bytes 393224 | tf_op jit(solution)/shard_map/ppermute | solution.py:107
  1.5 15.3 %collective-permute-start.1 = (f32[2,32,512]{2,1,0:T(8,128)}, f32[2,32,512]{2,1,0:T(8,128)S(1)}, u32[]{:S(2)}, u32[]{:S(2)}) collective-permute-start(f32[2,32,512]{2,1,0:T(8,128)} %param.6), channel_id=1, source_target_pairs={{0,8},{4,12},{8,0},{12,4},{16,24},{20,28},{24,16},{28,20},{1,9},{5... | collective-permute-start | bytes 393224 | tf_op jit(solution)/shard_map/ppermute | solution.py:107
  3.1 16.0 %collective-permute-start.2 = (f32[2,32,512]{2,1,0:T(8,128)}, f32[2,32,512]{2,1,0:T(8,128)S(1)}, u32[]{:S(2)}, u32[]{:S(2)}) collective-permute-start(f32[2,32,512]{2,1,0:T(8,128)} %param.6), channel_id=1, source_target_pairs={{0,12},{4,8},{8,4},{12,0},{16,28},{20,24},{24,20},{28,16},{1,13},{... | collective-permute-start | bytes 393224 | tf_op jit(solution)/shard_map/ppermute | solution.py:107
  3.5 16.2 %collective-permute-start.3 = (f32[2,32,512]{2,1,0:T(8,128)}, f32[2,32,512]{2,1,0:T(8,128)S(1)}, u32[]{:S(2)}, u32[]{:S(2)}) collective-permute-start(f32[2,32,512]{2,1,0:T(8,128)} %param.6), channel_id=1, source_target_pairs={{0,16},{4,20},{8,24},{12,28},{16,0},{20,4},{24,8},{28,12},{1,17},{... | collective-permute-start | bytes 393224 | tf_op jit(solution)/shard_map/ppermute | solution.py:107
  3.8 16.6 %collective-permute-start.4 = (f32[2,32,512]{2,1,0:T(8,128)}, f32[2,32,512]{2,1,0:T(8,128)S(1)}, u32[]{:S(2)}, u32[]{:S(2)}) collective-permute-start(f32[2,32,512]{2,1,0:T(8,128)} %param.6), channel_id=1, source_target_pairs={{0,20},{4,16},{8,28},{12,24},{16,4},{20,0},{24,12},{28,8},{1,21},{... | collective-permute-start | bytes 393224 | tf_op jit(solution)/shard_map/ppermute | solution.py:107
  15.7 11.6 %collective-permute-start.5 = (f32[2,32,512]{2,1,0:T(8,128)S(1)}, f32[2,32,512]{2,1,0:T(8,128)S(1)}, u32[]{:S(2)}, u32[]{:S(2)}) collective-permute-start(f32[2,32,512]{2,1,0:T(8,128)S(1)} %copy-done.2), channel_id=1, source_target_pairs={{0,24},{4,28},{8,16},{12,20},{16,8},{20,12},{24,0},{28,4},{1,25},{... | collective-permute-start | bytes 393224 | tf_op jit(solution)/shard_map/ppermute | solution.py:107
  16.9 12.9 %collective-permute-start.6 = (f32[2,32,512]{2,1,0:T(8,128)S(1)}, f32[2,32,512]{2,1,0:T(8,128)S(1)}, u32[]{:S(2)}, u32[]{:S(2)}) collective-permute-start(f32[2,32,512]{2,1,0:T(8,128)S(1)} %copy-done.2), channel_id=1, source_target_pairs={{0,28},{4,24},{8,20},{12,16},{16,12},{20,8},{24,4},{28,0},{1,29},{... | collective-permute-start | bytes 393224 | tf_op jit(solution)/shard_map/ppermute | solution.py:107
  35.8 23.8 %collective-permute-start.7 = (f32[16,4096]{1,0:T(8,128)}, f32[16,4096]{1,0:T(8,128)}, u32[]{:S(2)}, u32[]{:S(2)}) collective-permute-start(f32[16,4096]{1,0:T(8,128)} %bitcast.41), channel_id=1, source_target_pairs={{0,1},{1,2},{2,3},{4,5},{5,6},{6,7},{8,9},{9,10},{10,11},{12,13},{... | collective-permute-start | bytes 786440 | tf_op jit(solution)/shard_map/ppermute | solution.py:22
  42.9 18.7 %collective-permute-start.8 = (f32[16,4096]{1,0:T(8,128)}, f32[16,4096]{1,0:T(8,128)S(1)}, u32[]{:S(2)}, u32[]{:S(2)}) collective-permute-start(f32[16,4096]{1,0:T(8,128)} %bitcast.43), channel_id=1, source_target_pairs={{1,0},{2,1},{3,2},{5,4},{6,5},{7,6},{9,8},{10,9},{11,10},{13,12},{... | collective-permute-start | bytes 786440 | tf_op jit(solution)/shard_map/ppermute | solution.py:24
  64.1 0.9 %copy-start.3 = (f32[160,128]{1,0:T(8,128)S(1)}, f32[160,128]{1,0:T(8,128)}, u32[]{:S(2)}) copy-start(f32[160,128]{1,0:T(8,128)} %neg.5) | copy-start | bytes 245764
  64.1 0.9 %copy-start.4 = (f32[160,128]{1,0:T(8,128)S(1)}, f32[160,128]{1,0:T(8,128)}, u32[]{:S(2)}) copy-start(f32[160,128]{1,0:T(8,128)} %get-tuple-element.6) | copy-start | bytes 245764
  66.2 1.0 %copy-start = (f32[1,1,32,4096]{3,2,1,0:T(8,128)S(1)}, f32[1,1,32,4096]{3,2,1,0:T(8,128)}, u32[]{:S(2)}) copy-start(f32[1,1,32,4096]{3,2,1,0:T(8,128)} %cos.67) | copy-start | bytes 1572868
  66.2 1.2 %copy-start.1 = (f32[1,1,32,4096]{3,2,1,0:T(8,128)S(1)}, f32[1,1,32,4096]{3,2,1,0:T(8,128)}, u32[]{:S(2)}) copy-start(f32[1,1,32,4096]{3,2,1,0:T(8,128)} %sin.67) | copy-start | bytes 1572868
  67.6 8.6 %collective-permute-start.10 = (f32[2,1,16,4096]{3,2,1,0:T(8,128)S(1)}, f32[2,1,16,4096]{3,2,1,0:T(8,128)S(1)}, u32[]{:S(2)}, u32[]{:S(2)}) collective-permute-start(f32[2,1,16,4096]{3,2,1,0:T(8,128)S(1)} %get-tuple-element.18), channel_id=1, source_target_pairs={{1,0},{2,1},{3,2},{5,4},{6,5},{7,6},{9,8},{10,9},{11,10},{13,12},{... | collective-permute-start | bytes 1572872 | tf_op jit(solution)/shard_map/ppermute | solution.py:24
  69.5 10.5 %collective-permute-start.9 = (f32[2,1,16,4096]{3,2,1,0:T(8,128)S(1)}, f32[2,1,16,4096]{3,2,1,0:T(8,128)S(1)}, u32[]{:S(2)}, u32[]{:S(2)}) collective-permute-start(f32[2,1,16,4096]{3,2,1,0:T(8,128)S(1)} %get-tuple-element.17), channel_id=1, source_target_pairs={{0,1},{1,2},{2,3},{4,5},{5,6},{6,7},{8,9},{9,10},{10,11},{12,13},{... | collective-permute-start | bytes 1572872 | tf_op jit(solution)/shard_map/ppermute | solution.py:22

commit v5 on v4

--- a/solution.py
+++ b/solution.py
@@ -135,11 +135,15 @@
     across_sin = jnp.where(inside[None, :], jnp.sin(two_pi * across), 0.0)[:, :, None]
     along_cos = jnp.cos(two_pi * along)[:, None, :]
     along_sin = jnp.sin(two_pi * along)[:, None, :]
-    real = across_cos * along_cos - across_sin * along_sin
-    imag = across_sin * along_cos + across_cos * along_sin
+
+    def incident(rows):
+        real = across_cos[:, rows] * along_cos - across_sin[:, rows] * along_sin
+        imag = across_sin[:, rows] * along_cos + across_cos[:, rows] * along_sin
+        return real, imag
+
     halo = extended(screens[0], (("tile", 0),), HALF)
     pieces = [
-        transmit(real[:, rows], imag[:, rows], screen)
+        transmit(*incident(rows), screen)
         for rows, screen in (
             (slice(0, HALF), halo[:HALF]),
             (slice(HALF, HALF + local_rows), screens[0]),

time: 85.4 us -> 70 us (0.82)
  the two profiles are of different devices: /device:TPU:18 before, /device:TPU:1 now
where the time goes in v5:
time: 70 us; the launch traced here: 69 us
  starting transfers between devices  24.4 us (35%)
  local copies, waits for them, and re-layouts  18.4 us (26%)
  waiting for transfers between devices  12.6 us (18%)
  other arithmetic  9.25 us (13%)
  matrix products  3.64 us (5%)
    ppermute x2, starting transfers between devices, extended(): lax.ppermute(tail, axis, [(i, (i + 1) % count) for i in range(ends)])  10.3 us
    ppermute x7, starting transfers between devices, gather_screens(): lax.ppermute(stored_planes, axis, [(i, partner(i, k)) for i in range(coun...  10.3 us
    ppermute x7, waiting for transfers between devices, gather_screens(): lax.ppermute(stored_planes, axis, [(i, partner(i, k)) for i in range(coun...  6.7 us
    ppermute x2, waiting for transfers between devices, extended(): lax.ppermute(head, axis, [((i + 1) % count, i) for i in range(ends)])  4.74 us
    cos x7, local copies, waits for them, and re-layouts, transmit(): cosine = jnp.cos(screen)  4.61 us
    ppermute x2, starting transfers between devices, extended(): lax.ppermute(head, axis, [((i + 1) % count, i) for i in range(ends)])  3.83 us
    unnamed x38, local copies, waits for them, and re-layouts  3.46 us
    sin x5, local copies, waits for them, and re-layouts, transmit(): sine = jnp.sin(screen)  2.67 us
  transfers between devices with their start and end apart: 11, of which 4 were waited for; matrix products, arithmetic and copies ran while one was open for 27% of the time, Pallas kernels for 0%

profile of v5, /device:TPU:1, one launch (start us, length us, event | category | flops | bytes accessed | tf_op | source)
XLA Modules:
  0.0 69.0 jit_solution(8024759451965277475)
XLA Ops:
  0.0 2.1 %collective-permute-start = (f32[2,32,512]{2,1,0:T(8,128)}, f32[2,32,512]{2,1,0:T(8,128)S(1)}, u32[]{:S(2)}, u32[]{:S(2)}) collective-permute-start(f32[2,32,512]{2,1,0:T(8,128)} %param.6), channel_id=1, source_target_pairs={{0,4},{4,0},{8,12},{12,8},{16,20},{20,16},{24,28},{28,24},{1,5},{5... | collective-permute-start | bytes 393224 | tf_op jit(solution)/shard_map/ppermute | solution.py:107
  2.1 1.3 %collective-permute-start.1 = (f32[2,32,512]{2,1,0:T(8,128)}, f32[2,32,512]{2,1,0:T(8,128)S(1)}, u32[]{:S(2)}, u32[]{:S(2)}) collective-permute-start(f32[2,32,512]{2,1,0:T(8,128)} %param.6), channel_id=1, source_target_pairs={{0,8},{4,12},{8,0},{12,4},{16,24},{20,28},{24,16},{28,20},{1,9},{5... | collective-permute-start | bytes 393224 | tf_op jit(solution)/shard_map/ppermute | solution.py:107
  3.4 2.4 %collective-permute-start.3 = (f32[2,32,512]{2,1,0:T(8,128)}, f32[2,32,512]{2,1,0:T(8,128)S(1)}, u32[]{:S(2)}, u32[]{:S(2)}) collective-permute-start(f32[2,32,512]{2,1,0:T(8,128)} %param.6), channel_id=1, source_target_pairs={{0,16},{4,20},{8,24},{12,28},{16,0},{20,4},{24,8},{28,12},{1,17},{... | collective-permute-start | bytes 393224 | tf_op jit(solution)/shard_map/ppermute | solution.py:107
  5.8 1.0 %collective-permute-start.4 = (f32[2,32,512]{2,1,0:T(8,128)}, f32[2,32,512]{2,1,0:T(8,128)S(1)}, u32[]{:S(2)}, u32[]{:S(2)}) collective-permute-start(f32[2,32,512]{2,1,0:T(8,128)} %param.6), channel_id=1, source_target_pairs={{0,20},{4,16},{8,28},{12,24},{16,4},{20,0},{24,12},{28,8},{1,21},{... | collective-permute-start | bytes 393224 | tf_op jit(solution)/shard_map/ppermute | solution.py:107
  6.8 0.9 %bitcast_dynamic-update-slice_fusion.11 = f32[2,8,32,512]{3,2,0,1:T(8,128)S(1)} fusion(f32[2,32,512]{2,1,0:T(8,128)} %param.6), kind=kLoop, calls=%fused_computation.76 | loop fusion | bytes 262144
  7.8 1.3 %fusion.43 = (s32[1,1]{1,0:T(1,128)}, s32[1,1]{1,0:T(1,128)}) fusion(s32[1,2]{1,0:T(1,128)} %param.4), kind=kLoop, calls=%fused_computation.127 | loop fusion | bytes 16 | tf_op jit(solution)/shard_map/slice | solution.py:131
  9.1 0.7 %sine_select_fusion = (f32[1,64,1]{1,2,0:T(1,128)S(1)}, f32[1,64,1]{1,2,0:T(1,128)S(1)}) fusion(s32[]{:T(128)S(6)} %sub.149, s32[]{:T(128)} %bitcast), kind=kLoop, calls=%fused_computation.111 | loop fusion | flops 1280 | bytes 520 | tf_op jit(solution)/shard_map/jit(_where)/select_n | solution.py:135
  12.3 0.8 %slice_bitcast_fusion.15 = (f32[33]{0:T(128)S(1)}, f32[33]{0:T(128)S(1)}) fusion(f32[2,33]{1,0:T(2,128)} %param.5), kind=kLoop, calls=%fused_computation.105 | loop fusion | bytes 528 | tf_op jit(solution)/shard_map/squeeze | solution.py:74
  13.2 1.1 %select_reduce_fusion = (f32[160,128]{1,0:T(8,128)S(1)}, f32[160,128]{1,0:T(8,128)}) fusion(f32[33]{0:T(128)S(1)} %get-tuple-element.46, s32[160,128]{1,0:T(8,128)S(1)} %iota_subtract_fusion, f32[33]{0:T(128)S(1)} %get-tuple-element.45), kind=kLoop, calls=%fused_computation.4 | loop fusion | flops 3338240 | bytes 246024 | tf_op jit(solution)/shard_map/reduce_sum | solution.py:36
  14.4 0.8 %fusion.32 = (s32[8]{0:T(128)S(1)}, s32[8]{0:T(128)S(1)}) fusion(s32[2,8]{1,0:T(2,128)} %param.7, s32[]{:T(128)S(6)} %axis_index.25), kind=kLoop, calls=%fused_computation.103 | loop fusion | flops 64 | bytes 132 | tf_op jit(solution)/shard_map/select_n | solution.py:114
  17.0 0.7 %fusion.26 = (f32[4096]{0:T(1024)S(1)}, f32[4096]{0:T(1024)S(1)}) fusion(s32[]{:T(128)} %bitcast.2), kind=kLoop, calls=%fused_computation.89 | loop fusion | flops 57344 | bytes 32772 | tf_op jit(solution)/shard_map/sin | solution.py:137
  17.7 3.4 %collective-permute-start.5 = (f32[2,32,512]{2,1,0:T(8,128)}, f32[2,32,512]{2,1,0:T(8,128)S(1)}, u32[]{:S(2)}, u32[]{:S(2)}) collective-permute-start(f32[2,32,512]{2,1,0:T(8,128)} %param.6), channel_id=1, source_target_pairs={{0,24},{4,28},{8,16},{12,20},{16,8},{20,12},{24,0},{28,4},{1,25},{... | collective-permute-start | bytes 393224 | tf_op jit(solution)/shard_map/ppermute | solution.py:107
  21.3 2.5 %collective-permute-done.5 = f32[2,32,512]{2,1,0:T(8,128)S(1)} collective-permute-done((f32[2,32,512]{2,1,0:T(8,128)}, f32[2,32,512]{2,1,0:T(8,128)S(1)}, u32[]{:S(2)}, u32[]{:S(2)}) %collective-permute-start.5) | collective-permute-done | bytes 131104 | tf_op jit(solution)/shard_map/ppermute | solution.py:107
  23.8 4.2 %collective-permute-done.6 = f32[2,32,512]{2,1,0:T(8,128)S(1)} collective-permute-done((f32[2,32,512]{2,1,0:T(8,128)}, f32[2,32,512]{2,1,0:T(8,128)S(1)}, u32[]{:S(2)}, u32[]{:S(2)}) %collective-permute-start.6) | collective-permute-done | bytes 131104 | tf_op jit(solution)/shard_map/ppermute | solution.py:107
  28.7 1.9 %bitcast_cosine_fusion = (f32[32,8,512]{2,0,1:T(8,128)S(1)}, f32[32,8,512]{2,0,1:T(8,128)S(1)}) fusion(f32[8,32,512]{2,1,0:T(8,128)S(1)} %gather_fusion), kind=kLoop, calls=%fused_computation.120 | loop fusion | bytes 1572864 | tf_op jit(solution)/shard_map/cos | solution.py:81
  30.6 6.5 %collective-permute-start.7 = (f32[16,4096]{1,0:T(8,128)S(1)}, f32[16,4096]{1,0:T(8,128)S(1)}, u32[]{:S(2)}, u32[]{:S(2)}) collective-permute-start(f32[16,4096]{1,0:T(8,128)S(1)} %bitcast.164), channel_id=1, source_target_pairs={{0,1},{1,2},{2,3},{4,5},{5,6},{6,7},{8,9},{9,10},{10,11},{12,13},{... | collective-permute-start | bytes 786440 | tf_op jit(solution)/shard_map/ppermute | solution.py:22
  38.0 0.7 %copy.18 = f32[8,2,8,512]{3,2,0,1:T(8,128)} copy(f32[8,2,8,512]{3,2,1,0:T(8,128)S(1)} %get-tuple-element.35) | data formatting | bytes 524288 | tf_op jit(solution)/shard_map/slice | solution.py:18
  38.7 1.9 %collective-permute-start.8 = (f32[16,4096]{1,0:T(8,128)}, f32[16,4096]{1,0:T(8,128)S(1)}, u32[]{:S(2)}, u32[]{:S(2)}) collective-permute-start(f32[16,4096]{1,0:T(8,128)} %bitcast.49), channel_id=1, source_target_pairs={{1,0},{2,1},{3,2},{5,4},{6,5},{7,6},{9,8},{10,9},{11,10},{13,12},{... | collective-permute-start | bytes 786440 | tf_op jit(solution)/shard_map/ppermute | solution.py:24
  40.6 0.7 %gather_fusion.1 = f32[8,32,512]{2,1,0:T(8,128)S(1)} fusion(f32[8,32,512]{2,1,0:T(8,128)S(1)} %get-tuple-element.21, s32[1024]{0:T(1024)} %get-tuple-element.53), kind=kCustom, calls=%fused_computation.1 | custom fusion | bytes 1048608 | tf_op jit(solution)/shard_map/gather | solution.py:114
  41.4 1.9 %sine_bitcast_fusion = (f32[32,8,512]{2,0,1:T(8,128)S(1)}, f32[32,8,512]{2,0,1:T(8,128)S(1)}) fusion(f32[8,32,512]{2,1,0:T(8,128)S(1)} %gather_fusion.1), kind=kLoop, calls=%fused_computation.48 | loop fusion | bytes 1572864 | tf_op jit(solution)/shard_map/sin | solution.py:82
  44.1 1.0 %fusion.42 = (f32[16,4096]{1,0:T(8,128)S(1)}, f32[16,4096]{1,0:T(8,128)S(1)}) fusion(f32[16,4096]{1,0:T(8,128)S(1)} %collective-permute-done.7), kind=kLoop, calls=%fused_computation.126 | loop fusion | bytes 786432 | tf_op jit(solution)/shard_map/cos | solution.py:81
  45.1 0.9 %bitcast_dynamic-update-slice_fusion.3 = f32[1,128,4096]{2,1,0:T(8,128)S(1)} fusion(f32[16,4096]{1,0:T(8,128)S(1)} %get-tuple-element.42, f32[16,4096]{1,0:T(8,128)S(1)} %get-tuple-element.41, f32[4096]{0:T(1024)S(1)} %get-tuple-element.55, f32[16]{0:T(128)} %get-tuple-element.50, f32[4096]{0:T(1024)S(1)} %get-tuple-element.56, f32[16]{0:T(128)} %get-tuple-element.48), kind=kLoop, calls=%fused_computation.64 | loop fusion | flops 589823 | bytes 819328
  46.0 1.0 %subtract_dynamic-update-slice_fusion = f32[1,128,4096]{2,1,0:T(8,128)S(1)} fusion(f32[1,128,4096]{2,1,0:T(8,128)S(1)} %bitcast_dynamic-update-slice_fusion.3, f32[1,32,4096]{2,1,0:T(8,128)S(1)} %sin.70, f32[1,32,4096]{2,1,0:T(8,128)S(1)} %cos.70, f32[4096]{0:T(1024)S(1)} %get-tuple-element.55, f32[32]{0:T(128)} %slice_bitcast_fusion.18, ...), kind=kLoop, calls=%fused_computation.55 | loop fusion | flops 1179648 | bytes 1605888
  46.9 1.0 %fusion.41 = (f32[16,4096]{1,0:T(8,128)S(1)}, f32[16,4096]{1,0:T(8,128)S(1)}) fusion(f32[16,4096]{1,0:T(8,128)S(1)} %collective-permute-done.8), kind=kLoop, calls=%fused_computation.125 | loop fusion | bytes 786432 | tf_op jit(solution)/shard_map/cos | solution.py:81
  50.8 1.1 %fusion.18 = f32[1,32,32,256]{3,2,1,0:T(8,128)S(1)} fusion(f32[1,32,32,32]{3,2,1,0:T(8,128)S(1)} %bitcast.157, f32[1,32,32,128]{3,2,1,0:T(8,128)S(1)} %bitcast.163, f32[1,32,32,32]{3,2,1,0:T(8,128)S(1)} %bitcast.159, f32[1,32,32,128]{3,2,1,0:T(8,128)S(1)} %bitcast.161, f32[160,128]{1,0:T(8,128)S(1)} %copy-done.2, f32[160,128]{1,0:T(8,128)S(1)} %copy-done.1, ...), kind=kOutput, calls=%fused_computation.29 | convolution fusion | flops 504545280 | bytes 2605056 | tf_op jit(solution)/shard_map/...nj,jc->...nc/dot_general | solution.py:68
  52.5 1.9 %collective-permute-start.10 = (f32[2,1,16,4096]{3,2,1,0:T(8,128)S(1)}, f32[2,1,16,4096]{3,2,1,0:T(8,128)S(1)}, u32[]{:S(2)}, u32[]{:S(2)}) collective-permute-start(f32[2,1,16,4096]{3,2,1,0:T(8,128)S(1)} %get-tuple-element.18), channel_id=1, source_target_pairs={{1,0},{2,1},{3,2},{5,4},{6,5},{7,6},{9,8},{10,9},{11,10},{13,12},{... | collective-permute-start | bytes 1572872 | tf_op jit(solution)/shard_map/ppermute | solution.py:24
  54.5 3.8 %collective-permute-start.9 = (f32[2,1,16,4096]{3,2,1,0:T(8,128)S(1)}, f32[2,1,16,4096]{3,2,1,0:T(8,128)S(1)}, u32[]{:S(2)}, u32[]{:S(2)}) collective-permute-start(f32[2,1,16,4096]{3,2,1,0:T(8,128)S(1)} %get-tuple-element.17), channel_id=1, source_target_pairs={{0,1},{1,2},{2,3},{4,5},{5,6},{6,7},{8,9},{9,10},{10,11},{12,13},{... | collective-permute-start | bytes 1572872 | tf_op jit(solution)/shard_map/ppermute | solution.py:22
  58.3 4.7 %collective-permute-done.10 = f32[2,1,16,4096]{3,2,1,0:T(8,128)S(1)} collective-permute-done((f32[2,1,16,4096]{3,2,1,0:T(8,128)S(1)}, f32[2,1,16,4096]{3,2,1,0:T(8,128)S(1)}, u32[]{:S(2)}, u32[]{:S(2)}) %collective-permute-start.10) | collective-permute-done | bytes 524320 | tf_op jit(solution)/shard_map/ppermute | solution.py:24
  63.0 1.2 %collective-permute-done.9 = f32[2,1,16,4096]{3,2,1,0:T(8,128)S(1)} collective-permute-done((f32[2,1,16,4096]{3,2,1,0:T(8,128)S(1)}, f32[2,1,16,4096]{3,2,1,0:T(8,128)S(1)}, u32[]{:S(2)}, u32[]{:S(2)}) %collective-permute-start.9) | collective-permute-done | bytes 524320 | tf_op jit(solution)/shard_map/ppermute | solution.py:22
  64.6 0.7 convolution_bitcast_fusion
  66.4 1.1 %fusion.17 = f32[1,32,32,256]{3,2,1,0:T(8,128)S(1)} fusion(f32[1,32,32,32]{3,2,1,0:T(8,128)S(1)} %bitcast.156, f32[1,32,32,128]{3,2,1,0:T(8,128)S(1)} %bitcast.162, f32[1,32,32,32]{3,2,1,0:T(8,128)S(1)} %bitcast.158, f32[1,32,32,128]{3,2,1,0:T(8,128)S(1)} %bitcast.160, f32[160,128]{1,0:T(8,128)S(1)} %copy-done.2, f32[160,128]{1,0:T(8,128)S(1)} %copy-done.1, ...), kind=kOutput, calls=%fused_computation.28 | convolution fusion | flops 504545280 | bytes 2605056 | tf_op jit(solution)/shard_map/...nj,jc->...nc/dot_general | solution.py:68
  67.9 1.0 %pad_maximum_fusion.1 = f32[2,1,32,4096]{3,2,1,0:T(8,128)} fusion(f32[1,1,32,4096]{3,2,1,0:T(8,128)S(1)} %stack_reshape.7, f32[1,1,32,4096]{3,2,1,0:T(8,128)S(1)} %stack_reshape.6), kind=kLoop, calls=%fused_computation.34 | loop fusion | flops 262144 | bytes 2097152 | tf_op jit(solution)/shard_map/stack | solution.py:162
  (85 shorter events, 12.2 us)
Async XLA Ops:
  0.0 17.7 %collective-permute-start = (f32[2,32,512]{2,1,0:T(8,128)}, f32[2,32,512]{2,1,0:T(8,128)S(1)}, u32[]{:S(2)}, u32[]{:S(2)}) collective-permute-start(f32[2,32,512]{2,1,0:T(8,128)} %param.6), channel_id=1, source_target_pairs={{0,4},{4,0},{8,12},{12,8},{16,20},{20,16},{24,28},{28,24},{1,5},{5... | collective-permute-start | bytes 393224 | tf_op jit(solution)/shard_map/ppermute | solution.py:107
  2.1 19.0 %collective-permute-start.1 = (f32[2,32,512]{2,1,0:T(8,128)}, f32[2,32,512]{2,1,0:T(8,128)S(1)}, u32[]{:S(2)}, u32[]{:S(2)}) collective-permute-start(f32[2,32,512]{2,1,0:T(8,128)} %param.6), channel_id=1, source_target_pairs={{0,8},{4,12},{8,0},{12,4},{16,24},{20,28},{24,16},{28,20},{1,9},{5... | collective-permute-start | bytes 393224 | tf_op jit(solution)/shard_map/ppermute | solution.py:107
  3.4 17.8 %collective-permute-start.2 = (f32[2,32,512]{2,1,0:T(8,128)}, f32[2,32,512]{2,1,0:T(8,128)S(1)}, u32[]{:S(2)}, u32[]{:S(2)}) collective-permute-start(f32[2,32,512]{2,1,0:T(8,128)} %param.6), channel_id=1, source_target_pairs={{0,12},{4,8},{8,4},{12,0},{16,28},{20,24},{24,20},{28,16},{1,13},{... | collective-permute-start | bytes 393224 | tf_op jit(solution)/shard_map/ppermute | solution.py:107
  3.4 17.9 %collective-permute-start.3 = (f32[2,32,512]{2,1,0:T(8,128)}, f32[2,32,512]{2,1,0:T(8,128)S(1)}, u32[]{:S(2)}, u32[]{:S(2)}) collective-permute-start(f32[2,32,512]{2,1,0:T(8,128)} %param.6), channel_id=1, source_target_pairs={{0,16},{4,20},{8,24},{12,28},{16,0},{20,4},{24,8},{28,12},{1,17},{... | collective-permute-start | bytes 393224 | tf_op jit(solution)/shard_map/ppermute | solution.py:107
  5.8 15.5 %collective-permute-start.4 = (f32[2,32,512]{2,1,0:T(8,128)}, f32[2,32,512]{2,1,0:T(8,128)S(1)}, u32[]{:S(2)}, u32[]{:S(2)}) collective-permute-start(f32[2,32,512]{2,1,0:T(8,128)} %param.6), channel_id=1, source_target_pairs={{0,20},{4,16},{8,28},{12,24},{16,4},{20,0},{24,12},{28,8},{1,21},{... | collective-permute-start | bytes 393224 | tf_op jit(solution)/shard_map/ppermute | solution.py:107
  17.7 6.1 %collective-permute-start.5 = (f32[2,32,512]{2,1,0:T(8,128)}, f32[2,32,512]{2,1,0:T(8,128)S(1)}, u32[]{:S(2)}, u32[]{:S(2)}) collective-permute-start(f32[2,32,512]{2,1,0:T(8,128)} %param.6), channel_id=1, source_target_pairs={{0,24},{4,28},{8,16},{12,20},{16,8},{20,12},{24,0},{28,4},{1,25},{... | collective-permute-start | bytes 393224 | tf_op jit(solution)/shard_map/ppermute | solution.py:107
  21.1 6.9 %collective-permute-start.6 = (f32[2,32,512]{2,1,0:T(8,128)}, f32[2,32,512]{2,1,0:T(8,128)S(1)}, u32[]{:S(2)}, u32[]{:S(2)}) collective-permute-start(f32[2,32,512]{2,1,0:T(8,128)} %param.6), channel_id=1, source_target_pairs={{0,28},{4,24},{8,20},{12,16},{16,12},{20,8},{24,4},{28,0},{1,29},{... | collective-permute-start | bytes 393224 | tf_op jit(solution)/shard_map/ppermute | solution.py:107
  30.6 13.4 %collective-permute-start.7 = (f32[16,4096]{1,0:T(8,128)S(1)}, f32[16,4096]{1,0:T(8,128)S(1)}, u32[]{:S(2)}, u32[]{:S(2)}) collective-permute-start(f32[16,4096]{1,0:T(8,128)S(1)} %bitcast.164), channel_id=1, source_target_pairs={{0,1},{1,2},{2,3},{4,5},{5,6},{6,7},{8,9},{9,10},{10,11},{12,13},{... | collective-permute-start | bytes 786440 | tf_op jit(solution)/shard_map/ppermute | solution.py:22
  38.7 8.2 %collective-permute-start.8 = (f32[16,4096]{1,0:T(8,128)}, f32[16,4096]{1,0:T(8,128)S(1)}, u32[]{:S(2)}, u32[]{:S(2)}) collective-permute-start(f32[16,4096]{1,0:T(8,128)} %bitcast.49), channel_id=1, source_target_pairs={{1,0},{2,1},{3,2},{5,4},{6,5},{7,6},{9,8},{10,9},{11,10},{13,12},{... | collective-permute-start | bytes 786440 | tf_op jit(solution)/shard_map/ppermute | solution.py:24
  44.1 3.9 %copy-start.3 = (f32[16]{0:T(128)S(1)}, f32[16]{0:T(128)}, u32[]{:S(2)}) copy-start(f32[16]{0:T(128)} %get-tuple-element.49) | copy-start | bytes 196
  44.1 3.9 %copy-start.4 = (f32[16]{0:T(128)S(1)}, f32[16]{0:T(128)}, u32[]{:S(2)}) copy-start(f32[16]{0:T(128)} %get-tuple-element.47) | copy-start | bytes 196
  45.1 3.0 %copy-start.5 = (f32[16]{0:T(128)S(1)}, f32[16]{0:T(128)}, u32[]{:S(2)}) copy-start(f32[16]{0:T(128)} %get-tuple-element.50) | copy-start | bytes 196
  45.1 3.0 %copy-start.6 = (f32[16]{0:T(128)S(1)}, f32[16]{0:T(128)}, u32[]{:S(2)}) copy-start(f32[16]{0:T(128)} %get-tuple-element.48) | copy-start | bytes 196
  46.0 2.3 %copy-start.7 = (f32[32]{0:T(128)S(1)}, f32[32]{0:T(128)}, u32[]{:S(2)}) copy-start(f32[32]{0:T(128)} %slice_bitcast_fusion.18) | copy-start | bytes 388
  46.0 2.3 %copy-start.8 = (f32[32]{0:T(128)S(1)}, f32[32]{0:T(128)}, u32[]{:S(2)}) copy-start(f32[32]{0:T(128)} %slice_bitcast_fusion.19) | copy-start | bytes 388
  47.9 0.8 %copy-start = (f32[32,64]{1,0:T(8,128)S(1)}, f32[32,64]{1,0:T(8,128)}, u32[]{:S(2)}) copy-start(f32[32,64]{1,0:T(8,128)} %neg.4) | copy-start | bytes 24580
  49.9 0.9 %copy-start.1 = (f32[160,128]{1,0:T(8,128)S(1)}, f32[160,128]{1,0:T(8,128)}, u32[]{:S(2)}) copy-start(f32[160,128]{1,0:T(8,128)} %neg.5) | copy-start | bytes 245764
  49.9 0.9 %copy-start.2 = (f32[160,128]{1,0:T(8,128)S(1)}, f32[160,128]{1,0:T(8,128)}, u32[]{:S(2)}) copy-start(f32[160,128]{1,0:T(8,128)} %get-tuple-element.6) | copy-start | bytes 245764
  52.5 10.5 %collective-permute-start.10 = (f32[2,1,16,4096]{3,2,1,0:T(8,128)S(1)}, f32[2,1,16,4096]{3,2,1,0:T(8,128)S(1)}, u32[]{:S(2)}, u32[]{:S(2)}) collective-permute-start(f32[2,1,16,4096]{3,2,1,0:T(8,128)S(1)} %get-tuple-element.18), channel_id=1, source_target_pairs={{1,0},{2,1},{3,2},{5,4},{6,5},{7,6},{9,8},{10,9},{11,10},{13,12},{... | collective-permute-start | bytes 1572872 | tf_op jit(solution)/shard_map/ppermute | solution.py:24
  54.5 9.8 %collective-permute-start.9 = (f32[2,1,16,4096]{3,2,1,0:T(8,128)S(1)}, f32[2,1,16,4096]{3,2,1,0:T(8,128)S(1)}, u32[]{:S(2)}, u32[]{:S(2)}) collective-permute-start(f32[2,1,16,4096]{3,2,1,0:T(8,128)S(1)} %get-tuple-element.17), channel_id=1, source_target_pairs={{0,1},{1,2},{2,3},{4,5},{5,6},{6,7},{8,9},{9,10},{10,11},{12,13},{... | collective-permute-start | bytes 1572872 | tf_op jit(solution)/shard_map/ppermute | solution.py:22

commit v6 on v5

--- a/solution.py
+++ b/solution.py
@@ -94,7 +94,7 @@
     return jnp.stack(planes)
 
 
-def gather_screens(stored_planes, owner, axis):
+def gather_screen(stored, order, axis):
     count = lax.axis_size(axis)
     me = lax.axis_index(axis)
     paired = count & (count - 1) == 0
@@ -102,18 +102,13 @@
     def partner(i, k):
         return i ^ k if paired else (i + k) % count
 
-    parts = [stored_planes]
+    parts = [stored]
     for k in range(1, count):
-        parts.append(lax.ppermute(stored_planes, axis, [(i, partner(i, k)) for i in range(count)]))
-    stacked = jnp.stack(parts, axis=1)
-    rows = stored_planes.shape[1]
-    width = stored_planes.shape[2]
-    planes = []
-    for p in range(stored_planes.shape[0]):
-        source = jnp.bitwise_xor(me, owner[p]) if paired else jnp.mod(me - owner[p], count)
-        picked = stacked[p][source]
-        planes.append(jnp.transpose(picked, (1, 0, 2)).reshape(rows, count * width))
-    return jnp.stack(planes)
+        parts.append(lax.ppermute(stored, axis, [(i, partner(i, k)) for i in range(count)]))
+    stacked = jnp.stack(parts)
+    source = jnp.bitwise_xor(me, order) if paired else jnp.mod(me - order, count)
+    picked = stacked[source]
+    return jnp.transpose(picked, (1, 0, 2)).reshape(stored.shape[0], count * stored.shape[1])
 
 
 def body(tilts, taps, stored_planes, owner):
@@ -121,7 +116,7 @@
     total_rows = local_rows * lax.axis_size("tile")
     total_cols = NY
     first_row = lax.axis_index("tile") * local_rows
-    screens = gather_screens(stored_planes, owner, "illum")
+    screens = [gather_screen(stored_planes[0], owner[0], "illum")]
     extra = HALF
     span = local_rows + 2 * extra
     global_rows = first_row - extra + jnp.arange(span, dtype=jnp.int32)
@@ -142,6 +137,9 @@
         return real, imag
 
     halo = extended(screens[0], (("tile", 0),), HALF)
+    for plane in range(1, PLANES):
+        ready = halo[0, 0] * 0.0 + halo[span - 1, 0] * 0.0
+        screens.append(gather_screen(stored_planes[plane] + ready, owner[plane], "illum"))
     pieces = [
         transmit(*incident(rows), screen)
         for rows, screen in (

time: 70 us -> 79.1 us (1.13)
  starting transfers between devices: 24.4 us -> 34.7 us
  other arithmetic: 9.25 us -> 5.41 us
  waiting for transfers between devices: 12.6 us -> 16.3 us
  local copies, waits for them, and re-layouts: 18.4 us -> 16.8 us
  between operations: 0.63 us -> 1.86 us
    ppermute x7 -> x14, starting transfers between devices: 10.3 us -> 19.7 us  [gather_screen(): lax.ppermute(stored, axis, [(i, partner(i, k)) for i in range(count)])]
    ppermute x2, waiting for transfers between devices: 4.74 us -> 7.26 us  [extended(): lax.ppermute(head, axis, [((i + 1) % count, i) for i in range(ends)])]
    mul x4, local copies, waits for them, and re-layouts: 2.48 us -> 0.29 us  [incident(): real = across_cos[:, rows] * along_cos - across_sin[:, rows] * along_sin]
    unnamed x5, other arithmetic: 2.35 us -> 0.9 us
    ppermute x7 -> x14, waiting for transfers between devices: 6.7 us -> 7.81 us  [gather_screen(): lax.ppermute(stored, axis, [(i, partner(i, k)) for i in range(count)])]
    slice x0 -> x2, local copies, waits for them, and re-layouts: none -> 1.06 us  [body(): ready = halo[0, 0] * 0.0 + halo[span - 1, 0] * 0.0]
    ppermute x2, starting transfers between devices: 10.3 us -> 11.2 us  [extended(): lax.ppermute(tail, axis, [(i, (i + 1) % count) for i in range(ends)])]
    unnamed x38 -> x27, local copies, waits for them, and re-layouts: 3.46 us -> 3.07 us
  transfers between devices with their start and end apart: 11 -> 18, of which waited for: 4 -> 7; matrix products, arithmetic and copies ran while one was open for 27% -> 20% of each run, Pallas kernels for 0% -> 0%
where the time goes in v6:
time: 79.1 us; the launch traced here: 78.7 us
  starting transfers between devices  34.7 us (44%)
  local copies, waits for them, and re-layouts  16.8 us (21%)
  waiting for transfers between devices  16.3 us (21%)
  other arithmetic  5.41 us (7%)
  matrix products  3.64 us (5%)
  between operations  1.86 us (2%)
    ppermute x14, starting transfers between devices, gather_screen(): lax.ppermute(stored, axis, [(i, partner(i, k)) for i in range(count)])  19.7 us
    ppermute x2, starting transfers between devices, extended(): lax.ppermute(tail, axis, [(i, (i + 1) % count) for i in range(ends)])  11.2 us
    ppermute x14, waiting for transfers between devices, gather_screen(): lax.ppermute(stored, axis, [(i, partner(i, k)) for i in range(count)])  7.81 us
    ppermute x2, waiting for transfers between devices, extended(): lax.ppermute(head, axis, [((i + 1) % count, i) for i in range(ends)])  7.26 us
    cos x7, local copies, waits for them, and re-layouts, transmit(): cosine = jnp.cos(screen)  4.59 us
    ppermute x2, starting transfers between devices, extended(): lax.ppermute(head, axis, [((i + 1) % count, i) for i in range(ends)])  3.84 us
    unnamed x27, local copies, waits for them, and re-layouts  3.07 us
    sin x5, local copies, waits for them, and re-layouts, transmit(): sine = jnp.sin(screen)  2.67 us
  transfers between devices with their start and end apart: 18, of which 7 were waited for; matrix products, arithmetic and copies ran while one was open for 20% of the time, Pallas kernels for 0%

profile of v6, /device:TPU:1, one launch (start us, length us, event | category | flops | bytes accessed | tf_op | source)
XLA Modules:
  0.0 78.7 jit_solution(11012594022317189202)
XLA Ops:
  0.0 0.8 %slice_bitcast_fusion.12 = (f32[32,512]{1,0:T(8,128)S(1)}, f32[8,32,512]{2,1,0:T(8,128)S(1)}) fusion(f32[2,32,512]{2,1,0:T(8,128)} %param.6), kind=kLoop, calls=%fused_computation.84 | loop fusion | bytes 196608 | tf_op jit(solution)/shard_map/squeeze | solution.py:119
  0.9 2.1 %collective-permute-start = (f32[32,512]{1,0:T(8,128)S(1)}, f32[32,512]{1,0:T(8,128)S(1)}, u32[]{:S(2)}, u32[]{:S(2)}) collective-permute-start(f32[32,512]{1,0:T(8,128)S(1)} %get-tuple-element.43), channel_id=1, source_target_pairs={{0,4},{4,0},{8,12},{12,8},{16,20},{20,16},{24,28},{28,24},{1,5},{5... | collective-permute-start | bytes 196616 | tf_op jit(solution)/shard_map/ppermute | solution.py:107
  3.0 1.3 %collective-permute-start.1 = (f32[32,512]{1,0:T(8,128)S(1)}, f32[32,512]{1,0:T(8,128)S(1)}, u32[]{:S(2)}, u32[]{:S(2)}) collective-permute-start(f32[32,512]{1,0:T(8,128)S(1)} %get-tuple-element.43), channel_id=1, source_target_pairs={{0,8},{4,12},{8,0},{12,4},{16,24},{20,28},{24,16},{28,20},{1,9},{5... | collective-permute-start | bytes 196616 | tf_op jit(solution)/shard_map/ppermute | solution.py:107
  4.3 2.4 %collective-permute-start.3 = (f32[32,512]{1,0:T(8,128)S(1)}, f32[32,512]{1,0:T(8,128)S(1)}, u32[]{:S(2)}, u32[]{:S(2)}) collective-permute-start(f32[32,512]{1,0:T(8,128)S(1)} %get-tuple-element.43), channel_id=1, source_target_pairs={{0,16},{4,20},{8,24},{12,28},{16,0},{20,4},{24,8},{28,12},{1,17},{... | collective-permute-start | bytes 196616 | tf_op jit(solution)/shard_map/ppermute | solution.py:107
  6.7 1.0 %collective-permute-start.4 = (f32[32,512]{1,0:T(8,128)S(1)}, f32[32,512]{1,0:T(8,128)S(1)}, u32[]{:S(2)}, u32[]{:S(2)}) collective-permute-start(f32[32,512]{1,0:T(8,128)S(1)} %get-tuple-element.43), channel_id=1, source_target_pairs={{0,20},{4,16},{8,28},{12,24},{16,4},{20,0},{24,12},{28,8},{1,21},{... | collective-permute-start | bytes 196616 | tf_op jit(solution)/shard_map/ppermute | solution.py:107
  7.7 1.3 %fusion.45 = (s32[1,1]{1,0:T(1,128)}, s32[1,1]{1,0:T(1,128)}) fusion(s32[1,2]{1,0:T(1,128)} %param.4), kind=kLoop, calls=%fused_computation.136 | loop fusion | bytes 16 | tf_op jit(solution)/shard_map/slice | solution.py:126
  9.1 0.7 sine_select_fusion
  10.1 0.8 fusion.34
  10.8 0.7 fusion.28
  11.5 0.8 slice_bitcast_fusion.14
  13.1 3.4 %collective-permute-start.5 = (f32[32,512]{1,0:T(8,128)S(1)}, f32[32,512]{1,0:T(8,128)S(1)}, u32[]{:S(2)}, u32[]{:S(2)}) collective-permute-start(f32[32,512]{1,0:T(8,128)S(1)} %get-tuple-element.43), channel_id=1, source_target_pairs={{0,24},{4,28},{8,16},{12,20},{16,8},{20,12},{24,0},{28,4},{1,25},{... | collective-permute-start | bytes 196616 | tf_op jit(solution)/shard_map/ppermute | solution.py:107
  16.7 1.5 %collective-permute-done.5 = f32[32,512]{1,0:T(8,128)S(1)} collective-permute-done((f32[32,512]{1,0:T(8,128)S(1)}, f32[32,512]{1,0:T(8,128)S(1)}, u32[]{:S(2)}, u32[]{:S(2)}) %collective-permute-start.5) | collective-permute-done | bytes 65568 | tf_op jit(solution)/shard_map/ppermute | solution.py:107
  18.2 4.3 %collective-permute-done.6 = f32[32,512]{1,0:T(8,128)S(1)} collective-permute-done((f32[32,512]{1,0:T(8,128)S(1)}, f32[32,512]{1,0:T(8,128)S(1)}, u32[]{:S(2)}, u32[]{:S(2)}) %collective-permute-start.6) | collective-permute-done | bytes 65568 | tf_op jit(solution)/shard_map/ppermute | solution.py:107
  23.1 6.4 %collective-permute-start.7 = (f32[16,4096]{1,0:T(8,128)S(1)}, f32[16,4096]{1,0:T(8,128)S(1)}, u32[]{:S(2)}, u32[]{:S(2)}) collective-permute-start(f32[16,4096]{1,0:T(8,128)S(1)} %bitcast.177), channel_id=1, source_target_pairs={{0,1},{1,2},{2,3},{4,5},{5,6},{6,7},{8,9},{9,10},{10,11},{12,13},{... | collective-permute-start | bytes 786440 | tf_op jit(solution)/shard_map/ppermute | solution.py:22
  29.6 1.9 %collective-permute-start.8 = (f32[16,4096]{1,0:T(8,128)S(1)}, f32[16,4096]{1,0:T(8,128)S(1)}, u32[]{:S(2)}, u32[]{:S(2)}) collective-permute-start(f32[16,4096]{1,0:T(8,128)S(1)} %bitcast.178), channel_id=1, source_target_pairs={{1,0},{2,1},{3,2},{5,4},{6,5},{7,6},{9,8},{10,9},{11,10},{13,12},{... | collective-permute-start | bytes 786440 | tf_op jit(solution)/shard_map/ppermute | solution.py:24
  31.5 1.9 %bitcast_cosine_fusion = (f32[32,8,512]{2,0,1:T(8,128)S(1)}, f32[32,8,512]{2,0,1:T(8,128)S(1)}) fusion(f32[8,32,512]{2,1,0:T(8,128)S(1)} %gather_fusion), kind=kLoop, calls=%fused_computation.129 | loop fusion | bytes 1572864 | tf_op jit(solution)/shard_map/cos | solution.py:81
  34.8 2.5 %collective-permute-done.8 = f32[16,4096]{1,0:T(8,128)S(1)} collective-permute-done((f32[16,4096]{1,0:T(8,128)S(1)}, f32[16,4096]{1,0:T(8,128)S(1)}, u32[]{:S(2)}, u32[]{:S(2)}) %collective-permute-start.8) | collective-permute-done | bytes 262176 | tf_op jit(solution)/shard_map/ppermute | solution.py:24
  39.4 2.4 %collective-permute-start.11 = (f32[32,512]{1,0:T(8,128)S(1)}, f32[32,512]{1,0:T(8,128)S(1)}, u32[]{:S(2)}, u32[]{:S(2)}) collective-permute-start(f32[32,512]{1,0:T(8,128)S(1)} %get-tuple-element.41), channel_id=1, source_target_pairs={{0,12},{4,8},{8,4},{12,0},{16,28},{20,24},{24,20},{28,16},{1,13},{... | collective-permute-start | bytes 196616 | tf_op jit(solution)/shard_map/ppermute | solution.py:107
  41.9 2.3 %collective-permute-start.13 = (f32[32,512]{1,0:T(8,128)S(1)}, f32[32,512]{1,0:T(8,128)S(1)}, u32[]{:S(2)}, u32[]{:S(2)}) collective-permute-start(f32[32,512]{1,0:T(8,128)S(1)} %get-tuple-element.41), channel_id=1, source_target_pairs={{0,20},{4,16},{8,28},{12,24},{16,4},{20,0},{24,12},{28,8},{1,21},{... | collective-permute-start | bytes 196616 | tf_op jit(solution)/shard_map/ppermute | solution.py:107
  44.2 0.9 %fusion.44 = (f32[16,4096]{1,0:T(8,128)S(1)}, f32[16,4096]{1,0:T(8,128)S(1)}) fusion(f32[16,4096]{1,0:T(8,128)S(1)} %collective-permute-done.7), kind=kLoop, calls=%fused_computation.135 | loop fusion | bytes 786432 | tf_op jit(solution)/shard_map/cos | solution.py:81
  45.5 1.0 %fusion.43 = (f32[16,4096]{1,0:T(8,128)S(1)}, f32[16,4096]{1,0:T(8,128)S(1)}) fusion(f32[16,4096]{1,0:T(8,128)S(1)} %collective-permute-done.8), kind=kLoop, calls=%fused_computation.134 | loop fusion | bytes 786432 | tf_op jit(solution)/shard_map/cos | solution.py:81
  49.0 1.1 %fusion.18 = f32[1,32,32,256]{3,2,1,0:T(8,128)S(1)} fusion(f32[1,32,32,32]{3,2,1,0:T(8,128)S(1)} %bitcast.170, f32[1,32,32,128]{3,2,1,0:T(8,128)S(1)} %bitcast.172, f32[1,32,32,32]{3,2,1,0:T(8,128)S(1)} %bitcast.174, f32[1,32,32,128]{3,2,1,0:T(8,128)S(1)} %bitcast.176, f32[160,128]{1,0:T(8,128)S(1)} %get-tuple-element.6, f32[160,128]{1,0:T(8,128)S(1)} %neg.5, ...), kind=kOutput, calls=%fused_computation.29 | convolution fusion | flops 504545280 | bytes 2605056 | tf_op jit(solution)/shard_map/...nj,jc->...nc/dot_general | solution.py:68
  51.1 0.8 %bitcast_dynamic-update-slice_fusion.10 = f32[8,32,512]{2,1,0:T(8,128)S(1)} fusion(f32[8,32,512]{2,1,0:T(8,128)S(1)} %get-tuple-element.42, f32[32,512]{1,0:T(8,128)} %collective-permute-done.9), kind=kLoop, calls=%fused_computation.74 | loop fusion | bytes 131072
  51.9 3.8 %collective-permute-start.15 = (f32[32,512]{1,0:T(8,128)S(1)}, f32[32,512]{1,0:T(8,128)S(1)}, u32[]{:S(2)}, u32[]{:S(2)}) collective-permute-start(f32[32,512]{1,0:T(8,128)S(1)} %get-tuple-element.41), channel_id=1, source_target_pairs={{0,28},{4,24},{8,20},{12,16},{16,12},{20,8},{24,4},{28,0},{1,29},{... | collective-permute-start | bytes 196616 | tf_op jit(solution)/shard_map/ppermute | solution.py:107
  56.0 1.8 %collective-permute-done.15 = f32[32,512]{1,0:T(8,128)S(1)} collective-permute-done((f32[32,512]{1,0:T(8,128)S(1)}, f32[32,512]{1,0:T(8,128)S(1)}, u32[]{:S(2)}, u32[]{:S(2)}) %collective-permute-start.15) | collective-permute-done | bytes 65568 | tf_op jit(solution)/shard_map/ppermute | solution.py:107
  58.4 1.9 %sine_bitcast_fusion = (f32[32,8,512]{2,0,1:T(8,128)S(1)}, f32[32,8,512]{2,0,1:T(8,128)S(1)}) fusion(f32[8,32,512]{2,1,0:T(8,128)S(1)} %gather_fusion.1), kind=kLoop, calls=%fused_computation.46 | loop fusion | bytes 1572864 | tf_op jit(solution)/shard_map/sin | solution.py:82
  61.3 1.9 %collective-permute-start.17 = (f32[2,1,16,4096]{3,2,1,0:T(8,128)S(1)}, f32[2,1,16,4096]{3,2,1,0:T(8,128)S(1)}, u32[]{:S(2)}, u32[]{:S(2)}) collective-permute-start(f32[2,1,16,4096]{3,2,1,0:T(8,128)S(1)} %get-tuple-element.18), channel_id=1, source_target_pairs={{1,0},{2,1},{3,2},{5,4},{6,5},{7,6},{9,8},{10,9},{11,10},{13,12},{... | collective-permute-start | bytes 1572872 | tf_op jit(solution)/shard_map/ppermute | solution.py:24
  63.2 4.8 %collective-permute-start.16 = (f32[2,1,16,4096]{3,2,1,0:T(8,128)S(1)}, f32[2,1,16,4096]{3,2,1,0:T(8,128)S(1)}, u32[]{:S(2)}, u32[]{:S(2)}) collective-permute-start(f32[2,1,16,4096]{3,2,1,0:T(8,128)S(1)} %get-tuple-element.17), channel_id=1, source_target_pairs={{0,1},{1,2},{2,3},{4,5},{5,6},{6,7},{8,9},{9,10},{10,11},{12,13},{... | collective-permute-start | bytes 1572872 | tf_op jit(solution)/shard_map/ppermute | solution.py:22
  68.0 4.7 %collective-permute-done.17 = f32[2,1,16,4096]{3,2,1,0:T(8,128)S(1)} collective-permute-done((f32[2,1,16,4096]{3,2,1,0:T(8,128)S(1)}, f32[2,1,16,4096]{3,2,1,0:T(8,128)S(1)}, u32[]{:S(2)}, u32[]{:S(2)}) %collective-permute-start.17) | collective-permute-done | bytes 524320 | tf_op jit(solution)/shard_map/ppermute | solution.py:24
  72.7 1.2 %collective-permute-done.16 = f32[2,1,16,4096]{3,2,1,0:T(8,128)S(1)} collective-permute-done((f32[2,1,16,4096]{3,2,1,0:T(8,128)S(1)}, f32[2,1,16,4096]{3,2,1,0:T(8,128)S(1)}, u32[]{:S(2)}, u32[]{:S(2)}) %collective-permute-start.16) | collective-permute-done | bytes 524320 | tf_op jit(solution)/shard_map/ppermute | solution.py:22
  76.2 1.1 %fusion.17 = f32[1,32,32,256]{3,2,1,0:T(8,128)S(1)} fusion(f32[1,32,32,32]{3,2,1,0:T(8,128)S(1)} %bitcast.169, f32[1,32,32,128]{3,2,1,0:T(8,128)S(1)} %bitcast.171, f32[1,32,32,32]{3,2,1,0:T(8,128)S(1)} %bitcast.173, f32[1,32,32,128]{3,2,1,0:T(8,128)S(1)} %bitcast.175, f32[160,128]{1,0:T(8,128)S(1)} %get-tuple-element.6, f32[160,128]{1,0:T(8,128)S(1)} %neg.5, ...), kind=kOutput, calls=%fused_computation.28 | convolution fusion | flops 504545280 | bytes 2605056 | tf_op jit(solution)/shard_map/...nj,jc->...nc/dot_general | solution.py:68
  77.7 1.0 %pad_maximum_fusion.1 = f32[2,1,32,4096]{3,2,1,0:T(8,128)} fusion(f32[1,1,32,4096]{3,2,1,0:T(8,128)S(1)} %stack_reshape.7, f32[1,1,32,4096]{3,2,1,0:T(8,128)S(1)} %stack_reshape.6), kind=kLoop, calls=%fused_computation.34 | loop fusion | flops 262144 | bytes 2097152 | tf_op jit(solution)/shard_map/stack | solution.py:160
  (93 shorter events, 12.2 us)
Async XLA Ops:
  0.9 12.3 %collective-permute-start = (f32[32,512]{1,0:T(8,128)S(1)}, f32[32,512]{1,0:T(8,128)S(1)}, u32[]{:S(2)}, u32[]{:S(2)}) collective-permute-start(f32[32,512]{1,0:T(8,128)S(1)} %get-tuple-element.43), channel_id=1, source_target_pairs={{0,4},{4,0},{8,12},{12,8},{16,20},{20,16},{24,28},{28,24},{1,5},{5... | collective-permute-start | bytes 196616 | tf_op jit(solution)/shard_map/ppermute | solution.py:107
  3.0 13.5 %collective-permute-start.1 = (f32[32,512]{1,0:T(8,128)S(1)}, f32[32,512]{1,0:T(8,128)S(1)}, u32[]{:S(2)}, u32[]{:S(2)}) collective-permute-start(f32[32,512]{1,0:T(8,128)S(1)} %get-tuple-element.43), channel_id=1, source_target_pairs={{0,8},{4,12},{8,0},{12,4},{16,24},{20,28},{24,16},{28,20},{1,9},{5... | collective-permute-start | bytes 196616 | tf_op jit(solution)/shard_map/ppermute | solution.py:107
  4.3 12.3 %collective-permute-start.2 = (f32[32,512]{1,0:T(8,128)S(1)}, f32[32,512]{1,0:T(8,128)S(1)}, u32[]{:S(2)}, u32[]{:S(2)}) collective-permute-start(f32[32,512]{1,0:T(8,128)S(1)} %get-tuple-element.43), channel_id=1, source_target_pairs={{0,12},{4,8},{8,4},{12,0},{16,28},{20,24},{24,20},{28,16},{1,13},{... | collective-permute-start | bytes 196616 | tf_op jit(solution)/shard_map/ppermute | solution.py:107
  4.3 12.3 %collective-permute-start.3 = (f32[32,512]{1,0:T(8,128)S(1)}, f32[32,512]{1,0:T(8,128)S(1)}, u32[]{:S(2)}, u32[]{:S(2)}) collective-permute-start(f32[32,512]{1,0:T(8,128)S(1)} %get-tuple-element.43), channel_id=1, source_target_pairs={{0,16},{4,20},{8,24},{12,28},{16,0},{20,4},{24,8},{28,12},{1,17},{... | collective-permute-start | bytes 196616 | tf_op jit(solution)/shard_map/ppermute | solution.py:107
  6.7 10.0 %collective-permute-start.4 = (f32[32,512]{1,0:T(8,128)S(1)}, f32[32,512]{1,0:T(8,128)S(1)}, u32[]{:S(2)}, u32[]{:S(2)}) collective-permute-start(f32[32,512]{1,0:T(8,128)S(1)} %get-tuple-element.43), channel_id=1, source_target_pairs={{0,20},{4,16},{8,28},{12,24},{16,4},{20,0},{24,12},{28,8},{1,21},{... | collective-permute-start | bytes 196616 | tf_op jit(solution)/shard_map/ppermute | solution.py:107
  13.1 5.1 %collective-permute-start.5 = (f32[32,512]{1,0:T(8,128)S(1)}, f32[32,512]{1,0:T(8,128)S(1)}, u32[]{:S(2)}, u32[]{:S(2)}) collective-permute-start(f32[32,512]{1,0:T(8,128)S(1)} %get-tuple-element.43), channel_id=1, source_target_pairs={{0,24},{4,28},{8,16},{12,20},{16,8},{20,12},{24,0},{28,4},{1,25},{... | collective-permute-start | bytes 196616 | tf_op jit(solution)/shard_map/ppermute | solution.py:107
  16.5 5.9 %collective-permute-start.6 = (f32[32,512]{1,0:T(8,128)S(1)}, f32[32,512]{1,0:T(8,128)S(1)}, u32[]{:S(2)}, u32[]{:S(2)}) collective-permute-start(f32[32,512]{1,0:T(8,128)S(1)} %get-tuple-element.43), channel_id=1, source_target_pairs={{0,28},{4,24},{8,20},{12,16},{16,12},{20,8},{24,4},{28,0},{1,29},{... | collective-permute-start | bytes 196616 | tf_op jit(solution)/shard_map/ppermute | solution.py:107
  23.1 11.1 %collective-permute-start.7 = (f32[16,4096]{1,0:T(8,128)S(1)}, f32[16,4096]{1,0:T(8,128)S(1)}, u32[]{:S(2)}, u32[]{:S(2)}) collective-permute-start(f32[16,4096]{1,0:T(8,128)S(1)} %bitcast.177), channel_id=1, source_target_pairs={{0,1},{1,2},{2,3},{4,5},{5,6},{6,7},{8,9},{9,10},{10,11},{12,13},{... | collective-permute-start | bytes 786440 | tf_op jit(solution)/shard_map/ppermute | solution.py:22
  29.6 7.7 %collective-permute-start.8 = (f32[16,4096]{1,0:T(8,128)S(1)}, f32[16,4096]{1,0:T(8,128)S(1)}, u32[]{:S(2)}, u32[]{:S(2)}) collective-permute-start(f32[16,4096]{1,0:T(8,128)S(1)} %bitcast.178), channel_id=1, source_target_pairs={{1,0},{2,1},{3,2},{5,4},{6,5},{7,6},{9,8},{10,9},{11,10},{13,12},{... | collective-permute-start | bytes 786440 | tf_op jit(solution)/shard_map/ppermute | solution.py:24
  33.4 5.7 %copy-start = (f32[2,32,512]{2,1,0:T(8,128)S(1)}, f32[2,32,512]{2,1,0:T(8,128)}, u32[]{:S(2)}) copy-start(f32[2,32,512]{2,1,0:T(8,128)} %param.6) | copy-start | bytes 393220
  39.1 11.4 %collective-permute-start.9 = (f32[32,512]{1,0:T(8,128)S(1)}, f32[32,512]{1,0:T(8,128)}, u32[]{:S(2)}, u32[]{:S(2)}) collective-permute-start(f32[32,512]{1,0:T(8,128)S(1)} %get-tuple-element.41), channel_id=1, source_target_pairs={{0,4},{4,0},{8,12},{12,8},{16,20},{20,16},{24,28},{28,24},{1,5},{5... | collective-permute-start | bytes 196616 | tf_op jit(solution)/shard_map/ppermute | solution.py:107
  39.4 12.5 %collective-permute-start.10 = (f32[32,512]{1,0:T(8,128)S(1)}, f32[32,512]{1,0:T(8,128)S(1)}, u32[]{:S(2)}, u32[]{:S(2)}) collective-permute-start(f32[32,512]{1,0:T(8,128)S(1)} %get-tuple-element.41), channel_id=1, source_target_pairs={{0,8},{4,12},{8,0},{12,4},{16,24},{20,28},{24,16},{28,20},{1,9},{5... | collective-permute-start | bytes 196616 | tf_op jit(solution)/shard_map/ppermute | solution.py:107
  39.4 16.3 %collective-permute-start.11 = (f32[32,512]{1,0:T(8,128)S(1)}, f32[32,512]{1,0:T(8,128)S(1)}, u32[]{:S(2)}, u32[]{:S(2)}) collective-permute-start(f32[32,512]{1,0:T(8,128)S(1)} %get-tuple-element.41), channel_id=1, source_target_pairs={{0,12},{4,8},{8,4},{12,0},{16,28},{20,24},{24,20},{28,16},{1,13},{... | collective-permute-start | bytes 196616 | tf_op jit(solution)/shard_map/ppermute | solution.py:107
  41.8 13.9 %collective-permute-start.12 = (f32[32,512]{1,0:T(8,128)S(1)}, f32[32,512]{1,0:T(8,128)S(1)}, u32[]{:S(2)}, u32[]{:S(2)}) collective-permute-start(f32[32,512]{1,0:T(8,128)S(1)} %get-tuple-element.41), channel_id=1, source_target_pairs={{0,16},{4,20},{8,24},{12,28},{16,0},{20,4},{24,8},{28,12},{1,17},{... | collective-permute-start | bytes 196616 | tf_op jit(solution)/shard_map/ppermute | solution.py:107
  41.9 13.9 %collective-permute-start.13 = (f32[32,512]{1,0:T(8,128)S(1)}, f32[32,512]{1,0:T(8,128)S(1)}, u32[]{:S(2)}, u32[]{:S(2)}) collective-permute-start(f32[32,512]{1,0:T(8,128)S(1)} %get-tuple-element.41), channel_id=1, source_target_pairs={{0,20},{4,16},{8,28},{12,24},{16,4},{20,0},{24,12},{28,8},{1,21},{... | collective-permute-start | bytes 196616 | tf_op jit(solution)/shard_map/ppermute | solution.py:107
  50.5 5.5 %collective-permute-start.14 = (f32[32,512]{1,0:T(8,128)S(1)}, f32[32,512]{1,0:T(8,128)S(1)}, u32[]{:S(2)}, u32[]{:S(2)}) collective-permute-start(f32[32,512]{1,0:T(8,128)S(1)} %get-tuple-element.41), channel_id=1, source_target_pairs={{0,24},{4,28},{8,16},{12,20},{16,8},{20,12},{24,0},{28,4},{1,25},{... | collective-permute-start | bytes 196616 | tf_op jit(solution)/shard_map/ppermute | solution.py:107
  51.9 5.9 %collective-permute-start.15 = (f32[32,512]{1,0:T(8,128)S(1)}, f32[32,512]{1,0:T(8,128)S(1)}, u32[]{:S(2)}, u32[]{:S(2)}) collective-permute-start(f32[32,512]{1,0:T(8,128)S(1)} %get-tuple-element.41), channel_id=1, source_target_pairs={{0,28},{4,24},{8,20},{12,16},{16,12},{20,8},{24,4},{28,0},{1,29},{... | collective-permute-start | bytes 196616 | tf_op jit(solution)/shard_map/ppermute | solution.py:107
  61.3 11.4 %collective-permute-start.17 = (f32[2,1,16,4096]{3,2,1,0:T(8,128)S(1)}, f32[2,1,16,4096]{3,2,1,0:T(8,128)S(1)}, u32[]{:S(2)}, u32[]{:S(2)}) collective-permute-start(f32[2,1,16,4096]{3,2,1,0:T(8,128)S(1)} %get-tuple-element.18), channel_id=1, source_target_pairs={{1,0},{2,1},{3,2},{5,4},{6,5},{7,6},{9,8},{10,9},{11,10},{13,12},{... | collective-permute-start | bytes 1572872 | tf_op jit(solution)/shard_map/ppermute | solution.py:24
  63.2 10.7 %collective-permute-start.16 = (f32[2,1,16,4096]{3,2,1,0:T(8,128)S(1)}, f32[2,1,16,4096]{3,2,1,0:T(8,128)S(1)}, u32[]{:S(2)}, u32[]{:S(2)}) collective-permute-start(f32[2,1,16,4096]{3,2,1,0:T(8,128)S(1)} %get-tuple-element.17), channel_id=1, source_target_pairs={{0,1},{1,2},{2,3},{4,5},{5,6},{6,7},{8,9},{9,10},{10,11},{12,13},{... | collective-permute-start | bytes 1572872 | tf_op jit(solution)/shard_map/ppermute | solution.py:22

commit v7 on v3

--- a/solution.py
+++ b/solution.py
@@ -116,32 +116,86 @@
     return jnp.stack(planes)
 
 
+def around(arrays, reaches, axis):
+    count = lax.axis_size(axis)
+    local = arrays[0].shape[0]
+    below = [[] for _ in arrays]
+    above = [[] for _ in arrays]
+    for distance in range(1, max(-(-r // local) for r in reaches) + 1):
+        for down in (True, False):
+            spans = []
+            for x, reach in zip(arrays, reaches):
+                if down:
+                    lo, hi = max(distance * local - reach, 0), local
+                else:
+                    lo, hi = 0, min(local, reach - (distance - 1) * local)
+                spans.append((lo, hi) if hi > lo else None)
+            taken = [x[lo:hi] for x, span in zip(arrays, spans) if span for lo, hi in [span]]
+            if not taken:
+                continue
+            if down:
+                pairs = [(i, i + distance) for i in range(count - distance)]
+            else:
+                pairs = [(i + distance, i) for i in range(count - distance)]
+            got = lax.ppermute(jnp.concatenate(taken, axis=0), axis, pairs)
+            at = 0
+            for k, span in enumerate(spans):
+                if span:
+                    piece = got[at : at + span[1] - span[0]]
+                    at += span[1] - span[0]
+                    if down:
+                        below[k].insert(0, piece)
+                    else:
+                        above[k].append(piece)
+    return [(b, x, a) for b, x, a in zip(below, arrays, above)]
+
+
 def body(tilts, taps, stored_planes, owner):
     local_rows = stored_planes.shape[1]
     total_rows = local_rows * lax.axis_size("tile")
     total_cols = NY
     first_row = lax.axis_index("tile") * local_rows
     screens = gather_screens(stored_planes, owner, "illum")
-    extra = 0
-    span = local_rows + 2 * extra
-    global_rows = first_row - extra + jnp.arange(span, dtype=jnp.int32)
-    inside = (global_rows >= 0) & (global_rows < total_rows)
+    reaches = [(PLANES - plane) * HALF for plane in range(PLANES)]
+    extended_screens = around([screens[plane] for plane in range(PLANES)], reaches, "tile")
     cols = jnp.arange(total_cols, dtype=jnp.int32)
-    across = (
-        jnp.mod(tilts[:, 0:1] * global_rows[None, :], total_rows).astype(jnp.float32) / total_rows
-    )
     along = jnp.mod(tilts[:, 1:2] * cols[None, :], total_cols).astype(jnp.float32) / total_cols
-    across_cos = jnp.where(inside[None, :], jnp.cos(two_pi * across), 0.0)[:, :, None]
-    across_sin = jnp.where(inside[None, :], jnp.sin(two_pi * across), 0.0)[:, :, None]
     along_cos = jnp.cos(two_pi * along)[:, None, :]
     along_sin = jnp.sin(two_pi * along)[:, None, :]
-    real = across_cos * along_cos - across_sin * along_sin
-    imag = across_sin * along_cos + across_cos * along_sin
+
+    def rows_from(start, count):
+        global_rows = first_row + start + jnp.arange(count, dtype=jnp.int32)
+        return global_rows, (global_rows >= 0) & (global_rows < total_rows)
+
+    def incident(start, count):
+        global_rows, inside = rows_from(start, count)
+        across = jnp.mod(tilts[:, 0:1] * global_rows[None, :], total_rows).astype(jnp.float32) / total_rows
+        across_cos = jnp.where(inside[None, :], jnp.cos(two_pi * across), 0.0)[:, :, None]
+        across_sin = jnp.where(inside[None, :], jnp.sin(two_pi * across), 0.0)[:, :, None]
+        real = across_cos * along_cos - across_sin * along_sin
+        imag = across_sin * along_cos + across_cos * along_sin
+        return real, imag
+
+    reach = reaches[0]
+    pieces = []
+    start = -reach
+    for group in extended_screens[0]:
+        for screen in group if isinstance(group, list) else [group]:
+            pieces.append(transmit(*incident(start, screen.shape[0]), screen))
+            start += screen.shape[0]
+    real = jnp.concatenate([piece[0] for piece in pieces], axis=1)
+    imag = jnp.concatenate([piece[1] for piece in pieces], axis=1)
     for plane in range(PLANES):
-        real, imag = transmit(real, imag, screens[plane])
-        packed = extended(jnp.stack([real, imag]), (("tile", 2),), HALF)
-        real, imag = cross_pass(packed[0], packed[1], taps)
+        real, imag = cross_pass(real, imag, taps)
         real, imag = along_pass(real, imag, taps)
+        if plane + 1 < PLANES:
+            reach = reaches[plane + 1]
+            _, inside = rows_from(-reach, local_rows + 2 * reach)
+            below, own, above = extended_screens[plane + 1]
+            screen = jnp.concatenate(below + [own] + above, axis=0)
+            real = jnp.where(inside[None, :, None], real, 0.0)
+            imag = jnp.where(inside[None, :, None], imag, 0.0)
+            real, imag = transmit(real, imag, screen)
     return jnp.stack([real, imag])
 
 

time: 71.1 us -> 82.1 us (1.15)
  the two profiles are of different devices: /device:TPU:18 before, /device:TPU:17 now
where the time goes in v7:
time: 82.1 us; the launch traced here: 81.7 us
  other arithmetic  24.5 us (30%)
  waiting for transfers between devices  22.4 us (27%)
  local copies, waits for them, and re-layouts  14.6 us (18%)
  starting transfers between devices  14.4 us (18%)
  matrix products  5.31 us (6%)
    ppermute x7, waiting for transfers between devices, gather_screens(): lax.ppermute(stored_planes, axis, [(i, partner(i, k)) for i in range(coun...  15.5 us
    unnamed x5, other arithmetic  7.68 us
    ppermute x7, starting transfers between devices, gather_screens(): lax.ppermute(stored_planes, axis, [(i, partner(i, k)) for i in range(coun...  7.51 us
    ppermute x2, waiting for transfers between devices, around(): got = lax.ppermute(jnp.concatenate(taken, axis=0), axis, pairs)  6.9 us
    ppermute x2, starting transfers between devices, around(): got = lax.ppermute(jnp.concatenate(taken, axis=0), axis, pairs)  6.84 us
    sub x1, other arithmetic, transmit(): return (real * cosine - imag * sine, real * sine + imag * cosine)  5.13 us
    unnamed x40, local copies, waits for them, and re-layouts  4.11 us
    select_n x3, other arithmetic, incident(): jnp.where(inside[None, :], jnp.sin(two_pi * across), 0.0)[:, :, None]  3.71 us
  transfers between devices with their start and end apart: 9, of which 4 were waited for; matrix products, arithmetic and copies ran while one was open for 22% of the time, Pallas kernels for 0%

profile of v7, /device:TPU:17, one launch (start us, length us, event | category | flops | bytes accessed | tf_op | source)
XLA Modules:
  0.0 81.7 jit_solution(11700217869401694718)
XLA Ops:
  0.0 1.2 %collective-permute-start = (f32[2,32,512]{2,1,0:T(8,128)}, f32[2,32,512]{2,1,0:T(8,128)S(1)}, u32[]{:S(2)}, u32[]{:S(2)}) collective-permute-start(f32[2,32,512]{2,1,0:T(8,128)} %param.6), channel_id=1, source_target_pairs={{0,4},{4,0},{8,12},{12,8},{16,20},{20,16},{24,28},{28,24},{1,5},{5... | collective-permute-start | bytes 393224 | tf_op jit(solution)/shard_map/ppermute | solution.py:107
  1.2 1.3 %collective-permute-start.1 = (f32[2,32,512]{2,1,0:T(8,128)}, f32[2,32,512]{2,1,0:T(8,128)S(1)}, u32[]{:S(2)}, u32[]{:S(2)}) collective-permute-start(f32[2,32,512]{2,1,0:T(8,128)} %param.6), channel_id=1, source_target_pairs={{0,8},{4,12},{8,0},{12,4},{16,24},{20,28},{24,16},{28,20},{1,9},{5... | collective-permute-start | bytes 393224 | tf_op jit(solution)/shard_map/ppermute | solution.py:107
  2.7 3.3 %collective-permute-start.4 = (f32[2,32,512]{2,1,0:T(8,128)}, f32[2,32,512]{2,1,0:T(8,128)S(1)}, u32[]{:S(2)}, u32[]{:S(2)}) collective-permute-start(f32[2,32,512]{2,1,0:T(8,128)} %param.6), channel_id=1, source_target_pairs={{0,20},{4,16},{8,28},{12,24},{16,4},{20,0},{24,12},{28,8},{1,21},{... | collective-permute-start | bytes 393224 | tf_op jit(solution)/shard_map/ppermute | solution.py:107
  6.0 0.9 %bitcast_dynamic-update-slice_fusion.11 = f32[2,8,32,512]{3,2,0,1:T(8,128)S(1)} fusion(f32[2,32,512]{2,1,0:T(8,128)} %param.6), kind=kLoop, calls=%fused_computation.90 | loop fusion | bytes 262144
  7.0 0.8 slice_bitcast_fusion.15
  8.8 0.8 fusion.53
  9.6 1.3 %fusion.62 = (s32[1,1]{1,0:T(1,128)}, s32[1,1]{1,0:T(1,128)}) fusion(s32[1,2]{1,0:T(1,128)} %param.4), kind=kLoop, calls=%fused_computation.159 | loop fusion | bytes 16 | tf_op jit(solution)/shard_map/slice | solution.py:172
  11.8 1.3 %collective-permute-start.6 = (f32[2,32,512]{2,1,0:T(8,128)}, f32[2,32,512]{2,1,0:T(8,128)S(1)}, u32[]{:S(2)}, u32[]{:S(2)}) collective-permute-start(f32[2,32,512]{2,1,0:T(8,128)} %param.6), channel_id=1, source_target_pairs={{0,28},{4,24},{8,20},{12,16},{16,12},{20,8},{24,4},{28,0},{1,29},{... | collective-permute-start | bytes 393224 | tf_op jit(solution)/shard_map/ppermute | solution.py:107
  13.6 10.6 %collective-permute-done.5 = f32[2,32,512]{2,1,0:T(8,128)S(1)} collective-permute-done((f32[2,32,512]{2,1,0:T(8,128)}, f32[2,32,512]{2,1,0:T(8,128)S(1)}, u32[]{:S(2)}, u32[]{:S(2)}) %collective-permute-start.5) | collective-permute-done | bytes 131104 | tf_op jit(solution)/shard_map/ppermute | solution.py:107
  24.2 4.5 %collective-permute-done.6 = f32[2,32,512]{2,1,0:T(8,128)S(1)} collective-permute-done((f32[2,32,512]{2,1,0:T(8,128)}, f32[2,32,512]{2,1,0:T(8,128)S(1)}, u32[]{:S(2)}, u32[]{:S(2)}) %collective-permute-start.6) | collective-permute-done | bytes 131104 | tf_op jit(solution)/shard_map/ppermute | solution.py:107
  30.1 1.3 %pad_maximum_fusion.2 = (f32[48,4096]{1,0:T(8,128)}, f32[48,4096]{1,0:T(8,128)}) fusion(f32[32,4096]{1,0:T(8,128)S(1)} %bitcast.145, f32[16,4096]{1,0:T(8,128)S(1)} %bitcast.147, f32[16,4096]{1,0:T(8,128)S(1)} %bitcast.146), kind=kLoop, calls=%fused_computation.40 | loop fusion | flops 393216 | bytes 2621440 | tf_op jit(solution)/shard_map/concatenate | solution.py:140
  31.4 4.7 %collective-permute-start.7 = (f32[48,4096]{1,0:T(8,128)}, f32[48,4096]{1,0:T(8,128)S(1)}, u32[]{:S(2)}, u32[]{:S(2)}) collective-permute-start(f32[48,4096]{1,0:T(8,128)} %get-tuple-element.32), channel_id=1, source_target_pairs={{0,1},{1,2},{2,3},{4,5},{5,6},{6,7},{8,9},{9,10},{10,11},{12,13},{... | collective-permute-start | bytes 2359304 | tf_op jit(solution)/shard_map/ppermute | solution.py:140
  36.6 1.2 %sine_select_fusion.1 = (f32[32]{0:T(128)}, f32[32]{0:T(128)}) fusion(s32[]{:T(128)S(6)} %mul.439, s32[]{:T(128)} %bitcast), kind=kLoop, calls=%fused_computation.145 | loop fusion | flops 640 | bytes 264 | tf_op jit(solution)/shard_map/jit(_where)/select_n | solution.py:174
  37.8 1.3 %sine_select_fusion.2 = (f32[32]{0:T(128)}, f32[32]{0:T(128)}) fusion(s32[]{:T(128)S(6)} %add.212, s32[]{:T(128)} %bitcast), kind=kLoop, calls=%fused_computation.148 | loop fusion | flops 640 | bytes 264 | tf_op jit(solution)/shard_map/jit(_where)/select_n | solution.py:174
  39.1 1.2 %sine_select_fusion = (f32[32]{0:T(128)}, f32[32]{0:T(128)}) fusion(s32[]{:T(128)S(6)} %add.224, s32[]{:T(128)} %bitcast), kind=kLoop, calls=%fused_computation.142 | loop fusion | flops 640 | bytes 264 | tf_op jit(solution)/shard_map/jit(_where)/select_n | solution.py:174
  40.3 0.7 fusion.41
  41.4 1.9 %bitcast_cosine_fusion = (f32[32,8,512]{2,0,1:T(8,128)S(1)}, f32[32,8,512]{2,0,1:T(8,128)S(1)}) fusion(f32[8,32,512]{2,1,0:T(8,128)S(1)} %gather_fusion), kind=kLoop, calls=%fused_computation.53 | loop fusion | bytes 1572864 | tf_op jit(solution)/shard_map/cos | solution.py:81
  44.1 2.1 %collective-permute-start.8 = (f32[48,4096]{1,0:T(8,128)}, f32[48,4096]{1,0:T(8,128)S(1)}, u32[]{:S(2)}, u32[]{:S(2)}) collective-permute-start(f32[48,4096]{1,0:T(8,128)} %get-tuple-element.31), channel_id=1, source_target_pairs={{1,0},{2,1},{3,2},{5,4},{6,5},{7,6},{9,8},{10,9},{11,10},{13,12},{... | collective-permute-start | bytes 2359304 | tf_op jit(solution)/shard_map/ppermute | solution.py:140
  46.2 0.9 %concatenate.88 = f32[1,32,4096]{2,1,0:T(8,128)} reshape(f32[32,8,512]{2,1,0:T(8,128)S(1)} %copy.16) | data formatting | bytes 1048576 | tf_op jit(solution)/shard_map/concatenate | solution.py:195
  47.2 2.7 %bitcast_dynamic-update-slice_fusion.3 = f32[1,192,4096]{2,1,0:T(8,128)S(1)} fusion(f32[48,4096]{1,0:T(8,128)S(1)} %collective-permute-done.7, f32[4096]{0:T(1024)S(1)} %get-tuple-element.45, f32[32]{0:T(128)} %get-tuple-element.49, f32[4096]{0:T(1024)S(1)} %get-tuple-element.46, f32[32]{0:T(128)} %get-tuple-element.50), kind=kLoop, calls=%fused_computation.52 | loop fusion | flops 1179647 | bytes 1081600
  49.8 0.9 %subtract_dynamic-update-slice_fusion = f32[1,192,4096]{2,1,0:T(8,128)S(1)} fusion(f32[1,192,4096]{2,1,0:T(8,128)S(1)} %bitcast_dynamic-update-slice_fusion.3, f32[1,32,4096]{2,1,0:T(8,128)S(1)} %sin.78, f32[1,32,4096]{2,1,0:T(8,128)S(1)} %cos.78, f32[4096]{0:T(1024)S(1)} %get-tuple-element.45, f32[32]{0:T(128)} %get-tuple-element.47, ...), kind=kLoop, calls=%fused_computation.62 | loop fusion | flops 1179648 | bytes 1605888
  50.7 6.9 %collective-permute-done.8 = f32[48,4096]{1,0:T(8,128)S(1)} collective-permute-done((f32[48,4096]{1,0:T(8,128)}, f32[48,4096]{1,0:T(8,128)S(1)}, u32[]{:S(2)}, u32[]{:S(2)}) %collective-permute-start.8) | collective-permute-done | bytes 786464 | tf_op jit(solution)/shard_map/ppermute | solution.py:140
  57.6 2.0 %bitcast_dynamic-update-slice_fusion.2 = f32[1,192,4096]{2,1,0:T(8,128)S(1)} fusion(f32[1,192,4096]{2,1,0:T(8,128)S(1)} %subtract_dynamic-update-slice_fusion, f32[48,4096]{1,0:T(8,128)S(1)} %collective-permute-done.8, f32[32]{0:T(128)S(1)} %copy-done.3, f32[32]{0:T(128)S(1)} %copy-done.4, f32[4096]{0:T(1024)S(1)} %get-tuple-element.45, ...), kind=kLoop, calls=%fused_computation.51 | loop fusion | flops 1179648 | bytes 1082368
  59.6 2.0 %bitcast_dynamic-update-slice_fusion.1 = f32[1,192,4096]{2,1,0:T(8,128)S(1)} fusion(f32[1,192,4096]{2,1,0:T(8,128)S(1)} %bitcast_dynamic-update-slice_fusion.2, f32[48,4096]{1,0:T(8,128)S(1)} %collective-permute-done.7, f32[4096]{0:T(1024)S(1)} %get-tuple-element.45, f32[32]{0:T(128)S(1)} %copy-done.5, f32[4096]{0:T(1024)S(1)} %get-tuple-element.46, ...), kind=kLoop, calls=%fused_computation.50 | loop fusion | flops 1179648 | bytes 1082368
  61.8 2.0 %bitcast_dynamic-update-slice_fusion = f32[1,192,4096]{2,1,0:T(8,128)S(1)} fusion(f32[1,192,4096]{2,1,0:T(8,128)S(1)} %add_dynamic-update-slice_fusion, f32[48,4096]{1,0:T(8,128)S(1)} %collective-permute-done.8, f32[32]{0:T(128)S(1)} %copy-done.3, f32[32]{0:T(128)S(1)} %copy-done.4, f32[4096]{0:T(1024)S(1)} %get-tuple-element.45, f32[4096]{0:T(1024)S(1)} %get-tuple-element.46), kind=kLoop, calls=%fused_computation.49 | loop fusion | flops 1179648 | bytes 1082368 | tf_op jit(solution)/shard_map/concatenate | solution.py:75
  63.8 1.1 %convolution_bitcast_fusion = f32[1,128,4096]{2,1,0:T(8,128)S(1)} fusion(f32[1,192,4096]{2,1,0:T(8,128)S(1)} %bitcast_dynamic-update-slice_fusion, f32[64,96]{1,0:T(8,128)S(1)} %get-tuple-element.8, f32[64,96]{1,0:T(8,128)S(1)} %get-tuple-element.7, f32[64,96]{1,0:T(8,128)S(1)} %neg.12), kind=kOutput, calls=%fused_computation.2 | convolution fusion | flops 604053504 | bytes 5316608 | tf_op jit(solution)/shard_map/ij,ajy->aiy/dot_general | solution.py:76
  67.1 2.4 %fusion.10 = f32[1,64,32,256]{3,2,1,0:T(8,128)S(1)} fusion(f32[1,64,32,32]{3,2,1,0:T(8,128)S(1)} %bitcast.148, f32[1,64,32,128]{3,2,1,0:T(8,128)S(1)} %bitcast.151, f32[1,64,32,32]{3,2,1,0:T(8,128)S(1)} %bitcast.149, f32[1,64,32,128]{3,2,1,0:T(8,128)S(1)} %bitcast.150, f32[160,128]{1,0:T(8,128)S(1)} %get-tuple-element.6, f32[160,128]{1,0:T(8,128)S(1)} %neg.13, ...), kind=kOutput, calls=%fused_computation.19 | convolution fusion | flops 1008844800 | bytes 4964352 | tf_op jit(solution)/shard_map/...nj,jc->...nc/dot_general | solution.py:68
  70.2 1.0 %slice_bitcast_fusion.10 = f32[1,16,4096]{2,1,0:T(8,128)S(1)} fusion(f32[48,4096]{1,0:T(8,128)} %copy-done.1), kind=kLoop, calls=%fused_computation.72 | loop fusion | bytes 524288 | tf_op jit(solution)/shard_map/concatenate | solution.py:195
  71.1 1.0 %slice_bitcast_fusion.11 = f32[1,16,4096]{2,1,0:T(8,128)S(1)} fusion(f32[48,4096]{1,0:T(8,128)} %copy-done), kind=kLoop, calls=%fused_computation.73 | loop fusion | bytes 524288 | tf_op jit(solution)/shard_map/concatenate | solution.py:195
  72.1 5.1 %multiply_subtract_fusion = (f32[1,64,4096]{2,1,0:T(8,128)S(1)}, f32[1,64,4096]{2,1,0:T(8,128)S(1)}) fusion(f32[1,64,4096]{2,1,0:T(8,128)S(1)} %reshape.983, f32[1,64,4096]{2,1,0:T(8,128)S(1)} %reshape.982, f32[1,16,4096]{2,1,0:T(8,128)S(1)} %slice_bitcast_fusion.10, f32[1,32,4096]{2,1,0:T(8,128)} %concatenate.88, ...), kind=kLoop, calls=%fused_computation.35 | loop fusion | flops 2621440 | bytes 5242944 | tf_op jit(solution)/shard_map/sub | solution.py:83
  79.1 1.1 %fusion.18 = f32[1,32,32,256]{3,2,1,0:T(8,128)S(1)} fusion(f32[1,32,32,32]{3,2,1,0:T(8,128)S(1)} %bitcast.152, f32[1,32,32,128]{3,2,1,0:T(8,128)S(1)} %bitcast.155, f32[1,32,32,32]{3,2,1,0:T(8,128)S(1)} %bitcast.153, f32[1,32,32,128]{3,2,1,0:T(8,128)S(1)} %bitcast.154, f32[160,128]{1,0:T(8,128)S(1)} %get-tuple-element.6, f32[160,128]{1,0:T(8,128)S(1)} %neg.13, ...), kind=kOutput, calls=%fused_computation.28 | convolution fusion | flops 504545280 | bytes 2605056 | tf_op jit(solution)/shard_map/...nj,jc->...nc/dot_general | solution.py:68
  80.6 1.0 %pad_maximum_fusion.1 = f32[2,1,32,4096]{3,2,1,0:T(8,128)} fusion(f32[1,1,32,4096]{3,2,1,0:T(8,128)S(1)} %stack_reshape.7, f32[1,1,32,4096]{3,2,1,0:T(8,128)S(1)} %stack_reshape.6), kind=kLoop, calls=%fused_computation.33 | loop fusion | flops 262144 | bytes 2097152 | tf_op jit(solution)/shard_map/stack | solution.py:199
  (81 shorter events, 10.7 us)
Async XLA Ops:
  0.0 11.5 %collective-permute-start = (f32[2,32,512]{2,1,0:T(8,128)}, f32[2,32,512]{2,1,0:T(8,128)S(1)}, u32[]{:S(2)}, u32[]{:S(2)}) collective-permute-start(f32[2,32,512]{2,1,0:T(8,128)} %param.6), channel_id=1, source_target_pairs={{0,4},{4,0},{8,12},{12,8},{16,20},{20,16},{24,28},{28,24},{1,5},{5... | collective-permute-start | bytes 393224 | tf_op jit(solution)/shard_map/ppermute | solution.py:107
  1.2 10.5 %collective-permute-start.1 = (f32[2,32,512]{2,1,0:T(8,128)}, f32[2,32,512]{2,1,0:T(8,128)S(1)}, u32[]{:S(2)}, u32[]{:S(2)}) collective-permute-start(f32[2,32,512]{2,1,0:T(8,128)} %param.6), channel_id=1, source_target_pairs={{0,8},{4,12},{8,0},{12,4},{16,24},{20,28},{24,16},{28,20},{1,9},{5... | collective-permute-start | bytes 393224 | tf_op jit(solution)/shard_map/ppermute | solution.py:107
  2.5 10.6 %collective-permute-start.2 = (f32[2,32,512]{2,1,0:T(8,128)}, f32[2,32,512]{2,1,0:T(8,128)S(1)}, u32[]{:S(2)}, u32[]{:S(2)}) collective-permute-start(f32[2,32,512]{2,1,0:T(8,128)} %param.6), channel_id=1, source_target_pairs={{0,12},{4,8},{8,4},{12,0},{16,28},{20,24},{24,20},{28,16},{1,13},{... | collective-permute-start | bytes 393224 | tf_op jit(solution)/shard_map/ppermute | solution.py:107
  2.6 10.5 %collective-permute-start.3 = (f32[2,32,512]{2,1,0:T(8,128)}, f32[2,32,512]{2,1,0:T(8,128)S(1)}, u32[]{:S(2)}, u32[]{:S(2)}) collective-permute-start(f32[2,32,512]{2,1,0:T(8,128)} %param.6), channel_id=1, source_target_pairs={{0,16},{4,20},{8,24},{12,28},{16,0},{20,4},{24,8},{28,12},{1,17},{... | collective-permute-start | bytes 393224 | tf_op jit(solution)/shard_map/ppermute | solution.py:107
  2.7 10.9 %collective-permute-start.4 = (f32[2,32,512]{2,1,0:T(8,128)}, f32[2,32,512]{2,1,0:T(8,128)S(1)}, u32[]{:S(2)}, u32[]{:S(2)}) collective-permute-start(f32[2,32,512]{2,1,0:T(8,128)} %param.6), channel_id=1, source_target_pairs={{0,20},{4,16},{8,28},{12,24},{16,4},{20,0},{24,12},{28,8},{1,21},{... | collective-permute-start | bytes 393224 | tf_op jit(solution)/shard_map/ppermute | solution.py:107
  11.5 12.6 %collective-permute-start.5 = (f32[2,32,512]{2,1,0:T(8,128)}, f32[2,32,512]{2,1,0:T(8,128)S(1)}, u32[]{:S(2)}, u32[]{:S(2)}) collective-permute-start(f32[2,32,512]{2,1,0:T(8,128)} %param.6), channel_id=1, source_target_pairs={{0,24},{4,28},{8,16},{12,20},{16,8},{20,12},{24,0},{28,4},{1,25},{... | collective-permute-start | bytes 393224 | tf_op jit(solution)/shard_map/ppermute | solution.py:107
  11.8 16.9 %collective-permute-start.6 = (f32[2,32,512]{2,1,0:T(8,128)}, f32[2,32,512]{2,1,0:T(8,128)S(1)}, u32[]{:S(2)}, u32[]{:S(2)}) collective-permute-start(f32[2,32,512]{2,1,0:T(8,128)} %param.6), channel_id=1, source_target_pairs={{0,28},{4,24},{8,20},{12,16},{16,12},{20,8},{24,4},{28,0},{1,29},{... | collective-permute-start | bytes 393224 | tf_op jit(solution)/shard_map/ppermute | solution.py:107
  31.4 15.8 %collective-permute-start.7 = (f32[48,4096]{1,0:T(8,128)}, f32[48,4096]{1,0:T(8,128)S(1)}, u32[]{:S(2)}, u32[]{:S(2)}) collective-permute-start(f32[48,4096]{1,0:T(8,128)} %get-tuple-element.32), channel_id=1, source_target_pairs={{0,1},{1,2},{2,3},{4,5},{5,6},{6,7},{8,9},{9,10},{10,11},{12,13},{... | collective-permute-start | bytes 2359304 | tf_op jit(solution)/shard_map/ppermute | solution.py:140
  44.1 13.5 %collective-permute-start.8 = (f32[48,4096]{1,0:T(8,128)}, f32[48,4096]{1,0:T(8,128)S(1)}, u32[]{:S(2)}, u32[]{:S(2)}) collective-permute-start(f32[48,4096]{1,0:T(8,128)} %get-tuple-element.31), channel_id=1, source_target_pairs={{1,0},{2,1},{3,2},{5,4},{6,5},{7,6},{9,8},{10,9},{11,10},{13,12},{... | collective-permute-start | bytes 2359304 | tf_op jit(solution)/shard_map/ppermute | solution.py:140
  47.1 10.5 %copy-start.3 = (f32[32]{0:T(128)S(1)}, f32[32]{0:T(128)}, u32[]{:S(2)}) copy-start(f32[32]{0:T(128)} %get-tuple-element.51) | copy-start | bytes 388
  47.1 10.5 %copy-start.4 = (f32[32]{0:T(128)S(1)}, f32[32]{0:T(128)}, u32[]{:S(2)}) copy-start(f32[32]{0:T(128)} %get-tuple-element.52) | copy-start | bytes 388
  47.1 12.5 %copy-start.5 = (f32[32]{0:T(128)S(1)}, f32[32]{0:T(128)}, u32[]{:S(2)}) copy-start(f32[32]{0:T(128)} %get-tuple-element.49) | copy-start | bytes 388
  47.1 12.5 %copy-start.6 = (f32[32]{0:T(128)S(1)}, f32[32]{0:T(128)}, u32[]{:S(2)}) copy-start(f32[32]{0:T(128)} %get-tuple-element.50) | copy-start | bytes 388
  47.1 14.4 %copy-start.7 = (f32[32]{0:T(128)S(1)}, f32[32]{0:T(128)}, u32[]{:S(2)}) copy-start(f32[32]{0:T(128)} %get-tuple-element.47) | copy-start | bytes 388
  47.1 14.4 %copy-start.8 = (f32[32]{0:T(128)S(1)}, f32[32]{0:T(128)}, u32[]{:S(2)}) copy-start(f32[32]{0:T(128)} %get-tuple-element.48) | copy-start | bytes 388
  47.1 14.7 %copy-start = (f32[48,4096]{1,0:T(8,128)}, f32[48,4096]{1,0:T(8,128)S(1)}, u32[]{:S(2)}) copy-start(f32[48,4096]{1,0:T(8,128)S(1)} %collective-permute-done.7) | copy-start | bytes 2359300
  57.6 7.3 %copy-start.1 = (f32[48,4096]{1,0:T(8,128)}, f32[48,4096]{1,0:T(8,128)S(1)}, u32[]{:S(2)}) copy-start(f32[48,4096]{1,0:T(8,128)S(1)} %collective-permute-done.8) | copy-start | bytes 2359300
  69.8 2.4 %copy-start.9 = (pred[64]{0:T(512)(128)(4,1)S(1)}, pred[64]{0:T(512)(128)(4,1)}, u32[]{:S(2)}) copy-start(pred[64]{0:T(512)(128)(4,1)} %compare_and_fusion.3) | copy-start | bytes 196
  72.1 5.1 %copy-start.2 = (f32[32,64]{1,0:T(8,128)S(1)}, f32[32,64]{1,0:T(8,128)}, u32[]{:S(2)}) copy-start(f32[32,64]{1,0:T(8,128)} %neg.14) | copy-start | bytes 24580

commit v8 on v5

--- a/solution.py
+++ b/solution.py
@@ -102,9 +102,17 @@
     def partner(i, k):
         return i ^ k if paired else (i + k) % count
 
-    parts = [stored_planes]
-    for k in range(1, count):
-        parts.append(lax.ppermute(stored_planes, axis, [(i, partner(i, k)) for i in range(count)]))
+    def exchange(x, k):
+        return lax.ppermute(x, axis, [(i, partner(i, k)) for i in range(count)])
+
+    if count == 8:
+        one, two, four = (exchange(stored_planes, k) for k in (1, 2, 4))
+        three, five = exchange(jnp.stack([two, four]), 1)
+        six = exchange(four, 2)
+        seven = exchange(one, 6)
+        parts = [stored_planes, one, two, three, four, five, six, seven]
+    else:
+        parts = [stored_planes] + [exchange(stored_planes, k) for k in range(1, count)]
     stacked = jnp.stack(parts, axis=1)
     rows = stored_planes.shape[1]
     width = stored_planes.shape[2]

time: 70 us -> 66.4 us (0.949)
  starting transfers between devices: 24.4 us -> 20.1 us
  waiting for transfers between devices: 12.6 us -> 14.2 us
    ppermute x7 -> x6, starting transfers between devices: 10.3 us -> 7.2 us  [exchange(): return lax.ppermute(x, axis, [(i, partner(i, k)) for i in range(count)])]
    ppermute x2, waiting for transfers between devices: 1.18 us -> 4 us  [extended(): lax.ppermute(tail, axis, [(i, (i + 1) % count) for i in range(ends)])]
    ppermute x2, starting transfers between devices: 10.3 us -> 8.93 us  [extended(): lax.ppermute(tail, axis, [(i, (i + 1) % count) for i in range(ends)])]
    ppermute x7 -> x6, waiting for transfers between devices: 6.7 us -> 5.79 us  [exchange(): return lax.ppermute(x, axis, [(i, partner(i, k)) for i in range(count)])]
  transfers between devices with their start and end apart: 11 -> 10, of which waited for: 4 -> 4; matrix products, arithmetic and copies ran while one was open for 27% -> 28% of each run, Pallas kernels for 0% -> 0%
where the time goes in v8:
time: 66.4 us; the launch traced here: 66 us
  starting transfers between devices  20.1 us (30%)
  local copies, waits for them, and re-layouts  18.3 us (28%)
  waiting for transfers between devices  14.2 us (21%)
  other arithmetic  9.17 us (14%)
  matrix products  3.64 us (5%)
    ppermute x2, starting transfers between devices, extended(): lax.ppermute(tail, axis, [(i, (i + 1) % count) for i in range(ends)])  8.93 us
    ppermute x6, starting transfers between devices, exchange(): return lax.ppermute(x, axis, [(i, partner(i, k)) for i in range(count)])  7.2 us
    ppermute x6, waiting for transfers between devices, exchange(): return lax.ppermute(x, axis, [(i, partner(i, k)) for i in range(count)])  5.79 us
    cos x7, local copies, waits for them, and re-layouts, transmit(): cosine = jnp.cos(screen)  4.61 us
    ppermute x2, waiting for transfers between devices, extended(): lax.ppermute(head, axis, [((i + 1) % count, i) for i in range(ends)])  4.4 us
    ppermute x2, starting transfers between devices, extended(): lax.ppermute(head, axis, [((i + 1) % count, i) for i in range(ends)])  4.01 us
    ppermute x2, waiting for transfers between devices, extended(): lax.ppermute(tail, axis, [(i, (i + 1) % count) for i in range(ends)])  4 us
    unnamed x38, local copies, waits for them, and re-layouts  3.46 us
  transfers between devices with their start and end apart: 10, of which 4 were waited for; matrix products, arithmetic and copies ran while one was open for 28% of the time, Pallas kernels for 0%

profile of v8, /device:TPU:1, one launch (start us, length us, event | category | flops | bytes accessed | tf_op | source)
XLA Modules:
  0.0 66.0 jit_solution(16263988716971486697)
XLA Ops:
  0.0 3.1 %collective-permute-start.2 = (f32[2,32,512]{2,1,0:T(8,128)}, f32[2,32,512]{2,1,0:T(8,128)S(1)}, u32[]{:S(2)}, u32[]{:S(2)}) collective-permute-start(f32[2,32,512]{2,1,0:T(8,128)} %param.6), channel_id=1, source_target_pairs={{0,16},{4,20},{8,24},{12,28},{16,0},{20,4},{24,8},{28,12},{1,17},{... | collective-permute-start | bytes 393224 | tf_op jit(solution)/shard_map/ppermute | solution.py:106
  3.1 1.3 %collective-permute-start.1 = (f32[2,32,512]{2,1,0:T(8,128)}, f32[2,32,512]{2,1,0:T(8,128)S(1)}, u32[]{:S(2)}, u32[]{:S(2)}) collective-permute-start(f32[2,32,512]{2,1,0:T(8,128)} %param.6), channel_id=1, source_target_pairs={{0,8},{4,12},{8,0},{12,4},{16,24},{20,28},{24,16},{28,20},{1,9},{5... | collective-permute-start | bytes 393224 | tf_op jit(solution)/shard_map/ppermute | solution.py:106
  4.4 1.2 %collective-permute-start = (f32[2,32,512]{2,1,0:T(8,128)}, f32[2,32,512]{2,1,0:T(8,128)S(1)}, u32[]{:S(2)}, u32[]{:S(2)}) collective-permute-start(f32[2,32,512]{2,1,0:T(8,128)} %param.6), channel_id=1, source_target_pairs={{0,4},{4,0},{8,12},{12,8},{16,20},{20,16},{24,28},{28,24},{1,5},{5... | collective-permute-start | bytes 393224 | tf_op jit(solution)/shard_map/ppermute | solution.py:106
  5.7 0.9 %bitcast_dynamic-update-slice_fusion.9 = f32[2,8,32,512]{3,2,0,1:T(8,128)S(1)} fusion(f32[2,32,512]{2,1,0:T(8,128)} %param.6), kind=kLoop, calls=%fused_computation.79 | loop fusion | bytes 262144
  6.6 1.3 %fusion.45 = (s32[1,1]{1,0:T(1,128)}, s32[1,1]{1,0:T(1,128)}) fusion(s32[1,2]{1,0:T(1,128)} %param.4), kind=kLoop, calls=%fused_computation.130 | loop fusion | bytes 16 | tf_op jit(solution)/shard_map/slice | solution.py:139
  8.0 0.7 %sine_select_fusion = (f32[1,64,1]{1,2,0:T(1,128)S(1)}, f32[1,64,1]{1,2,0:T(1,128)S(1)}) fusion(s32[]{:T(128)S(6)} %sub.149, s32[]{:T(128)} %bitcast), kind=kLoop, calls=%fused_computation.114 | loop fusion | flops 1280 | bytes 520 | tf_op jit(solution)/shard_map/jit(_where)/select_n | solution.py:143
  11.0 0.8 %slice_bitcast_fusion.17 = (f32[33]{0:T(128)S(1)}, f32[33]{0:T(128)S(1)}) fusion(f32[2,33]{1,0:T(2,128)} %param.5), kind=kLoop, calls=%fused_computation.108 | loop fusion | bytes 528 | tf_op jit(solution)/shard_map/squeeze | solution.py:74
  12.0 1.1 %select_reduce_fusion = (f32[160,128]{1,0:T(8,128)S(1)}, f32[160,128]{1,0:T(8,128)}) fusion(f32[33]{0:T(128)S(1)} %get-tuple-element.46, s32[160,128]{1,0:T(8,128)S(1)} %iota_subtract_fusion, f32[33]{0:T(128)S(1)} %get-tuple-element.45), kind=kLoop, calls=%fused_computation.4 | loop fusion | flops 3338240 | bytes 246024 | tf_op jit(solution)/shard_map/reduce_sum | solution.py:36
  13.1 0.8 %fusion.34 = (s32[8]{0:T(128)S(1)}, s32[8]{0:T(128)S(1)}) fusion(s32[2,8]{1,0:T(2,128)} %param.7, s32[]{:T(128)S(6)} %axis_index.25), kind=kLoop, calls=%fused_computation.106 | loop fusion | flops 64 | bytes 132 | tf_op jit(solution)/shard_map/select_n | solution.py:122
  13.8 0.7 %fusion.28 = (f32[4096]{0:T(1024)S(1)}, f32[4096]{0:T(1024)S(1)}) fusion(s32[]{:T(128)} %bitcast.2), kind=kLoop, calls=%fused_computation.92 | loop fusion | flops 57344 | bytes 32772 | tf_op jit(solution)/shard_map/sin | solution.py:145
  16.9 1.1 %collective-permute-start.5 = (f32[2,32,512]{2,1,0:T(8,128)S(1)}, f32[2,32,512]{2,1,0:T(8,128)S(1)}, u32[]{:S(2)}, u32[]{:S(2)}) collective-permute-start(f32[2,32,512]{2,1,0:T(8,128)S(1)} %collective-permute-done), channel_id=1, source_target_pairs={{0,24},{4,28},{8,16},{12,20},{16,8},{20,12},{24,0},{28,4},{1,25},{... | collective-permute-start | bytes 393224 | tf_op jit(solution)/shard_map/ppermute | solution.py:106
  18.0 4.8 %collective-permute-done.3 = f32[2,2,32,512]{3,2,1,0:T(8,128)S(1)} collective-permute-done((f32[2,2,32,512]{3,2,1,0:T(8,128)S(1)}, f32[2,2,32,512]{3,2,1,0:T(8,128)S(1)}, u32[]{:S(2)}, u32[]{:S(2)}) %collective-permute-start.3) | collective-permute-done | bytes 262176 | tf_op jit(solution)/shard_map/ppermute | solution.py:106
  22.8 1.0 %collective-permute-done.5 = f32[2,32,512]{2,1,0:T(8,128)S(1)} collective-permute-done((f32[2,32,512]{2,1,0:T(8,128)S(1)}, f32[2,32,512]{2,1,0:T(8,128)S(1)}, u32[]{:S(2)}, u32[]{:S(2)}) %collective-permute-start.5) | collective-permute-done | bytes 131104 | tf_op jit(solution)/shard_map/ppermute | solution.py:106
  24.5 1.9 %bitcast_cosine_fusion = (f32[32,8,512]{2,0,1:T(8,128)S(1)}, f32[32,8,512]{2,0,1:T(8,128)S(1)}) fusion(f32[8,32,512]{2,1,0:T(8,128)S(1)} %gather_fusion), kind=kLoop, calls=%fused_computation.123 | loop fusion | bytes 1572864 | tf_op jit(solution)/shard_map/cos | solution.py:81
  26.5 5.3 %collective-permute-start.6 = (f32[16,4096]{1,0:T(8,128)S(1)}, f32[16,4096]{1,0:T(8,128)S(1)}, u32[]{:S(2)}, u32[]{:S(2)}) collective-permute-start(f32[16,4096]{1,0:T(8,128)S(1)} %bitcast.172), channel_id=1, source_target_pairs={{0,1},{1,2},{2,3},{4,5},{5,6},{6,7},{8,9},{9,10},{10,11},{12,13},{... | collective-permute-start | bytes 786440 | tf_op jit(solution)/shard_map/ppermute | solution.py:22
  32.6 0.7 %copy.18 = f32[8,2,8,512]{3,2,0,1:T(8,128)} copy(f32[8,2,8,512]{3,2,1,0:T(8,128)S(1)} %get-tuple-element.35) | data formatting | bytes 524288 | tf_op jit(solution)/shard_map/slice | solution.py:18
  33.3 1.9 %collective-permute-start.7 = (f32[16,4096]{1,0:T(8,128)}, f32[16,4096]{1,0:T(8,128)S(1)}, u32[]{:S(2)}, u32[]{:S(2)}) collective-permute-start(f32[16,4096]{1,0:T(8,128)} %bitcast.51), channel_id=1, source_target_pairs={{1,0},{2,1},{3,2},{5,4},{6,5},{7,6},{9,8},{10,9},{11,10},{13,12},{... | collective-permute-start | bytes 786440 | tf_op jit(solution)/shard_map/ppermute | solution.py:24
  35.2 0.7 %gather_fusion.1 = f32[8,32,512]{2,1,0:T(8,128)S(1)} fusion(f32[8,32,512]{2,1,0:T(8,128)S(1)} %get-tuple-element.21, s32[1024]{0:T(1024)} %get-tuple-element.53), kind=kCustom, calls=%fused_computation.1 | custom fusion | bytes 1048608 | tf_op jit(solution)/shard_map/gather | solution.py:122
  36.0 1.9 %sine_bitcast_fusion = (f32[32,8,512]{2,0,1:T(8,128)S(1)}, f32[32,8,512]{2,0,1:T(8,128)S(1)}) fusion(f32[8,32,512]{2,1,0:T(8,128)S(1)} %gather_fusion.1), kind=kLoop, calls=%fused_computation.48 | loop fusion | bytes 1572864 | tf_op jit(solution)/shard_map/sin | solution.py:82
  38.7 1.0 %fusion.44 = (f32[16,4096]{1,0:T(8,128)S(1)}, f32[16,4096]{1,0:T(8,128)S(1)}) fusion(f32[16,4096]{1,0:T(8,128)S(1)} %collective-permute-done.6), kind=kLoop, calls=%fused_computation.129 | loop fusion | bytes 786432 | tf_op jit(solution)/shard_map/cos | solution.py:81
  39.7 0.9 %bitcast_dynamic-update-slice_fusion.3 = f32[1,128,4096]{2,1,0:T(8,128)S(1)} fusion(f32[16,4096]{1,0:T(8,128)S(1)} %get-tuple-element.42, f32[16,4096]{1,0:T(8,128)S(1)} %get-tuple-element.41, f32[4096]{0:T(1024)S(1)} %get-tuple-element.55, f32[16]{0:T(128)} %get-tuple-element.50, f32[4096]{0:T(1024)S(1)} %get-tuple-element.56, f32[16]{0:T(128)} %get-tuple-element.48), kind=kLoop, calls=%fused_computation.65 | loop fusion | flops 589823 | bytes 819328
  40.6 0.9 %subtract_dynamic-update-slice_fusion = f32[1,128,4096]{2,1,0:T(8,128)S(1)} fusion(f32[1,128,4096]{2,1,0:T(8,128)S(1)} %bitcast_dynamic-update-slice_fusion.3, f32[1,32,4096]{2,1,0:T(8,128)S(1)} %sin.70, f32[1,32,4096]{2,1,0:T(8,128)S(1)} %cos.70, f32[4096]{0:T(1024)S(1)} %get-tuple-element.55, f32[32]{0:T(128)} %slice_bitcast_fusion.20, ...), kind=kLoop, calls=%fused_computation.55 | loop fusion | flops 1179648 | bytes 1605888
  41.5 1.0 %fusion.43 = (f32[16,4096]{1,0:T(8,128)S(1)}, f32[16,4096]{1,0:T(8,128)S(1)}) fusion(f32[16,4096]{1,0:T(8,128)S(1)} %collective-permute-done.7), kind=kLoop, calls=%fused_computation.128 | loop fusion | bytes 786432 | tf_op jit(solution)/shard_map/cos | solution.py:81
  43.3 0.7 %convolution_bitcast_fusion.1 = f32[1,64,4096]{2,1,0:T(8,128)S(1)} fusion(f32[1,128,4096]{2,1,0:T(8,128)S(1)} %bitcast_dynamic-update-slice_fusion, f32[32,64]{1,0:T(8,128)S(1)} %get-tuple-element.8, f32[32,64]{1,0:T(8,128)S(1)} %get-tuple-element.7, f32[32,64]{1,0:T(8,128)S(1)} %copy-done), kind=kOutput, calls=%fused_computation.3 | convolution fusion | flops 201351168 | bytes 3170304 | tf_op jit(solution)/shard_map/ij,ajy->aiy/dot_general | solution.py:76
  45.4 1.1 %fusion.18 = f32[1,32,32,256]{3,2,1,0:T(8,128)S(1)} fusion(f32[1,32,32,32]{3,2,1,0:T(8,128)S(1)} %bitcast.163, f32[1,32,32,128]{3,2,1,0:T(8,128)S(1)} %bitcast.169, f32[1,32,32,32]{3,2,1,0:T(8,128)S(1)} %bitcast.165, f32[1,32,32,128]{3,2,1,0:T(8,128)S(1)} %bitcast.167, f32[160,128]{1,0:T(8,128)S(1)} %copy-done.2, f32[160,128]{1,0:T(8,128)S(1)} %copy-done.1, ...), kind=kOutput, calls=%fused_computation.29 | convolution fusion | flops 504545280 | bytes 2605056 | tf_op jit(solution)/shard_map/...nj,jc->...nc/dot_general | solution.py:68
  47.1 3.6 %collective-permute-start.8 = (f32[2,1,16,4096]{3,2,1,0:T(8,128)S(1)}, f32[2,1,16,4096]{3,2,1,0:T(8,128)S(1)}, u32[]{:S(2)}, u32[]{:S(2)}) collective-permute-start(f32[2,1,16,4096]{3,2,1,0:T(8,128)S(1)} %get-tuple-element.17), channel_id=1, source_target_pairs={{0,1},{1,2},{2,3},{4,5},{5,6},{6,7},{8,9},{9,10},{10,11},{12,13},{... | collective-permute-start | bytes 1572872 | tf_op jit(solution)/shard_map/ppermute | solution.py:22
  50.7 2.1 %collective-permute-start.9 = (f32[2,1,16,4096]{3,2,1,0:T(8,128)S(1)}, f32[2,1,16,4096]{3,2,1,0:T(8,128)S(1)}, u32[]{:S(2)}, u32[]{:S(2)}) collective-permute-start(f32[2,1,16,4096]{3,2,1,0:T(8,128)S(1)} %get-tuple-element.18), channel_id=1, source_target_pairs={{1,0},{2,1},{3,2},{5,4},{6,5},{7,6},{9,8},{10,9},{11,10},{13,12},{... | collective-permute-start | bytes 1572872 | tf_op jit(solution)/shard_map/ppermute | solution.py:24
  52.8 4.0 %collective-permute-done.8 = f32[2,1,16,4096]{3,2,1,0:T(8,128)S(1)} collective-permute-done((f32[2,1,16,4096]{3,2,1,0:T(8,128)S(1)}, f32[2,1,16,4096]{3,2,1,0:T(8,128)S(1)}, u32[]{:S(2)}, u32[]{:S(2)}) %collective-permute-start.8) | collective-permute-done | bytes 524320 | tf_op jit(solution)/shard_map/ppermute | solution.py:22
  56.8 4.4 %collective-permute-done.9 = f32[2,1,16,4096]{3,2,1,0:T(8,128)S(1)} collective-permute-done((f32[2,1,16,4096]{3,2,1,0:T(8,128)S(1)}, f32[2,1,16,4096]{3,2,1,0:T(8,128)S(1)}, u32[]{:S(2)}, u32[]{:S(2)}) %collective-permute-start.9) | collective-permute-done | bytes 524320 | tf_op jit(solution)/shard_map/ppermute | solution.py:24
  61.6 0.7 %convolution_bitcast_fusion = f32[1,64,4096]{2,1,0:T(8,128)S(1)} fusion(f32[1,64,4096]{2,1,0:T(8,128)S(1)} %get-tuple-element.10, f32[1,64,4096]{2,1,0:T(8,128)S(1)} %get-tuple-element.9, f32[32,64]{1,0:T(8,128)S(1)} %get-tuple-element.8, f32[32,64]{1,0:T(8,128)S(1)} %get-tuple-element.7, f32[32,64]{1,0:T(8,128)S(1)} %copy-done), kind=kOutput, calls=%fused_computation.2 | convolution fusion | flops 201875456 | bytes 3170304 | tf_op jit(solution)/shard_map/ij,ajy->aiy/dot_general | solution.py:76
  63.5 1.1 %fusion.17 = f32[1,32,32,256]{3,2,1,0:T(8,128)S(1)} fusion(f32[1,32,32,32]{3,2,1,0:T(8,128)S(1)} %bitcast.162, f32[1,32,32,128]{3,2,1,0:T(8,128)S(1)} %bitcast.168, f32[1,32,32,32]{3,2,1,0:T(8,128)S(1)} %bitcast.164, f32[1,32,32,128]{3,2,1,0:T(8,128)S(1)} %bitcast.166, f32[160,128]{1,0:T(8,128)S(1)} %copy-done.2, f32[160,128]{1,0:T(8,128)S(1)} %copy-done.1, ...), kind=kOutput, calls=%fused_computation.28 | convolution fusion | flops 504545280 | bytes 2605056 | tf_op jit(solution)/shard_map/...nj,jc->...nc/dot_general | solution.py:68
  65.0 1.0 %pad_maximum_fusion.1 = f32[2,1,32,4096]{3,2,1,0:T(8,128)} fusion(f32[1,1,32,4096]{3,2,1,0:T(8,128)S(1)} %stack_reshape.7, f32[1,1,32,4096]{3,2,1,0:T(8,128)S(1)} %stack_reshape.6), kind=kLoop, calls=%fused_computation.34 | loop fusion | flops 262144 | bytes 2097152 | tf_op jit(solution)/shard_map/stack | solution.py:170
  (84 shorter events, 11.7 us)
Async XLA Ops:
  0.0 16.4 %collective-permute-start.2 = (f32[2,32,512]{2,1,0:T(8,128)}, f32[2,32,512]{2,1,0:T(8,128)S(1)}, u32[]{:S(2)}, u32[]{:S(2)}) collective-permute-start(f32[2,32,512]{2,1,0:T(8,128)} %param.6), channel_id=1, source_target_pairs={{0,16},{4,20},{8,24},{12,28},{16,0},{20,4},{24,8},{28,12},{1,17},{... | collective-permute-start | bytes 393224 | tf_op jit(solution)/shard_map/ppermute | solution.py:106
  3.1 13.2 %collective-permute-start.1 = (f32[2,32,512]{2,1,0:T(8,128)}, f32[2,32,512]{2,1,0:T(8,128)S(1)}, u32[]{:S(2)}, u32[]{:S(2)}) collective-permute-start(f32[2,32,512]{2,1,0:T(8,128)} %param.6), channel_id=1, source_target_pairs={{0,8},{4,12},{8,0},{12,4},{16,24},{20,28},{24,16},{28,20},{1,9},{5... | collective-permute-start | bytes 393224 | tf_op jit(solution)/shard_map/ppermute | solution.py:106
  4.4 12.4 %collective-permute-start = (f32[2,32,512]{2,1,0:T(8,128)}, f32[2,32,512]{2,1,0:T(8,128)S(1)}, u32[]{:S(2)}, u32[]{:S(2)}) collective-permute-start(f32[2,32,512]{2,1,0:T(8,128)} %param.6), channel_id=1, source_target_pairs={{0,4},{4,0},{8,12},{12,8},{16,20},{20,16},{24,28},{28,24},{1,5},{5... | collective-permute-start | bytes 393224 | tf_op jit(solution)/shard_map/ppermute | solution.py:106
  16.4 6.3 %collective-permute-start.3 = (f32[2,2,32,512]{3,2,1,0:T(8,128)S(1)}, f32[2,2,32,512]{3,2,1,0:T(8,128)S(1)}, u32[]{:S(2)}, u32[]{:S(2)}) collective-permute-start(f32[2,2,32,512]{3,2,1,0:T(8,128)S(1)} %pad_maximum_fusion.3), channel_id=1, source_target_pairs={{0,4},{4,0},{8,12},{12,8},{16,20},{20,16},{24,28},{28,24},{1,5},{5... | collective-permute-start | bytes 786440 | tf_op jit(solution)/shard_map/ppermute | solution.py:106
  16.7 6.1 %collective-permute-start.4 = (f32[2,32,512]{2,1,0:T(8,128)S(1)}, f32[2,32,512]{2,1,0:T(8,128)S(1)}, u32[]{:S(2)}, u32[]{:S(2)}) collective-permute-start(f32[2,32,512]{2,1,0:T(8,128)S(1)} %collective-permute-done.2), channel_id=1, source_target_pairs={{0,8},{4,12},{8,0},{12,4},{16,24},{20,28},{24,16},{28,20},{1,9},{5... | collective-permute-start | bytes 393224 | tf_op jit(solution)/shard_map/ppermute | solution.py:106
  16.9 7.0 %collective-permute-start.5 = (f32[2,32,512]{2,1,0:T(8,128)S(1)}, f32[2,32,512]{2,1,0:T(8,128)S(1)}, u32[]{:S(2)}, u32[]{:S(2)}) collective-permute-start(f32[2,32,512]{2,1,0:T(8,128)S(1)} %collective-permute-done), channel_id=1, source_target_pairs={{0,24},{4,28},{8,16},{12,20},{16,8},{20,12},{24,0},{28,4},{1,25},{... | collective-permute-start | bytes 393224 | tf_op jit(solution)/shard_map/ppermute | solution.py:106
  26.5 12.2 %collective-permute-start.6 = (f32[16,4096]{1,0:T(8,128)S(1)}, f32[16,4096]{1,0:T(8,128)S(1)}, u32[]{:S(2)}, u32[]{:S(2)}) collective-permute-start(f32[16,4096]{1,0:T(8,128)S(1)} %bitcast.172), channel_id=1, source_target_pairs={{0,1},{1,2},{2,3},{4,5},{5,6},{6,7},{8,9},{9,10},{10,11},{12,13},{... | collective-permute-start | bytes 786440 | tf_op jit(solution)/shard_map/ppermute | solution.py:22
  33.3 8.2 %collective-permute-start.7 = (f32[16,4096]{1,0:T(8,128)}, f32[16,4096]{1,0:T(8,128)S(1)}, u32[]{:S(2)}, u32[]{:S(2)}) collective-permute-start(f32[16,4096]{1,0:T(8,128)} %bitcast.51), channel_id=1, source_target_pairs={{1,0},{2,1},{3,2},{5,4},{6,5},{7,6},{9,8},{10,9},{11,10},{13,12},{... | collective-permute-start | bytes 786440 | tf_op jit(solution)/shard_map/ppermute | solution.py:24
  38.7 3.8 %copy-start.3 = (f32[16]{0:T(128)S(1)}, f32[16]{0:T(128)}, u32[]{:S(2)}) copy-start(f32[16]{0:T(128)} %get-tuple-element.49) | copy-start | bytes 196
  38.7 3.8 %copy-start.4 = (f32[16]{0:T(128)S(1)}, f32[16]{0:T(128)}, u32[]{:S(2)}) copy-start(f32[16]{0:T(128)} %get-tuple-element.47) | copy-start | bytes 196
  39.7 3.0 %copy-start.5 = (f32[16]{0:T(128)S(1)}, f32[16]{0:T(128)}, u32[]{:S(2)}) copy-start(f32[16]{0:T(128)} %get-tuple-element.50) | copy-start | bytes 196
  39.7 3.0 %copy-start.6 = (f32[16]{0:T(128)S(1)}, f32[16]{0:T(128)}, u32[]{:S(2)}) copy-start(f32[16]{0:T(128)} %get-tuple-element.48) | copy-start | bytes 196
  40.6 2.3 %copy-start.7 = (f32[32]{0:T(128)S(1)}, f32[32]{0:T(128)}, u32[]{:S(2)}) copy-start(f32[32]{0:T(128)} %slice_bitcast_fusion.20) | copy-start | bytes 388
  40.6 2.3 %copy-start.8 = (f32[32]{0:T(128)S(1)}, f32[32]{0:T(128)}, u32[]{:S(2)}) copy-start(f32[32]{0:T(128)} %slice_bitcast_fusion.21) | copy-start | bytes 388
  42.5 0.8 %copy-start = (f32[32,64]{1,0:T(8,128)S(1)}, f32[32,64]{1,0:T(8,128)}, u32[]{:S(2)}) copy-start(f32[32,64]{1,0:T(8,128)} %neg.4) | copy-start | bytes 24580
  44.5 0.9 %copy-start.1 = (f32[160,128]{1,0:T(8,128)S(1)}, f32[160,128]{1,0:T(8,128)}, u32[]{:S(2)}) copy-start(f32[160,128]{1,0:T(8,128)} %neg.5) | copy-start | bytes 245764
  44.5 0.9 %copy-start.2 = (f32[160,128]{1,0:T(8,128)S(1)}, f32[160,128]{1,0:T(8,128)}, u32[]{:S(2)}) copy-start(f32[160,128]{1,0:T(8,128)} %get-tuple-element.6) | copy-start | bytes 245764
  47.1 9.8 %collective-permute-start.8 = (f32[2,1,16,4096]{3,2,1,0:T(8,128)S(1)}, f32[2,1,16,4096]{3,2,1,0:T(8,128)S(1)}, u32[]{:S(2)}, u32[]{:S(2)}) collective-permute-start(f32[2,1,16,4096]{3,2,1,0:T(8,128)S(1)} %get-tuple-element.17), channel_id=1, source_target_pairs={{0,1},{1,2},{2,3},{4,5},{5,6},{6,7},{8,9},{9,10},{10,11},{12,13},{... | collective-permute-start | bytes 1572872 | tf_op jit(solution)/shard_map/ppermute | solution.py:22
  50.7 10.5 %collective-permute-start.9 = (f32[2,1,16,4096]{3,2,1,0:T(8,128)S(1)}, f32[2,1,16,4096]{3,2,1,0:T(8,128)S(1)}, u32[]{:S(2)}, u32[]{:S(2)}) collective-permute-start(f32[2,1,16,4096]{3,2,1,0:T(8,128)S(1)} %get-tuple-element.18), channel_id=1, source_target_pairs={{1,0},{2,1},{3,2},{5,4},{6,5},{7,6},{9,8},{10,9},{11,10},{13,12},{... | collective-permute-start | bytes 1572872 | tf_op jit(solution)/shard_map/ppermute | solution.py:24

commit v9 on v8

--- a/solution.py
+++ b/solution.py
@@ -94,7 +94,7 @@
     return jnp.stack(planes)
 
 
-def gather_screens(stored_planes, owner, axis):
+def gather_screens(stored_planes, selections, axis):
     count = lax.axis_size(axis)
     me = lax.axis_index(axis)
     paired = count & (count - 1) == 0
@@ -113,15 +113,14 @@
         parts = [stored_planes, one, two, three, four, five, six, seven]
     else:
         parts = [stored_planes] + [exchange(stored_planes, k) for k in range(1, count)]
-    stacked = jnp.stack(parts, axis=1)
-    rows = stored_planes.shape[1]
-    width = stored_planes.shape[2]
-    planes = []
-    for p in range(stored_planes.shape[0]):
-        source = jnp.bitwise_xor(me, owner[p]) if paired else jnp.mod(me - owner[p], count)
-        picked = stacked[p][source]
-        planes.append(jnp.transpose(picked, (1, 0, 2)).reshape(rows, count * width))
-    return jnp.stack(planes)
+    stacked = jnp.stack(parts)
+    width = stored_planes.shape[1]
+    screens = []
+    for lo, hi, order in selections:
+        source = jnp.bitwise_xor(me, order) if paired else jnp.mod(me - order, count)
+        picked = stacked[:, lo:hi][source]
+        screens.append(jnp.transpose(picked, (1, 0, 2)).reshape(hi - lo, count * width))
+    return screens
 
 
 def body(tilts, taps, stored_planes, owner):
@@ -129,8 +128,14 @@
     total_rows = local_rows * lax.axis_size("tile")
     total_cols = NY
     first_row = lax.axis_index("tile") * local_rows
-    screens = gather_screens(stored_planes, owner, "illum")
     extra = HALF
+    first_block = extended(stored_planes[0], (("tile", 0),), HALF)
+    block = jnp.concatenate([first_block] + [stored_planes[plane] for plane in range(1, PLANES)], axis=0)
+    selections = [(0, local_rows + 2 * extra, owner[0])]
+    for plane in range(1, PLANES):
+        lo = local_rows + 2 * extra + (plane - 1) * local_rows
+        selections.append((lo, lo + local_rows, owner[plane]))
+    screens = gather_screens(block, selections, "illum")
     span = local_rows + 2 * extra
     global_rows = first_row - extra + jnp.arange(span, dtype=jnp.int32)
     inside = (global_rows >= 0) & (global_rows < total_rows)
@@ -149,17 +154,7 @@
         imag = across_sin[:, rows] * along_cos + across_cos[:, rows] * along_sin
         return real, imag
 
-    halo = extended(screens[0], (("tile", 0),), HALF)
-    pieces = [
-        transmit(*incident(rows), screen)
-        for rows, screen in (
-            (slice(0, HALF), halo[:HALF]),
-            (slice(HALF, HALF + local_rows), screens[0]),
-            (slice(HALF + local_rows, span), halo[HALF + local_rows :]),
-        )
-    ]
-    real = jnp.concatenate([piece[0] for piece in pieces], axis=1)
-    imag = jnp.concatenate([piece[1] for piece in pieces], axis=1)
+    real, imag = transmit(*incident(slice(0, span)), screens[0])
     real, imag = cross_pass(real, imag, taps)
     real, imag = along_pass(real, imag, taps)
     for plane in range(1, PLANES):

time: 66.4 us -> 71.4 us (1.075)
  waiting for transfers between devices: 14.2 us -> 23.7 us
  other arithmetic: 9.17 us -> 4.92 us
    ppermute x6, waiting for transfers between devices: 5.79 us -> 15.9 us  [exchange(): return lax.ppermute(x, axis, [(i, partner(i, k)) for i in range(count)])]
    sin x5 -> x6, local copies, waits for them, and re-layouts: 2.67 us -> 7.56 us  [transmit(): sine = jnp.sin(screen)]
    cos x7 -> x4, local copies, waits for them, and re-layouts: 4.61 us -> 2.02 us  [transmit(): cosine = jnp.cos(screen)]
    ppermute x2, starting transfers between devices: 8.93 us -> 6.42 us  [extended(): lax.ppermute(tail, axis, [(i, (i + 1) % count) for i in range(ends)])]
    mul x4 -> x0, local copies, waits for them, and re-layouts: 2.34 us -> none  [incident(): real = across_cos[:, rows] * along_cos - across_sin[:, rows] * along_sin]
    unnamed x5 -> x1, other arithmetic: 2.31 us -> 0.01 us
    ppermute x6, starting transfers between devices: 7.2 us -> 8.47 us  [exchange(): return lax.ppermute(x, axis, [(i, partner(i, k)) for i in range(count)])]
    squeeze x1, local copies, waits for them, and re-layouts: 0.09 us -> 0.88 us  [body(): first_block = extended(stored_planes[0], (('tile', 0),), HALF)]
  transfers between devices with their start and end apart: 10 -> 10, of which waited for: 4 -> 6; matrix products, arithmetic and copies ran while one was open for 28% -> 9% of each run, Pallas kernels for 0% -> 0%
where the time goes in v9:
time: 71.4 us; the launch traced here: 71 us
  waiting for transfers between devices  23.7 us (33%)
  starting transfers between devices  19.4 us (27%)
  local copies, waits for them, and re-layouts  18.8 us (26%)
  other arithmetic  4.92 us (7%)
  matrix products  3.65 us (5%)
    ppermute x6, waiting for transfers between devices, exchange(): return lax.ppermute(x, axis, [(i, partner(i, k)) for i in range(count)])  15.9 us
    ppermute x6, starting transfers between devices, exchange(): return lax.ppermute(x, axis, [(i, partner(i, k)) for i in range(count)])  8.47 us
    sin x6, local copies, waits for them, and re-layouts, transmit(): sine = jnp.sin(screen)  7.56 us
    ppermute x2, starting transfers between devices, extended(): lax.ppermute(tail, axis, [(i, (i + 1) % count) for i in range(ends)])  6.42 us
    ppermute x2, starting transfers between devices, extended(): lax.ppermute(head, axis, [((i + 1) % count, i) for i in range(ends)])  4.54 us
    ppermute x2, waiting for transfers between devices, extended(): lax.ppermute(head, axis, [((i + 1) % count, i) for i in range(ends)])  4.4 us
    ppermute x2, waiting for transfers between devices, extended(): lax.ppermute(tail, axis, [(i, (i + 1) % count) for i in range(ends)])  3.48 us
    unnamed x22, local copies, waits for them, and re-layouts  3.18 us
  transfers between devices with their start and end apart: 10, of which 6 were waited for; matrix products, arithmetic and copies ran while one was open for 9% of the time, Pallas kernels for 0%

profile of v9, /device:TPU:1, one launch (start us, length us, event | category | flops | bytes accessed | tf_op | source)
XLA Modules:
  0.0 71.0 jit_solution(8211672714231529783)
XLA Ops:
  0.0 0.8 %slice_bitcast_fusion.13 = (f32[16,512]{1,0:T(8,128)S(1)}, f32[16,512]{1,0:T(8,128)S(1)}) fusion(f32[2,32,512]{2,1,0:T(8,128)} %param.6), kind=kLoop, calls=%fused_computation.74 | loop fusion | bytes 131072 | tf_op jit(solution)/shard_map/slice | solution.py:19
  0.8 4.5 %collective-permute-start = (f32[16,512]{1,0:T(8,128)S(1)}, f32[16,512]{1,0:T(8,128)S(1)}, u32[]{:S(2)}, u32[]{:S(2)}) collective-permute-start(f32[16,512]{1,0:T(8,128)S(1)} %get-tuple-element.37), channel_id=1, source_target_pairs={{0,1},{1,2},{2,3},{4,5},{5,6},{6,7},{8,9},{9,10},{10,11},{12,13},{... | collective-permute-start | bytes 98312 | tf_op jit(solution)/shard_map/ppermute | solution.py:22
  5.3 1.9 %collective-permute-start.1 = (f32[16,512]{1,0:T(8,128)S(1)}, f32[16,512]{1,0:T(8,128)S(1)}, u32[]{:S(2)}, u32[]{:S(2)}) collective-permute-start(f32[16,512]{1,0:T(8,128)S(1)} %get-tuple-element.38), channel_id=1, source_target_pairs={{1,0},{2,1},{3,2},{5,4},{6,5},{7,6},{9,8},{10,9},{11,10},{13,12},{... | collective-permute-start | bytes 98312 | tf_op jit(solution)/shard_map/ppermute | solution.py:24
  7.2 0.9 %slice_bitcast_fusion.11 = (f32[32,512]{1,0:T(8,128)S(1)}, f32[32,512]{1,0:T(8,128)S(1)}) fusion(f32[2,32,512]{2,1,0:T(8,128)} %param.6), kind=kLoop, calls=%fused_computation.71 | loop fusion | bytes 262144 | tf_op jit(solution)/shard_map/squeeze | solution.py:132
  8.1 1.3 %fusion.42 = (s32[1,1]{1,0:T(1,128)}, s32[1,1]{1,0:T(1,128)}) fusion(s32[1,2]{1,0:T(1,128)} %param.4), kind=kLoop, calls=%fused_computation.115 | loop fusion | bytes 16 | tf_op jit(solution)/shard_map/slice | solution.py:144
  9.5 0.8 %slice_bitcast_fusion.15 = (f32[33]{0:T(128)S(1)}, f32[33]{0:T(128)S(1)}) fusion(f32[2,33]{1,0:T(2,128)} %param.5), kind=kLoop, calls=%fused_computation.103 | loop fusion | bytes 528 | tf_op jit(solution)/shard_map/squeeze | solution.py:74
  10.2 0.7 fusion.27
  11.7 0.8 %fusion.33 = (s32[8]{0:T(128)S(1)}, s32[8]{0:T(128)S(1)}) fusion(s32[2,8]{1,0:T(2,128)} %param.7, s32[]{:T(128)S(6)} %axis_index.25), kind=kLoop, calls=%fused_computation.101 | loop fusion | flops 64 | bytes 132 | tf_op jit(solution)/shard_map/select_n | solution.py:121
  12.5 1.4 %collective-permute-start.3 = (f32[96,512]{1,0:T(8,128)S(1)}, f32[96,512]{1,0:T(8,128)S(1)}, u32[]{:S(2)}, u32[]{:S(2)}) collective-permute-start(f32[96,512]{1,0:T(8,128)S(1)} %pad_maximum_fusion.4), channel_id=1, source_target_pairs={{0,8},{4,12},{8,0},{12,4},{16,24},{20,28},{24,16},{28,20},{1,9},{5... | collective-permute-start | bytes 589832 | tf_op jit(solution)/shard_map/ppermute | solution.py:106
  13.9 2.3 %collective-permute-start.4 = (f32[96,512]{1,0:T(8,128)S(1)}, f32[96,512]{1,0:T(8,128)S(1)}, u32[]{:S(2)}, u32[]{:S(2)}) collective-permute-start(f32[96,512]{1,0:T(8,128)S(1)} %pad_maximum_fusion.4), channel_id=1, source_target_pairs={{0,16},{4,20},{8,24},{12,28},{16,0},{20,4},{24,8},{28,12},{1,17},{... | collective-permute-start | bytes 589832 | tf_op jit(solution)/shard_map/ppermute | solution.py:106
  16.2 0.7 sine_select_fusion
  16.9 1.3 %collective-permute-start.2 = (f32[96,512]{1,0:T(8,128)S(1)}, f32[96,512]{1,0:T(8,128)S(1)}, u32[]{:S(2)}, u32[]{:S(2)}) collective-permute-start(f32[96,512]{1,0:T(8,128)S(1)} %pad_maximum_fusion.4), channel_id=1, source_target_pairs={{0,4},{4,0},{8,12},{12,8},{16,20},{20,16},{24,28},{28,24},{1,5},{5... | collective-permute-start | bytes 589832 | tf_op jit(solution)/shard_map/ppermute | solution.py:106
  18.2 2.9 %collective-permute-done.3 = f32[96,512]{1,0:T(8,128)S(1)} collective-permute-done((f32[96,512]{1,0:T(8,128)S(1)}, f32[96,512]{1,0:T(8,128)S(1)}, u32[]{:S(2)}, u32[]{:S(2)}) %collective-permute-start.3) | collective-permute-done | bytes 196640 | tf_op jit(solution)/shard_map/ppermute | solution.py:106
  21.1 3.4 %collective-permute-done.4 = f32[96,512]{1,0:T(8,128)S(1)} collective-permute-done((f32[96,512]{1,0:T(8,128)S(1)}, f32[96,512]{1,0:T(8,128)S(1)}, u32[]{:S(2)}, u32[]{:S(2)}) %collective-permute-start.4) | collective-permute-done | bytes 196640 | tf_op jit(solution)/shard_map/ppermute | solution.py:106
  24.6 1.3 %collective-permute-start.5 = (f32[2,96,512]{2,1,0:T(8,128)S(1)}, f32[2,96,512]{2,1,0:T(8,128)S(1)}, u32[]{:S(2)}, u32[]{:S(2)}) collective-permute-start(f32[2,96,512]{2,1,0:T(8,128)S(1)} %pad_maximum_fusion.3), channel_id=1, source_target_pairs={{0,4},{4,0},{8,12},{12,8},{16,20},{20,16},{24,28},{28,24},{1,5},{5... | collective-permute-start | bytes 1179656 | tf_op jit(solution)/shard_map/ppermute | solution.py:106
  25.9 2.2 %collective-permute-start.7 = (f32[96,512]{1,0:T(8,128)S(1)}, f32[96,512]{1,0:T(8,128)S(1)}, u32[]{:S(2)}, u32[]{:S(2)}) collective-permute-start(f32[96,512]{1,0:T(8,128)S(1)} %collective-permute-done.2), channel_id=1, source_target_pairs={{0,24},{4,28},{8,16},{12,20},{16,8},{20,12},{24,0},{28,4},{1,25},{... | collective-permute-start | bytes 589832 | tf_op jit(solution)/shard_map/ppermute | solution.py:106
  28.1 4.0 %collective-permute-done.5 = f32[2,96,512]{2,1,0:T(8,128)S(1)} collective-permute-done((f32[2,96,512]{2,1,0:T(8,128)S(1)}, f32[2,96,512]{2,1,0:T(8,128)S(1)}, u32[]{:S(2)}, u32[]{:S(2)}) %collective-permute-start.5) | collective-permute-done | bytes 393248 | tf_op jit(solution)/shard_map/ppermute | solution.py:106
  32.2 5.5 %collective-permute-done.7 = f32[96,512]{1,0:T(8,128)S(1)} collective-permute-done((f32[96,512]{1,0:T(8,128)S(1)}, f32[96,512]{1,0:T(8,128)S(1)}, u32[]{:S(2)}, u32[]{:S(2)}) %collective-permute-start.7) | collective-permute-done | bytes 196640 | tf_op jit(solution)/shard_map/ppermute | solution.py:106
  38.5 1.9 %sine_bitcast_fusion.1 = (f32[32,8,512]{2,0,1:T(8,128)S(1)}, f32[32,8,512]{2,0,1:T(8,128)S(1)}) fusion(f32[8,32,512]{2,1,0:T(8,128)S(1)} %gather_fusion.1), kind=kLoop, calls=%fused_computation.54 | loop fusion | bytes 1572864 | tf_op jit(solution)/shard_map/sin | solution.py:82
  40.7 0.9 %sin.67 = f32[1,1,32,4096]{3,2,1,0:T(8,128)} reshape(f32[32,8,512]{2,1,0:T(8,128)S(1)} %copy.12) | data formatting | bytes 1048576 | tf_op jit(solution)/shard_map/sin | solution.py:82
  41.9 0.9 %cos.67 = f32[1,1,32,4096]{3,2,1,0:T(8,128)} reshape(f32[32,8,512]{2,1,0:T(8,128)S(1)} %copy.11) | data formatting | bytes 1048576 | tf_op jit(solution)/shard_map/cos | solution.py:81
  43.4 3.7 %sine_bitcast_fusion = (f32[64,8,512]{2,0,1:T(8,128)S(1)}, f32[64,8,512]{2,0,1:T(8,128)S(1)}) fusion(f32[8,64,512]{2,1,0:T(8,128)S(1)} %gather_fusion), kind=kLoop, calls=%fused_computation.39 | loop fusion | bytes 3145728 | tf_op jit(solution)/shard_map/sin | solution.py:82
  49.3 0.7 convolution_bitcast_fusion.1
  51.1 1.1 %fusion.19 = f32[1,32,32,256]{3,2,1,0:T(8,128)S(1)} fusion(f32[1,32,32,32]{3,2,1,0:T(8,128)S(1)} %bitcast.139, f32[1,32,32,128]{3,2,1,0:T(8,128)S(1)} %bitcast.137, f32[1,32,32,32]{3,2,1,0:T(8,128)S(1)} %bitcast.135, f32[1,32,32,128]{3,2,1,0:T(8,128)S(1)} %bitcast.133, f32[160,128]{1,0:T(8,128)S(1)} %get-tuple-element.6, f32[160,128]{1,0:T(8,128)S(1)} %neg.5, ...), kind=kOutput, calls=%fused_computation.31 | convolution fusion | flops 504545280 | bytes 2605056 | tf_op jit(solution)/shard_map/...nj,jc->...nc/dot_general | solution.py:68
  52.7 0.8 %copy-done = f32[1,1,32,4096]{3,2,1,0:T(8,128)S(1)} copy-done((f32[1,1,32,4096]{3,2,1,0:T(8,128)S(1)}, f32[1,1,32,4096]{3,2,1,0:T(8,128)}, u32[]{:S(2)}) %copy-start) | copy-done | bytes 524312
  53.8 1.9 %collective-permute-start.8 = (f32[2,1,16,4096]{3,2,1,0:T(8,128)S(1)}, f32[2,1,16,4096]{3,2,1,0:T(8,128)S(1)}, u32[]{:S(2)}, u32[]{:S(2)}) collective-permute-start(f32[2,1,16,4096]{3,2,1,0:T(8,128)S(1)} %get-tuple-element.19), channel_id=1, source_target_pairs={{0,1},{1,2},{2,3},{4,5},{5,6},{6,7},{8,9},{9,10},{10,11},{12,13},{... | collective-permute-start | bytes 1572872 | tf_op jit(solution)/shard_map/ppermute | solution.py:22
  55.8 2.6 %collective-permute-start.9 = (f32[2,1,16,4096]{3,2,1,0:T(8,128)S(1)}, f32[2,1,16,4096]{3,2,1,0:T(8,128)S(1)}, u32[]{:S(2)}, u32[]{:S(2)}) collective-permute-start(f32[2,1,16,4096]{3,2,1,0:T(8,128)S(1)} %get-tuple-element.20), channel_id=1, source_target_pairs={{1,0},{2,1},{3,2},{5,4},{6,5},{7,6},{9,8},{10,9},{11,10},{13,12},{... | collective-permute-start | bytes 1572872 | tf_op jit(solution)/shard_map/ppermute | solution.py:24
  58.4 3.5 %collective-permute-done.8 = f32[2,1,16,4096]{3,2,1,0:T(8,128)S(1)} collective-permute-done((f32[2,1,16,4096]{3,2,1,0:T(8,128)S(1)}, f32[2,1,16,4096]{3,2,1,0:T(8,128)S(1)}, u32[]{:S(2)}, u32[]{:S(2)}) %collective-permute-start.8) | collective-permute-done | bytes 524320 | tf_op jit(solution)/shard_map/ppermute | solution.py:22
  61.9 4.4 %collective-permute-done.9 = f32[2,1,16,4096]{3,2,1,0:T(8,128)S(1)} collective-permute-done((f32[2,1,16,4096]{3,2,1,0:T(8,128)S(1)}, f32[2,1,16,4096]{3,2,1,0:T(8,128)S(1)}, u32[]{:S(2)}, u32[]{:S(2)}) %collective-permute-start.9) | collective-permute-done | bytes 524320 | tf_op jit(solution)/shard_map/ppermute | solution.py:24
  66.6 0.7 convolution_bitcast_fusion
  68.5 1.1 %fusion.18 = f32[1,32,32,256]{3,2,1,0:T(8,128)S(1)} fusion(f32[1,32,32,32]{3,2,1,0:T(8,128)S(1)} %bitcast.138, f32[1,32,32,128]{3,2,1,0:T(8,128)S(1)} %bitcast.136, f32[1,32,32,32]{3,2,1,0:T(8,128)S(1)} %bitcast.134, f32[1,32,32,128]{3,2,1,0:T(8,128)S(1)} %bitcast.132, f32[160,128]{1,0:T(8,128)S(1)} %get-tuple-element.6, f32[160,128]{1,0:T(8,128)S(1)} %neg.5, ...), kind=kOutput, calls=%fused_computation.30 | convolution fusion | flops 504545280 | bytes 2605056 | tf_op jit(solution)/shard_map/...nj,jc->...nc/dot_general | solution.py:68
  70.0 1.0 %pad_maximum_fusion.1 = f32[2,1,32,4096]{3,2,1,0:T(8,128)} fusion(f32[1,1,32,4096]{3,2,1,0:T(8,128)S(1)} %stack_reshape.7, f32[1,1,32,4096]{3,2,1,0:T(8,128)S(1)} %stack_reshape.6), kind=kLoop, calls=%fused_computation.36 | loop fusion | flops 262144 | bytes 2097152 | tf_op jit(solution)/shard_map/stack | solution.py:165
  (60 shorter events, 8.6 us)
Async XLA Ops:
  0.8 11.7 %collective-permute-start = (f32[16,512]{1,0:T(8,128)S(1)}, f32[16,512]{1,0:T(8,128)S(1)}, u32[]{:S(2)}, u32[]{:S(2)}) collective-permute-start(f32[16,512]{1,0:T(8,128)S(1)} %get-tuple-element.37), channel_id=1, source_target_pairs={{0,1},{1,2},{2,3},{4,5},{5,6},{6,7},{8,9},{9,10},{10,11},{12,13},{... | collective-permute-start | bytes 98312 | tf_op jit(solution)/shard_map/ppermute | solution.py:22
  5.3 7.2 %collective-permute-start.1 = (f32[16,512]{1,0:T(8,128)S(1)}, f32[16,512]{1,0:T(8,128)S(1)}, u32[]{:S(2)}, u32[]{:S(2)}) collective-permute-start(f32[16,512]{1,0:T(8,128)S(1)} %get-tuple-element.38), channel_id=1, source_target_pairs={{1,0},{2,1},{3,2},{5,4},{6,5},{7,6},{9,8},{10,9},{11,10},{13,12},{... | collective-permute-start | bytes 98312 | tf_op jit(solution)/shard_map/ppermute | solution.py:24
  12.5 8.6 %collective-permute-start.3 = (f32[96,512]{1,0:T(8,128)S(1)}, f32[96,512]{1,0:T(8,128)S(1)}, u32[]{:S(2)}, u32[]{:S(2)}) collective-permute-start(f32[96,512]{1,0:T(8,128)S(1)} %pad_maximum_fusion.4), channel_id=1, source_target_pairs={{0,8},{4,12},{8,0},{12,4},{16,24},{20,28},{24,16},{28,20},{1,9},{5... | collective-permute-start | bytes 589832 | tf_op jit(solution)/shard_map/ppermute | solution.py:106
  13.9 10.6 %collective-permute-start.4 = (f32[96,512]{1,0:T(8,128)S(1)}, f32[96,512]{1,0:T(8,128)S(1)}, u32[]{:S(2)}, u32[]{:S(2)}) collective-permute-start(f32[96,512]{1,0:T(8,128)S(1)} %pad_maximum_fusion.4), channel_id=1, source_target_pairs={{0,16},{4,20},{8,24},{12,28},{16,0},{20,4},{24,8},{28,12},{1,17},{... | collective-permute-start | bytes 589832 | tf_op jit(solution)/shard_map/ppermute | solution.py:106
  16.9 9.0 %collective-permute-start.2 = (f32[96,512]{1,0:T(8,128)S(1)}, f32[96,512]{1,0:T(8,128)S(1)}, u32[]{:S(2)}, u32[]{:S(2)}) collective-permute-start(f32[96,512]{1,0:T(8,128)S(1)} %pad_maximum_fusion.4), channel_id=1, source_target_pairs={{0,4},{4,0},{8,12},{12,8},{16,20},{20,16},{24,28},{28,24},{1,5},{5... | collective-permute-start | bytes 589832 | tf_op jit(solution)/shard_map/ppermute | solution.py:106
  24.6 7.6 %collective-permute-start.5 = (f32[2,96,512]{2,1,0:T(8,128)S(1)}, f32[2,96,512]{2,1,0:T(8,128)S(1)}, u32[]{:S(2)}, u32[]{:S(2)}) collective-permute-start(f32[2,96,512]{2,1,0:T(8,128)S(1)} %pad_maximum_fusion.3), channel_id=1, source_target_pairs={{0,4},{4,0},{8,12},{12,8},{16,20},{20,16},{24,28},{28,24},{1,5},{5... | collective-permute-start | bytes 1179656 | tf_op jit(solution)/shard_map/ppermute | solution.py:106
  25.9 6.3 %collective-permute-start.6 = (f32[96,512]{1,0:T(8,128)S(1)}, f32[96,512]{1,0:T(8,128)S(1)}, u32[]{:S(2)}, u32[]{:S(2)}) collective-permute-start(f32[96,512]{1,0:T(8,128)S(1)} %collective-permute-done.4), channel_id=1, source_target_pairs={{0,8},{4,12},{8,0},{12,4},{16,24},{20,28},{24,16},{28,20},{1,9},{5... | collective-permute-start | bytes 589832 | tf_op jit(solution)/shard_map/ppermute | solution.py:106
  25.9 11.9 %collective-permute-start.7 = (f32[96,512]{1,0:T(8,128)S(1)}, f32[96,512]{1,0:T(8,128)S(1)}, u32[]{:S(2)}, u32[]{:S(2)}) collective-permute-start(f32[96,512]{1,0:T(8,128)S(1)} %collective-permute-done.2), channel_id=1, source_target_pairs={{0,24},{4,28},{8,16},{12,20},{16,8},{20,12},{24,0},{28,4},{1,25},{... | collective-permute-start | bytes 589832 | tf_op jit(solution)/shard_map/ppermute | solution.py:106
  52.4 1.1 %copy-start = (f32[1,1,32,4096]{3,2,1,0:T(8,128)S(1)}, f32[1,1,32,4096]{3,2,1,0:T(8,128)}, u32[]{:S(2)}) copy-start(f32[1,1,32,4096]{3,2,1,0:T(8,128)} %sin.67) | copy-start | bytes 1572868
  52.4 1.2 %copy-start.1 = (f32[1,1,32,4096]{3,2,1,0:T(8,128)S(1)}, f32[1,1,32,4096]{3,2,1,0:T(8,128)}, u32[]{:S(2)}) copy-start(f32[1,1,32,4096]{3,2,1,0:T(8,128)} %cos.67) | copy-start | bytes 1572868
  53.8 8.0 %collective-permute-start.8 = (f32[2,1,16,4096]{3,2,1,0:T(8,128)S(1)}, f32[2,1,16,4096]{3,2,1,0:T(8,128)S(1)}, u32[]{:S(2)}, u32[]{:S(2)}) collective-permute-start(f32[2,1,16,4096]{3,2,1,0:T(8,128)S(1)} %get-tuple-element.19), channel_id=1, source_target_pairs={{0,1},{1,2},{2,3},{4,5},{5,6},{6,7},{8,9},{9,10},{10,11},{12,13},{... | collective-permute-start | bytes 1572872 | tf_op jit(solution)/shard_map/ppermute | solution.py:22
  55.8 10.5 %collective-permute-start.9 = (f32[2,1,16,4096]{3,2,1,0:T(8,128)S(1)}, f32[2,1,16,4096]{3,2,1,0:T(8,128)S(1)}, u32[]{:S(2)}, u32[]{:S(2)}) collective-permute-start(f32[2,1,16,4096]{3,2,1,0:T(8,128)S(1)} %get-tuple-element.20), channel_id=1, source_target_pairs={{1,0},{2,1},{3,2},{5,4},{6,5},{7,6},{9,8},{10,9},{11,10},{13,12},{... | collective-permute-start | bytes 1572872 | tf_op jit(solution)/shard_map/ppermute | solution.py:24

commit v10 on v8

--- a/solution.py
+++ b/solution.py
@@ -111,8 +111,11 @@
         six = exchange(four, 2)
         seven = exchange(one, 6)
         parts = [stored_planes, one, two, three, four, five, six, seven]
+        first = [three, six, seven]
     else:
         parts = [stored_planes] + [exchange(stored_planes, k) for k in range(1, count)]
+        first = parts[1:]
+    landed = sum(part[0, 0, 0] for part in first) * 0.0
     stacked = jnp.stack(parts, axis=1)
     rows = stored_planes.shape[1]
     width = stored_planes.shape[2]
@@ -121,7 +124,7 @@
         source = jnp.bitwise_xor(me, owner[p]) if paired else jnp.mod(me - owner[p], count)
         picked = stacked[p][source]
         planes.append(jnp.transpose(picked, (1, 0, 2)).reshape(rows, count * width))
-    return jnp.stack(planes)
+    return jnp.stack(planes), landed
 
 
 def body(tilts, taps, stored_planes, owner):
@@ -129,7 +132,8 @@
     total_rows = local_rows * lax.axis_size("tile")
     total_cols = NY
     first_row = lax.axis_index("tile") * local_rows
-    screens = gather_screens(stored_planes, owner, "illum")
+    screens, landed = gather_screens(stored_planes, owner, "illum")
+    taps = taps + landed
     extra = HALF
     span = local_rows + 2 * extra
     global_rows = first_row - extra + jnp.arange(span, dtype=jnp.int32)

time: 66.4 us -> 65.5 us (0.986)
  other arithmetic: 9.17 us -> 5.97 us
  between operations: 0.6 us -> 2.33 us
  local copies, waits for them, and re-layouts: 18.3 us -> 19.1 us
  waiting for transfers between devices: 14.2 us -> 13.5 us
    slice x0 -> x3, local copies, waits for them, and re-layouts: none -> 1.54 us  [gather_screens(): landed = sum((part[0, 0, 0] for part in first)) * 0.0]
    unnamed x5, other arithmetic: 2.31 us -> 0.9 us
    ppermute x6, starting transfers between devices: 7.2 us -> 8.34 us  [exchange(): return lax.ppermute(x, axis, [(i, partner(i, k)) for i in range(count)])]
    squeeze x1, local copies, waits for them, and re-layouts: 0.76 us -> 0.01 us  [cross_pass(): taps[0]]
    slice x1, local copies, waits for them, and re-layouts: 0.02 us -> 0.72 us  [extended(): lax.slice_in_dim(cells, cells.shape[dim] - width, cells.shape[dim], axis=...]
    ppermute x6, waiting for transfers between devices: 5.79 us -> 5.12 us  [exchange(): return lax.ppermute(x, axis, [(i, partner(i, k)) for i in range(count)])]
    unnamed x38 -> x30, local copies, waits for them, and re-layouts: 3.46 us -> 3.41 us
  transfers between devices with their start and end apart: 10 -> 10, of which waited for: 4 -> 4; matrix products, arithmetic and copies ran while one was open for 28% -> 24% of each run, Pallas kernels for 0% -> 0%
where the time goes in v10:
time: 65.5 us; the launch traced here: 65.2 us
  starting transfers between devices  20.6 us (31%)
  local copies, waits for them, and re-layouts  19.1 us (29%)
  waiting for transfers between devices  13.5 us (21%)
  other arithmetic  5.97 us (9%)
  matrix products  3.64 us (6%)
  between operations  2.33 us (4%)
    ppermute x6, starting transfers between devices, exchange(): return lax.ppermute(x, axis, [(i, partner(i, k)) for i in range(count)])  8.34 us
    ppermute x2, starting transfers between devices, extended(): lax.ppermute(tail, axis, [(i, (i + 1) % count) for i in range(ends)])  8.27 us
    ppermute x6, waiting for transfers between devices, exchange(): return lax.ppermute(x, axis, [(i, partner(i, k)) for i in range(count)])  5.12 us
    cos x7, local copies, waits for them, and re-layouts, transmit(): cosine = jnp.cos(screen)  4.61 us
    ppermute x2, waiting for transfers between devices, extended(): lax.ppermute(head, axis, [((i + 1) % count, i) for i in range(ends)])  4.4 us
    ppermute x2, starting transfers between devices, extended(): lax.ppermute(head, axis, [((i + 1) % count, i) for i in range(ends)])  4.01 us
    ppermute x2, waiting for transfers between devices, extended(): lax.ppermute(tail, axis, [(i, (i + 1) % count) for i in range(ends)])  4 us
    unnamed x30, local copies, waits for them, and re-layouts  3.41 us
  transfers between devices with their start and end apart: 10, of which 4 were waited for; matrix products, arithmetic and copies ran while one was open for 24% of the time, Pallas kernels for 0%

profile of v10, /device:TPU:1, one launch (start us, length us, event | category | flops | bytes accessed | tf_op | source)
XLA Modules:
  0.0 65.2 jit_solution(616789456661387314)
XLA Ops:
  0.0 3.1 %collective-permute-start.2 = (f32[2,32,512]{2,1,0:T(8,128)}, f32[2,32,512]{2,1,0:T(8,128)S(1)}, u32[]{:S(2)}, u32[]{:S(2)}) collective-permute-start(f32[2,32,512]{2,1,0:T(8,128)} %param.6), channel_id=1, source_target_pairs={{0,16},{4,20},{8,24},{12,28},{16,0},{20,4},{24,8},{28,12},{1,17},{... | collective-permute-start | bytes 393224 | tf_op jit(solution)/shard_map/ppermute | solution.py:106
  3.1 1.3 %collective-permute-start.1 = (f32[2,32,512]{2,1,0:T(8,128)}, f32[2,32,512]{2,1,0:T(8,128)S(1)}, u32[]{:S(2)}, u32[]{:S(2)}) collective-permute-start(f32[2,32,512]{2,1,0:T(8,128)} %param.6), channel_id=1, source_target_pairs={{0,8},{4,12},{8,0},{12,4},{16,24},{20,28},{24,16},{28,20},{1,9},{5... | collective-permute-start | bytes 393224 | tf_op jit(solution)/shard_map/ppermute | solution.py:106
  4.4 1.2 %collective-permute-start = (f32[2,32,512]{2,1,0:T(8,128)}, f32[2,32,512]{2,1,0:T(8,128)S(1)}, u32[]{:S(2)}, u32[]{:S(2)}) collective-permute-start(f32[2,32,512]{2,1,0:T(8,128)} %param.6), channel_id=1, source_target_pairs={{0,4},{4,0},{8,12},{12,8},{16,20},{20,16},{24,28},{28,24},{1,5},{5... | collective-permute-start | bytes 393224 | tf_op jit(solution)/shard_map/ppermute | solution.py:106
  5.7 0.9 %bitcast_dynamic-update-slice_fusion.10 = f32[2,8,32,512]{3,2,0,1:T(8,128)S(1)} fusion(f32[2,32,512]{2,1,0:T(8,128)} %param.6), kind=kLoop, calls=%fused_computation.78 | loop fusion | bytes 262144
  6.6 1.3 %fusion.44 = (s32[1,1]{1,0:T(1,128)}, s32[1,1]{1,0:T(1,128)}) fusion(s32[1,2]{1,0:T(1,128)} %param.4), kind=kLoop, calls=%fused_computation.131 | loop fusion | bytes 16 | tf_op jit(solution)/shard_map/slice | solution.py:143
  8.0 0.7 %sine_select_fusion = (f32[1,64,1]{1,2,0:T(1,128)S(1)}, f32[1,64,1]{1,2,0:T(1,128)S(1)}) fusion(s32[]{:T(128)S(6)} %sub.149, s32[]{:T(128)} %bitcast), kind=kLoop, calls=%fused_computation.115 | loop fusion | flops 1280 | bytes 520 | tf_op jit(solution)/shard_map/jit(_where)/select_n | solution.py:147
  8.7 0.6 slice_bitcast_fusion.20
  9.9 0.6 slice_bitcast_fusion.21
  10.5 0.7 %fusion.27 = (f32[4096]{0:T(1024)S(1)}, f32[4096]{0:T(1024)S(1)}) fusion(s32[]{:T(128)} %bitcast.2), kind=kLoop, calls=%fused_computation.92 | loop fusion | flops 57344 | bytes 32772 | tf_op jit(solution)/shard_map/sin | solution.py:149
  11.2 0.8 %fusion.33 = (s32[8]{0:T(128)S(1)}, s32[8]{0:T(128)S(1)}) fusion(s32[2,8]{1,0:T(2,128)} %param.7, s32[]{:T(128)S(6)} %axis_index.25), kind=kLoop, calls=%fused_computation.106 | loop fusion | flops 64 | bytes 132 | tf_op jit(solution)/shard_map/select_n | solution.py:125
  12.5 2.2 %collective-permute-start.5 = (f32[2,32,512]{2,1,0:T(8,128)S(1)}, f32[2,32,512]{2,1,0:T(8,128)S(1)}, u32[]{:S(2)}, u32[]{:S(2)}) collective-permute-start(f32[2,32,512]{2,1,0:T(8,128)S(1)} %collective-permute-done), channel_id=1, source_target_pairs={{0,24},{4,28},{8,16},{12,20},{16,8},{20,12},{24,0},{28,4},{1,25},{... | collective-permute-start | bytes 393224 | tf_op jit(solution)/shard_map/ppermute | solution.py:106
  14.7 1.4 %collective-permute-done.4 = f32[2,32,512]{2,1,0:T(8,128)S(1)} collective-permute-done((f32[2,32,512]{2,1,0:T(8,128)S(1)}, f32[2,32,512]{2,1,0:T(8,128)S(1)}, u32[]{:S(2)}, u32[]{:S(2)}) %collective-permute-start.4) | collective-permute-done | bytes 131104 | tf_op jit(solution)/shard_map/ppermute | solution.py:106
  16.7 3.7 %collective-permute-done.5 = f32[2,32,512]{2,1,0:T(8,128)S(1)} collective-permute-done((f32[2,32,512]{2,1,0:T(8,128)S(1)}, f32[2,32,512]{2,1,0:T(8,128)S(1)}, u32[]{:S(2)}, u32[]{:S(2)}) %collective-permute-start.5) | collective-permute-done | bytes 131104 | tf_op jit(solution)/shard_map/ppermute | solution.py:106
  21.1 0.6 gather_fusion
  21.7 1.9 %bitcast_cosine_fusion = (f32[32,8,512]{2,0,1:T(8,128)S(1)}, f32[32,8,512]{2,0,1:T(8,128)S(1)}) fusion(f32[8,32,512]{2,1,0:T(8,128)S(1)} %gather_fusion), kind=kLoop, calls=%fused_computation.124 | loop fusion | bytes 1572864 | tf_op jit(solution)/shard_map/cos | solution.py:81
  23.6 0.7 %copy.17 = f32[8,2,8,512]{3,2,0,1:T(8,128)} copy(f32[8,2,8,512]{3,2,1,0:T(8,128)S(1)} %get-tuple-element.36) | data formatting | bytes 524288 | tf_op jit(solution)/shard_map/slice | solution.py:19
  24.3 4.6 %collective-permute-start.6 = (f32[16,4096]{1,0:T(8,128)}, f32[16,4096]{1,0:T(8,128)S(1)}, u32[]{:S(2)}, u32[]{:S(2)}) collective-permute-start(f32[16,4096]{1,0:T(8,128)} %bitcast.51), channel_id=1, source_target_pairs={{0,1},{1,2},{2,3},{4,5},{5,6},{6,7},{8,9},{9,10},{10,11},{12,13},{... | collective-permute-start | bytes 786440 | tf_op jit(solution)/shard_map/ppermute | solution.py:22
  29.8 0.7 %copy.18 = f32[8,2,8,512]{3,2,0,1:T(8,128)} copy(f32[8,2,8,512]{3,2,1,0:T(8,128)S(1)} %get-tuple-element.35) | data formatting | bytes 524288 | tf_op jit(solution)/shard_map/slice | solution.py:18
  30.6 1.9 %collective-permute-start.7 = (f32[16,4096]{1,0:T(8,128)}, f32[16,4096]{1,0:T(8,128)S(1)}, u32[]{:S(2)}, u32[]{:S(2)}) collective-permute-start(f32[16,4096]{1,0:T(8,128)} %bitcast.53), channel_id=1, source_target_pairs={{1,0},{2,1},{3,2},{5,4},{6,5},{7,6},{9,8},{10,9},{11,10},{13,12},{... | collective-permute-start | bytes 786440 | tf_op jit(solution)/shard_map/ppermute | solution.py:24
  34.9 1.1 %select_reduce_fusion = (f32[160,128]{1,0:T(8,128)S(1)}, f32[160,128]{1,0:T(8,128)}) fusion(f32[33]{0:T(128)S(1)} %get-tuple-element.46, s32[160,128]{1,0:T(8,128)S(1)} %iota_subtract_fusion, f32[33]{0:T(128)S(1)} %get-tuple-element.45), kind=kLoop, calls=%fused_computation.4 | loop fusion | flops 3338240 | bytes 246024 | tf_op jit(solution)/shard_map/reduce_sum | solution.py:36
  36.6 1.9 %sine_bitcast_fusion = (f32[32,8,512]{2,0,1:T(8,128)S(1)}, f32[32,8,512]{2,0,1:T(8,128)S(1)}) fusion(f32[8,32,512]{2,1,0:T(8,128)S(1)} %gather_fusion.1), kind=kLoop, calls=%fused_computation.48 | loop fusion | bytes 1572864 | tf_op jit(solution)/shard_map/sin | solution.py:82
  39.4 1.0 %fusion.43 = (f32[16,4096]{1,0:T(8,128)S(1)}, f32[16,4096]{1,0:T(8,128)S(1)}) fusion(f32[16,4096]{1,0:T(8,128)S(1)} %collective-permute-done.6), kind=kLoop, calls=%fused_computation.130 | loop fusion | bytes 786432 | tf_op jit(solution)/shard_map/cos | solution.py:81
  40.8 1.0 %fusion.42 = (f32[16,4096]{1,0:T(8,128)S(1)}, f32[16,4096]{1,0:T(8,128)S(1)}) fusion(f32[16,4096]{1,0:T(8,128)S(1)} %collective-permute-done.7), kind=kLoop, calls=%fused_computation.129 | loop fusion | bytes 786432 | tf_op jit(solution)/shard_map/cos | solution.py:81
  42.5 0.7 %convolution_bitcast_fusion.1 = f32[1,64,4096]{2,1,0:T(8,128)S(1)} fusion(f32[1,128,4096]{2,1,0:T(8,128)S(1)} %bitcast_dynamic-update-slice_fusion, f32[32,64]{1,0:T(8,128)S(1)} %get-tuple-element.8, f32[32,64]{1,0:T(8,128)S(1)} %get-tuple-element.7, f32[32,64]{1,0:T(8,128)S(1)} %neg.4), kind=kOutput, calls=%fused_computation.3 | convolution fusion | flops 201351168 | bytes 3170304 | tf_op jit(solution)/shard_map/ij,ajy->aiy/dot_general | solution.py:76
  44.5 1.1 %fusion.18 = f32[1,32,32,256]{3,2,1,0:T(8,128)S(1)} fusion(f32[1,32,32,32]{3,2,1,0:T(8,128)S(1)} %bitcast.164, f32[1,32,32,128]{3,2,1,0:T(8,128)S(1)} %bitcast.170, f32[1,32,32,32]{3,2,1,0:T(8,128)S(1)} %bitcast.166, f32[1,32,32,128]{3,2,1,0:T(8,128)S(1)} %bitcast.168, f32[160,128]{1,0:T(8,128)S(1)} %copy-done, f32[160,128]{1,0:T(8,128)S(1)} %neg.5, ...), kind=kOutput, calls=%fused_computation.29 | convolution fusion | flops 504545280 | bytes 2605056 | tf_op jit(solution)/shard_map/...nj,jc->...nc/dot_general | solution.py:68
  46.2 3.6 %collective-permute-start.8 = (f32[2,1,16,4096]{3,2,1,0:T(8,128)S(1)}, f32[2,1,16,4096]{3,2,1,0:T(8,128)S(1)}, u32[]{:S(2)}, u32[]{:S(2)}) collective-permute-start(f32[2,1,16,4096]{3,2,1,0:T(8,128)S(1)} %get-tuple-element.17), channel_id=1, source_target_pairs={{0,1},{1,2},{2,3},{4,5},{5,6},{6,7},{8,9},{9,10},{10,11},{12,13},{... | collective-permute-start | bytes 1572872 | tf_op jit(solution)/shard_map/ppermute | solution.py:22
  49.9 2.1 %collective-permute-start.9 = (f32[2,1,16,4096]{3,2,1,0:T(8,128)S(1)}, f32[2,1,16,4096]{3,2,1,0:T(8,128)S(1)}, u32[]{:S(2)}, u32[]{:S(2)}) collective-permute-start(f32[2,1,16,4096]{3,2,1,0:T(8,128)S(1)} %get-tuple-element.18), channel_id=1, source_target_pairs={{1,0},{2,1},{3,2},{5,4},{6,5},{7,6},{9,8},{10,9},{11,10},{13,12},{... | collective-permute-start | bytes 1572872 | tf_op jit(solution)/shard_map/ppermute | solution.py:24
  52.0 4.0 %collective-permute-done.8 = f32[2,1,16,4096]{3,2,1,0:T(8,128)S(1)} collective-permute-done((f32[2,1,16,4096]{3,2,1,0:T(8,128)S(1)}, f32[2,1,16,4096]{3,2,1,0:T(8,128)S(1)}, u32[]{:S(2)}, u32[]{:S(2)}) %collective-permute-start.8) | collective-permute-done | bytes 524320 | tf_op jit(solution)/shard_map/ppermute | solution.py:22
  56.0 4.4 %collective-permute-done.9 = f32[2,1,16,4096]{3,2,1,0:T(8,128)S(1)} collective-permute-done((f32[2,1,16,4096]{3,2,1,0:T(8,128)S(1)}, f32[2,1,16,4096]{3,2,1,0:T(8,128)S(1)}, u32[]{:S(2)}, u32[]{:S(2)}) %collective-permute-start.9) | collective-permute-done | bytes 524320 | tf_op jit(solution)/shard_map/ppermute | solution.py:24
  60.8 0.7 %convolution_bitcast_fusion = f32[1,64,4096]{2,1,0:T(8,128)S(1)} fusion(f32[1,64,4096]{2,1,0:T(8,128)S(1)} %get-tuple-element.10, f32[1,64,4096]{2,1,0:T(8,128)S(1)} %get-tuple-element.9, f32[32,64]{1,0:T(8,128)S(1)} %get-tuple-element.8, f32[32,64]{1,0:T(8,128)S(1)} %get-tuple-element.7, f32[32,64]{1,0:T(8,128)S(1)} %neg.4), kind=kOutput, calls=%fused_computation.2 | convolution fusion | flops 201875456 | bytes 3170304 | tf_op jit(solution)/shard_map/ij,ajy->aiy/dot_general | solution.py:76
  62.6 1.1 %fusion.17 = f32[1,32,32,256]{3,2,1,0:T(8,128)S(1)} fusion(f32[1,32,32,32]{3,2,1,0:T(8,128)S(1)} %bitcast.163, f32[1,32,32,128]{3,2,1,0:T(8,128)S(1)} %bitcast.169, f32[1,32,32,32]{3,2,1,0:T(8,128)S(1)} %bitcast.165, f32[1,32,32,128]{3,2,1,0:T(8,128)S(1)} %bitcast.167, f32[160,128]{1,0:T(8,128)S(1)} %copy-done, f32[160,128]{1,0:T(8,128)S(1)} %neg.5, ...), kind=kOutput, calls=%fused_computation.28 | convolution fusion | flops 504545280 | bytes 2605056 | tf_op jit(solution)/shard_map/...nj,jc->...nc/dot_general | solution.py:68
  64.1 1.0 %pad_maximum_fusion.1 = f32[2,1,32,4096]{3,2,1,0:T(8,128)} fusion(f32[1,1,32,4096]{3,2,1,0:T(8,128)S(1)} %stack_reshape.7, f32[1,1,32,4096]{3,2,1,0:T(8,128)S(1)} %stack_reshape.6), kind=kLoop, calls=%fused_computation.34 | loop fusion | flops 262144 | bytes 2097152 | tf_op jit(solution)/shard_map/stack | solution.py:174
  (81 shorter events, 10.0 us)
Async XLA Ops:
  0.0 12.0 %collective-permute-start.2 = (f32[2,32,512]{2,1,0:T(8,128)}, f32[2,32,512]{2,1,0:T(8,128)S(1)}, u32[]{:S(2)}, u32[]{:S(2)}) collective-permute-start(f32[2,32,512]{2,1,0:T(8,128)} %param.6), channel_id=1, source_target_pairs={{0,16},{4,20},{8,24},{12,28},{16,0},{20,4},{24,8},{28,12},{1,17},{... | collective-permute-start | bytes 393224 | tf_op jit(solution)/shard_map/ppermute | solution.py:106
  3.1 8.9 %collective-permute-start.1 = (f32[2,32,512]{2,1,0:T(8,128)}, f32[2,32,512]{2,1,0:T(8,128)S(1)}, u32[]{:S(2)}, u32[]{:S(2)}) collective-permute-start(f32[2,32,512]{2,1,0:T(8,128)} %param.6), channel_id=1, source_target_pairs={{0,8},{4,12},{8,0},{12,4},{16,24},{20,28},{24,16},{28,20},{1,9},{5... | collective-permute-start | bytes 393224 | tf_op jit(solution)/shard_map/ppermute | solution.py:106
  4.4 8.1 %collective-permute-start = (f32[2,32,512]{2,1,0:T(8,128)}, f32[2,32,512]{2,1,0:T(8,128)S(1)}, u32[]{:S(2)}, u32[]{:S(2)}) collective-permute-start(f32[2,32,512]{2,1,0:T(8,128)} %param.6), channel_id=1, source_target_pairs={{0,4},{4,0},{8,12},{12,8},{16,20},{20,16},{24,28},{28,24},{1,5},{5... | collective-permute-start | bytes 393224 | tf_op jit(solution)/shard_map/ppermute | solution.py:106
  12.0 8.9 %collective-permute-start.3 = (f32[2,2,32,512]{3,2,1,0:T(8,128)S(1)}, f32[2,2,32,512]{3,2,1,0:T(8,128)S(1)}, u32[]{:S(2)}, u32[]{:S(2)}) collective-permute-start(f32[2,2,32,512]{3,2,1,0:T(8,128)S(1)} %pad_maximum_fusion.3), channel_id=1, source_target_pairs={{0,4},{4,0},{8,12},{12,8},{16,20},{20,16},{24,28},{28,24},{1,5},{5... | collective-permute-start | bytes 786440 | tf_op jit(solution)/shard_map/ppermute | solution.py:106
  12.3 3.8 %collective-permute-start.4 = (f32[2,32,512]{2,1,0:T(8,128)S(1)}, f32[2,32,512]{2,1,0:T(8,128)S(1)}, u32[]{:S(2)}, u32[]{:S(2)}) collective-permute-start(f32[2,32,512]{2,1,0:T(8,128)S(1)} %collective-permute-done.2), channel_id=1, source_target_pairs={{0,8},{4,12},{8,0},{12,4},{16,24},{20,28},{24,16},{28,20},{1,9},{5... | collective-permute-start | bytes 393224 | tf_op jit(solution)/shard_map/ppermute | solution.py:106
  12.5 7.9 %collective-permute-start.5 = (f32[2,32,512]{2,1,0:T(8,128)S(1)}, f32[2,32,512]{2,1,0:T(8,128)S(1)}, u32[]{:S(2)}, u32[]{:S(2)}) collective-permute-start(f32[2,32,512]{2,1,0:T(8,128)S(1)} %collective-permute-done), channel_id=1, source_target_pairs={{0,24},{4,28},{8,16},{12,20},{16,8},{20,12},{24,0},{28,4},{1,25},{... | collective-permute-start | bytes 393224 | tf_op jit(solution)/shard_map/ppermute | solution.py:106
  24.3 15.1 %collective-permute-start.6 = (f32[16,4096]{1,0:T(8,128)}, f32[16,4096]{1,0:T(8,128)S(1)}, u32[]{:S(2)}, u32[]{:S(2)}) collective-permute-start(f32[16,4096]{1,0:T(8,128)} %bitcast.51), channel_id=1, source_target_pairs={{0,1},{1,2},{2,3},{4,5},{5,6},{6,7},{8,9},{9,10},{10,11},{12,13},{... | collective-permute-start | bytes 786440 | tf_op jit(solution)/shard_map/ppermute | solution.py:22
  29.3 5.4 %copy-start.4 = (f32[2,33]{1,0:T(2,128)S(1)}, f32[2,33]{1,0:T(2,128)}, u32[]{:S(2)}) copy-start(f32[2,33]{1,0:T(2,128)} %param.5) | copy-start | bytes 796
  30.6 10.2 %collective-permute-start.7 = (f32[16,4096]{1,0:T(8,128)}, f32[16,4096]{1,0:T(8,128)S(1)}, u32[]{:S(2)}, u32[]{:S(2)}) collective-permute-start(f32[16,4096]{1,0:T(8,128)} %bitcast.53), channel_id=1, source_target_pairs={{1,0},{2,1},{3,2},{5,4},{6,5},{7,6},{9,8},{10,9},{11,10},{13,12},{... | collective-permute-start | bytes 786440 | tf_op jit(solution)/shard_map/ppermute | solution.py:24
  38.8 1.5 %copy-start.1 = (f32[16]{0:T(128)S(1)}, f32[16]{0:T(128)}, u32[]{:S(2)}) copy-start(f32[16]{0:T(128)} %get-tuple-element.48) | copy-start | bytes 196
  38.9 1.6 %copy-start.2 = (f32[32]{0:T(128)S(1)}, f32[32]{0:T(128)}, u32[]{:S(2)}) copy-start(f32[32]{0:T(128)} %slice_bitcast_fusion.20) | copy-start | bytes 388
  39.0 1.6 %copy-start.3 = (f32[32]{0:T(128)S(1)}, f32[32]{0:T(128)}, u32[]{:S(2)}) copy-start(f32[32]{0:T(128)} %slice_bitcast_fusion.21) | copy-start | bytes 388
  43.7 0.9 %copy-start = (f32[160,128]{1,0:T(8,128)S(1)}, f32[160,128]{1,0:T(8,128)}, u32[]{:S(2)}) copy-start(f32[160,128]{1,0:T(8,128)} %get-tuple-element.6) | copy-start | bytes 245764
  46.2 9.8 %collective-permute-start.8 = (f32[2,1,16,4096]{3,2,1,0:T(8,128)S(1)}, f32[2,1,16,4096]{3,2,1,0:T(8,128)S(1)}, u32[]{:S(2)}, u32[]{:S(2)}) collective-permute-start(f32[2,1,16,4096]{3,2,1,0:T(8,128)S(1)} %get-tuple-element.17), channel_id=1, source_target_pairs={{0,1},{1,2},{2,3},{4,5},{5,6},{6,7},{8,9},{9,10},{10,11},{12,13},{... | collective-permute-start | bytes 1572872 | tf_op jit(solution)/shard_map/ppermute | solution.py:22
  49.9 10.5 %collective-permute-start.9 = (f32[2,1,16,4096]{3,2,1,0:T(8,128)S(1)}, f32[2,1,16,4096]{3,2,1,0:T(8,128)S(1)}, u32[]{:S(2)}, u32[]{:S(2)}) collective-permute-start(f32[2,1,16,4096]{3,2,1,0:T(8,128)S(1)} %get-tuple-element.18), channel_id=1, source_target_pairs={{1,0},{2,1},{3,2},{5,4},{6,5},{7,6},{9,8},{10,9},{11,10},{13,12},{... | collective-permute-start | bytes 1572872 | tf_op jit(solution)/shard_map/ppermute | solution.py:24

commit v11 on v10

--- a/solution.py
+++ b/solution.py
@@ -61,20 +61,20 @@
     return jnp.concatenate([top, bottom], axis=0)
 
 
-def along_pass(real, imag, taps):
-    block = min(128, real.shape[-1])
-    win = jnp.concatenate([windows(real, block), windows(imag, block)], axis=-1)
+def along_pass(packed, taps):
+    block = min(128, packed.shape[-1])
+    win = windows(packed, block)
     kern = complex_stack(toeplitz(taps[0], block), -toeplitz(taps[1], block))
-    out = jnp.einsum("...nj,jc->...nc", win, kern, precision=lax.Precision.HIGH)
-    return out[..., :block].reshape(real.shape), out[..., block:].reshape(real.shape)
+    kern = kern.reshape(2, block + 2 * HALF, 2, block)
+    out = jnp.einsum("q...nj,qjpc->p...nc", win, kern, precision=lax.Precision.HIGH)
+    return out.reshape(packed.shape)
 
 
-def cross_pass(real, imag, taps):
-    count = real.shape[1] - 2 * HALF
+def cross_pass(packed, taps):
+    count = packed.shape[-2] - 2 * HALF
     band = complex_stack(band_matrix(taps[0], count), band_matrix(taps[1], count))
-    field = jnp.concatenate([real, imag], axis=1)
-    out = jnp.einsum("ij,ajy->aiy", band, field, precision=lax.Precision.HIGH)
-    return out[:, :count], out[:, count:]
+    band = band.reshape(2, count, 2, count + 2 * HALF)
+    return jnp.einsum("piqj,q...jy->p...iy", band, packed, precision=lax.Precision.HIGH)
 
 
 def transmit(real, imag, screen):
@@ -164,14 +164,12 @@
     ]
     real = jnp.concatenate([piece[0] for piece in pieces], axis=1)
     imag = jnp.concatenate([piece[1] for piece in pieces], axis=1)
-    real, imag = cross_pass(real, imag, taps)
-    real, imag = along_pass(real, imag, taps)
+    packed = along_pass(cross_pass(jnp.stack([real, imag]), taps), taps)
     for plane in range(1, PLANES):
-        real, imag = transmit(real, imag, screens[plane])
+        real, imag = transmit(packed[0], packed[1], screens[plane])
         packed = extended(jnp.stack([real, imag]), (("tile", 2),), HALF)
-        real, imag = cross_pass(packed[0], packed[1], taps)
-        real, imag = along_pass(real, imag, taps)
-    return jnp.stack([real, imag])
+        packed = along_pass(cross_pass(packed, taps), taps)
+    return packed
 
 
 def solution(mesh):

time: 65.5 us -> 68 us (1.038)
  local copies, waits for them, and re-layouts: 19.1 us -> 22.1 us
  other arithmetic: 5.97 us -> 5.16 us
    sin x5 -> x8, local copies, waits for them, and re-layouts: 2.67 us -> 8.25 us  [transmit(): sine = jnp.sin(screen)]
    cos x7 -> x4, local copies, waits for them, and re-layouts: 4.61 us -> 0.81 us  [transmit(): cosine = jnp.cos(screen)]
    unnamed x30, local copies, waits for them, and re-layouts: 3.41 us -> 1.85 us
    reshape x2 -> x3, local copies, waits for them, and re-layouts: 0.2 us -> 1.43 us  [the longest x1 1.16 us: along_pass(): return out.reshape(packed.shape)]
    ppermute x2, starting transfers between devices: 8.27 us -> 9.42 us  [extended(): lax.ppermute(tail, axis, [(i, (i + 1) % count) for i in range(ends)])]
    ppermute x6, starting transfers between devices: 8.34 us -> 7.2 us  [exchange(): return lax.ppermute(x, axis, [(i, partner(i, k)) for i in range(count)])]
    another operation x1 -> x2, other arithmetic: 1.04 us -> 0.14 us  [body(): packed = along_pass(cross_pass(jnp.stack([real, imag]), taps), taps)]
    unnamed x5 -> x0, other arithmetic: 0.9 us -> none
  transfers between devices with their start and end apart: 10 -> 10, of which waited for: 4 -> 4; matrix products, arithmetic and copies ran while one was open for 24% -> 27% of each run, Pallas kernels for 0% -> 0%
where the time goes in v11:
time: 68 us; the launch traced here: 67.7 us
  local copies, waits for them, and re-layouts  22.1 us (32%)
  starting transfers between devices  20.6 us (30%)
  waiting for transfers between devices  13.7 us (20%)
  other arithmetic  5.16 us (8%)
  matrix products  3.45 us (5%)
  between operations  2.54 us (4%)
    ppermute x2, starting transfers between devices, extended(): lax.ppermute(tail, axis, [(i, (i + 1) % count) for i in range(ends)])  9.42 us
    sin x8, local copies, waits for them, and re-layouts, transmit(): sine = jnp.sin(screen)  8.25 us
    ppermute x6, starting transfers between devices, exchange(): return lax.ppermute(x, axis, [(i, partner(i, k)) for i in range(count)])  7.2 us
    ppermute x6, waiting for transfers between devices, exchange(): return lax.ppermute(x, axis, [(i, partner(i, k)) for i in range(count)])  5.34 us
    ppermute x2, waiting for transfers between devices, extended(): lax.ppermute(head, axis, [((i + 1) % count, i) for i in range(ends)])  4.4 us
    ppermute x2, starting transfers between devices, extended(): lax.ppermute(head, axis, [((i + 1) % count, i) for i in range(ends)])  4.01 us
    ppermute x2, waiting for transfers between devices, extended(): lax.ppermute(tail, axis, [(i, (i + 1) % count) for i in range(ends)])  4 us
    mul x4, local copies, waits for them, and re-layouts, incident(): real = across_cos[:, rows] * along_cos - across_sin[:, rows] * along_sin  2.46 us
  transfers between devices with their start and end apart: 10, of which 4 were waited for; matrix products, arithmetic and copies ran while one was open for 27% of the time, Pallas kernels for 0%

profile of v11, /device:TPU:1, one launch (start us, length us, event | category | flops | bytes accessed | tf_op | source)
XLA Modules:
  0.0 67.7 jit_solution(13975585609705459750)
XLA Ops:
  0.0 3.1 %collective-permute-start.1 = (f32[2,32,512]{2,1,0:T(8,128)}, f32[2,32,512]{2,1,0:T(8,128)S(1)}, u32[]{:S(2)}, u32[]{:S(2)}) collective-permute-start(f32[2,32,512]{2,1,0:T(8,128)} %param.6), channel_id=1, source_target_pairs={{0,16},{4,20},{8,24},{12,28},{16,0},{20,4},{24,8},{28,12},{1,17},{... | collective-permute-start | bytes 393224 | tf_op jit(solution)/shard_map/ppermute | solution.py:106
  3.1 1.3 %collective-permute-start = (f32[2,32,512]{2,1,0:T(8,128)}, f32[2,32,512]{2,1,0:T(8,128)S(1)}, u32[]{:S(2)}, u32[]{:S(2)}) collective-permute-start(f32[2,32,512]{2,1,0:T(8,128)} %param.6), channel_id=1, source_target_pairs={{0,8},{4,12},{8,0},{12,4},{16,24},{20,28},{24,16},{28,20},{1,9},{5... | collective-permute-start | bytes 393224 | tf_op jit(solution)/shard_map/ppermute | solution.py:106
  4.4 1.2 %collective-permute-start.4 = (f32[2,32,512]{2,1,0:T(8,128)}, f32[2,32,512]{2,1,0:T(8,128)S(1)}, u32[]{:S(2)}, u32[]{:S(2)}) collective-permute-start(f32[2,32,512]{2,1,0:T(8,128)} %param.6), channel_id=1, source_target_pairs={{0,4},{4,0},{8,12},{12,8},{16,20},{20,16},{24,28},{28,24},{1,5},{5... | collective-permute-start | bytes 393224 | tf_op jit(solution)/shard_map/ppermute | solution.py:106
  5.7 0.9 %bitcast_dynamic-update-slice_fusion.6 = f32[2,8,32,512]{3,2,0,1:T(8,128)S(1)} fusion(f32[2,32,512]{2,1,0:T(8,128)} %param.6), kind=kLoop, calls=%fused_computation.74 | loop fusion | bytes 262144
  6.6 1.3 %fusion.38 = (s32[1,1]{1,0:T(1,128)}, s32[1,1]{1,0:T(1,128)}) fusion(s32[1,2]{1,0:T(1,128)} %param.4), kind=kLoop, calls=%fused_computation.124 | loop fusion | bytes 16 | tf_op jit(solution)/shard_map/slice | solution.py:145
  7.9 0.7 sine_select_fusion
  8.6 0.7 slice_bitcast_fusion.10
  9.3 0.6 slice_bitcast_fusion.8
  9.9 0.6 slice_bitcast_fusion.11
  11.1 1.3 %fusion.26 = (f32[4096]{0:T(1024)S(1)}, f32[4096]{0:T(1024)}) fusion(s32[]{:T(128)} %bitcast.10), kind=kLoop, calls=%fused_computation.90 | loop fusion | flops 57344 | bytes 32772 | tf_op jit(solution)/shard_map/sin | solution.py:149
  12.4 0.8 %fusion.31 = (s32[8]{0:T(128)S(1)}, s32[8]{0:T(128)S(1)}) fusion(s32[2,8]{1,0:T(2,128)} %param.7, s32[]{:T(128)S(6)} %axis_index.25), kind=kLoop, calls=%fused_computation.103 | loop fusion | flops 64 | bytes 132 | tf_op jit(solution)/shard_map/select_n | solution.py:125
  14.3 1.1 %collective-permute-start.5 = (f32[2,32,512]{2,1,0:T(8,128)S(1)}, f32[2,32,512]{2,1,0:T(8,128)S(1)}, u32[]{:S(2)}, u32[]{:S(2)}) collective-permute-start(f32[2,32,512]{2,1,0:T(8,128)S(1)} %collective-permute-done.4), channel_id=1, source_target_pairs={{0,24},{4,28},{8,16},{12,20},{16,8},{20,12},{24,0},{28,4},{1,25},{... | collective-permute-start | bytes 393224 | tf_op jit(solution)/shard_map/ppermute | solution.py:106
  15.4 2.5 %collective-permute-done.3 = f32[2,32,512]{2,1,0:T(8,128)S(1)} collective-permute-done((f32[2,32,512]{2,1,0:T(8,128)S(1)}, f32[2,32,512]{2,1,0:T(8,128)S(1)}, u32[]{:S(2)}, u32[]{:S(2)}) %collective-permute-start.3) | collective-permute-done | bytes 131104 | tf_op jit(solution)/shard_map/ppermute | solution.py:106
  18.5 2.8 %collective-permute-done.5 = f32[2,32,512]{2,1,0:T(8,128)S(1)} collective-permute-done((f32[2,32,512]{2,1,0:T(8,128)S(1)}, f32[2,32,512]{2,1,0:T(8,128)S(1)}, u32[]{:S(2)}, u32[]{:S(2)}) %collective-permute-start.5) | collective-permute-done | bytes 131104 | tf_op jit(solution)/shard_map/ppermute | solution.py:106
  22.6 1.9 %bitcast_sine_fusion = (f32[32,8,512]{2,0,1:T(8,128)S(1)}, f32[32,8,512]{2,0,1:T(8,128)S(1)}) fusion(f32[8,32,512]{2,1,0:T(8,128)S(1)} %gather_fusion), kind=kLoop, calls=%fused_computation.119 | loop fusion | bytes 1572864 | tf_op jit(solution)/shard_map/sin | solution.py:82
  24.5 0.7 %copy.75 = f32[8,2,8,512]{3,2,0,1:T(8,128)} copy(f32[8,2,8,512]{3,2,1,0:T(8,128)S(1)} %get-tuple-element.29) | data formatting | bytes 524288 | tf_op jit(solution)/shard_map/slice | solution.py:19
  25.2 5.8 %collective-permute-start.6 = (f32[16,4096]{1,0:T(8,128)}, f32[16,4096]{1,0:T(8,128)}, u32[]{:S(2)}, u32[]{:S(2)}) collective-permute-start(f32[16,4096]{1,0:T(8,128)} %bitcast.75), channel_id=1, source_target_pairs={{0,1},{1,2},{2,3},{4,5},{5,6},{6,7},{8,9},{9,10},{10,11},{12,13},{... | collective-permute-start | bytes 786440 | tf_op jit(solution)/shard_map/ppermute | solution.py:22
  31.0 0.7 %copy.76 = f32[8,2,8,512]{3,2,0,1:T(8,128)} copy(f32[8,2,8,512]{3,2,1,0:T(8,128)S(1)} %get-tuple-element.30) | data formatting | bytes 524288 | tf_op jit(solution)/shard_map/slice | solution.py:18
  31.8 1.9 %collective-permute-start.7 = (f32[16,4096]{1,0:T(8,128)}, f32[16,4096]{1,0:T(8,128)}, u32[]{:S(2)}, u32[]{:S(2)}) collective-permute-start(f32[16,4096]{1,0:T(8,128)} %bitcast.77), channel_id=1, source_target_pairs={{1,0},{2,1},{3,2},{5,4},{6,5},{7,6},{9,8},{10,9},{11,10},{13,12},{... | collective-permute-start | bytes 786440 | tf_op jit(solution)/shard_map/ppermute | solution.py:24
  38.3 0.7 %gather_fusion.1 = f32[8,32,512]{2,1,0:T(8,128)S(1)} fusion(f32[8,32,512]{2,1,0:T(8,128)S(1)} %get-tuple-element.22, s32[1024]{0:T(1024)} %get-tuple-element.49), kind=kCustom, calls=%fused_computation.1 | custom fusion | bytes 1048608 | tf_op jit(solution)/shard_map/gather | solution.py:125
  39.4 1.9 %sine_bitcast_fusion = (f32[32,8,512]{2,0,1:T(8,128)S(1)}, f32[32,8,512]{2,0,1:T(8,128)S(1)}) fusion(f32[8,32,512]{2,1,0:T(8,128)S(1)} %gather_fusion.1), kind=kLoop, calls=%fused_computation.46 | loop fusion | bytes 1572864 | tf_op jit(solution)/shard_map/sin | solution.py:82
  42.1 1.9 %fusion.36 = (f32[16,4096]{1,0:T(8,128)S(1)}, f32[16,4096]{1,0:T(8,128)S(1)}) fusion(f32[16,4096]{1,0:T(8,128)} %collective-permute-done.6), kind=kLoop, calls=%fused_computation.122 | loop fusion | bytes 786432 | tf_op jit(solution)/shard_map/sin | solution.py:82
  44.0 1.9 %fusion.37 = (f32[16,4096]{1,0:T(8,128)S(1)}, f32[16,4096]{1,0:T(8,128)S(1)}) fusion(f32[16,4096]{1,0:T(8,128)} %collective-permute-done.7), kind=kLoop, calls=%fused_computation.123 | loop fusion | bytes 786432 | tf_op jit(solution)/shard_map/sin | solution.py:82
  46.4 0.7 convolution_bitcast_fusion.1
  48.1 1.0 %fusion.10 = f32[2,1,32,32,128]{4,3,2,0,1:T(8,128)S(1)} fusion(f32[2,160,2,128,1]{3,2,1,0,4:T(2,128)S(1)} %bitcast.196, f32[2,1,32,32,32]{4,3,2,0,1:T(8,128)S(1)} %bitcast.191, f32[2,1,32,32,128]{4,3,2,0,1:T(8,128)S(1)} %bitcast.193), kind=kOutput, calls=%fused_computation.23 | convolution fusion | flops 503644160 | bytes 2686976 | tf_op jit(solution)/shard_map/q...nj,qjpc->p...nc/dot_general | solution.py:69
  49.6 3.6 %collective-permute-start.8 = (f32[2,1,16,4096]{3,2,0,1:T(8,128)S(1)}, f32[2,1,16,4096]{3,2,0,1:T(8,128)S(1)}, u32[]{:S(2)}, u32[]{:S(2)}) collective-permute-start(f32[2,1,16,4096]{3,2,0,1:T(8,128)S(1)} %get-tuple-element.15), channel_id=1, source_target_pairs={{0,1},{1,2},{2,3},{4,5},{5,6},{6,7},{8,9},{9,10},{10,11},{12,13},{... | collective-permute-start | bytes 1572872 | tf_op jit(solution)/shard_map/ppermute | solution.py:22
  53.3 2.1 %collective-permute-start.9 = (f32[2,1,16,4096]{3,2,0,1:T(8,128)S(1)}, f32[2,1,16,4096]{3,2,0,1:T(8,128)S(1)}, u32[]{:S(2)}, u32[]{:S(2)}) collective-permute-start(f32[2,1,16,4096]{3,2,0,1:T(8,128)S(1)} %get-tuple-element.16), channel_id=1, source_target_pairs={{1,0},{2,1},{3,2},{5,4},{6,5},{7,6},{9,8},{10,9},{11,10},{13,12},{... | collective-permute-start | bytes 1572872 | tf_op jit(solution)/shard_map/ppermute | solution.py:24
  55.4 4.0 %collective-permute-done.8 = f32[2,1,16,4096]{3,2,0,1:T(8,128)S(1)} collective-permute-done((f32[2,1,16,4096]{3,2,0,1:T(8,128)S(1)}, f32[2,1,16,4096]{3,2,0,1:T(8,128)S(1)}, u32[]{:S(2)}, u32[]{:S(2)}) %collective-permute-start.8) | collective-permute-done | bytes 524320 | tf_op jit(solution)/shard_map/ppermute | solution.py:22
  59.4 4.4 %collective-permute-done.9 = f32[2,1,16,4096]{3,2,0,1:T(8,128)S(1)} collective-permute-done((f32[2,1,16,4096]{3,2,0,1:T(8,128)S(1)}, f32[2,1,16,4096]{3,2,0,1:T(8,128)S(1)}, u32[]{:S(2)}, u32[]{:S(2)}) %collective-permute-start.9) | collective-permute-done | bytes 524320 | tf_op jit(solution)/shard_map/ppermute | solution.py:24
  63.8 0.7 %convolution_bitcast_fusion = f32[2,1,32,4096]{3,2,0,1:T(8,128)S(1)} fusion(f32[2,1,16,4096]{3,2,0,1:T(8,128)S(1)} %collective-permute-done.9, f32[1,1,32,4096]{3,2,0,1:T(8,128)S(1)} %get-tuple-element.10, f32[1,1,32,4096]{3,2,0,1:T(8,128)S(1)} %get-tuple-element.9, f32[2,1,16,4096]{3,2,0,1:T(8,128)S(1)} %collective-permute-done.8, ...), kind=kOutput, calls=%fused_computation.2 | convolution fusion | flops 202899456 | bytes 3178496 | tf_op jit(solution)/shard_map/piqj,q...jy->p...iy/dot_general | solution.py:77
  65.4 1.0 %fusion.11 = f32[2,1,32,32,128]{4,3,2,0,1:T(8,128)S(1)} fusion(f32[2,160,2,128,1]{3,2,1,0,4:T(2,128)S(1)} %bitcast.197, f32[2,1,32,32,32]{4,3,2,0,1:T(8,128)S(1)} %bitcast.192, f32[2,1,32,32,128]{4,3,2,0,1:T(8,128)S(1)} %bitcast.190), kind=kOutput, calls=%fused_computation.24 | convolution fusion | flops 503644160 | bytes 2686976 | tf_op jit(solution)/shard_map/q...nj,qjpc->p...nc/dot_general | solution.py:69
  66.5 1.2 %reshape.851 = f32[2,1,32,4096]{3,2,0,1:T(8,128)} reshape(f32[2,1,32,32,128]{4,3,2,0,1:T(8,128)S(1)} %fusion.11) | data formatting | bytes 2097152 | tf_op jit(solution)/shard_map/reshape | solution.py:70
  (78 shorter events, 10.1 us)
Async XLA Ops:
  0.0 13.8 %collective-permute-start.1 = (f32[2,32,512]{2,1,0:T(8,128)}, f32[2,32,512]{2,1,0:T(8,128)S(1)}, u32[]{:S(2)}, u32[]{:S(2)}) collective-permute-start(f32[2,32,512]{2,1,0:T(8,128)} %param.6), channel_id=1, source_target_pairs={{0,16},{4,20},{8,24},{12,28},{16,0},{20,4},{24,8},{28,12},{1,17},{... | collective-permute-start | bytes 393224 | tf_op jit(solution)/shard_map/ppermute | solution.py:106
  3.1 10.6 %collective-permute-start = (f32[2,32,512]{2,1,0:T(8,128)}, f32[2,32,512]{2,1,0:T(8,128)S(1)}, u32[]{:S(2)}, u32[]{:S(2)}) collective-permute-start(f32[2,32,512]{2,1,0:T(8,128)} %param.6), channel_id=1, source_target_pairs={{0,8},{4,12},{8,0},{12,4},{16,24},{20,28},{24,16},{28,20},{1,9},{5... | collective-permute-start | bytes 393224 | tf_op jit(solution)/shard_map/ppermute | solution.py:106
  4.4 9.8 %collective-permute-start.4 = (f32[2,32,512]{2,1,0:T(8,128)}, f32[2,32,512]{2,1,0:T(8,128)S(1)}, u32[]{:S(2)}, u32[]{:S(2)}) collective-permute-start(f32[2,32,512]{2,1,0:T(8,128)} %param.6), channel_id=1, source_target_pairs={{0,4},{4,0},{8,12},{12,8},{16,20},{20,16},{24,28},{28,24},{1,5},{5... | collective-permute-start | bytes 393224 | tf_op jit(solution)/shard_map/ppermute | solution.py:106
  13.8 8.0 %collective-permute-start.2 = (f32[2,2,32,512]{3,2,1,0:T(8,128)S(1)}, f32[2,2,32,512]{3,2,1,0:T(8,128)S(1)}, u32[]{:S(2)}, u32[]{:S(2)}) collective-permute-start(f32[2,2,32,512]{3,2,1,0:T(8,128)S(1)} %pad_maximum_fusion.3), channel_id=1, source_target_pairs={{0,4},{4,0},{8,12},{12,8},{16,20},{20,16},{24,28},{28,24},{1,5},{5... | collective-permute-start | bytes 786440 | tf_op jit(solution)/shard_map/ppermute | solution.py:106
  14.1 3.8 %collective-permute-start.3 = (f32[2,32,512]{2,1,0:T(8,128)S(1)}, f32[2,32,512]{2,1,0:T(8,128)S(1)}, u32[]{:S(2)}, u32[]{:S(2)}) collective-permute-start(f32[2,32,512]{2,1,0:T(8,128)S(1)} %collective-permute-done.1), channel_id=1, source_target_pairs={{0,8},{4,12},{8,0},{12,4},{16,24},{20,28},{24,16},{28,20},{1,9},{5... | collective-permute-start | bytes 393224 | tf_op jit(solution)/shard_map/ppermute | solution.py:106
  14.3 7.0 %collective-permute-start.5 = (f32[2,32,512]{2,1,0:T(8,128)S(1)}, f32[2,32,512]{2,1,0:T(8,128)S(1)}, u32[]{:S(2)}, u32[]{:S(2)}) collective-permute-start(f32[2,32,512]{2,1,0:T(8,128)S(1)} %collective-permute-done.4), channel_id=1, source_target_pairs={{0,24},{4,28},{8,16},{12,20},{16,8},{20,12},{24,0},{28,4},{1,25},{... | collective-permute-start | bytes 393224 | tf_op jit(solution)/shard_map/ppermute | solution.py:106
  25.2 16.9 %collective-permute-start.6 = (f32[16,4096]{1,0:T(8,128)}, f32[16,4096]{1,0:T(8,128)}, u32[]{:S(2)}, u32[]{:S(2)}) collective-permute-start(f32[16,4096]{1,0:T(8,128)} %bitcast.75), channel_id=1, source_target_pairs={{0,1},{1,2},{2,3},{4,5},{5,6},{6,7},{8,9},{9,10},{10,11},{12,13},{... | collective-permute-start | bytes 786440 | tf_op jit(solution)/shard_map/ppermute | solution.py:22
  31.8 12.2 %collective-permute-start.7 = (f32[16,4096]{1,0:T(8,128)}, f32[16,4096]{1,0:T(8,128)}, u32[]{:S(2)}, u32[]{:S(2)}) collective-permute-start(f32[16,4096]{1,0:T(8,128)} %bitcast.77), channel_id=1, source_target_pairs={{1,0},{2,1},{3,2},{5,4},{6,5},{7,6},{9,8},{10,9},{11,10},{13,12},{... | collective-permute-start | bytes 786440 | tf_op jit(solution)/shard_map/ppermute | solution.py:24
  34.1 3.0 %copy-start.6 = (f32[2,33]{1,0:T(2,128)S(1)}, f32[2,33]{1,0:T(2,128)}, u32[]{:S(2)}) copy-start(f32[2,33]{1,0:T(2,128)} %param.5) | copy-start | bytes 796
  38.1 0.9 %copy-start = (f32[4096]{0:T(1024)S(1)}, f32[4096]{0:T(1024)}, u32[]{:S(2)}) copy-start(f32[4096]{0:T(1024)} %get-tuple-element.52) | copy-start | bytes 49156
  38.1 0.9 %copy-start.7 = (f32[32]{0:T(128)S(1)}, f32[32]{0:T(128)}, u32[]{:S(2)}) copy-start(f32[32]{0:T(128)} %slice_bitcast_fusion.8) | copy-start | bytes 388
  38.1 0.9 %copy-start.8 = (f32[32]{0:T(128)S(1)}, f32[32]{0:T(128)}, u32[]{:S(2)}) copy-start(f32[32]{0:T(128)} %slice_bitcast_fusion.9) | copy-start | bytes 388
  42.1 3.8 %copy-start.1 = (f32[4096]{0:T(1024)S(1)}, f32[4096]{0:T(1024)}, u32[]{:S(2)}) copy-start(f32[4096]{0:T(1024)} %get-tuple-element.52) | copy-start | bytes 49156
  42.1 3.8 %copy-start.2 = (f32[16]{0:T(128)S(1)}, f32[16]{0:T(128)}, u32[]{:S(2)}) copy-start(f32[16]{0:T(128)} %get-tuple-element.45) | copy-start | bytes 196
  42.1 3.8 %copy-start.3 = (f32[16]{0:T(128)S(1)}, f32[16]{0:T(128)}, u32[]{:S(2)}) copy-start(f32[16]{0:T(128)} %get-tuple-element.46) | copy-start | bytes 196
  42.1 3.8 %copy-start.4 = (f32[16]{0:T(128)S(1)}, f32[16]{0:T(128)}, u32[]{:S(2)}) copy-start(f32[16]{0:T(128)} %get-tuple-element.43) | copy-start | bytes 196
  42.1 3.8 %copy-start.5 = (f32[16]{0:T(128)S(1)}, f32[16]{0:T(128)}, u32[]{:S(2)}) copy-start(f32[16]{0:T(128)} %get-tuple-element.44) | copy-start | bytes 196
  49.6 9.8 %collective-permute-start.8 = (f32[2,1,16,4096]{3,2,0,1:T(8,128)S(1)}, f32[2,1,16,4096]{3,2,0,1:T(8,128)S(1)}, u32[]{:S(2)}, u32[]{:S(2)}) collective-permute-start(f32[2,1,16,4096]{3,2,0,1:T(8,128)S(1)} %get-tuple-element.15), channel_id=1, source_target_pairs={{0,1},{1,2},{2,3},{4,5},{5,6},{6,7},{8,9},{9,10},{10,11},{12,13},{... | collective-permute-start | bytes 1572872 | tf_op jit(solution)/shard_map/ppermute | solution.py:22
  53.3 10.5 %collective-permute-start.9 = (f32[2,1,16,4096]{3,2,0,1:T(8,128)S(1)}, f32[2,1,16,4096]{3,2,0,1:T(8,128)S(1)}, u32[]{:S(2)}, u32[]{:S(2)}) collective-permute-start(f32[2,1,16,4096]{3,2,0,1:T(8,128)S(1)} %get-tuple-element.16), channel_id=1, source_target_pairs={{1,0},{2,1},{3,2},{5,4},{6,5},{7,6},{9,8},{10,9},{11,10},{13,12},{... | collective-permute-start | bytes 1572872 | tf_op jit(solution)/shard_map/ppermute | solution.py:24

commit v12 on v10

--- a/solution.py
+++ b/solution.py
@@ -78,8 +78,10 @@
 
 
 def transmit(real, imag, screen):
-    cosine = jnp.cos(screen)
-    sine = jnp.sin(screen)
+    return rotate(real, imag, jnp.cos(screen), jnp.sin(screen))
+
+
+def rotate(real, imag, cosine, sine):
     return (real * cosine - imag * sine, real * sine + imag * cosine)
 
 
@@ -153,13 +155,14 @@
         imag = across_sin[:, rows] * along_cos + across_cos[:, rows] * along_sin
         return real, imag
 
-    halo = extended(screens[0], (("tile", 0),), HALF)
+    cosine, sine = jnp.cos(screens[0]), jnp.sin(screens[0])
+    halo = extended(jnp.stack([cosine, sine]), (("tile", 1),), HALF)
     pieces = [
-        transmit(*incident(rows), screen)
-        for rows, screen in (
-            (slice(0, HALF), halo[:HALF]),
-            (slice(HALF, HALF + local_rows), screens[0]),
-            (slice(HALF + local_rows, span), halo[HALF + local_rows :]),
+        rotate(*incident(rows), *parts)
+        for rows, parts in (
+            (slice(0, HALF), (halo[0, :HALF], halo[1, :HALF])),
+            (slice(HALF, HALF + local_rows), (cosine, sine)),
+            (slice(HALF + local_rows, span), (halo[0, HALF + local_rows :], halo[1, HALF + local_rows :])),
         )
     ]
     real = jnp.concatenate([piece[0] for piece in pieces], axis=1)

time: 65.5 us -> 65 us (level)
  local copies, waits for them, and re-layouts: 19.1 us -> 17.5 us
  waiting for transfers between devices: 13.5 us -> 14.7 us
    cos x7 -> x4, local copies, waits for them, and re-layouts: 4.61 us -> 1.61 us  [the longest x2 1.2 us: transmit(): return rotate(real, imag, jnp.cos(screen), jnp.sin(screen))]
    sin x5 -> x6, local copies, waits for them, and re-layouts: 2.67 us -> 4.53 us  [the longest x3 2.27 us: body(): cosine, sine = (jnp.cos(screens[0]), jnp.sin(screens[0]))]
    ppermute x6, starting transfers between devices: 8.34 us -> 9.94 us  [exchange(): return lax.ppermute(x, axis, [(i, partner(i, k)) for i in range(count)])]
    mul x4, local copies, waits for them, and re-layouts: 1.82 us -> 0.29 us  [incident(): real = across_cos[:, rows] * along_cos - across_sin[:, rows] * along_sin]
    ppermute x2, starting transfers between devices: 8.27 us -> 7.05 us  [extended(): lax.ppermute(tail, axis, [(i, (i + 1) % count) for i in range(ends)])]
    ppermute x2, waiting for transfers between devices: 4.4 us -> 5.43 us  [extended(): lax.ppermute(head, axis, [((i + 1) % count, i) for i in range(ends)])]
    squeeze x1, local copies, waits for them, and re-layouts: 0.09 us -> 0.89 us  [gather_screens(): picked = stacked[p][source]]
    slice x1 -> x0, local copies, waits for them, and re-layouts: 0.72 us -> none  [extended(): lax.slice_in_dim(cells, cells.shape[dim] - width, cells.shape[dim], axis=...]
  transfers between devices with their start and end apart: 10 -> 10, of which waited for: 4 -> 4; matrix products, arithmetic and copies ran while one was open for 24% -> 18% of each run, Pallas kernels for 0% -> 0%
where the time goes in v12:
time: 65 us; the launch traced here: 64.7 us
  starting transfers between devices  21 us (32%)
  local copies, waits for them, and re-layouts  17.5 us (27%)
  waiting for transfers between devices  14.7 us (23%)
  other arithmetic  5.37 us (8%)
  matrix products  3.64 us (6%)
  between operations  2.43 us (4%)
    ppermute x6, starting transfers between devices, exchange(): return lax.ppermute(x, axis, [(i, partner(i, k)) for i in range(count)])  9.94 us
    ppermute x2, starting transfers between devices, extended(): lax.ppermute(tail, axis, [(i, (i + 1) % count) for i in range(ends)])  7.05 us
    ppermute x2, waiting for transfers between devices, extended(): lax.ppermute(head, axis, [((i + 1) % count, i) for i in range(ends)])  5.43 us
    ppermute x6, waiting for transfers between devices, exchange(): return lax.ppermute(x, axis, [(i, partner(i, k)) for i in range(count)])  5.31 us
    ppermute x2, starting transfers between devices, extended(): lax.ppermute(head, axis, [((i + 1) % count, i) for i in range(ends)])  4.02 us
    ppermute x2, waiting for transfers between devices, extended(): lax.ppermute(tail, axis, [(i, (i + 1) % count) for i in range(ends)])  4 us
    unnamed x26, local copies, waits for them, and re-layouts  3.85 us
    dot_general x2, matrix products, along_pass(): out = jnp.einsum('...nj,jc->...nc', win, kern, precision=lax.Precision.HIGH)  2.27 us
  transfers between devices with their start and end apart: 10, of which 4 were waited for; matrix products, arithmetic and copies ran while one was open for 18% of the time, Pallas kernels for 0%

profile of v12, /device:TPU:1, one launch (start us, length us, event | category | flops | bytes accessed | tf_op | source)
XLA Modules:
  0.0 64.7 jit_solution(10653498941587720936)
XLA Ops:
  0.0 3.1 %collective-permute-start.2 = (f32[2,32,512]{2,1,0:T(8,128)}, f32[2,32,512]{2,1,0:T(8,128)S(1)}, u32[]{:S(2)}, u32[]{:S(2)}) collective-permute-start(f32[2,32,512]{2,1,0:T(8,128)} %param.6), channel_id=1, source_target_pairs={{0,16},{4,20},{8,24},{12,28},{16,0},{20,4},{24,8},{28,12},{1,17},{... | collective-permute-start | bytes 393224 | tf_op jit(solution)/shard_map/ppermute | solution.py:108
  3.1 1.3 %collective-permute-start.1 = (f32[2,32,512]{2,1,0:T(8,128)}, f32[2,32,512]{2,1,0:T(8,128)S(1)}, u32[]{:S(2)}, u32[]{:S(2)}) collective-permute-start(f32[2,32,512]{2,1,0:T(8,128)} %param.6), channel_id=1, source_target_pairs={{0,8},{4,12},{8,0},{12,4},{16,24},{20,28},{24,16},{28,20},{1,9},{5... | collective-permute-start | bytes 393224 | tf_op jit(solution)/shard_map/ppermute | solution.py:108
  4.4 1.2 %collective-permute-start = (f32[2,32,512]{2,1,0:T(8,128)}, f32[2,32,512]{2,1,0:T(8,128)S(1)}, u32[]{:S(2)}, u32[]{:S(2)}) collective-permute-start(f32[2,32,512]{2,1,0:T(8,128)} %param.6), channel_id=1, source_target_pairs={{0,4},{4,0},{8,12},{12,8},{16,20},{20,16},{24,28},{28,24},{1,5},{5... | collective-permute-start | bytes 393224 | tf_op jit(solution)/shard_map/ppermute | solution.py:108
  5.7 0.9 %bitcast_dynamic-update-slice_fusion.6 = f32[2,8,32,512]{3,2,0,1:T(8,128)S(1)} fusion(f32[2,32,512]{2,1,0:T(8,128)} %param.6), kind=kLoop, calls=%fused_computation.78 | loop fusion | bytes 262144
  6.6 1.3 %fusion.43 = (s32[1,1]{1,0:T(1,128)}, s32[1,1]{1,0:T(1,128)}) fusion(s32[1,2]{1,0:T(1,128)} %param.4), kind=kLoop, calls=%fused_computation.130 | loop fusion | bytes 16 | tf_op jit(solution)/shard_map/slice | solution.py:145
  7.9 0.7 %sine_select_fusion = (f32[1,64,1]{1,2,0:T(1,128)S(1)}, f32[1,64,1]{1,2,0:T(1,128)S(1)}) fusion(s32[]{:T(128)S(6)} %sub.157, s32[]{:T(128)} %bitcast), kind=kLoop, calls=%fused_computation.117 | loop fusion | flops 1280 | bytes 520 | tf_op jit(solution)/shard_map/jit(_where)/select_n | solution.py:149
  9.0 0.7 %fusion.27 = (f32[4096]{0:T(1024)S(1)}, f32[4096]{0:T(1024)S(1)}) fusion(s32[]{:T(128)} %bitcast.2), kind=kLoop, calls=%fused_computation.94 | loop fusion | flops 57344 | bytes 32772 | tf_op jit(solution)/shard_map/sin | solution.py:151
  9.6 0.8 %fusion.33 = (s32[8]{0:T(128)S(1)}, s32[8]{0:T(128)S(1)}) fusion(s32[2,8]{1,0:T(2,128)} %param.7, s32[]{:T(128)S(6)} %axis_index.25), kind=kLoop, calls=%fused_computation.108 | loop fusion | flops 64 | bytes 132 | tf_op jit(solution)/shard_map/select_n | solution.py:127
  10.7 1.3 %collective-permute-start.4 = (f32[2,32,512]{2,1,0:T(8,128)S(1)}, f32[2,32,512]{2,1,0:T(8,128)S(1)}, u32[]{:S(2)}, u32[]{:S(2)}) collective-permute-start(f32[2,32,512]{2,1,0:T(8,128)S(1)} %collective-permute-done.2), channel_id=1, source_target_pairs={{0,8},{4,12},{8,0},{12,4},{16,24},{20,28},{24,16},{28,20},{1,9},{5... | collective-permute-start | bytes 393224 | tf_op jit(solution)/shard_map/ppermute | solution.py:108
  12.0 2.7 %collective-permute-start.5 = (f32[2,32,512]{2,1,0:T(8,128)S(1)}, f32[2,32,512]{2,1,0:T(8,128)S(1)}, u32[]{:S(2)}, u32[]{:S(2)}) collective-permute-start(f32[2,32,512]{2,1,0:T(8,128)S(1)} %collective-permute-done), channel_id=1, source_target_pairs={{0,24},{4,28},{8,16},{12,20},{16,8},{20,12},{24,0},{28,4},{1,25},{... | collective-permute-start | bytes 393224 | tf_op jit(solution)/shard_map/ppermute | solution.py:108
  14.8 0.6 slice.212
  15.3 5.3 %collective-permute-done.5 = f32[2,32,512]{2,1,0:T(8,128)S(1)} collective-permute-done((f32[2,32,512]{2,1,0:T(8,128)S(1)}, f32[2,32,512]{2,1,0:T(8,128)S(1)}, u32[]{:S(2)}, u32[]{:S(2)}) %collective-permute-start.5) | collective-permute-done | bytes 131104 | tf_op jit(solution)/shard_map/ppermute | solution.py:108
  21.3 0.9 %slice_bitcast_fusion.2 = (f32[8,32,512]{2,1,0:T(8,128)}, f32[8,32,512]{2,1,0:T(8,128)S(1)}) fusion(f32[2,8,32,512]{3,2,0,1:T(8,128)S(1)} %bitcast_dynamic-update-slice_fusion), kind=kLoop, calls=%fused_computation.40 | loop fusion | bytes 2097152 | tf_op jit(solution)/shard_map/squeeze | solution.py:127
  22.2 0.6 gather_fusion
  22.8 1.9 %sine_bitcast_fusion.1 = (f32[32,8,512]{2,0,1:T(8,128)S(1)}, f32[32,8,512]{2,0,1:T(8,128)S(1)}) fusion(f32[8,32,512]{2,1,0:T(8,128)S(1)} %gather_fusion), kind=kLoop, calls=%fused_computation.58 | loop fusion | bytes 1572864 | tf_op jit(solution)/shard_map/sin | solution.py:158
  25.6 1.1 %fusion.42 = (f32[2,16,4096]{2,1,0:T(8,128)}, f32[2,16,4096]{2,1,0:T(8,128)}) fusion(f32[2,32,4096]{2,1,0:T(8,128)S(1)} %constant_dynamic-update-slice_fusion), kind=kLoop, calls=%fused_computation.129 | loop fusion | bytes 2097152 | tf_op jit(solution)/shard_map/slice | solution.py:18
  26.7 4.4 %collective-permute-start.6 = (f32[2,16,4096]{2,1,0:T(8,128)}, f32[2,16,4096]{2,1,0:T(8,128)S(1)}, u32[]{:S(2)}, u32[]{:S(2)}) collective-permute-start(f32[2,16,4096]{2,1,0:T(8,128)} %get-tuple-element.26), channel_id=1, source_target_pairs={{0,1},{1,2},{2,3},{4,5},{5,6},{6,7},{8,9},{9,10},{10,11},{12,13},{... | collective-permute-start | bytes 1572872 | tf_op jit(solution)/shard_map/ppermute | solution.py:22
  31.1 1.9 %collective-permute-start.7 = (f32[2,16,4096]{2,1,0:T(8,128)}, f32[2,16,4096]{2,1,0:T(8,128)S(1)}, u32[]{:S(2)}, u32[]{:S(2)}) collective-permute-start(f32[2,16,4096]{2,1,0:T(8,128)} %get-tuple-element.25), channel_id=1, source_target_pairs={{1,0},{2,1},{3,2},{5,4},{6,5},{7,6},{9,8},{10,9},{11,10},{13,12},{... | collective-permute-start | bytes 1572872 | tf_op jit(solution)/shard_map/ppermute | solution.py:24
  36.3 0.6 gather_fusion.1
  36.9 1.9 %sine_bitcast_fusion = (f32[32,8,512]{2,0,1:T(8,128)S(1)}, f32[32,8,512]{2,0,1:T(8,128)S(1)}) fusion(f32[8,32,512]{2,1,0:T(8,128)S(1)} %gather_fusion.1), kind=kLoop, calls=%fused_computation.48 | loop fusion | bytes 1572864 | tf_op jit(solution)/shard_map/sin | solution.py:81
  39.1 0.9 %cos.74 = f32[1,1,32,4096]{3,2,1,0:T(8,128)} reshape(f32[32,8,512]{2,1,0:T(8,128)S(1)} %copy.11) | data formatting | bytes 1048576 | tf_op jit(solution)/shard_map/cos | solution.py:81
  40.8 1.0 %collective-permute-done.7 = f32[2,16,4096]{2,1,0:T(8,128)S(1)} collective-permute-done((f32[2,16,4096]{2,1,0:T(8,128)}, f32[2,16,4096]{2,1,0:T(8,128)S(1)}, u32[]{:S(2)}, u32[]{:S(2)}) %collective-permute-start.7) | collective-permute-done | bytes 524320 | tf_op jit(solution)/shard_map/ppermute | solution.py:24
  42.5 0.7 %convolution_bitcast_fusion.1 = f32[1,64,4096]{2,1,0:T(8,128)S(1)} fusion(f32[1,128,4096]{2,1,0:T(8,128)S(1)} %add_dynamic-update-slice_fusion.1, f32[32,64]{1,0:T(8,128)S(1)} %get-tuple-element.8, f32[32,64]{1,0:T(8,128)S(1)} %get-tuple-element.7, f32[32,64]{1,0:T(8,128)S(1)} %neg.4), kind=kOutput, calls=%fused_computation.3 | convolution fusion | flops 201351168 | bytes 3170304 | tf_op jit(solution)/shard_map/ij,ajy->aiy/dot_general | solution.py:76
  44.4 1.1 %fusion.18 = f32[1,32,32,256]{3,2,1,0:T(8,128)S(1)} fusion(f32[1,32,32,32]{3,2,1,0:T(8,128)S(1)} %bitcast.150, f32[1,32,32,128]{3,2,1,0:T(8,128)S(1)} %bitcast.156, f32[1,32,32,32]{3,2,1,0:T(8,128)S(1)} %bitcast.152, f32[1,32,32,128]{3,2,1,0:T(8,128)S(1)} %bitcast.154, f32[160,128]{1,0:T(8,128)S(1)} %get-tuple-element.6, f32[160,128]{1,0:T(8,128)S(1)} %neg.5, ...), kind=kOutput, calls=%fused_computation.29 | convolution fusion | flops 504545280 | bytes 2605056 | tf_op jit(solution)/shard_map/...nj,jc->...nc/dot_general | solution.py:68
  45.9 0.7 %copy-done = f32[1,1,32,4096]{3,2,1,0:T(8,128)S(1)} copy-done((f32[1,1,32,4096]{3,2,1,0:T(8,128)S(1)}, f32[1,1,32,4096]{3,2,1,0:T(8,128)}, u32[]{:S(2)}) %copy-start) | copy-done | bytes 524312
  46.8 2.6 %collective-permute-start.8 = (f32[2,1,16,4096]{3,2,1,0:T(8,128)S(1)}, f32[2,1,16,4096]{3,2,1,0:T(8,128)S(1)}, u32[]{:S(2)}, u32[]{:S(2)}) collective-permute-start(f32[2,1,16,4096]{3,2,1,0:T(8,128)S(1)} %get-tuple-element.17), channel_id=1, source_target_pairs={{0,1},{1,2},{2,3},{4,5},{5,6},{6,7},{8,9},{9,10},{10,11},{12,13},{... | collective-permute-start | bytes 1572872 | tf_op jit(solution)/shard_map/ppermute | solution.py:22
  49.4 2.1 %collective-permute-start.9 = (f32[2,1,16,4096]{3,2,1,0:T(8,128)S(1)}, f32[2,1,16,4096]{3,2,1,0:T(8,128)S(1)}, u32[]{:S(2)}, u32[]{:S(2)}) collective-permute-start(f32[2,1,16,4096]{3,2,1,0:T(8,128)S(1)} %get-tuple-element.18), channel_id=1, source_target_pairs={{1,0},{2,1},{3,2},{5,4},{6,5},{7,6},{9,8},{10,9},{11,10},{13,12},{... | collective-permute-start | bytes 1572872 | tf_op jit(solution)/shard_map/ppermute | solution.py:24
  51.5 4.0 %collective-permute-done.8 = f32[2,1,16,4096]{3,2,1,0:T(8,128)S(1)} collective-permute-done((f32[2,1,16,4096]{3,2,1,0:T(8,128)S(1)}, f32[2,1,16,4096]{3,2,1,0:T(8,128)S(1)}, u32[]{:S(2)}, u32[]{:S(2)}) %collective-permute-start.8) | collective-permute-done | bytes 524320 | tf_op jit(solution)/shard_map/ppermute | solution.py:22
  55.5 4.4 %collective-permute-done.9 = f32[2,1,16,4096]{3,2,1,0:T(8,128)S(1)} collective-permute-done((f32[2,1,16,4096]{3,2,1,0:T(8,128)S(1)}, f32[2,1,16,4096]{3,2,1,0:T(8,128)S(1)}, u32[]{:S(2)}, u32[]{:S(2)}) %collective-permute-start.9) | collective-permute-done | bytes 524320 | tf_op jit(solution)/shard_map/ppermute | solution.py:24
  60.3 0.7 %convolution_bitcast_fusion = f32[1,64,4096]{2,1,0:T(8,128)S(1)} fusion(f32[1,64,4096]{2,1,0:T(8,128)S(1)} %get-tuple-element.10, f32[1,64,4096]{2,1,0:T(8,128)S(1)} %get-tuple-element.9, f32[32,64]{1,0:T(8,128)S(1)} %get-tuple-element.8, f32[32,64]{1,0:T(8,128)S(1)} %get-tuple-element.7, f32[32,64]{1,0:T(8,128)S(1)} %neg.4), kind=kOutput, calls=%fused_computation.2 | convolution fusion | flops 201875456 | bytes 3170304 | tf_op jit(solution)/shard_map/ij,ajy->aiy/dot_general | solution.py:76
  62.1 1.1 %fusion.17 = f32[1,32,32,256]{3,2,1,0:T(8,128)S(1)} fusion(f32[1,32,32,32]{3,2,1,0:T(8,128)S(1)} %bitcast.149, f32[1,32,32,128]{3,2,1,0:T(8,128)S(1)} %bitcast.155, f32[1,32,32,32]{3,2,1,0:T(8,128)S(1)} %bitcast.151, f32[1,32,32,128]{3,2,1,0:T(8,128)S(1)} %bitcast.153, f32[160,128]{1,0:T(8,128)S(1)} %get-tuple-element.6, f32[160,128]{1,0:T(8,128)S(1)} %neg.5, ...), kind=kOutput, calls=%fused_computation.28 | convolution fusion | flops 504545280 | bytes 2605056 | tf_op jit(solution)/shard_map/...nj,jc->...nc/dot_general | solution.py:68
  63.6 1.0 %pad_maximum_fusion.1 = f32[2,1,32,4096]{3,2,1,0:T(8,128)} fusion(f32[1,1,32,4096]{3,2,1,0:T(8,128)S(1)} %stack_reshape.7, f32[1,1,32,4096]{3,2,1,0:T(8,128)S(1)} %stack_reshape.6), kind=kLoop, calls=%fused_computation.34 | loop fusion | flops 262144 | bytes 2097152 | tf_op jit(solution)/shard_map/stack | solution.py:177
  (75 shorter events, 8.7 us)
Async XLA Ops:
  0.0 10.4 %collective-permute-start.2 = (f32[2,32,512]{2,1,0:T(8,128)}, f32[2,32,512]{2,1,0:T(8,128)S(1)}, u32[]{:S(2)}, u32[]{:S(2)}) collective-permute-start(f32[2,32,512]{2,1,0:T(8,128)} %param.6), channel_id=1, source_target_pairs={{0,16},{4,20},{8,24},{12,28},{16,0},{20,4},{24,8},{28,12},{1,17},{... | collective-permute-start | bytes 393224 | tf_op jit(solution)/shard_map/ppermute | solution.py:108
  3.1 7.3 %collective-permute-start.1 = (f32[2,32,512]{2,1,0:T(8,128)}, f32[2,32,512]{2,1,0:T(8,128)S(1)}, u32[]{:S(2)}, u32[]{:S(2)}) collective-permute-start(f32[2,32,512]{2,1,0:T(8,128)} %param.6), channel_id=1, source_target_pairs={{0,8},{4,12},{8,0},{12,4},{16,24},{20,28},{24,16},{28,20},{1,9},{5... | collective-permute-start | bytes 393224 | tf_op jit(solution)/shard_map/ppermute | solution.py:108
  4.4 7.6 %collective-permute-start = (f32[2,32,512]{2,1,0:T(8,128)}, f32[2,32,512]{2,1,0:T(8,128)S(1)}, u32[]{:S(2)}, u32[]{:S(2)}) collective-permute-start(f32[2,32,512]{2,1,0:T(8,128)} %param.6), channel_id=1, source_target_pairs={{0,4},{4,0},{8,12},{12,8},{16,20},{20,16},{24,28},{28,24},{1,5},{5... | collective-permute-start | bytes 393224 | tf_op jit(solution)/shard_map/ppermute | solution.py:108
  10.4 10.8 %collective-permute-start.3 = (f32[2,2,32,512]{3,2,1,0:T(8,128)S(1)}, f32[2,2,32,512]{3,2,1,0:T(8,128)S(1)}, u32[]{:S(2)}, u32[]{:S(2)}) collective-permute-start(f32[2,2,32,512]{3,2,1,0:T(8,128)S(1)} %pad_maximum_fusion.3), channel_id=1, source_target_pairs={{0,4},{4,0},{8,12},{12,8},{16,20},{20,16},{24,28},{28,24},{1,5},{5... | collective-permute-start | bytes 786440 | tf_op jit(solution)/shard_map/ppermute | solution.py:108
  10.7 4.0 %collective-permute-start.4 = (f32[2,32,512]{2,1,0:T(8,128)S(1)}, f32[2,32,512]{2,1,0:T(8,128)S(1)}, u32[]{:S(2)}, u32[]{:S(2)}) collective-permute-start(f32[2,32,512]{2,1,0:T(8,128)S(1)} %collective-permute-done.2), channel_id=1, source_target_pairs={{0,8},{4,12},{8,0},{12,4},{16,24},{20,28},{24,16},{28,20},{1,9},{5... | collective-permute-start | bytes 393224 | tf_op jit(solution)/shard_map/ppermute | solution.py:108
  12.0 8.6 %collective-permute-start.5 = (f32[2,32,512]{2,1,0:T(8,128)S(1)}, f32[2,32,512]{2,1,0:T(8,128)S(1)}, u32[]{:S(2)}, u32[]{:S(2)}) collective-permute-start(f32[2,32,512]{2,1,0:T(8,128)S(1)} %collective-permute-done), channel_id=1, source_target_pairs={{0,24},{4,28},{8,16},{12,20},{16,8},{20,12},{24,0},{28,4},{1,25},{... | collective-permute-start | bytes 393224 | tf_op jit(solution)/shard_map/ppermute | solution.py:108
  25.4 10.1 %copy-start.2 = (f32[2,33]{1,0:T(2,128)S(1)}, f32[2,33]{1,0:T(2,128)}, u32[]{:S(2)}) copy-start(f32[2,33]{1,0:T(2,128)} %param.5) | copy-start | bytes 796
  25.5 10.8 %copy-start.1 = (f32[8,32,512]{2,1,0:T(8,128)S(1)}, f32[8,32,512]{2,1,0:T(8,128)}, u32[]{:S(2)}) copy-start(f32[8,32,512]{2,1,0:T(8,128)} %get-tuple-element.21) | copy-start | bytes 1572868
  26.7 13.7 %collective-permute-start.6 = (f32[2,16,4096]{2,1,0:T(8,128)}, f32[2,16,4096]{2,1,0:T(8,128)S(1)}, u32[]{:S(2)}, u32[]{:S(2)}) collective-permute-start(f32[2,16,4096]{2,1,0:T(8,128)} %get-tuple-element.26), channel_id=1, source_target_pairs={{0,1},{1,2},{2,3},{4,5},{5,6},{6,7},{8,9},{9,10},{10,11},{12,13},{... | collective-permute-start | bytes 1572872 | tf_op jit(solution)/shard_map/ppermute | solution.py:22
  31.1 10.7 %collective-permute-start.7 = (f32[2,16,4096]{2,1,0:T(8,128)}, f32[2,16,4096]{2,1,0:T(8,128)S(1)}, u32[]{:S(2)}, u32[]{:S(2)}) collective-permute-start(f32[2,16,4096]{2,1,0:T(8,128)} %get-tuple-element.25), channel_id=1, source_target_pairs={{1,0},{2,1},{3,2},{5,4},{6,5},{7,6},{9,8},{10,9},{11,10},{13,12},{... | collective-permute-start | bytes 1572872 | tf_op jit(solution)/shard_map/ppermute | solution.py:24
  45.5 1.0 %copy-start = (f32[1,1,32,4096]{3,2,1,0:T(8,128)S(1)}, f32[1,1,32,4096]{3,2,1,0:T(8,128)}, u32[]{:S(2)}) copy-start(f32[1,1,32,4096]{3,2,1,0:T(8,128)} %cos.74) | copy-start | bytes 1572868
  46.8 8.7 %collective-permute-start.8 = (f32[2,1,16,4096]{3,2,1,0:T(8,128)S(1)}, f32[2,1,16,4096]{3,2,1,0:T(8,128)S(1)}, u32[]{:S(2)}, u32[]{:S(2)}) collective-permute-start(f32[2,1,16,4096]{3,2,1,0:T(8,128)S(1)} %get-tuple-element.17), channel_id=1, source_target_pairs={{0,1},{1,2},{2,3},{4,5},{5,6},{6,7},{8,9},{9,10},{10,11},{12,13},{... | collective-permute-start | bytes 1572872 | tf_op jit(solution)/shard_map/ppermute | solution.py:22
  49.4 10.5 %collective-permute-start.9 = (f32[2,1,16,4096]{3,2,1,0:T(8,128)S(1)}, f32[2,1,16,4096]{3,2,1,0:T(8,128)S(1)}, u32[]{:S(2)}, u32[]{:S(2)}) collective-permute-start(f32[2,1,16,4096]{3,2,1,0:T(8,128)S(1)} %get-tuple-element.18), channel_id=1, source_target_pairs={{1,0},{2,1},{3,2},{5,4},{6,5},{7,6},{9,8},{10,9},{11,10},{13,12},{... | collective-permute-start | bytes 1572872 | tf_op jit(solution)/shard_map/ppermute | solution.py:24

commit v13 on v12

--- a/solution.py
+++ b/solution.py
@@ -143,8 +143,9 @@
     cols = jnp.arange(total_cols, dtype=jnp.int32)
     across = (
         jnp.mod(tilts[:, 0:1] * global_rows[None, :], total_rows).astype(jnp.float32) / total_rows
+     + landed
     )
-    along = jnp.mod(tilts[:, 1:2] * cols[None, :], total_cols).astype(jnp.float32) / total_cols
+    along = jnp.mod(tilts[:, 1:2] * cols[None, :], total_cols).astype(jnp.float32) / total_cols + landed
     across_cos = jnp.where(inside[None, :], jnp.cos(two_pi * across), 0.0)[:, :, None]
     across_sin = jnp.where(inside[None, :], jnp.sin(two_pi * across), 0.0)[:, :, None]
     along_cos = jnp.cos(two_pi * along)[:, None, :]

time: 65 us -> 67.4 us (1.037)
  waiting for transfers between devices: 14.7 us -> 16.2 us
  starting transfers between devices: 21 us -> 22.1 us
    ppermute x2, waiting for transfers between devices: 5.43 us -> 7.03 us  [extended(): lax.ppermute(head, axis, [((i + 1) % count, i) for i in range(ends)])]
    ppermute x6, starting transfers between devices: 9.94 us -> 11.2 us  [exchange(): return lax.ppermute(x, axis, [(i, partner(i, k)) for i in range(count)])]
    ppermute x2, starting transfers between devices: 7.05 us -> 6.36 us  [extended(): lax.ppermute(tail, axis, [(i, (i + 1) % count) for i in range(ends)])]
  transfers between devices with their start and end apart: 10 -> 10, of which waited for: 4 -> 5; matrix products, arithmetic and copies ran while one was open for 18% -> 17% of each run, Pallas kernels for 0% -> 0%
where the time goes in v13:
time: 67.4 us; the launch traced here: 67 us
  starting transfers between devices  22.1 us (33%)
  local copies, waits for them, and re-layouts  17.4 us (26%)
  waiting for transfers between devices  16.2 us (24%)
  other arithmetic  5.4 us (8%)
  matrix products  3.64 us (5%)
  between operations  2.29 us (3%)
    ppermute x6, starting transfers between devices, exchange(): return lax.ppermute(x, axis, [(i, partner(i, k)) for i in range(count)])  11.2 us
    ppermute x2, waiting for transfers between devices, extended(): lax.ppermute(head, axis, [((i + 1) % count, i) for i in range(ends)])  7.03 us
    ppermute x2, starting transfers between devices, extended(): lax.ppermute(tail, axis, [(i, (i + 1) % count) for i in range(ends)])  6.36 us
    ppermute x6, waiting for transfers between devices, exchange(): return lax.ppermute(x, axis, [(i, partner(i, k)) for i in range(count)])  5.69 us
    ppermute x2, starting transfers between devices, extended(): lax.ppermute(head, axis, [((i + 1) % count, i) for i in range(ends)])  4.53 us
    unnamed x26, local copies, waits for them, and re-layouts  3.85 us
    ppermute x2, waiting for transfers between devices, extended(): lax.ppermute(tail, axis, [(i, (i + 1) % count) for i in range(ends)])  3.48 us
    dot_general x2, matrix products, along_pass(): out = jnp.einsum('...nj,jc->...nc', win, kern, precision=lax.Precision.HIGH)  2.27 us
  transfers between devices with their start and end apart: 10, of which 5 were waited for; matrix products, arithmetic and copies ran while one was open for 17% of the time, Pallas kernels for 0%

profile of v13, /device:TPU:1, one launch (start us, length us, event | category | flops | bytes accessed | tf_op | source)
XLA Modules:
  0.0 67.0 jit_solution(13068363989436410059)
XLA Ops:
  0.0 3.1 %collective-permute-start.1 = (f32[2,32,512]{2,1,0:T(8,128)}, f32[2,32,512]{2,1,0:T(8,128)S(1)}, u32[]{:S(2)}, u32[]{:S(2)}) collective-permute-start(f32[2,32,512]{2,1,0:T(8,128)} %param.6), channel_id=1, source_target_pairs={{0,16},{4,20},{8,24},{12,28},{16,0},{20,4},{24,8},{28,12},{1,17},{... | collective-permute-start | bytes 393224 | tf_op jit(solution)/shard_map/ppermute | solution.py:108
  3.1 1.3 %collective-permute-start = (f32[2,32,512]{2,1,0:T(8,128)}, f32[2,32,512]{2,1,0:T(8,128)S(1)}, u32[]{:S(2)}, u32[]{:S(2)}) collective-permute-start(f32[2,32,512]{2,1,0:T(8,128)} %param.6), channel_id=1, source_target_pairs={{0,8},{4,12},{8,0},{12,4},{16,24},{20,28},{24,16},{28,20},{1,9},{5... | collective-permute-start | bytes 393224 | tf_op jit(solution)/shard_map/ppermute | solution.py:108
  4.4 1.2 %collective-permute-start.4 = (f32[2,32,512]{2,1,0:T(8,128)}, f32[2,32,512]{2,1,0:T(8,128)S(1)}, u32[]{:S(2)}, u32[]{:S(2)}) collective-permute-start(f32[2,32,512]{2,1,0:T(8,128)} %param.6), channel_id=1, source_target_pairs={{0,4},{4,0},{8,12},{12,8},{16,20},{20,16},{24,28},{28,24},{1,5},{5... | collective-permute-start | bytes 393224 | tf_op jit(solution)/shard_map/ppermute | solution.py:108
  5.7 0.9 %bitcast_dynamic-update-slice_fusion.6 = f32[2,8,32,512]{3,2,0,1:T(8,128)S(1)} fusion(f32[2,32,512]{2,1,0:T(8,128)} %param.6), kind=kLoop, calls=%fused_computation.78 | loop fusion | bytes 262144
  6.7 0.8 %fusion.37 = (s32[8]{0:T(128)S(1)}, s32[8]{0:T(128)S(1)}) fusion(s32[2,8]{1,0:T(2,128)} %param.7, s32[]{:T(128)S(6)} %axis_index.25), kind=kLoop, calls=%fused_computation.112 | loop fusion | flops 64 | bytes 132 | tf_op jit(solution)/shard_map/select_n | solution.py:127
  7.4 1.4 %fusion.47 = (s32[1,1]{1,0:T(1,128)}, s32[1,1]{1,0:T(1,128)}) fusion(s32[1,2]{1,0:T(1,128)} %param.4), kind=kLoop, calls=%fused_computation.134 | loop fusion | bytes 16 | tf_op jit(solution)/shard_map/slice | solution.py:145
  9.2 0.8 %collective-permute-start.2 = (f32[2,2,32,512]{3,2,1,0:T(8,128)S(1)}, f32[2,2,32,512]{3,2,1,0:T(8,128)S(1)}, u32[]{:S(2)}, u32[]{:S(2)}) collective-permute-start(f32[2,2,32,512]{3,2,1,0:T(8,128)S(1)} %pad_maximum_fusion.3), channel_id=1, source_target_pairs={{0,4},{4,0},{8,12},{12,8},{16,20},{20,16},{24,28},{28,24},{1,5},{5... | collective-permute-start | bytes 786440 | tf_op jit(solution)/shard_map/ppermute | solution.py:108
  10.0 2.0 %collective-permute-start.3 = (f32[2,32,512]{2,1,0:T(8,128)S(1)}, f32[2,32,512]{2,1,0:T(8,128)S(1)}, u32[]{:S(2)}, u32[]{:S(2)}) collective-permute-start(f32[2,32,512]{2,1,0:T(8,128)S(1)} %collective-permute-done.1), channel_id=1, source_target_pairs={{0,8},{4,12},{8,0},{12,4},{16,24},{20,28},{24,16},{28,20},{1,9},{5... | collective-permute-start | bytes 393224 | tf_op jit(solution)/shard_map/ppermute | solution.py:108
  12.0 2.7 %collective-permute-start.5 = (f32[2,32,512]{2,1,0:T(8,128)S(1)}, f32[2,32,512]{2,1,0:T(8,128)S(1)}, u32[]{:S(2)}, u32[]{:S(2)}) collective-permute-start(f32[2,32,512]{2,1,0:T(8,128)S(1)} %collective-permute-done.4), channel_id=1, source_target_pairs={{0,24},{4,28},{8,16},{12,20},{16,8},{20,12},{24,0},{28,4},{1,25},{... | collective-permute-start | bytes 393224 | tf_op jit(solution)/shard_map/ppermute | solution.py:108
  15.3 5.4 %collective-permute-done.5 = f32[2,32,512]{2,1,0:T(8,128)S(1)} collective-permute-done((f32[2,32,512]{2,1,0:T(8,128)S(1)}, f32[2,32,512]{2,1,0:T(8,128)S(1)}, u32[]{:S(2)}, u32[]{:S(2)}) %collective-permute-start.5) | collective-permute-done | bytes 131104 | tf_op jit(solution)/shard_map/ppermute | solution.py:108
  21.3 0.9 %slice_bitcast_fusion.2 = (f32[8,32,512]{2,1,0:T(8,128)}, f32[8,32,512]{2,1,0:T(8,128)S(1)}) fusion(f32[2,8,32,512]{3,2,0,1:T(8,128)S(1)} %bitcast_dynamic-update-slice_fusion), kind=kLoop, calls=%fused_computation.40 | loop fusion | bytes 2097152 | tf_op jit(solution)/shard_map/squeeze | solution.py:127
  22.2 0.6 gather_fusion
  22.7 1.9 %sine_bitcast_fusion.1 = (f32[32,8,512]{2,0,1:T(8,128)S(1)}, f32[32,8,512]{2,0,1:T(8,128)S(1)}) fusion(f32[8,32,512]{2,1,0:T(8,128)S(1)} %gather_fusion), kind=kLoop, calls=%fused_computation.58 | loop fusion | bytes 1572864 | tf_op jit(solution)/shard_map/sin | solution.py:159
  25.6 1.1 %fusion.46 = (f32[2,16,4096]{2,1,0:T(8,128)}, f32[2,16,4096]{2,1,0:T(8,128)}) fusion(f32[2,32,4096]{2,1,0:T(8,128)S(1)} %constant_dynamic-update-slice_fusion), kind=kLoop, calls=%fused_computation.133 | loop fusion | bytes 2097152 | tf_op jit(solution)/shard_map/slice | solution.py:18
  26.7 4.4 %collective-permute-start.6 = (f32[2,16,4096]{2,1,0:T(8,128)}, f32[2,16,4096]{2,1,0:T(8,128)S(1)}, u32[]{:S(2)}, u32[]{:S(2)}) collective-permute-start(f32[2,16,4096]{2,1,0:T(8,128)} %get-tuple-element.26), channel_id=1, source_target_pairs={{0,1},{1,2},{2,3},{4,5},{5,6},{6,7},{8,9},{9,10},{10,11},{12,13},{... | collective-permute-start | bytes 1572872 | tf_op jit(solution)/shard_map/ppermute | solution.py:22
  33.4 0.7 %sine_select_fusion = (f32[1,64,1]{1,2,0:T(1,128)S(1)}, f32[1,64,1]{1,2,0:T(1,128)S(1)}) fusion(s32[]{:T(128)S(6)} %sub.157, f32[]{:T(128)} %bitcast.4, s32[]{:T(128)} %bitcast), kind=kLoop, calls=%fused_computation.121 | loop fusion | flops 1408 | bytes 524 | tf_op jit(solution)/shard_map/jit(_where)/select_n | solution.py:150
  34.2 1.9 %collective-permute-start.7 = (f32[2,16,4096]{2,1,0:T(8,128)}, f32[2,16,4096]{2,1,0:T(8,128)S(1)}, u32[]{:S(2)}, u32[]{:S(2)}) collective-permute-start(f32[2,16,4096]{2,1,0:T(8,128)} %get-tuple-element.25), channel_id=1, source_target_pairs={{1,0},{2,1},{3,2},{5,4},{6,5},{7,6},{9,8},{10,9},{11,10},{13,12},{... | collective-permute-start | bytes 1572872 | tf_op jit(solution)/shard_map/ppermute | solution.py:24
  37.0 0.6 gather_fusion.1
  37.5 1.9 %sine_bitcast_fusion = (f32[32,8,512]{2,0,1:T(8,128)S(1)}, f32[32,8,512]{2,0,1:T(8,128)S(1)}) fusion(f32[8,32,512]{2,1,0:T(8,128)S(1)} %gather_fusion.1), kind=kLoop, calls=%fused_computation.48 | loop fusion | bytes 1572864 | tf_op jit(solution)/shard_map/sin | solution.py:81
  39.7 0.9 %cos.74 = f32[1,1,32,4096]{3,2,1,0:T(8,128)} reshape(f32[32,8,512]{2,1,0:T(8,128)S(1)} %copy.11) | data formatting | bytes 1048576 | tf_op jit(solution)/shard_map/cos | solution.py:81
  41.0 0.7 %fusion.29 = (f32[4096]{0:T(1024)S(1)}, f32[4096]{0:T(1024)S(1)}) fusion(f32[]{:T(128)} %bitcast.4, s32[]{:T(128)} %bitcast.6), kind=kLoop, calls=%fused_computation.96 | loop fusion | flops 65536 | bytes 32776 | tf_op jit(solution)/shard_map/sin | solution.py:152
  42.3 2.6 %collective-permute-done.7 = f32[2,16,4096]{2,1,0:T(8,128)S(1)} collective-permute-done((f32[2,16,4096]{2,1,0:T(8,128)}, f32[2,16,4096]{2,1,0:T(8,128)S(1)}, u32[]{:S(2)}, u32[]{:S(2)}) %collective-permute-start.7) | collective-permute-done | bytes 524320 | tf_op jit(solution)/shard_map/ppermute | solution.py:24
  45.6 0.7 %convolution_bitcast_fusion.1 = f32[1,64,4096]{2,1,0:T(8,128)S(1)} fusion(f32[1,128,4096]{2,1,0:T(8,128)S(1)} %add_dynamic-update-slice_fusion.1, f32[32,64]{1,0:T(8,128)S(1)} %get-tuple-element.8, f32[32,64]{1,0:T(8,128)S(1)} %get-tuple-element.7, f32[32,64]{1,0:T(8,128)S(1)} %neg.4), kind=kOutput, calls=%fused_computation.3 | convolution fusion | flops 201351168 | bytes 3170304 | tf_op jit(solution)/shard_map/ij,ajy->aiy/dot_general | solution.py:76
  47.4 1.1 %fusion.18 = f32[1,32,32,256]{3,2,1,0:T(8,128)S(1)} fusion(f32[1,32,32,32]{3,2,1,0:T(8,128)S(1)} %bitcast.150, f32[1,32,32,128]{3,2,1,0:T(8,128)S(1)} %bitcast.156, f32[1,32,32,32]{3,2,1,0:T(8,128)S(1)} %bitcast.152, f32[1,32,32,128]{3,2,1,0:T(8,128)S(1)} %bitcast.154, f32[160,128]{1,0:T(8,128)S(1)} %get-tuple-element.6, f32[160,128]{1,0:T(8,128)S(1)} %neg.5, ...), kind=kOutput, calls=%fused_computation.29 | convolution fusion | flops 504545280 | bytes 2605056 | tf_op jit(solution)/shard_map/...nj,jc->...nc/dot_general | solution.py:68
  49.0 0.7 %copy-done = f32[1,1,32,4096]{3,2,1,0:T(8,128)S(1)} copy-done((f32[1,1,32,4096]{3,2,1,0:T(8,128)S(1)}, f32[1,1,32,4096]{3,2,1,0:T(8,128)}, u32[]{:S(2)}) %copy-start) | copy-done | bytes 524312
  49.8 1.9 %collective-permute-start.8 = (f32[2,1,16,4096]{3,2,1,0:T(8,128)S(1)}, f32[2,1,16,4096]{3,2,1,0:T(8,128)S(1)}, u32[]{:S(2)}, u32[]{:S(2)}) collective-permute-start(f32[2,1,16,4096]{3,2,1,0:T(8,128)S(1)} %get-tuple-element.17), channel_id=1, source_target_pairs={{0,1},{1,2},{2,3},{4,5},{5,6},{6,7},{8,9},{9,10},{10,11},{12,13},{... | collective-permute-start | bytes 1572872 | tf_op jit(solution)/shard_map/ppermute | solution.py:22
  51.8 2.6 %collective-permute-start.9 = (f32[2,1,16,4096]{3,2,1,0:T(8,128)S(1)}, f32[2,1,16,4096]{3,2,1,0:T(8,128)S(1)}, u32[]{:S(2)}, u32[]{:S(2)}) collective-permute-start(f32[2,1,16,4096]{3,2,1,0:T(8,128)S(1)} %get-tuple-element.18), channel_id=1, source_target_pairs={{1,0},{2,1},{3,2},{5,4},{6,5},{7,6},{9,8},{10,9},{11,10},{13,12},{... | collective-permute-start | bytes 1572872 | tf_op jit(solution)/shard_map/ppermute | solution.py:24
  54.4 3.5 %collective-permute-done.8 = f32[2,1,16,4096]{3,2,1,0:T(8,128)S(1)} collective-permute-done((f32[2,1,16,4096]{3,2,1,0:T(8,128)S(1)}, f32[2,1,16,4096]{3,2,1,0:T(8,128)S(1)}, u32[]{:S(2)}, u32[]{:S(2)}) %collective-permute-start.8) | collective-permute-done | bytes 524320 | tf_op jit(solution)/shard_map/ppermute | solution.py:22
  57.9 4.4 %collective-permute-done.9 = f32[2,1,16,4096]{3,2,1,0:T(8,128)S(1)} collective-permute-done((f32[2,1,16,4096]{3,2,1,0:T(8,128)S(1)}, f32[2,1,16,4096]{3,2,1,0:T(8,128)S(1)}, u32[]{:S(2)}, u32[]{:S(2)}) %collective-permute-start.9) | collective-permute-done | bytes 524320 | tf_op jit(solution)/shard_map/ppermute | solution.py:24
  62.6 0.7 %convolution_bitcast_fusion = f32[1,64,4096]{2,1,0:T(8,128)S(1)} fusion(f32[1,64,4096]{2,1,0:T(8,128)S(1)} %get-tuple-element.10, f32[1,64,4096]{2,1,0:T(8,128)S(1)} %get-tuple-element.9, f32[32,64]{1,0:T(8,128)S(1)} %get-tuple-element.8, f32[32,64]{1,0:T(8,128)S(1)} %get-tuple-element.7, f32[32,64]{1,0:T(8,128)S(1)} %neg.4), kind=kOutput, calls=%fused_computation.2 | convolution fusion | flops 201875456 | bytes 3170304 | tf_op jit(solution)/shard_map/ij,ajy->aiy/dot_general | solution.py:76
  64.5 1.1 %fusion.17 = f32[1,32,32,256]{3,2,1,0:T(8,128)S(1)} fusion(f32[1,32,32,32]{3,2,1,0:T(8,128)S(1)} %bitcast.149, f32[1,32,32,128]{3,2,1,0:T(8,128)S(1)} %bitcast.155, f32[1,32,32,32]{3,2,1,0:T(8,128)S(1)} %bitcast.151, f32[1,32,32,128]{3,2,1,0:T(8,128)S(1)} %bitcast.153, f32[160,128]{1,0:T(8,128)S(1)} %get-tuple-element.6, f32[160,128]{1,0:T(8,128)S(1)} %neg.5, ...), kind=kOutput, calls=%fused_computation.28 | convolution fusion | flops 504545280 | bytes 2605056 | tf_op jit(solution)/shard_map/...nj,jc->...nc/dot_general | solution.py:68
  66.0 1.0 %pad_maximum_fusion.1 = f32[2,1,32,4096]{3,2,1,0:T(8,128)} fusion(f32[1,1,32,4096]{3,2,1,0:T(8,128)S(1)} %stack_reshape.7, f32[1,1,32,4096]{3,2,1,0:T(8,128)S(1)} %stack_reshape.6), kind=kLoop, calls=%fused_computation.34 | loop fusion | flops 262144 | bytes 2097152 | tf_op jit(solution)/shard_map/stack | solution.py:178
  (75 shorter events, 9.2 us)
Async XLA Ops:
  0.0 9.1 %collective-permute-start.1 = (f32[2,32,512]{2,1,0:T(8,128)}, f32[2,32,512]{2,1,0:T(8,128)S(1)}, u32[]{:S(2)}, u32[]{:S(2)}) collective-permute-start(f32[2,32,512]{2,1,0:T(8,128)} %param.6), channel_id=1, source_target_pairs={{0,16},{4,20},{8,24},{12,28},{16,0},{20,4},{24,8},{28,12},{1,17},{... | collective-permute-start | bytes 393224 | tf_op jit(solution)/shard_map/ppermute | solution.py:108
  3.1 6.0 %collective-permute-start = (f32[2,32,512]{2,1,0:T(8,128)}, f32[2,32,512]{2,1,0:T(8,128)S(1)}, u32[]{:S(2)}, u32[]{:S(2)}) collective-permute-start(f32[2,32,512]{2,1,0:T(8,128)} %param.6), channel_id=1, source_target_pairs={{0,8},{4,12},{8,0},{12,4},{16,24},{20,28},{24,16},{28,20},{1,9},{5... | collective-permute-start | bytes 393224 | tf_op jit(solution)/shard_map/ppermute | solution.py:108
  4.4 7.6 %collective-permute-start.4 = (f32[2,32,512]{2,1,0:T(8,128)}, f32[2,32,512]{2,1,0:T(8,128)S(1)}, u32[]{:S(2)}, u32[]{:S(2)}) collective-permute-start(f32[2,32,512]{2,1,0:T(8,128)} %param.6), channel_id=1, source_target_pairs={{0,4},{4,0},{8,12},{12,8},{16,20},{20,16},{24,28},{28,24},{1,5},{5... | collective-permute-start | bytes 393224 | tf_op jit(solution)/shard_map/ppermute | solution.py:108
  9.2 12.0 %collective-permute-start.2 = (f32[2,2,32,512]{3,2,1,0:T(8,128)S(1)}, f32[2,2,32,512]{3,2,1,0:T(8,128)S(1)}, u32[]{:S(2)}, u32[]{:S(2)}) collective-permute-start(f32[2,2,32,512]{3,2,1,0:T(8,128)S(1)} %pad_maximum_fusion.3), channel_id=1, source_target_pairs={{0,4},{4,0},{8,12},{12,8},{16,20},{20,16},{24,28},{28,24},{1,5},{5... | collective-permute-start | bytes 786440 | tf_op jit(solution)/shard_map/ppermute | solution.py:108
  10.0 4.8 %collective-permute-start.3 = (f32[2,32,512]{2,1,0:T(8,128)S(1)}, f32[2,32,512]{2,1,0:T(8,128)S(1)}, u32[]{:S(2)}, u32[]{:S(2)}) collective-permute-start(f32[2,32,512]{2,1,0:T(8,128)S(1)} %collective-permute-done.1), channel_id=1, source_target_pairs={{0,8},{4,12},{8,0},{12,4},{16,24},{20,28},{24,16},{28,20},{1,9},{5... | collective-permute-start | bytes 393224 | tf_op jit(solution)/shard_map/ppermute | solution.py:108
  12.0 8.6 %collective-permute-start.5 = (f32[2,32,512]{2,1,0:T(8,128)S(1)}, f32[2,32,512]{2,1,0:T(8,128)S(1)}, u32[]{:S(2)}, u32[]{:S(2)}) collective-permute-start(f32[2,32,512]{2,1,0:T(8,128)S(1)} %collective-permute-done.4), channel_id=1, source_target_pairs={{0,24},{4,28},{8,16},{12,20},{16,8},{20,12},{24,0},{28,4},{1,25},{... | collective-permute-start | bytes 393224 | tf_op jit(solution)/shard_map/ppermute | solution.py:108
  25.4 10.7 %copy-start.2 = (f32[2,33]{1,0:T(2,128)S(1)}, f32[2,33]{1,0:T(2,128)}, u32[]{:S(2)}) copy-start(f32[2,33]{1,0:T(2,128)} %param.5) | copy-start | bytes 796
  25.5 11.4 %copy-start.1 = (f32[8,32,512]{2,1,0:T(8,128)S(1)}, f32[8,32,512]{2,1,0:T(8,128)}, u32[]{:S(2)}) copy-start(f32[8,32,512]{2,1,0:T(8,128)} %get-tuple-element.21) | copy-start | bytes 1572868
  26.7 15.2 %collective-permute-start.6 = (f32[2,16,4096]{2,1,0:T(8,128)}, f32[2,16,4096]{2,1,0:T(8,128)S(1)}, u32[]{:S(2)}, u32[]{:S(2)}) collective-permute-start(f32[2,16,4096]{2,1,0:T(8,128)} %get-tuple-element.26), channel_id=1, source_target_pairs={{0,1},{1,2},{2,3},{4,5},{5,6},{6,7},{8,9},{9,10},{10,11},{12,13},{... | collective-permute-start | bytes 1572872 | tf_op jit(solution)/shard_map/ppermute | solution.py:22
  34.2 10.7 %collective-permute-start.7 = (f32[2,16,4096]{2,1,0:T(8,128)}, f32[2,16,4096]{2,1,0:T(8,128)S(1)}, u32[]{:S(2)}, u32[]{:S(2)}) collective-permute-start(f32[2,16,4096]{2,1,0:T(8,128)} %get-tuple-element.25), channel_id=1, source_target_pairs={{1,0},{2,1},{3,2},{5,4},{6,5},{7,6},{9,8},{10,9},{11,10},{13,12},{... | collective-permute-start | bytes 1572872 | tf_op jit(solution)/shard_map/ppermute | solution.py:24
  48.6 1.0 %copy-start = (f32[1,1,32,4096]{3,2,1,0:T(8,128)S(1)}, f32[1,1,32,4096]{3,2,1,0:T(8,128)}, u32[]{:S(2)}) copy-start(f32[1,1,32,4096]{3,2,1,0:T(8,128)} %cos.74) | copy-start | bytes 1572868
  49.8 8.0 %collective-permute-start.8 = (f32[2,1,16,4096]{3,2,1,0:T(8,128)S(1)}, f32[2,1,16,4096]{3,2,1,0:T(8,128)S(1)}, u32[]{:S(2)}, u32[]{:S(2)}) collective-permute-start(f32[2,1,16,4096]{3,2,1,0:T(8,128)S(1)} %get-tuple-element.17), channel_id=1, source_target_pairs={{0,1},{1,2},{2,3},{4,5},{5,6},{6,7},{8,9},{9,10},{10,11},{12,13},{... | collective-permute-start | bytes 1572872 | tf_op jit(solution)/shard_map/ppermute | solution.py:22
  51.8 10.5 %collective-permute-start.9 = (f32[2,1,16,4096]{3,2,1,0:T(8,128)S(1)}, f32[2,1,16,4096]{3,2,1,0:T(8,128)S(1)}, u32[]{:S(2)}, u32[]{:S(2)}) collective-permute-start(f32[2,1,16,4096]{3,2,1,0:T(8,128)S(1)} %get-tuple-element.18), channel_id=1, source_target_pairs={{1,0},{2,1},{3,2},{5,4},{6,5},{7,6},{9,8},{10,9},{11,10},{13,12},{... | collective-permute-start | bytes 1572872 | tf_op jit(solution)/shard_map/ppermute | solution.py:24

commit v14 on v12

--- a/solution.py
+++ b/solution.py
@@ -111,7 +111,7 @@
         one, two, four = (exchange(stored_planes, k) for k in (1, 2, 4))
         three, five = exchange(jnp.stack([two, four]), 1)
         six = exchange(four, 2)
-        seven = exchange(one, 6)
+        seven = exchange(four, 3)
         parts = [stored_planes, one, two, three, four, five, six, seven]
         first = [three, six, seven]
     else:

time: 65 us -> 64.4 us (level)
  waiting for transfers between devices: 14.7 us -> 13.3 us
  starting transfers between devices: 21 us -> 21.9 us
    ppermute x2, starting transfers between devices: 7.05 us -> 9.45 us  [extended(): lax.ppermute(tail, axis, [(i, (i + 1) % count) for i in range(ends)])]
    ppermute x6, starting transfers between devices: 9.94 us -> 8.39 us  [exchange(): return lax.ppermute(x, axis, [(i, partner(i, k)) for i in range(count)])]
    ppermute x6, waiting for transfers between devices: 5.31 us -> 3.86 us  [exchange(): return lax.ppermute(x, axis, [(i, partner(i, k)) for i in range(count)])]
  transfers between devices with their start and end apart: 10 -> 10, of which waited for: 4 -> 6; matrix products, arithmetic and copies ran while one was open for 18% -> 18% of each run, Pallas kernels for 0% -> 0%
where the time goes in v14:
time: 64.4 us; the launch traced here: 64.1 us
  starting transfers between devices  21.9 us (34%)
  local copies, waits for them, and re-layouts  17.5 us (27%)
  waiting for transfers between devices  13.3 us (21%)
  other arithmetic  5.37 us (8%)
  matrix products  3.64 us (6%)
  between operations  2.43 us (4%)
    ppermute x2, starting transfers between devices, extended(): lax.ppermute(tail, axis, [(i, (i + 1) % count) for i in range(ends)])  9.45 us
    ppermute x6, starting transfers between devices, exchange(): return lax.ppermute(x, axis, [(i, partner(i, k)) for i in range(count)])  8.39 us
    ppermute x2, waiting for transfers between devices, extended(): lax.ppermute(head, axis, [((i + 1) % count, i) for i in range(ends)])  5.43 us
    ppermute x2, starting transfers between devices, extended(): lax.ppermute(head, axis, [((i + 1) % count, i) for i in range(ends)])  4.02 us
    ppermute x2, waiting for transfers between devices, extended(): lax.ppermute(tail, axis, [(i, (i + 1) % count) for i in range(ends)])  4 us
    ppermute x6, waiting for transfers between devices, exchange(): return lax.ppermute(x, axis, [(i, partner(i, k)) for i in range(count)])  3.86 us
    unnamed x26, local copies, waits for them, and re-layouts  3.85 us
    dot_general x2, matrix products, along_pass(): out = jnp.einsum('...nj,jc->...nc', win, kern, precision=lax.Precision.HIGH)  2.27 us
  transfers between devices with their start and end apart: 10, of which 6 were waited for; matrix products, arithmetic and copies ran while one was open for 18% of the time, Pallas kernels for 0%

profile of v14, /device:TPU:1, one launch (start us, length us, event | category | flops | bytes accessed | tf_op | source)
XLA Modules:
  0.0 64.1 jit_solution(9044496587760417421)
XLA Ops:
  0.0 3.1 %collective-permute-start.2 = (f32[2,32,512]{2,1,0:T(8,128)}, f32[2,32,512]{2,1,0:T(8,128)S(1)}, u32[]{:S(2)}, u32[]{:S(2)}) collective-permute-start(f32[2,32,512]{2,1,0:T(8,128)} %param.6), channel_id=1, source_target_pairs={{0,16},{4,20},{8,24},{12,28},{16,0},{20,4},{24,8},{28,12},{1,17},{... | collective-permute-start | bytes 393224 | tf_op jit(solution)/shard_map/ppermute | solution.py:108
  3.1 1.3 %collective-permute-start.1 = (f32[2,32,512]{2,1,0:T(8,128)}, f32[2,32,512]{2,1,0:T(8,128)S(1)}, u32[]{:S(2)}, u32[]{:S(2)}) collective-permute-start(f32[2,32,512]{2,1,0:T(8,128)} %param.6), channel_id=1, source_target_pairs={{0,8},{4,12},{8,0},{12,4},{16,24},{20,28},{24,16},{28,20},{1,9},{5... | collective-permute-start | bytes 393224 | tf_op jit(solution)/shard_map/ppermute | solution.py:108
  4.4 1.2 %collective-permute-start = (f32[2,32,512]{2,1,0:T(8,128)}, f32[2,32,512]{2,1,0:T(8,128)S(1)}, u32[]{:S(2)}, u32[]{:S(2)}) collective-permute-start(f32[2,32,512]{2,1,0:T(8,128)} %param.6), channel_id=1, source_target_pairs={{0,4},{4,0},{8,12},{12,8},{16,20},{20,16},{24,28},{28,24},{1,5},{5... | collective-permute-start | bytes 393224 | tf_op jit(solution)/shard_map/ppermute | solution.py:108
  5.7 0.9 %bitcast_dynamic-update-slice_fusion.6 = f32[2,8,32,512]{3,2,0,1:T(8,128)S(1)} fusion(f32[2,32,512]{2,1,0:T(8,128)} %param.6), kind=kLoop, calls=%fused_computation.78 | loop fusion | bytes 262144
  6.6 1.3 %fusion.43 = (s32[1,1]{1,0:T(1,128)}, s32[1,1]{1,0:T(1,128)}) fusion(s32[1,2]{1,0:T(1,128)} %param.4), kind=kLoop, calls=%fused_computation.130 | loop fusion | bytes 16 | tf_op jit(solution)/shard_map/slice | solution.py:145
  7.9 0.7 %sine_select_fusion = (f32[1,64,1]{1,2,0:T(1,128)S(1)}, f32[1,64,1]{1,2,0:T(1,128)S(1)}) fusion(s32[]{:T(128)S(6)} %sub.157, s32[]{:T(128)} %bitcast), kind=kLoop, calls=%fused_computation.117 | loop fusion | flops 1280 | bytes 520 | tf_op jit(solution)/shard_map/jit(_where)/select_n | solution.py:149
  9.0 0.7 %fusion.27 = (f32[4096]{0:T(1024)S(1)}, f32[4096]{0:T(1024)S(1)}) fusion(s32[]{:T(128)} %bitcast.2), kind=kLoop, calls=%fused_computation.94 | loop fusion | flops 57344 | bytes 32772 | tf_op jit(solution)/shard_map/sin | solution.py:151
  9.6 0.8 %fusion.33 = (s32[8]{0:T(128)S(1)}, s32[8]{0:T(128)S(1)}) fusion(s32[2,8]{1,0:T(2,128)} %param.7, s32[]{:T(128)S(6)} %axis_index.25), kind=kLoop, calls=%fused_computation.108 | loop fusion | flops 64 | bytes 132 | tf_op jit(solution)/shard_map/select_n | solution.py:127
  10.7 1.3 %collective-permute-start.4 = (f32[2,32,512]{2,1,0:T(8,128)S(1)}, f32[2,32,512]{2,1,0:T(8,128)S(1)}, u32[]{:S(2)}, u32[]{:S(2)}) collective-permute-start(f32[2,32,512]{2,1,0:T(8,128)S(1)} %collective-permute-done.2), channel_id=1, source_target_pairs={{0,8},{4,12},{8,0},{12,4},{16,24},{20,28},{24,16},{28,20},{1,9},{5... | collective-permute-start | bytes 393224 | tf_op jit(solution)/shard_map/ppermute | solution.py:108
  12.0 1.2 %collective-permute-start.5 = (f32[2,32,512]{2,1,0:T(8,128)S(1)}, f32[2,32,512]{2,1,0:T(8,128)S(1)}, u32[]{:S(2)}, u32[]{:S(2)}) collective-permute-start(f32[2,32,512]{2,1,0:T(8,128)S(1)} %collective-permute-done.2), channel_id=1, source_target_pairs={{0,12},{4,8},{8,4},{12,0},{16,28},{20,24},{24,20},{28,16},{1,13},{... | collective-permute-start | bytes 393224 | tf_op jit(solution)/shard_map/ppermute | solution.py:108
  13.2 1.4 %collective-permute-done.4 = f32[2,32,512]{2,1,0:T(8,128)S(1)} collective-permute-done((f32[2,32,512]{2,1,0:T(8,128)S(1)}, f32[2,32,512]{2,1,0:T(8,128)S(1)}, u32[]{:S(2)}, u32[]{:S(2)}) %collective-permute-start.4) | collective-permute-done | bytes 131104 | tf_op jit(solution)/shard_map/ppermute | solution.py:108
  15.1 2.3 %collective-permute-done.5 = f32[2,32,512]{2,1,0:T(8,128)S(1)} collective-permute-done((f32[2,32,512]{2,1,0:T(8,128)S(1)}, f32[2,32,512]{2,1,0:T(8,128)S(1)}, u32[]{:S(2)}, u32[]{:S(2)}) %collective-permute-start.5) | collective-permute-done | bytes 131104 | tf_op jit(solution)/shard_map/ppermute | solution.py:108
  18.3 0.9 %slice_bitcast_fusion.2 = (f32[8,32,512]{2,1,0:T(8,128)}, f32[8,32,512]{2,1,0:T(8,128)S(1)}) fusion(f32[2,8,32,512]{3,2,0,1:T(8,128)S(1)} %bitcast_dynamic-update-slice_fusion), kind=kLoop, calls=%fused_computation.40 | loop fusion | bytes 2097152 | tf_op jit(solution)/shard_map/squeeze | solution.py:127
  19.2 0.6 gather_fusion
  19.8 1.9 %sine_bitcast_fusion.1 = (f32[32,8,512]{2,0,1:T(8,128)S(1)}, f32[32,8,512]{2,0,1:T(8,128)S(1)}) fusion(f32[8,32,512]{2,1,0:T(8,128)S(1)} %gather_fusion), kind=kLoop, calls=%fused_computation.58 | loop fusion | bytes 1572864 | tf_op jit(solution)/shard_map/sin | solution.py:158
  22.6 1.1 %fusion.42 = (f32[2,16,4096]{2,1,0:T(8,128)}, f32[2,16,4096]{2,1,0:T(8,128)}) fusion(f32[2,32,4096]{2,1,0:T(8,128)S(1)} %constant_dynamic-update-slice_fusion), kind=kLoop, calls=%fused_computation.129 | loop fusion | bytes 2097152 | tf_op jit(solution)/shard_map/slice | solution.py:18
  23.7 6.8 %collective-permute-start.6 = (f32[2,16,4096]{2,1,0:T(8,128)}, f32[2,16,4096]{2,1,0:T(8,128)S(1)}, u32[]{:S(2)}, u32[]{:S(2)}) collective-permute-start(f32[2,16,4096]{2,1,0:T(8,128)} %get-tuple-element.26), channel_id=1, source_target_pairs={{0,1},{1,2},{2,3},{4,5},{5,6},{6,7},{8,9},{9,10},{10,11},{12,13},{... | collective-permute-start | bytes 1572872 | tf_op jit(solution)/shard_map/ppermute | solution.py:22
  30.5 1.9 %collective-permute-start.7 = (f32[2,16,4096]{2,1,0:T(8,128)}, f32[2,16,4096]{2,1,0:T(8,128)S(1)}, u32[]{:S(2)}, u32[]{:S(2)}) collective-permute-start(f32[2,16,4096]{2,1,0:T(8,128)} %get-tuple-element.25), channel_id=1, source_target_pairs={{1,0},{2,1},{3,2},{5,4},{6,5},{7,6},{9,8},{10,9},{11,10},{13,12},{... | collective-permute-start | bytes 1572872 | tf_op jit(solution)/shard_map/ppermute | solution.py:24
  35.7 0.6 gather_fusion.1
  36.3 1.9 %sine_bitcast_fusion = (f32[32,8,512]{2,0,1:T(8,128)S(1)}, f32[32,8,512]{2,0,1:T(8,128)S(1)}) fusion(f32[8,32,512]{2,1,0:T(8,128)S(1)} %gather_fusion.1), kind=kLoop, calls=%fused_computation.48 | loop fusion | bytes 1572864 | tf_op jit(solution)/shard_map/sin | solution.py:81
  38.5 0.9 %cos.74 = f32[1,1,32,4096]{3,2,1,0:T(8,128)} reshape(f32[32,8,512]{2,1,0:T(8,128)S(1)} %copy.11) | data formatting | bytes 1048576 | tf_op jit(solution)/shard_map/cos | solution.py:81
  40.2 1.0 %collective-permute-done.7 = f32[2,16,4096]{2,1,0:T(8,128)S(1)} collective-permute-done((f32[2,16,4096]{2,1,0:T(8,128)}, f32[2,16,4096]{2,1,0:T(8,128)S(1)}, u32[]{:S(2)}, u32[]{:S(2)}) %collective-permute-start.7) | collective-permute-done | bytes 524320 | tf_op jit(solution)/shard_map/ppermute | solution.py:24
  41.9 0.7 %convolution_bitcast_fusion.1 = f32[1,64,4096]{2,1,0:T(8,128)S(1)} fusion(f32[1,128,4096]{2,1,0:T(8,128)S(1)} %add_dynamic-update-slice_fusion.1, f32[32,64]{1,0:T(8,128)S(1)} %get-tuple-element.8, f32[32,64]{1,0:T(8,128)S(1)} %get-tuple-element.7, f32[32,64]{1,0:T(8,128)S(1)} %neg.4), kind=kOutput, calls=%fused_computation.3 | convolution fusion | flops 201351168 | bytes 3170304 | tf_op jit(solution)/shard_map/ij,ajy->aiy/dot_general | solution.py:76
  43.8 1.1 %fusion.18 = f32[1,32,32,256]{3,2,1,0:T(8,128)S(1)} fusion(f32[1,32,32,32]{3,2,1,0:T(8,128)S(1)} %bitcast.150, f32[1,32,32,128]{3,2,1,0:T(8,128)S(1)} %bitcast.156, f32[1,32,32,32]{3,2,1,0:T(8,128)S(1)} %bitcast.152, f32[1,32,32,128]{3,2,1,0:T(8,128)S(1)} %bitcast.154, f32[160,128]{1,0:T(8,128)S(1)} %get-tuple-element.6, f32[160,128]{1,0:T(8,128)S(1)} %neg.5, ...), kind=kOutput, calls=%fused_computation.29 | convolution fusion | flops 504545280 | bytes 2605056 | tf_op jit(solution)/shard_map/...nj,jc->...nc/dot_general | solution.py:68
  45.3 0.7 %copy-done = f32[1,1,32,4096]{3,2,1,0:T(8,128)S(1)} copy-done((f32[1,1,32,4096]{3,2,1,0:T(8,128)S(1)}, f32[1,1,32,4096]{3,2,1,0:T(8,128)}, u32[]{:S(2)}) %copy-start) | copy-done | bytes 524312
  46.2 2.6 %collective-permute-start.8 = (f32[2,1,16,4096]{3,2,1,0:T(8,128)S(1)}, f32[2,1,16,4096]{3,2,1,0:T(8,128)S(1)}, u32[]{:S(2)}, u32[]{:S(2)}) collective-permute-start(f32[2,1,16,4096]{3,2,1,0:T(8,128)S(1)} %get-tuple-element.17), channel_id=1, source_target_pairs={{0,1},{1,2},{2,3},{4,5},{5,6},{6,7},{8,9},{9,10},{10,11},{12,13},{... | collective-permute-start | bytes 1572872 | tf_op jit(solution)/shard_map/ppermute | solution.py:22
  48.8 2.1 %collective-permute-start.9 = (f32[2,1,16,4096]{3,2,1,0:T(8,128)S(1)}, f32[2,1,16,4096]{3,2,1,0:T(8,128)S(1)}, u32[]{:S(2)}, u32[]{:S(2)}) collective-permute-start(f32[2,1,16,4096]{3,2,1,0:T(8,128)S(1)} %get-tuple-element.18), channel_id=1, source_target_pairs={{1,0},{2,1},{3,2},{5,4},{6,5},{7,6},{9,8},{10,9},{11,10},{13,12},{... | collective-permute-start | bytes 1572872 | tf_op jit(solution)/shard_map/ppermute | solution.py:24
  50.9 4.0 %collective-permute-done.8 = f32[2,1,16,4096]{3,2,1,0:T(8,128)S(1)} collective-permute-done((f32[2,1,16,4096]{3,2,1,0:T(8,128)S(1)}, f32[2,1,16,4096]{3,2,1,0:T(8,128)S(1)}, u32[]{:S(2)}, u32[]{:S(2)}) %collective-permute-start.8) | collective-permute-done | bytes 524320 | tf_op jit(solution)/shard_map/ppermute | solution.py:22
  54.9 4.4 %collective-permute-done.9 = f32[2,1,16,4096]{3,2,1,0:T(8,128)S(1)} collective-permute-done((f32[2,1,16,4096]{3,2,1,0:T(8,128)S(1)}, f32[2,1,16,4096]{3,2,1,0:T(8,128)S(1)}, u32[]{:S(2)}, u32[]{:S(2)}) %collective-permute-start.9) | collective-permute-done | bytes 524320 | tf_op jit(solution)/shard_map/ppermute | solution.py:24
  59.7 0.7 %convolution_bitcast_fusion = f32[1,64,4096]{2,1,0:T(8,128)S(1)} fusion(f32[1,64,4096]{2,1,0:T(8,128)S(1)} %get-tuple-element.10, f32[1,64,4096]{2,1,0:T(8,128)S(1)} %get-tuple-element.9, f32[32,64]{1,0:T(8,128)S(1)} %get-tuple-element.8, f32[32,64]{1,0:T(8,128)S(1)} %get-tuple-element.7, f32[32,64]{1,0:T(8,128)S(1)} %neg.4), kind=kOutput, calls=%fused_computation.2 | convolution fusion | flops 201875456 | bytes 3170304 | tf_op jit(solution)/shard_map/ij,ajy->aiy/dot_general | solution.py:76
  61.5 1.1 %fusion.17 = f32[1,32,32,256]{3,2,1,0:T(8,128)S(1)} fusion(f32[1,32,32,32]{3,2,1,0:T(8,128)S(1)} %bitcast.149, f32[1,32,32,128]{3,2,1,0:T(8,128)S(1)} %bitcast.155, f32[1,32,32,32]{3,2,1,0:T(8,128)S(1)} %bitcast.151, f32[1,32,32,128]{3,2,1,0:T(8,128)S(1)} %bitcast.153, f32[160,128]{1,0:T(8,128)S(1)} %get-tuple-element.6, f32[160,128]{1,0:T(8,128)S(1)} %neg.5, ...), kind=kOutput, calls=%fused_computation.28 | convolution fusion | flops 504545280 | bytes 2605056 | tf_op jit(solution)/shard_map/...nj,jc->...nc/dot_general | solution.py:68
  63.0 1.0 %pad_maximum_fusion.1 = f32[2,1,32,4096]{3,2,1,0:T(8,128)} fusion(f32[1,1,32,4096]{3,2,1,0:T(8,128)S(1)} %stack_reshape.7, f32[1,1,32,4096]{3,2,1,0:T(8,128)S(1)} %stack_reshape.6), kind=kLoop, calls=%fused_computation.34 | loop fusion | flops 262144 | bytes 2097152 | tf_op jit(solution)/shard_map/stack | solution.py:177
  (75 shorter events, 9.5 us)
Async XLA Ops:
  0.0 10.4 %collective-permute-start.2 = (f32[2,32,512]{2,1,0:T(8,128)}, f32[2,32,512]{2,1,0:T(8,128)S(1)}, u32[]{:S(2)}, u32[]{:S(2)}) collective-permute-start(f32[2,32,512]{2,1,0:T(8,128)} %param.6), channel_id=1, source_target_pairs={{0,16},{4,20},{8,24},{12,28},{16,0},{20,4},{24,8},{28,12},{1,17},{... | collective-permute-start | bytes 393224 | tf_op jit(solution)/shard_map/ppermute | solution.py:108
  3.1 7.3 %collective-permute-start.1 = (f32[2,32,512]{2,1,0:T(8,128)}, f32[2,32,512]{2,1,0:T(8,128)S(1)}, u32[]{:S(2)}, u32[]{:S(2)}) collective-permute-start(f32[2,32,512]{2,1,0:T(8,128)} %param.6), channel_id=1, source_target_pairs={{0,8},{4,12},{8,0},{12,4},{16,24},{20,28},{24,16},{28,20},{1,9},{5... | collective-permute-start | bytes 393224 | tf_op jit(solution)/shard_map/ppermute | solution.py:108
  4.4 8.7 %collective-permute-start = (f32[2,32,512]{2,1,0:T(8,128)}, f32[2,32,512]{2,1,0:T(8,128)S(1)}, u32[]{:S(2)}, u32[]{:S(2)}) collective-permute-start(f32[2,32,512]{2,1,0:T(8,128)} %param.6), channel_id=1, source_target_pairs={{0,4},{4,0},{8,12},{12,8},{16,20},{20,16},{24,28},{28,24},{1,5},{5... | collective-permute-start | bytes 393224 | tf_op jit(solution)/shard_map/ppermute | solution.py:108
  10.4 7.8 %collective-permute-start.3 = (f32[2,2,32,512]{3,2,1,0:T(8,128)S(1)}, f32[2,2,32,512]{3,2,1,0:T(8,128)S(1)}, u32[]{:S(2)}, u32[]{:S(2)}) collective-permute-start(f32[2,2,32,512]{3,2,1,0:T(8,128)S(1)} %pad_maximum_fusion.3), channel_id=1, source_target_pairs={{0,4},{4,0},{8,12},{12,8},{16,20},{20,16},{24,28},{28,24},{1,5},{5... | collective-permute-start | bytes 786440 | tf_op jit(solution)/shard_map/ppermute | solution.py:108
  10.7 3.8 %collective-permute-start.4 = (f32[2,32,512]{2,1,0:T(8,128)S(1)}, f32[2,32,512]{2,1,0:T(8,128)S(1)}, u32[]{:S(2)}, u32[]{:S(2)}) collective-permute-start(f32[2,32,512]{2,1,0:T(8,128)S(1)} %collective-permute-done.2), channel_id=1, source_target_pairs={{0,8},{4,12},{8,0},{12,4},{16,24},{20,28},{24,16},{28,20},{1,9},{5... | collective-permute-start | bytes 393224 | tf_op jit(solution)/shard_map/ppermute | solution.py:108
  12.0 5.4 %collective-permute-start.5 = (f32[2,32,512]{2,1,0:T(8,128)S(1)}, f32[2,32,512]{2,1,0:T(8,128)S(1)}, u32[]{:S(2)}, u32[]{:S(2)}) collective-permute-start(f32[2,32,512]{2,1,0:T(8,128)S(1)} %collective-permute-done.2), channel_id=1, source_target_pairs={{0,12},{4,8},{8,4},{12,0},{16,28},{20,24},{24,20},{28,16},{1,13},{... | collective-permute-start | bytes 393224 | tf_op jit(solution)/shard_map/ppermute | solution.py:108
  22.4 12.5 %copy-start.2 = (f32[2,33]{1,0:T(2,128)S(1)}, f32[2,33]{1,0:T(2,128)}, u32[]{:S(2)}) copy-start(f32[2,33]{1,0:T(2,128)} %param.5) | copy-start | bytes 796
  22.5 13.2 %copy-start.1 = (f32[8,32,512]{2,1,0:T(8,128)S(1)}, f32[8,32,512]{2,1,0:T(8,128)}, u32[]{:S(2)}) copy-start(f32[8,32,512]{2,1,0:T(8,128)} %get-tuple-element.21) | copy-start | bytes 1572868
  23.7 16.1 %collective-permute-start.6 = (f32[2,16,4096]{2,1,0:T(8,128)}, f32[2,16,4096]{2,1,0:T(8,128)S(1)}, u32[]{:S(2)}, u32[]{:S(2)}) collective-permute-start(f32[2,16,4096]{2,1,0:T(8,128)} %get-tuple-element.26), channel_id=1, source_target_pairs={{0,1},{1,2},{2,3},{4,5},{5,6},{6,7},{8,9},{9,10},{10,11},{12,13},{... | collective-permute-start | bytes 1572872 | tf_op jit(solution)/shard_map/ppermute | solution.py:22
  30.5 10.7 %collective-permute-start.7 = (f32[2,16,4096]{2,1,0:T(8,128)}, f32[2,16,4096]{2,1,0:T(8,128)S(1)}, u32[]{:S(2)}, u32[]{:S(2)}) collective-permute-start(f32[2,16,4096]{2,1,0:T(8,128)} %get-tuple-element.25), channel_id=1, source_target_pairs={{1,0},{2,1},{3,2},{5,4},{6,5},{7,6},{9,8},{10,9},{11,10},{13,12},{... | collective-permute-start | bytes 1572872 | tf_op jit(solution)/shard_map/ppermute | solution.py:24
  44.9 1.0 %copy-start = (f32[1,1,32,4096]{3,2,1,0:T(8,128)S(1)}, f32[1,1,32,4096]{3,2,1,0:T(8,128)}, u32[]{:S(2)}) copy-start(f32[1,1,32,4096]{3,2,1,0:T(8,128)} %cos.74) | copy-start | bytes 1572868
  46.2 8.7 %collective-permute-start.8 = (f32[2,1,16,4096]{3,2,1,0:T(8,128)S(1)}, f32[2,1,16,4096]{3,2,1,0:T(8,128)S(1)}, u32[]{:S(2)}, u32[]{:S(2)}) collective-permute-start(f32[2,1,16,4096]{3,2,1,0:T(8,128)S(1)} %get-tuple-element.17), channel_id=1, source_target_pairs={{0,1},{1,2},{2,3},{4,5},{5,6},{6,7},{8,9},{9,10},{10,11},{12,13},{... | collective-permute-start | bytes 1572872 | tf_op jit(solution)/shard_map/ppermute | solution.py:22
  48.8 10.5 %collective-permute-start.9 = (f32[2,1,16,4096]{3,2,1,0:T(8,128)S(1)}, f32[2,1,16,4096]{3,2,1,0:T(8,128)S(1)}, u32[]{:S(2)}, u32[]{:S(2)}) collective-permute-start(f32[2,1,16,4096]{3,2,1,0:T(8,128)S(1)} %get-tuple-element.18), channel_id=1, source_target_pairs={{1,0},{2,1},{3,2},{5,4},{6,5},{7,6},{9,8},{10,9},{11,10},{13,12},{... | collective-permute-start | bytes 1572872 | tf_op jit(solution)/shard_map/ppermute | solution.py:24

commit v15 on v14

--- a/solution.py
+++ b/solution.py
@@ -14,17 +14,16 @@
 def extended(cells, sides, width):
     for axis, dim in sides:
         count = lax.axis_size(axis)
-        ends = count - 1
+        odd = lax.axis_index(axis) % 2 == 1
         head = lax.slice_in_dim(cells, 0, width, axis=dim)
         tail = lax.slice_in_dim(cells, cells.shape[dim] - width, cells.shape[dim], axis=dim)
-        cells = jnp.concatenate(
-            [
-                lax.ppermute(tail, axis, [(i, (i + 1) % count) for i in range(ends)]),
-                cells,
-                lax.ppermute(head, axis, [((i + 1) % count, i) for i in range(ends)]),
-            ],
-            axis=dim,
-        )
+        across = [(i, i + 1) for i in range(1, count - 1, 2)] + [(i + 1, i) for i in range(1, count - 1, 2)]
+        within = [(i, i + 1) for i in range(0, count - 1, 2)] + [(i + 1, i) for i in range(0, count - 1, 2)]
+        got_across = lax.ppermute(jnp.where(odd, tail, head), axis, across)
+        got_within = lax.ppermute(jnp.where(odd, head, tail), axis, within)
+        before = jnp.where(odd, got_within, got_across)
+        after = jnp.where(odd, got_across, got_within)
+        cells = jnp.concatenate([before, cells, after], axis=dim)
     return cells
 
 

time: 64.4 us -> 61 us (0.947)
  starting transfers between devices: 21.9 us -> 18.5 us
  other arithmetic: 5.37 us -> 8.42 us
  local copies, waits for them, and re-layouts: 17.5 us -> 15.8 us
  waiting for transfers between devices: 13.3 us -> 12 us
    ppermute x4, starting transfers between devices: 13.5 us -> 10.1 us  [the longest x2 6.19 us: extended(): got_across = lax.ppermute(jnp.where(odd, tail, head), axis, across)]
    select_n x0 -> x4, other arithmetic: none -> 2.51 us  [the longest x1 1.28 us: extended(): after = jnp.where(odd, got_across, got_within)]
    mul x4, local copies, waits for them, and re-layouts: 0.29 us -> 1.81 us  [incident(): real = across_cos[:, rows] * along_cos - across_sin[:, rows] * along_sin]
    ppermute x4, waiting for transfers between devices: 9.43 us -> 8.04 us  [the longest x2 8.03 us: extended(): got_across = lax.ppermute(jnp.where(odd, tail, head), axis, across)]
    slice x1 -> x0, local copies, waits for them, and re-layouts: 1.09 us -> none  [extended(): head = lax.slice_in_dim(cells, 0, width, axis=dim)]
    squeeze x1, local copies, waits for them, and re-layouts: 0.89 us -> 0.09 us  [gather_screens(): picked = stacked[p][source]]
    cos x2, local copies, waits for them, and re-layouts: 1.2 us -> 0.41 us  [transmit(): return rotate(real, imag, jnp.cos(screen), jnp.sin(screen))]
    unnamed x26 -> x30, local copies, waits for them, and re-layouts: 3.85 us -> 3.41 us
  transfers between devices with their start and end apart: 10 -> 10, of which waited for: 6 -> 5; matrix products, arithmetic and copies ran while one was open for 18% -> 21% of each run, Pallas kernels for 0% -> 0%
where the time goes in v15:
time: 61 us; the launch traced here: 60.7 us
  starting transfers between devices  18.5 us (30%)
  local copies, waits for them, and re-layouts  15.8 us (26%)
  waiting for transfers between devices  12 us (20%)
  other arithmetic  8.42 us (14%)
  matrix products  3.64 us (6%)
  between operations  2.39 us (4%)
    ppermute x6, starting transfers between devices, exchange(): return lax.ppermute(x, axis, [(i, partner(i, k)) for i in range(count)])  8.39 us
    ppermute x2, waiting for transfers between devices, extended(): got_across = lax.ppermute(jnp.where(odd, tail, head), axis, across)  8.03 us
    ppermute x2, starting transfers between devices, extended(): got_across = lax.ppermute(jnp.where(odd, tail, head), axis, across)  6.19 us
    ppermute x6, waiting for transfers between devices, exchange(): return lax.ppermute(x, axis, [(i, partner(i, k)) for i in range(count)])  3.98 us
    ppermute x2, starting transfers between devices, extended(): got_within = lax.ppermute(jnp.where(odd, head, tail), axis, within)  3.92 us
    unnamed x30, local copies, waits for them, and re-layouts  3.41 us
    dot_general x2, matrix products, along_pass(): out = jnp.einsum('...nj,jc->...nc', win, kern, precision=lax.Precision.HIGH)  2.27 us
    sin x3, local copies, waits for them, and re-layouts, transmit(): return rotate(real, imag, jnp.cos(screen), jnp.sin(screen))  2.27 us
  transfers between devices with their start and end apart: 10, of which 5 were waited for; matrix products, arithmetic and copies ran while one was open for 21% of the time, Pallas kernels for 0%

profile of v15, /device:TPU:1, one launch (start us, length us, event | category | flops | bytes accessed | tf_op | source)
XLA Modules:
  0.0 60.7 jit_solution(8329320105920017863)
XLA Ops:
  0.0 3.1 %collective-permute-start.2 = (f32[2,32,512]{2,1,0:T(8,128)}, f32[2,32,512]{2,1,0:T(8,128)S(1)}, u32[]{:S(2)}, u32[]{:S(2)}) collective-permute-start(f32[2,32,512]{2,1,0:T(8,128)} %param.6), channel_id=1, source_target_pairs={{0,16},{4,20},{8,24},{12,28},{16,0},{20,4},{24,8},{28,12},{1,17},{... | collective-permute-start | bytes 393224 | tf_op jit(solution)/shard_map/ppermute | solution.py:107
  3.1 1.3 %collective-permute-start.1 = (f32[2,32,512]{2,1,0:T(8,128)}, f32[2,32,512]{2,1,0:T(8,128)S(1)}, u32[]{:S(2)}, u32[]{:S(2)}) collective-permute-start(f32[2,32,512]{2,1,0:T(8,128)} %param.6), channel_id=1, source_target_pairs={{0,8},{4,12},{8,0},{12,4},{16,24},{20,28},{24,16},{28,20},{1,9},{5... | collective-permute-start | bytes 393224 | tf_op jit(solution)/shard_map/ppermute | solution.py:107
  4.4 1.2 %collective-permute-start = (f32[2,32,512]{2,1,0:T(8,128)}, f32[2,32,512]{2,1,0:T(8,128)S(1)}, u32[]{:S(2)}, u32[]{:S(2)}) collective-permute-start(f32[2,32,512]{2,1,0:T(8,128)} %param.6), channel_id=1, source_target_pairs={{0,4},{4,0},{8,12},{12,8},{16,20},{20,16},{24,28},{28,24},{1,5},{5... | collective-permute-start | bytes 393224 | tf_op jit(solution)/shard_map/ppermute | solution.py:107
  5.7 0.9 %bitcast_dynamic-update-slice_fusion.6 = f32[2,8,32,512]{3,2,0,1:T(8,128)S(1)} fusion(f32[2,32,512]{2,1,0:T(8,128)} %param.6), kind=kLoop, calls=%fused_computation.86 | loop fusion | bytes 262144
  6.6 1.3 %fusion.42 = (s32[1,1]{1,0:T(1,128)}, s32[1,1]{1,0:T(1,128)}) fusion(s32[1,2]{1,0:T(1,128)} %param.4), kind=kLoop, calls=%fused_computation.137 | loop fusion | bytes 16 | tf_op jit(solution)/shard_map/slice | solution.py:144
  8.0 0.7 %sine_select_fusion = (f32[1,64,1]{1,2,0:T(1,128)S(1)}, f32[1,64,1]{1,2,0:T(1,128)S(1)}) fusion(s32[]{:T(128)S(6)} %sub.157, s32[]{:T(128)} %bitcast), kind=kLoop, calls=%fused_computation.125 | loop fusion | flops 1280 | bytes 520 | tf_op jit(solution)/shard_map/jit(_where)/select_n | solution.py:148
  8.7 0.6 %slice_bitcast_fusion.18 = f32[32]{0:T(128)} fusion(f32[1,64,1]{1,2,0:T(1,128)S(1)} %get-tuple-element.57), kind=kLoop, calls=%fused_computation.122 | loop fusion | bytes 256 | tf_op jit(solution)/shard_map/mul | solution.py:153
  9.9 0.6 slice_bitcast_fusion.19
  10.5 0.7 %fusion.27 = (f32[4096]{0:T(1024)S(1)}, f32[4096]{0:T(1024)S(1)}) fusion(s32[]{:T(128)} %bitcast.2), kind=kLoop, calls=%fused_computation.102 | loop fusion | flops 57344 | bytes 32772 | tf_op jit(solution)/shard_map/sin | solution.py:150
  11.2 0.8 %fusion.33 = (s32[8]{0:T(128)S(1)}, s32[8]{0:T(128)S(1)}) fusion(s32[2,8]{1,0:T(2,128)} %param.7, s32[]{:T(128)S(6)} %axis_index.33), kind=kLoop, calls=%fused_computation.116 | loop fusion | flops 64 | bytes 132 | tf_op jit(solution)/shard_map/select_n | solution.py:126
  12.5 2.3 %collective-permute-start.5 = (f32[2,32,512]{2,1,0:T(8,128)S(1)}, f32[2,32,512]{2,1,0:T(8,128)S(1)}, u32[]{:S(2)}, u32[]{:S(2)}) collective-permute-start(f32[2,32,512]{2,1,0:T(8,128)S(1)} %collective-permute-done.2), channel_id=1, source_target_pairs={{0,12},{4,8},{8,4},{12,0},{16,28},{20,24},{24,20},{28,16},{1,13},{... | collective-permute-start | bytes 393224 | tf_op jit(solution)/shard_map/ppermute | solution.py:107
  14.8 1.4 %collective-permute-done.4 = f32[2,32,512]{2,1,0:T(8,128)S(1)} collective-permute-done((f32[2,32,512]{2,1,0:T(8,128)S(1)}, f32[2,32,512]{2,1,0:T(8,128)S(1)}, u32[]{:S(2)}, u32[]{:S(2)}) %collective-permute-start.4) | collective-permute-done | bytes 131104 | tf_op jit(solution)/shard_map/ppermute | solution.py:107
  16.2 0.5 slice.212
  16.7 2.3 %collective-permute-done.5 = f32[2,32,512]{2,1,0:T(8,128)S(1)} collective-permute-done((f32[2,32,512]{2,1,0:T(8,128)S(1)}, f32[2,32,512]{2,1,0:T(8,128)S(1)}, u32[]{:S(2)}, u32[]{:S(2)}) %collective-permute-start.5) | collective-permute-done | bytes 131104 | tf_op jit(solution)/shard_map/ppermute | solution.py:107
  20.0 0.6 gather_fusion
  20.6 1.9 %sine_bitcast_fusion.1 = (f32[32,8,512]{2,0,1:T(8,128)S(1)}, f32[32,8,512]{2,0,1:T(8,128)S(1)}) fusion(f32[8,32,512]{2,1,0:T(8,128)S(1)} %gather_fusion), kind=kLoop, calls=%fused_computation.58 | loop fusion | bytes 1572864 | tf_op jit(solution)/shard_map/sin | solution.py:157
  23.4 1.1 %slice_select_fusion = (f32[2,16,4096]{2,1,0:T(8,128)}, f32[2,16,4096]{2,1,0:T(8,128)}) fusion(f32[2,32,4096]{2,1,0:T(8,128)S(1)} %constant_dynamic-update-slice_fusion, pred[]{:T(512)S(6)} %eq.33), kind=kLoop, calls=%fused_computation.60 | loop fusion | flops 262144 | bytes 2097153 | tf_op jit(solution)/shard_map/jit(_where)/select_n | solution.py:22
  24.5 3.8 %collective-permute-start.6 = (f32[2,16,4096]{2,1,0:T(8,128)}, f32[2,16,4096]{2,1,0:T(8,128)}, u32[]{:S(2)}, u32[]{:S(2)}) collective-permute-start(f32[2,16,4096]{2,1,0:T(8,128)} %get-tuple-element.30), channel_id=1, source_target_pairs={{0,1},{2,3},{1,0},{3,2},{4,5},{6,7},{5,4},{7,6},{8,9},{10,11},{9,8... | collective-permute-start | bytes 1572872 | tf_op jit(solution)/shard_map/ppermute | solution.py:23
  28.3 3.0 %collective-permute-start.7 = (f32[2,16,4096]{2,1,0:T(8,128)}, f32[2,16,4096]{2,1,0:T(8,128)}, u32[]{:S(2)}, u32[]{:S(2)}) collective-permute-start(f32[2,16,4096]{2,1,0:T(8,128)} %get-tuple-element.29), channel_id=1, source_target_pairs={{1,2},{2,1},{5,6},{6,5},{9,10},{10,9},{13,14},{14,13},{17,18},{18,... | collective-permute-start | bytes 1572872 | tf_op jit(solution)/shard_map/ppermute | solution.py:22
  31.3 0.5 slice.211
  33.9 1.1 %select_reduce_fusion = (f32[160,128]{1,0:T(8,128)S(1)}, f32[160,128]{1,0:T(8,128)}) fusion(f32[33]{0:T(128)S(1)} %get-tuple-element.46, s32[160,128]{1,0:T(8,128)S(1)} %iota_subtract_fusion, f32[33]{0:T(128)S(1)} %get-tuple-element.45), kind=kLoop, calls=%fused_computation.4 | loop fusion | flops 3338240 | bytes 246024 | tf_op jit(solution)/shard_map/reduce_sum | solution.py:35
  35.0 0.6 gather_fusion.1
  35.6 1.9 %sine_bitcast_fusion = (f32[32,8,512]{2,0,1:T(8,128)S(1)}, f32[32,8,512]{2,0,1:T(8,128)S(1)}) fusion(f32[8,32,512]{2,1,0:T(8,128)S(1)} %gather_fusion.1), kind=kLoop, calls=%fused_computation.48 | loop fusion | bytes 1572864 | tf_op jit(solution)/shard_map/sin | solution.py:80
  38.4 0.7 %collective-permute-done.7 = f32[2,16,4096]{2,1,0:T(8,128)} collective-permute-done((f32[2,16,4096]{2,1,0:T(8,128)}, f32[2,16,4096]{2,1,0:T(8,128)}, u32[]{:S(2)}, u32[]{:S(2)}) %collective-permute-start.7) | collective-permute-done | bytes 524320 | tf_op jit(solution)/shard_map/ppermute | solution.py:22
  39.1 1.3 %broadcast_select_fusion = (f32[2,16,4096]{2,1,0:T(8,128)S(1)}, f32[2,16,4096]{2,1,0:T(8,128)S(1)}) fusion(f32[2,16,4096]{2,1,0:T(8,128)} %collective-permute-done.7, f32[2,16,4096]{2,1,0:T(8,128)} %collective-permute-done.6, pred[]{:T(512)S(6)} %eq.33), kind=kLoop, calls=%fused_computation.72 | loop fusion | flops 262144 | bytes 2097153 | tf_op jit(solution)/shard_map/jit(_where)/select_n | solution.py:25
  41.5 0.7 %convolution_bitcast_fusion.1 = f32[1,64,4096]{2,1,0:T(8,128)S(1)} fusion(f32[1,128,4096]{2,1,0:T(8,128)S(1)} %add_dynamic-update-slice_fusion.1, f32[32,64]{1,0:T(8,128)S(1)} %get-tuple-element.8, f32[32,64]{1,0:T(8,128)S(1)} %get-tuple-element.7, f32[32,64]{1,0:T(8,128)S(1)} %neg.4), kind=kOutput, calls=%fused_computation.3 | convolution fusion | flops 201351168 | bytes 3170304 | tf_op jit(solution)/shard_map/ij,ajy->aiy/dot_general | solution.py:75
  43.6 1.1 %fusion.18 = f32[1,32,32,256]{3,2,1,0:T(8,128)S(1)} fusion(f32[1,32,32,32]{3,2,1,0:T(8,128)S(1)} %bitcast.150, f32[1,32,32,128]{3,2,1,0:T(8,128)S(1)} %bitcast.156, f32[1,32,32,32]{3,2,1,0:T(8,128)S(1)} %bitcast.152, f32[1,32,32,128]{3,2,1,0:T(8,128)S(1)} %bitcast.154, f32[160,128]{1,0:T(8,128)S(1)} %copy-done, f32[160,128]{1,0:T(8,128)S(1)} %neg.5, ...), kind=kOutput, calls=%fused_computation.29 | convolution fusion | flops 504545280 | bytes 2605056 | tf_op jit(solution)/shard_map/...nj,jc->...nc/dot_general | solution.py:67
  45.4 3.2 %collective-permute-start.9 = (f32[2,1,16,4096]{3,2,1,0:T(8,128)S(1)}, f32[2,1,16,4096]{3,2,1,0:T(8,128)S(1)}, u32[]{:S(2)}, u32[]{:S(2)}) collective-permute-start(f32[2,1,16,4096]{3,2,1,0:T(8,128)S(1)} %get-tuple-element.20), channel_id=1, source_target_pairs={{1,2},{2,1},{5,6},{6,5},{9,10},{10,9},{13,14},{14,13},{17,18},{18,... | collective-permute-start | bytes 1572872 | tf_op jit(solution)/shard_map/ppermute | solution.py:22
  48.6 7.3 %collective-permute-done.9 = f32[2,1,16,4096]{3,2,1,0:T(8,128)S(1)} collective-permute-done((f32[2,1,16,4096]{3,2,1,0:T(8,128)S(1)}, f32[2,1,16,4096]{3,2,1,0:T(8,128)S(1)}, u32[]{:S(2)}, u32[]{:S(2)}) %collective-permute-start.9) | collective-permute-done | bytes 524320 | tf_op jit(solution)/shard_map/ppermute | solution.py:22
  56.3 0.7 %convolution_bitcast_fusion = f32[1,64,4096]{2,1,0:T(8,128)S(1)} fusion(f32[1,64,4096]{2,1,0:T(8,128)S(1)} %get-tuple-element.10, f32[1,64,4096]{2,1,0:T(8,128)S(1)} %get-tuple-element.9, f32[32,64]{1,0:T(8,128)S(1)} %get-tuple-element.8, f32[32,64]{1,0:T(8,128)S(1)} %get-tuple-element.7, f32[32,64]{1,0:T(8,128)S(1)} %neg.4), kind=kOutput, calls=%fused_computation.2 | convolution fusion | flops 201875456 | bytes 3170304 | tf_op jit(solution)/shard_map/ij,ajy->aiy/dot_general | solution.py:75
  58.2 1.1 %fusion.17 = f32[1,32,32,256]{3,2,1,0:T(8,128)S(1)} fusion(f32[1,32,32,32]{3,2,1,0:T(8,128)S(1)} %bitcast.149, f32[1,32,32,128]{3,2,1,0:T(8,128)S(1)} %bitcast.155, f32[1,32,32,32]{3,2,1,0:T(8,128)S(1)} %bitcast.151, f32[1,32,32,128]{3,2,1,0:T(8,128)S(1)} %bitcast.153, f32[160,128]{1,0:T(8,128)S(1)} %copy-done, f32[160,128]{1,0:T(8,128)S(1)} %neg.5, ...), kind=kOutput, calls=%fused_computation.28 | convolution fusion | flops 504545280 | bytes 2605056 | tf_op jit(solution)/shard_map/...nj,jc->...nc/dot_general | solution.py:67
  59.7 1.0 %pad_maximum_fusion.1 = f32[2,1,32,4096]{3,2,1,0:T(8,128)} fusion(f32[1,1,32,4096]{3,2,1,0:T(8,128)S(1)} %stack_reshape.7, f32[1,1,32,4096]{3,2,1,0:T(8,128)S(1)} %stack_reshape.6), kind=kLoop, calls=%fused_computation.34 | loop fusion | flops 262144 | bytes 2097152 | tf_op jit(solution)/shard_map/stack | solution.py:176
  (81 shorter events, 8.9 us)
Async XLA Ops:
  0.0 12.0 %collective-permute-start.2 = (f32[2,32,512]{2,1,0:T(8,128)}, f32[2,32,512]{2,1,0:T(8,128)S(1)}, u32[]{:S(2)}, u32[]{:S(2)}) collective-permute-start(f32[2,32,512]{2,1,0:T(8,128)} %param.6), channel_id=1, source_target_pairs={{0,16},{4,20},{8,24},{12,28},{16,0},{20,4},{24,8},{28,12},{1,17},{... | collective-permute-start | bytes 393224 | tf_op jit(solution)/shard_map/ppermute | solution.py:107
  3.1 8.9 %collective-permute-start.1 = (f32[2,32,512]{2,1,0:T(8,128)}, f32[2,32,512]{2,1,0:T(8,128)S(1)}, u32[]{:S(2)}, u32[]{:S(2)}) collective-permute-start(f32[2,32,512]{2,1,0:T(8,128)} %param.6), channel_id=1, source_target_pairs={{0,8},{4,12},{8,0},{12,4},{16,24},{20,28},{24,16},{28,20},{1,9},{5... | collective-permute-start | bytes 393224 | tf_op jit(solution)/shard_map/ppermute | solution.py:107
  4.4 10.3 %collective-permute-start = (f32[2,32,512]{2,1,0:T(8,128)}, f32[2,32,512]{2,1,0:T(8,128)S(1)}, u32[]{:S(2)}, u32[]{:S(2)}) collective-permute-start(f32[2,32,512]{2,1,0:T(8,128)} %param.6), channel_id=1, source_target_pairs={{0,4},{4,0},{8,12},{12,8},{16,20},{20,16},{24,28},{28,24},{1,5},{5... | collective-permute-start | bytes 393224 | tf_op jit(solution)/shard_map/ppermute | solution.py:107
  12.0 7.8 %collective-permute-start.3 = (f32[2,2,32,512]{3,2,1,0:T(8,128)S(1)}, f32[2,2,32,512]{3,2,1,0:T(8,128)S(1)}, u32[]{:S(2)}, u32[]{:S(2)}) collective-permute-start(f32[2,2,32,512]{3,2,1,0:T(8,128)S(1)} %pad_maximum_fusion.3), channel_id=1, source_target_pairs={{0,4},{4,0},{8,12},{12,8},{16,20},{20,16},{24,28},{28,24},{1,5},{5... | collective-permute-start | bytes 786440 | tf_op jit(solution)/shard_map/ppermute | solution.py:107
  12.3 3.8 %collective-permute-start.4 = (f32[2,32,512]{2,1,0:T(8,128)S(1)}, f32[2,32,512]{2,1,0:T(8,128)S(1)}, u32[]{:S(2)}, u32[]{:S(2)}) collective-permute-start(f32[2,32,512]{2,1,0:T(8,128)S(1)} %collective-permute-done.2), channel_id=1, source_target_pairs={{0,8},{4,12},{8,0},{12,4},{16,24},{20,28},{24,16},{28,20},{1,9},{5... | collective-permute-start | bytes 393224 | tf_op jit(solution)/shard_map/ppermute | solution.py:107
  12.5 6.5 %collective-permute-start.5 = (f32[2,32,512]{2,1,0:T(8,128)S(1)}, f32[2,32,512]{2,1,0:T(8,128)S(1)}, u32[]{:S(2)}, u32[]{:S(2)}) collective-permute-start(f32[2,32,512]{2,1,0:T(8,128)S(1)} %collective-permute-done.2), channel_id=1, source_target_pairs={{0,12},{4,8},{8,4},{12,0},{16,28},{20,24},{24,20},{28,16},{1,13},{... | collective-permute-start | bytes 393224 | tf_op jit(solution)/shard_map/ppermute | solution.py:107
  23.3 10.3 %copy-start.4 = (f32[2,33]{1,0:T(2,128)S(1)}, f32[2,33]{1,0:T(2,128)}, u32[]{:S(2)}) copy-start(f32[2,33]{1,0:T(2,128)} %param.5) | copy-start | bytes 796
  24.5 13.9 %collective-permute-start.6 = (f32[2,16,4096]{2,1,0:T(8,128)}, f32[2,16,4096]{2,1,0:T(8,128)}, u32[]{:S(2)}, u32[]{:S(2)}) collective-permute-start(f32[2,16,4096]{2,1,0:T(8,128)} %get-tuple-element.30), channel_id=1, source_target_pairs={{0,1},{2,3},{1,0},{3,2},{4,5},{6,7},{5,4},{7,6},{8,9},{10,11},{9,8... | collective-permute-start | bytes 1572872 | tf_op jit(solution)/shard_map/ppermute | solution.py:23
  28.3 10.8 %collective-permute-start.7 = (f32[2,16,4096]{2,1,0:T(8,128)}, f32[2,16,4096]{2,1,0:T(8,128)}, u32[]{:S(2)}, u32[]{:S(2)}) collective-permute-start(f32[2,16,4096]{2,1,0:T(8,128)} %get-tuple-element.29), channel_id=1, source_target_pairs={{1,2},{2,1},{5,6},{6,5},{9,10},{10,9},{13,14},{14,13},{17,18},{18,... | collective-permute-start | bytes 1572872 | tf_op jit(solution)/shard_map/ppermute | solution.py:22
  37.9 2.5 %copy-start.1 = (f32[16]{0:T(128)S(1)}, f32[16]{0:T(128)}, u32[]{:S(2)}) copy-start(f32[16]{0:T(128)} %get-tuple-element.48) | copy-start | bytes 196
  38.2 2.3 %copy-start.2 = (f32[32]{0:T(128)S(1)}, f32[32]{0:T(128)}, u32[]{:S(2)}) copy-start(f32[32]{0:T(128)} %slice_bitcast_fusion.18) | copy-start | bytes 388
  38.3 2.3 %copy-start.3 = (f32[32]{0:T(128)S(1)}, f32[32]{0:T(128)}, u32[]{:S(2)}) copy-start(f32[32]{0:T(128)} %slice_bitcast_fusion.19) | copy-start | bytes 388
  42.7 0.9 %copy-start = (f32[160,128]{1,0:T(8,128)S(1)}, f32[160,128]{1,0:T(8,128)}, u32[]{:S(2)}) copy-start(f32[160,128]{1,0:T(8,128)} %get-tuple-element.6) | copy-start | bytes 245764
  45.3 3.3 %collective-permute-start.8 = (f32[2,1,16,4096]{3,2,1,0:T(8,128)S(1)}, f32[2,1,16,4096]{3,2,1,0:T(8,128)S(1)}, u32[]{:S(2)}, u32[]{:S(2)}) collective-permute-start(f32[2,1,16,4096]{3,2,1,0:T(8,128)S(1)} %get-tuple-element.19), channel_id=1, source_target_pairs={{0,1},{2,3},{1,0},{3,2},{4,5},{6,7},{5,4},{7,6},{8,9},{10,11},{9,8... | collective-permute-start | bytes 1572872 | tf_op jit(solution)/shard_map/ppermute | solution.py:23
  45.4 10.5 %collective-permute-start.9 = (f32[2,1,16,4096]{3,2,1,0:T(8,128)S(1)}, f32[2,1,16,4096]{3,2,1,0:T(8,128)S(1)}, u32[]{:S(2)}, u32[]{:S(2)}) collective-permute-start(f32[2,1,16,4096]{3,2,1,0:T(8,128)S(1)} %get-tuple-element.20), channel_id=1, source_target_pairs={{1,2},{2,1},{5,6},{6,5},{9,10},{10,9},{13,14},{14,13},{17,18},{18,... | collective-permute-start | bytes 1572872 | tf_op jit(solution)/shard_map/ppermute | solution.py:22

commit v16 on v15

--- a/solution.py
+++ b/solution.py
@@ -19,8 +19,8 @@
         tail = lax.slice_in_dim(cells, cells.shape[dim] - width, cells.shape[dim], axis=dim)
         across = [(i, i + 1) for i in range(1, count - 1, 2)] + [(i + 1, i) for i in range(1, count - 1, 2)]
         within = [(i, i + 1) for i in range(0, count - 1, 2)] + [(i + 1, i) for i in range(0, count - 1, 2)]
+        got_within = lax.ppermute(jnp.where(odd, head, tail), axis, within)
         got_across = lax.ppermute(jnp.where(odd, tail, head), axis, across)
-        got_within = lax.ppermute(jnp.where(odd, head, tail), axis, within)
         before = jnp.where(odd, got_within, got_across)
         after = jnp.where(odd, got_across, got_within)
         cells = jnp.concatenate([before, cells, after], axis=dim)

time: 61 us -> 61 us (level)
  no operation moved by 1% of the time
where the time goes in v16:
time: 61 us; the launch traced here: 60.7 us
  starting transfers between devices  18.5 us (30%)
  local copies, waits for them, and re-layouts  15.8 us (26%)
  waiting for transfers between devices  12 us (20%)
  other arithmetic  8.42 us (14%)
  matrix products  3.64 us (6%)
  between operations  2.39 us (4%)
    ppermute x6, starting transfers between devices, exchange(): return lax.ppermute(x, axis, [(i, partner(i, k)) for i in range(count)])  8.39 us
    ppermute x2, waiting for transfers between devices, extended(): got_across = lax.ppermute(jnp.where(odd, tail, head), axis, across)  8.03 us
    ppermute x2, starting transfers between devices, extended(): got_across = lax.ppermute(jnp.where(odd, tail, head), axis, across)  6.19 us
    ppermute x6, waiting for transfers between devices, exchange(): return lax.ppermute(x, axis, [(i, partner(i, k)) for i in range(count)])  3.98 us
    ppermute x2, starting transfers between devices, extended(): got_within = lax.ppermute(jnp.where(odd, head, tail), axis, within)  3.92 us
    unnamed x30, local copies, waits for them, and re-layouts  3.41 us
    dot_general x2, matrix products, along_pass(): out = jnp.einsum('...nj,jc->...nc', win, kern, precision=lax.Precision.HIGH)  2.27 us
    sin x3, local copies, waits for them, and re-layouts, transmit(): return rotate(real, imag, jnp.cos(screen), jnp.sin(screen))  2.27 us
  transfers between devices with their start and end apart: 10, of which 5 were waited for; matrix products, arithmetic and copies ran while one was open for 21% of the time, Pallas kernels for 0%

profile of v16, /device:TPU:1, one launch (start us, length us, event | category | flops | bytes accessed | tf_op | source)
XLA Modules:
  0.0 60.7 jit_solution(8329320105920017863)
XLA Ops:
  0.0 3.1 %collective-permute-start.2 = (f32[2,32,512]{2,1,0:T(8,128)}, f32[2,32,512]{2,1,0:T(8,128)S(1)}, u32[]{:S(2)}, u32[]{:S(2)}) collective-permute-start(f32[2,32,512]{2,1,0:T(8,128)} %param.6), channel_id=1, source_target_pairs={{0,16},{4,20},{8,24},{12,28},{16,0},{20,4},{24,8},{28,12},{1,17},{... | collective-permute-start | bytes 393224 | tf_op jit(solution)/shard_map/ppermute | solution.py:107
  3.1 1.3 %collective-permute-start.1 = (f32[2,32,512]{2,1,0:T(8,128)}, f32[2,32,512]{2,1,0:T(8,128)S(1)}, u32[]{:S(2)}, u32[]{:S(2)}) collective-permute-start(f32[2,32,512]{2,1,0:T(8,128)} %param.6), channel_id=1, source_target_pairs={{0,8},{4,12},{8,0},{12,4},{16,24},{20,28},{24,16},{28,20},{1,9},{5... | collective-permute-start | bytes 393224 | tf_op jit(solution)/shard_map/ppermute | solution.py:107
  4.4 1.2 %collective-permute-start = (f32[2,32,512]{2,1,0:T(8,128)}, f32[2,32,512]{2,1,0:T(8,128)S(1)}, u32[]{:S(2)}, u32[]{:S(2)}) collective-permute-start(f32[2,32,512]{2,1,0:T(8,128)} %param.6), channel_id=1, source_target_pairs={{0,4},{4,0},{8,12},{12,8},{16,20},{20,16},{24,28},{28,24},{1,5},{5... | collective-permute-start | bytes 393224 | tf_op jit(solution)/shard_map/ppermute | solution.py:107
  5.7 0.9 %bitcast_dynamic-update-slice_fusion.6 = f32[2,8,32,512]{3,2,0,1:T(8,128)S(1)} fusion(f32[2,32,512]{2,1,0:T(8,128)} %param.6), kind=kLoop, calls=%fused_computation.86 | loop fusion | bytes 262144
  6.6 1.3 %fusion.42 = (s32[1,1]{1,0:T(1,128)}, s32[1,1]{1,0:T(1,128)}) fusion(s32[1,2]{1,0:T(1,128)} %param.4), kind=kLoop, calls=%fused_computation.137 | loop fusion | bytes 16 | tf_op jit(solution)/shard_map/slice | solution.py:144
  8.0 0.7 %sine_select_fusion = (f32[1,64,1]{1,2,0:T(1,128)S(1)}, f32[1,64,1]{1,2,0:T(1,128)S(1)}) fusion(s32[]{:T(128)S(6)} %sub.157, s32[]{:T(128)} %bitcast), kind=kLoop, calls=%fused_computation.125 | loop fusion | flops 1280 | bytes 520 | tf_op jit(solution)/shard_map/jit(_where)/select_n | solution.py:148
  8.7 0.6 %slice_bitcast_fusion.18 = f32[32]{0:T(128)} fusion(f32[1,64,1]{1,2,0:T(1,128)S(1)} %get-tuple-element.57), kind=kLoop, calls=%fused_computation.122 | loop fusion | bytes 256 | tf_op jit(solution)/shard_map/mul | solution.py:153
  9.9 0.6 slice_bitcast_fusion.19
  10.5 0.7 %fusion.27 = (f32[4096]{0:T(1024)S(1)}, f32[4096]{0:T(1024)S(1)}) fusion(s32[]{:T(128)} %bitcast.2), kind=kLoop, calls=%fused_computation.102 | loop fusion | flops 57344 | bytes 32772 | tf_op jit(solution)/shard_map/sin | solution.py:150
  11.2 0.8 %fusion.33 = (s32[8]{0:T(128)S(1)}, s32[8]{0:T(128)S(1)}) fusion(s32[2,8]{1,0:T(2,128)} %param.7, s32[]{:T(128)S(6)} %axis_index.33), kind=kLoop, calls=%fused_computation.116 | loop fusion | flops 64 | bytes 132 | tf_op jit(solution)/shard_map/select_n | solution.py:126
  12.5 2.3 %collective-permute-start.5 = (f32[2,32,512]{2,1,0:T(8,128)S(1)}, f32[2,32,512]{2,1,0:T(8,128)S(1)}, u32[]{:S(2)}, u32[]{:S(2)}) collective-permute-start(f32[2,32,512]{2,1,0:T(8,128)S(1)} %collective-permute-done.2), channel_id=1, source_target_pairs={{0,12},{4,8},{8,4},{12,0},{16,28},{20,24},{24,20},{28,16},{1,13},{... | collective-permute-start | bytes 393224 | tf_op jit(solution)/shard_map/ppermute | solution.py:107
  14.8 1.4 %collective-permute-done.4 = f32[2,32,512]{2,1,0:T(8,128)S(1)} collective-permute-done((f32[2,32,512]{2,1,0:T(8,128)S(1)}, f32[2,32,512]{2,1,0:T(8,128)S(1)}, u32[]{:S(2)}, u32[]{:S(2)}) %collective-permute-start.4) | collective-permute-done | bytes 131104 | tf_op jit(solution)/shard_map/ppermute | solution.py:107
  16.2 0.5 slice.212
  16.7 2.3 %collective-permute-done.5 = f32[2,32,512]{2,1,0:T(8,128)S(1)} collective-permute-done((f32[2,32,512]{2,1,0:T(8,128)S(1)}, f32[2,32,512]{2,1,0:T(8,128)S(1)}, u32[]{:S(2)}, u32[]{:S(2)}) %collective-permute-start.5) | collective-permute-done | bytes 131104 | tf_op jit(solution)/shard_map/ppermute | solution.py:107
  20.0 0.6 gather_fusion
  20.6 1.9 %sine_bitcast_fusion.1 = (f32[32,8,512]{2,0,1:T(8,128)S(1)}, f32[32,8,512]{2,0,1:T(8,128)S(1)}) fusion(f32[8,32,512]{2,1,0:T(8,128)S(1)} %gather_fusion), kind=kLoop, calls=%fused_computation.58 | loop fusion | bytes 1572864 | tf_op jit(solution)/shard_map/sin | solution.py:157
  23.4 1.1 %slice_select_fusion = (f32[2,16,4096]{2,1,0:T(8,128)}, f32[2,16,4096]{2,1,0:T(8,128)}) fusion(f32[2,32,4096]{2,1,0:T(8,128)S(1)} %constant_dynamic-update-slice_fusion, pred[]{:T(512)S(6)} %eq.33), kind=kLoop, calls=%fused_computation.60 | loop fusion | flops 262144 | bytes 2097153 | tf_op jit(solution)/shard_map/jit(_where)/select_n | solution.py:23
  24.5 3.8 %collective-permute-start.6 = (f32[2,16,4096]{2,1,0:T(8,128)}, f32[2,16,4096]{2,1,0:T(8,128)}, u32[]{:S(2)}, u32[]{:S(2)}) collective-permute-start(f32[2,16,4096]{2,1,0:T(8,128)} %get-tuple-element.30), channel_id=1, source_target_pairs={{0,1},{2,3},{1,0},{3,2},{4,5},{6,7},{5,4},{7,6},{8,9},{10,11},{9,8... | collective-permute-start | bytes 1572872 | tf_op jit(solution)/shard_map/ppermute | solution.py:22
  28.3 3.0 %collective-permute-start.7 = (f32[2,16,4096]{2,1,0:T(8,128)}, f32[2,16,4096]{2,1,0:T(8,128)}, u32[]{:S(2)}, u32[]{:S(2)}) collective-permute-start(f32[2,16,4096]{2,1,0:T(8,128)} %get-tuple-element.29), channel_id=1, source_target_pairs={{1,2},{2,1},{5,6},{6,5},{9,10},{10,9},{13,14},{14,13},{17,18},{18,... | collective-permute-start | bytes 1572872 | tf_op jit(solution)/shard_map/ppermute | solution.py:23
  31.3 0.5 slice.211
  33.9 1.1 %select_reduce_fusion = (f32[160,128]{1,0:T(8,128)S(1)}, f32[160,128]{1,0:T(8,128)}) fusion(f32[33]{0:T(128)S(1)} %get-tuple-element.46, s32[160,128]{1,0:T(8,128)S(1)} %iota_subtract_fusion, f32[33]{0:T(128)S(1)} %get-tuple-element.45), kind=kLoop, calls=%fused_computation.4 | loop fusion | flops 3338240 | bytes 246024 | tf_op jit(solution)/shard_map/reduce_sum | solution.py:35
  35.0 0.6 gather_fusion.1
  35.6 1.9 %sine_bitcast_fusion = (f32[32,8,512]{2,0,1:T(8,128)S(1)}, f32[32,8,512]{2,0,1:T(8,128)S(1)}) fusion(f32[8,32,512]{2,1,0:T(8,128)S(1)} %gather_fusion.1), kind=kLoop, calls=%fused_computation.48 | loop fusion | bytes 1572864 | tf_op jit(solution)/shard_map/sin | solution.py:80
  38.4 0.7 %collective-permute-done.7 = f32[2,16,4096]{2,1,0:T(8,128)} collective-permute-done((f32[2,16,4096]{2,1,0:T(8,128)}, f32[2,16,4096]{2,1,0:T(8,128)}, u32[]{:S(2)}, u32[]{:S(2)}) %collective-permute-start.7) | collective-permute-done | bytes 524320 | tf_op jit(solution)/shard_map/ppermute | solution.py:23
  39.1 1.3 %broadcast_select_fusion = (f32[2,16,4096]{2,1,0:T(8,128)S(1)}, f32[2,16,4096]{2,1,0:T(8,128)S(1)}) fusion(f32[2,16,4096]{2,1,0:T(8,128)} %collective-permute-done.7, f32[2,16,4096]{2,1,0:T(8,128)} %collective-permute-done.6, pred[]{:T(512)S(6)} %eq.33), kind=kLoop, calls=%fused_computation.72 | loop fusion | flops 262144 | bytes 2097153 | tf_op jit(solution)/shard_map/jit(_where)/select_n | solution.py:25
  41.5 0.7 %convolution_bitcast_fusion.1 = f32[1,64,4096]{2,1,0:T(8,128)S(1)} fusion(f32[1,128,4096]{2,1,0:T(8,128)S(1)} %add_dynamic-update-slice_fusion.1, f32[32,64]{1,0:T(8,128)S(1)} %get-tuple-element.8, f32[32,64]{1,0:T(8,128)S(1)} %get-tuple-element.7, f32[32,64]{1,0:T(8,128)S(1)} %neg.4), kind=kOutput, calls=%fused_computation.3 | convolution fusion | flops 201351168 | bytes 3170304 | tf_op jit(solution)/shard_map/ij,ajy->aiy/dot_general | solution.py:75
  43.6 1.1 %fusion.18 = f32[1,32,32,256]{3,2,1,0:T(8,128)S(1)} fusion(f32[1,32,32,32]{3,2,1,0:T(8,128)S(1)} %bitcast.150, f32[1,32,32,128]{3,2,1,0:T(8,128)S(1)} %bitcast.156, f32[1,32,32,32]{3,2,1,0:T(8,128)S(1)} %bitcast.152, f32[1,32,32,128]{3,2,1,0:T(8,128)S(1)} %bitcast.154, f32[160,128]{1,0:T(8,128)S(1)} %copy-done, f32[160,128]{1,0:T(8,128)S(1)} %neg.5, ...), kind=kOutput, calls=%fused_computation.29 | convolution fusion | flops 504545280 | bytes 2605056 | tf_op jit(solution)/shard_map/...nj,jc->...nc/dot_general | solution.py:67
  45.4 3.2 %collective-permute-start.9 = (f32[2,1,16,4096]{3,2,1,0:T(8,128)S(1)}, f32[2,1,16,4096]{3,2,1,0:T(8,128)S(1)}, u32[]{:S(2)}, u32[]{:S(2)}) collective-permute-start(f32[2,1,16,4096]{3,2,1,0:T(8,128)S(1)} %get-tuple-element.20), channel_id=1, source_target_pairs={{1,2},{2,1},{5,6},{6,5},{9,10},{10,9},{13,14},{14,13},{17,18},{18,... | collective-permute-start | bytes 1572872 | tf_op jit(solution)/shard_map/ppermute | solution.py:23
  48.6 7.3 %collective-permute-done.9 = f32[2,1,16,4096]{3,2,1,0:T(8,128)S(1)} collective-permute-done((f32[2,1,16,4096]{3,2,1,0:T(8,128)S(1)}, f32[2,1,16,4096]{3,2,1,0:T(8,128)S(1)}, u32[]{:S(2)}, u32[]{:S(2)}) %collective-permute-start.9) | collective-permute-done | bytes 524320 | tf_op jit(solution)/shard_map/ppermute | solution.py:23
  56.3 0.7 %convolution_bitcast_fusion = f32[1,64,4096]{2,1,0:T(8,128)S(1)} fusion(f32[1,64,4096]{2,1,0:T(8,128)S(1)} %get-tuple-element.10, f32[1,64,4096]{2,1,0:T(8,128)S(1)} %get-tuple-element.9, f32[32,64]{1,0:T(8,128)S(1)} %get-tuple-element.8, f32[32,64]{1,0:T(8,128)S(1)} %get-tuple-element.7, f32[32,64]{1,0:T(8,128)S(1)} %neg.4), kind=kOutput, calls=%fused_computation.2 | convolution fusion | flops 201875456 | bytes 3170304 | tf_op jit(solution)/shard_map/ij,ajy->aiy/dot_general | solution.py:75
  58.2 1.1 %fusion.17 = f32[1,32,32,256]{3,2,1,0:T(8,128)S(1)} fusion(f32[1,32,32,32]{3,2,1,0:T(8,128)S(1)} %bitcast.149, f32[1,32,32,128]{3,2,1,0:T(8,128)S(1)} %bitcast.155, f32[1,32,32,32]{3,2,1,0:T(8,128)S(1)} %bitcast.151, f32[1,32,32,128]{3,2,1,0:T(8,128)S(1)} %bitcast.153, f32[160,128]{1,0:T(8,128)S(1)} %copy-done, f32[160,128]{1,0:T(8,128)S(1)} %neg.5, ...), kind=kOutput, calls=%fused_computation.28 | convolution fusion | flops 504545280 | bytes 2605056 | tf_op jit(solution)/shard_map/...nj,jc->...nc/dot_general | solution.py:67
  59.7 1.0 %pad_maximum_fusion.1 = f32[2,1,32,4096]{3,2,1,0:T(8,128)} fusion(f32[1,1,32,4096]{3,2,1,0:T(8,128)S(1)} %stack_reshape.7, f32[1,1,32,4096]{3,2,1,0:T(8,128)S(1)} %stack_reshape.6), kind=kLoop, calls=%fused_computation.34 | loop fusion | flops 262144 | bytes 2097152 | tf_op jit(solution)/shard_map/stack | solution.py:176
  (81 shorter events, 8.9 us)
Async XLA Ops:
  0.0 12.0 %collective-permute-start.2 = (f32[2,32,512]{2,1,0:T(8,128)}, f32[2,32,512]{2,1,0:T(8,128)S(1)}, u32[]{:S(2)}, u32[]{:S(2)}) collective-permute-start(f32[2,32,512]{2,1,0:T(8,128)} %param.6), channel_id=1, source_target_pairs={{0,16},{4,20},{8,24},{12,28},{16,0},{20,4},{24,8},{28,12},{1,17},{... | collective-permute-start | bytes 393224 | tf_op jit(solution)/shard_map/ppermute | solution.py:107
  3.1 8.9 %collective-permute-start.1 = (f32[2,32,512]{2,1,0:T(8,128)}, f32[2,32,512]{2,1,0:T(8,128)S(1)}, u32[]{:S(2)}, u32[]{:S(2)}) collective-permute-start(f32[2,32,512]{2,1,0:T(8,128)} %param.6), channel_id=1, source_target_pairs={{0,8},{4,12},{8,0},{12,4},{16,24},{20,28},{24,16},{28,20},{1,9},{5... | collective-permute-start | bytes 393224 | tf_op jit(solution)/shard_map/ppermute | solution.py:107
  4.4 10.3 %collective-permute-start = (f32[2,32,512]{2,1,0:T(8,128)}, f32[2,32,512]{2,1,0:T(8,128)S(1)}, u32[]{:S(2)}, u32[]{:S(2)}) collective-permute-start(f32[2,32,512]{2,1,0:T(8,128)} %param.6), channel_id=1, source_target_pairs={{0,4},{4,0},{8,12},{12,8},{16,20},{20,16},{24,28},{28,24},{1,5},{5... | collective-permute-start | bytes 393224 | tf_op jit(solution)/shard_map/ppermute | solution.py:107
  12.0 7.8 %collective-permute-start.3 = (f32[2,2,32,512]{3,2,1,0:T(8,128)S(1)}, f32[2,2,32,512]{3,2,1,0:T(8,128)S(1)}, u32[]{:S(2)}, u32[]{:S(2)}) collective-permute-start(f32[2,2,32,512]{3,2,1,0:T(8,128)S(1)} %pad_maximum_fusion.3), channel_id=1, source_target_pairs={{0,4},{4,0},{8,12},{12,8},{16,20},{20,16},{24,28},{28,24},{1,5},{5... | collective-permute-start | bytes 786440 | tf_op jit(solution)/shard_map/ppermute | solution.py:107
  12.3 3.8 %collective-permute-start.4 = (f32[2,32,512]{2,1,0:T(8,128)S(1)}, f32[2,32,512]{2,1,0:T(8,128)S(1)}, u32[]{:S(2)}, u32[]{:S(2)}) collective-permute-start(f32[2,32,512]{2,1,0:T(8,128)S(1)} %collective-permute-done.2), channel_id=1, source_target_pairs={{0,8},{4,12},{8,0},{12,4},{16,24},{20,28},{24,16},{28,20},{1,9},{5... | collective-permute-start | bytes 393224 | tf_op jit(solution)/shard_map/ppermute | solution.py:107
  12.5 6.5 %collective-permute-start.5 = (f32[2,32,512]{2,1,0:T(8,128)S(1)}, f32[2,32,512]{2,1,0:T(8,128)S(1)}, u32[]{:S(2)}, u32[]{:S(2)}) collective-permute-start(f32[2,32,512]{2,1,0:T(8,128)S(1)} %collective-permute-done.2), channel_id=1, source_target_pairs={{0,12},{4,8},{8,4},{12,0},{16,28},{20,24},{24,20},{28,16},{1,13},{... | collective-permute-start | bytes 393224 | tf_op jit(solution)/shard_map/ppermute | solution.py:107
  23.3 10.3 %copy-start.4 = (f32[2,33]{1,0:T(2,128)S(1)}, f32[2,33]{1,0:T(2,128)}, u32[]{:S(2)}) copy-start(f32[2,33]{1,0:T(2,128)} %param.5) | copy-start | bytes 796
  24.5 13.9 %collective-permute-start.6 = (f32[2,16,4096]{2,1,0:T(8,128)}, f32[2,16,4096]{2,1,0:T(8,128)}, u32[]{:S(2)}, u32[]{:S(2)}) collective-permute-start(f32[2,16,4096]{2,1,0:T(8,128)} %get-tuple-element.30), channel_id=1, source_target_pairs={{0,1},{2,3},{1,0},{3,2},{4,5},{6,7},{5,4},{7,6},{8,9},{10,11},{9,8... | collective-permute-start | bytes 1572872 | tf_op jit(solution)/shard_map/ppermute | solution.py:22
  28.3 10.8 %collective-permute-start.7 = (f32[2,16,4096]{2,1,0:T(8,128)}, f32[2,16,4096]{2,1,0:T(8,128)}, u32[]{:S(2)}, u32[]{:S(2)}) collective-permute-start(f32[2,16,4096]{2,1,0:T(8,128)} %get-tuple-element.29), channel_id=1, source_target_pairs={{1,2},{2,1},{5,6},{6,5},{9,10},{10,9},{13,14},{14,13},{17,18},{18,... | collective-permute-start | bytes 1572872 | tf_op jit(solution)/shard_map/ppermute | solution.py:23
  37.9 2.5 %copy-start.1 = (f32[16]{0:T(128)S(1)}, f32[16]{0:T(128)}, u32[]{:S(2)}) copy-start(f32[16]{0:T(128)} %get-tuple-element.48) | copy-start | bytes 196
  38.2 2.3 %copy-start.2 = (f32[32]{0:T(128)S(1)}, f32[32]{0:T(128)}, u32[]{:S(2)}) copy-start(f32[32]{0:T(128)} %slice_bitcast_fusion.18) | copy-start | bytes 388
  38.3 2.3 %copy-start.3 = (f32[32]{0:T(128)S(1)}, f32[32]{0:T(128)}, u32[]{:S(2)}) copy-start(f32[32]{0:T(128)} %slice_bitcast_fusion.19) | copy-start | bytes 388
  42.7 0.9 %copy-start = (f32[160,128]{1,0:T(8,128)S(1)}, f32[160,128]{1,0:T(8,128)}, u32[]{:S(2)}) copy-start(f32[160,128]{1,0:T(8,128)} %get-tuple-element.6) | copy-start | bytes 245764
  45.3 3.3 %collective-permute-start.8 = (f32[2,1,16,4096]{3,2,1,0:T(8,128)S(1)}, f32[2,1,16,4096]{3,2,1,0:T(8,128)S(1)}, u32[]{:S(2)}, u32[]{:S(2)}) collective-permute-start(f32[2,1,16,4096]{3,2,1,0:T(8,128)S(1)} %get-tuple-element.19), channel_id=1, source_target_pairs={{0,1},{2,3},{1,0},{3,2},{4,5},{6,7},{5,4},{7,6},{8,9},{10,11},{9,8... | collective-permute-start | bytes 1572872 | tf_op jit(solution)/shard_map/ppermute | solution.py:22
  45.4 10.5 %collective-permute-start.9 = (f32[2,1,16,4096]{3,2,1,0:T(8,128)S(1)}, f32[2,1,16,4096]{3,2,1,0:T(8,128)S(1)}, u32[]{:S(2)}, u32[]{:S(2)}) collective-permute-start(f32[2,1,16,4096]{3,2,1,0:T(8,128)S(1)} %get-tuple-element.20), channel_id=1, source_target_pairs={{1,2},{2,1},{5,6},{6,5},{9,10},{10,9},{13,14},{14,13},{17,18},{18,... | collective-permute-start | bytes 1572872 | tf_op jit(solution)/shard_map/ppermute | solution.py:23

commit v17 on v16

--- a/solution.py
+++ b/solution.py
@@ -154,14 +154,13 @@
         imag = across_sin[:, rows] * along_cos + across_cos[:, rows] * along_sin
         return real, imag
 
-    cosine, sine = jnp.cos(screens[0]), jnp.sin(screens[0])
-    halo = extended(jnp.stack([cosine, sine]), (("tile", 1),), HALF)
+    halo = extended(screens[0], (("tile", 0),), HALF)
     pieces = [
-        rotate(*incident(rows), *parts)
-        for rows, parts in (
-            (slice(0, HALF), (halo[0, :HALF], halo[1, :HALF])),
-            (slice(HALF, HALF + local_rows), (cosine, sine)),
-            (slice(HALF + local_rows, span), (halo[0, HALF + local_rows :], halo[1, HALF + local_rows :])),
+        transmit(*incident(rows), screen)
+        for rows, screen in (
+            (slice(0, HALF), halo[:HALF]),
+            (slice(HALF, HALF + local_rows), screens[0]),
+            (slice(HALF + local_rows, span), halo[HALF + local_rows :]),
         )
     ]
     real = jnp.concatenate([piece[0] for piece in pieces], axis=1)

time: 61 us -> 60.5 us (level)
    unnamed x5 -> x6, other arithmetic: 0.9 us -> 3.49 us
    select_n x2 -> x0, other arithmetic: 2.36 us -> none  [the longest x1 1.28 us: extended(): after = jnp.where(odd, got_across, got_within)]
    sin x3 -> x0, local copies, waits for them, and re-layouts: 2.27 us -> none  [body(): cosine, sine = (jnp.cos(screens[0]), jnp.sin(screens[0]))]
    cos x2 -> x5, local copies, waits for them, and re-layouts: 0.41 us -> 2.67 us  [transmit(): return rotate(real, imag, jnp.cos(screen), jnp.sin(screen))]
    mul x4, local copies, waits for them, and re-layouts: 1.81 us -> 0.29 us  [incident(): real = across_cos[:, rows] * along_cos - across_sin[:, rows] * along_sin]
    select_n x0 -> x2, local copies, waits for them, and re-layouts: none -> 1.44 us  [the longest x1 0.72 us: extended(): got_within = lax.ppermute(jnp.where(odd, head, tail), axis, within)]
    concatenate x1, other arithmetic: 0.15 us -> 1 us  [cross_pass(): field = jnp.concatenate([real, imag], axis=1)]
    sin x3 -> x5, local copies, waits for them, and re-layouts: 2.27 us -> 2.67 us  [transmit(): return rotate(real, imag, jnp.cos(screen), jnp.sin(screen))]
  transfers between devices with their start and end apart: 10 -> 10, of which waited for: 5 -> 4; matrix products, arithmetic and copies ran while one was open for 21% -> 20% of each run, Pallas kernels for 0% -> 0%
where the time goes in v17:
time: 60.5 us; the launch traced here: 60.3 us
  starting transfers between devices  18 us (30%)
  local copies, waits for them, and re-layouts  15.5 us (26%)
  waiting for transfers between devices  11.7 us (19%)
  other arithmetic  9.02 us (15%)
  matrix products  3.64 us (6%)
  between operations  2.41 us (4%)
    ppermute x6, starting transfers between devices, exchange(): return lax.ppermute(x, axis, [(i, partner(i, k)) for i in range(count)])  8.39 us
    ppermute x2, waiting for transfers between devices, extended(): got_across = lax.ppermute(jnp.where(odd, tail, head), axis, across)  7.75 us
    ppermute x2, starting transfers between devices, extended(): got_across = lax.ppermute(jnp.where(odd, tail, head), axis, across)  5.73 us
    ppermute x6, waiting for transfers between devices, exchange(): return lax.ppermute(x, axis, [(i, partner(i, k)) for i in range(count)])  3.95 us
    ppermute x2, starting transfers between devices, extended(): got_within = lax.ppermute(jnp.where(odd, head, tail), axis, within)  3.92 us
    unnamed x6, other arithmetic  3.49 us
    unnamed x21, local copies, waits for them, and re-layouts  3.12 us
    sin x5, local copies, waits for them, and re-layouts, transmit(): return rotate(real, imag, jnp.cos(screen), jnp.sin(screen))  2.67 us
  transfers between devices with their start and end apart: 10, of which 4 were waited for; matrix products, arithmetic and copies ran while one was open for 20% of the time, Pallas kernels for 0%

profile of v17, /device:TPU:1, one launch (start us, length us, event | category | flops | bytes accessed | tf_op | source)
XLA Modules:
  0.0 60.3 jit_solution(8922175054815375649)
XLA Ops:
  0.0 3.1 %collective-permute-start.2 = (f32[2,32,512]{2,1,0:T(8,128)}, f32[2,32,512]{2,1,0:T(8,128)S(1)}, u32[]{:S(2)}, u32[]{:S(2)}) collective-permute-start(f32[2,32,512]{2,1,0:T(8,128)} %param.6), channel_id=1, source_target_pairs={{0,16},{4,20},{8,24},{12,28},{16,0},{20,4},{24,8},{28,12},{1,17},{... | collective-permute-start | bytes 393224 | tf_op jit(solution)/shard_map/ppermute | solution.py:107
  3.1 1.3 %collective-permute-start.1 = (f32[2,32,512]{2,1,0:T(8,128)}, f32[2,32,512]{2,1,0:T(8,128)S(1)}, u32[]{:S(2)}, u32[]{:S(2)}) collective-permute-start(f32[2,32,512]{2,1,0:T(8,128)} %param.6), channel_id=1, source_target_pairs={{0,8},{4,12},{8,0},{12,4},{16,24},{20,28},{24,16},{28,20},{1,9},{5... | collective-permute-start | bytes 393224 | tf_op jit(solution)/shard_map/ppermute | solution.py:107
  4.4 1.2 %collective-permute-start = (f32[2,32,512]{2,1,0:T(8,128)}, f32[2,32,512]{2,1,0:T(8,128)S(1)}, u32[]{:S(2)}, u32[]{:S(2)}) collective-permute-start(f32[2,32,512]{2,1,0:T(8,128)} %param.6), channel_id=1, source_target_pairs={{0,4},{4,0},{8,12},{12,8},{16,20},{20,16},{24,28},{28,24},{1,5},{5... | collective-permute-start | bytes 393224 | tf_op jit(solution)/shard_map/ppermute | solution.py:107
  5.7 0.9 %bitcast_dynamic-update-slice_fusion.10 = f32[2,8,32,512]{3,2,0,1:T(8,128)S(1)} fusion(f32[2,32,512]{2,1,0:T(8,128)} %param.6), kind=kLoop, calls=%fused_computation.82 | loop fusion | bytes 262144
  6.6 1.4 %fusion.46 = (s32[1,1]{1,0:T(1,128)}, s32[1,1]{1,0:T(1,128)}) fusion(s32[1,2]{1,0:T(1,128)} %param.4), kind=kLoop, calls=%fused_computation.139 | loop fusion | bytes 16 | tf_op jit(solution)/shard_map/slice | solution.py:144
  8.0 0.7 %sine_select_fusion = (f32[1,64,1]{1,2,0:T(1,128)S(1)}, f32[1,64,1]{1,2,0:T(1,128)S(1)}) fusion(s32[]{:T(128)S(6)} %sub.149, s32[]{:T(128)} %bitcast), kind=kLoop, calls=%fused_computation.125 | loop fusion | flops 1280 | bytes 520 | tf_op jit(solution)/shard_map/jit(_where)/select_n | solution.py:148
  9.0 0.8 %fusion.31 = (f32[4096]{0:T(1024)S(1)}, f32[4096]{0:T(1024)S(1)}) fusion(s32[]{:T(128)} %bitcast.2), kind=kLoop, calls=%fused_computation.102 | loop fusion | flops 57344 | bytes 32772 | tf_op jit(solution)/shard_map/sin | solution.py:150
  9.8 0.8 %fusion.37 = (s32[8]{0:T(128)S(1)}, s32[8]{0:T(128)S(1)}) fusion(s32[2,8]{1,0:T(2,128)} %param.7, s32[]{:T(128)S(6)} %axis_index.33), kind=kLoop, calls=%fused_computation.116 | loop fusion | flops 64 | bytes 132 | tf_op jit(solution)/shard_map/select_n | solution.py:126
  10.9 1.1 %collective-permute-start.4 = (f32[2,32,512]{2,1,0:T(8,128)S(1)}, f32[2,32,512]{2,1,0:T(8,128)S(1)}, u32[]{:S(2)}, u32[]{:S(2)}) collective-permute-start(f32[2,32,512]{2,1,0:T(8,128)S(1)} %collective-permute-done.2), channel_id=1, source_target_pairs={{0,8},{4,12},{8,0},{12,4},{16,24},{20,28},{24,16},{28,20},{1,9},{5... | collective-permute-start | bytes 393224 | tf_op jit(solution)/shard_map/ppermute | solution.py:107
  12.0 1.4 %collective-permute-start.5 = (f32[2,32,512]{2,1,0:T(8,128)S(1)}, f32[2,32,512]{2,1,0:T(8,128)S(1)}, u32[]{:S(2)}, u32[]{:S(2)}) collective-permute-start(f32[2,32,512]{2,1,0:T(8,128)S(1)} %collective-permute-done.2), channel_id=1, source_target_pairs={{0,12},{4,8},{8,4},{12,0},{16,28},{20,24},{24,20},{28,16},{1,13},{... | collective-permute-start | bytes 393224 | tf_op jit(solution)/shard_map/ppermute | solution.py:107
  13.4 1.4 %collective-permute-done.4 = f32[2,32,512]{2,1,0:T(8,128)S(1)} collective-permute-done((f32[2,32,512]{2,1,0:T(8,128)S(1)}, f32[2,32,512]{2,1,0:T(8,128)S(1)}, u32[]{:S(2)}, u32[]{:S(2)}) %collective-permute-start.4) | collective-permute-done | bytes 131104 | tf_op jit(solution)/shard_map/ppermute | solution.py:107
  15.3 2.3 %collective-permute-done.5 = f32[2,32,512]{2,1,0:T(8,128)S(1)} collective-permute-done((f32[2,32,512]{2,1,0:T(8,128)S(1)}, f32[2,32,512]{2,1,0:T(8,128)S(1)}, u32[]{:S(2)}, u32[]{:S(2)}) %collective-permute-start.5) | collective-permute-done | bytes 131104 | tf_op jit(solution)/shard_map/ppermute | solution.py:107
  18.6 0.6 gather_fusion
  19.2 1.9 %bitcast_cosine_fusion = (f32[32,8,512]{2,0,1:T(8,128)S(1)}, f32[32,8,512]{2,0,1:T(8,128)S(1)}) fusion(f32[8,32,512]{2,1,0:T(8,128)S(1)} %gather_fusion), kind=kLoop, calls=%fused_computation.134 | loop fusion | bytes 1572864 | tf_op jit(solution)/shard_map/cos | solution.py:80
  21.1 0.7 %copy.17 = f32[8,2,8,512]{3,2,0,1:T(8,128)} copy(f32[8,2,8,512]{3,2,1,0:T(8,128)S(1)} %get-tuple-element.40) | data formatting | bytes 524288 | tf_op jit(solution)/shard_map/jit(_where)/select_n | solution.py:22
  21.8 3.8 %collective-permute-start.6 = (f32[16,4096]{1,0:T(8,128)}, f32[16,4096]{1,0:T(8,128)S(1)}, u32[]{:S(2)}, u32[]{:S(2)}) collective-permute-start(f32[16,4096]{1,0:T(8,128)} %bitcast.51), channel_id=1, source_target_pairs={{0,1},{2,3},{1,0},{3,2},{4,5},{6,7},{5,4},{7,6},{8,9},{10,11},{9,8... | collective-permute-start | bytes 786440 | tf_op jit(solution)/shard_map/ppermute | solution.py:22
  25.7 0.7 %copy.18 = f32[8,2,8,512]{3,2,0,1:T(8,128)} copy(f32[8,2,8,512]{3,2,1,0:T(8,128)S(1)} %get-tuple-element.39) | data formatting | bytes 524288 | tf_op jit(solution)/shard_map/jit(_where)/select_n | solution.py:23
  26.4 3.0 %collective-permute-start.7 = (f32[16,4096]{1,0:T(8,128)}, f32[16,4096]{1,0:T(8,128)S(1)}, u32[]{:S(2)}, u32[]{:S(2)}) collective-permute-start(f32[16,4096]{1,0:T(8,128)} %bitcast.53), channel_id=1, source_target_pairs={{1,2},{2,1},{5,6},{6,5},{9,10},{10,9},{13,14},{14,13},{17,18},{18,... | collective-permute-start | bytes 786440 | tf_op jit(solution)/shard_map/ppermute | solution.py:23
  32.9 0.6 select_reduce_fusion
  33.5 0.6 gather_fusion.1
  34.1 1.9 %sine_bitcast_fusion = (f32[32,8,512]{2,0,1:T(8,128)S(1)}, f32[32,8,512]{2,0,1:T(8,128)S(1)}) fusion(f32[8,32,512]{2,1,0:T(8,128)S(1)} %gather_fusion.1), kind=kLoop, calls=%fused_computation.48 | loop fusion | bytes 1572864 | tf_op jit(solution)/shard_map/sin | solution.py:80
  36.8 1.0 %bitcast_dynamic-update-slice_fusion.3 = f32[1,128,4096]{2,1,0:T(8,128)S(1)} fusion(f32[4096]{0:T(1024)S(1)} %get-tuple-element.51, f32[16]{0:T(128)S(1)} %get-tuple-element.48, f32[4096]{0:T(1024)S(1)} %get-tuple-element.52, f32[16]{0:T(128)S(1)} %get-tuple-element.46, f32[16,4096]{1,0:T(8,128)S(1)} %collective-permute-done.6, ...), kind=kLoop, calls=%fused_computation.63 | loop fusion | flops 655359 | bytes 819329
  38.0 1.0 %bitcast_dynamic-update-slice_fusion.2 = f32[1,128,4096]{2,1,0:T(8,128)S(1)} fusion(f32[1,128,4096]{2,1,0:T(8,128)S(1)} %subtract_dynamic-update-slice_fusion, f32[16]{0:T(128)S(1)} %get-tuple-element.47, f32[16]{0:T(128)S(1)} %get-tuple-element.45, f32[4096]{0:T(1024)S(1)} %get-tuple-element.51, f32[4096]{0:T(1024)S(1)} %get-tuple-element.52, ...), kind=kLoop, calls=%fused_computation.62 | loop fusion | flops 655360 | bytes 820225
  39.0 1.0 %bitcast_dynamic-update-slice_fusion.1 = f32[1,128,4096]{2,1,0:T(8,128)S(1)} fusion(f32[1,128,4096]{2,1,0:T(8,128)S(1)} %bitcast_dynamic-update-slice_fusion.2, f32[4096]{0:T(1024)S(1)} %get-tuple-element.51, f32[16]{0:T(128)S(1)} %get-tuple-element.48, f32[4096]{0:T(1024)S(1)} %get-tuple-element.52, f32[16]{0:T(128)S(1)} %get-tuple-element.46, ...), kind=kLoop, calls=%fused_computation.61 | loop fusion | flops 655360 | bytes 820225
  40.3 1.0 %bitcast_dynamic-update-slice_fusion = f32[1,128,4096]{2,1,0:T(8,128)S(1)} fusion(f32[1,128,4096]{2,1,0:T(8,128)S(1)} %add_dynamic-update-slice_fusion, f32[16]{0:T(128)S(1)} %get-tuple-element.47, f32[16]{0:T(128)S(1)} %get-tuple-element.45, f32[4096]{0:T(1024)S(1)} %get-tuple-element.51, f32[4096]{0:T(1024)S(1)} %get-tuple-element.52, ...), kind=kLoop, calls=%fused_computation.60 | loop fusion | flops 655360 | bytes 820225 | tf_op jit(solution)/shard_map/concatenate | solution.py:74
  41.3 0.7 %convolution_bitcast_fusion.1 = f32[1,64,4096]{2,1,0:T(8,128)S(1)} fusion(f32[1,128,4096]{2,1,0:T(8,128)S(1)} %bitcast_dynamic-update-slice_fusion, f32[32,64]{1,0:T(8,128)S(1)} %get-tuple-element.8, f32[32,64]{1,0:T(8,128)S(1)} %get-tuple-element.7, f32[32,64]{1,0:T(8,128)S(1)} %neg.4), kind=kOutput, calls=%fused_computation.3 | convolution fusion | flops 201351168 | bytes 3170304 | tf_op jit(solution)/shard_map/ij,ajy->aiy/dot_general | solution.py:75
  43.1 1.1 %fusion.18 = f32[1,32,32,256]{3,2,1,0:T(8,128)S(1)} fusion(f32[1,32,32,32]{3,2,1,0:T(8,128)S(1)} %bitcast.164, f32[1,32,32,128]{3,2,1,0:T(8,128)S(1)} %bitcast.170, f32[1,32,32,32]{3,2,1,0:T(8,128)S(1)} %bitcast.166, f32[1,32,32,128]{3,2,1,0:T(8,128)S(1)} %bitcast.168, f32[160,128]{1,0:T(8,128)S(1)} %get-tuple-element.6, f32[160,128]{1,0:T(8,128)S(1)} %neg.5, ...), kind=kOutput, calls=%fused_computation.29 | convolution fusion | flops 504545280 | bytes 2605056 | tf_op jit(solution)/shard_map/...nj,jc->...nc/dot_general | solution.py:67
  44.9 2.7 %collective-permute-start.9 = (f32[2,1,16,4096]{3,2,1,0:T(8,128)S(1)}, f32[2,1,16,4096]{3,2,1,0:T(8,128)S(1)}, u32[]{:S(2)}, u32[]{:S(2)}) collective-permute-start(f32[2,1,16,4096]{3,2,1,0:T(8,128)S(1)} %get-tuple-element.20), channel_id=1, source_target_pairs={{1,2},{2,1},{5,6},{6,5},{9,10},{10,9},{13,14},{14,13},{17,18},{18,... | collective-permute-start | bytes 1572872 | tf_op jit(solution)/shard_map/ppermute | solution.py:23
  47.7 7.7 %collective-permute-done.9 = f32[2,1,16,4096]{3,2,1,0:T(8,128)S(1)} collective-permute-done((f32[2,1,16,4096]{3,2,1,0:T(8,128)S(1)}, f32[2,1,16,4096]{3,2,1,0:T(8,128)S(1)}, u32[]{:S(2)}, u32[]{:S(2)}) %collective-permute-start.9) | collective-permute-done | bytes 524320 | tf_op jit(solution)/shard_map/ppermute | solution.py:23
  55.9 0.7 %convolution_bitcast_fusion = f32[1,64,4096]{2,1,0:T(8,128)S(1)} fusion(f32[1,64,4096]{2,1,0:T(8,128)S(1)} %get-tuple-element.10, f32[1,64,4096]{2,1,0:T(8,128)S(1)} %get-tuple-element.9, f32[32,64]{1,0:T(8,128)S(1)} %get-tuple-element.8, f32[32,64]{1,0:T(8,128)S(1)} %get-tuple-element.7, f32[32,64]{1,0:T(8,128)S(1)} %neg.4), kind=kOutput, calls=%fused_computation.2 | convolution fusion | flops 201875456 | bytes 3170304 | tf_op jit(solution)/shard_map/ij,ajy->aiy/dot_general | solution.py:75
  57.7 1.1 %fusion.17 = f32[1,32,32,256]{3,2,1,0:T(8,128)S(1)} fusion(f32[1,32,32,32]{3,2,1,0:T(8,128)S(1)} %bitcast.163, f32[1,32,32,128]{3,2,1,0:T(8,128)S(1)} %bitcast.169, f32[1,32,32,32]{3,2,1,0:T(8,128)S(1)} %bitcast.165, f32[1,32,32,128]{3,2,1,0:T(8,128)S(1)} %bitcast.167, f32[160,128]{1,0:T(8,128)S(1)} %get-tuple-element.6, f32[160,128]{1,0:T(8,128)S(1)} %neg.5, ...), kind=kOutput, calls=%fused_computation.28 | convolution fusion | flops 504545280 | bytes 2605056 | tf_op jit(solution)/shard_map/...nj,jc->...nc/dot_general | solution.py:67
  59.2 1.0 %pad_maximum_fusion.1 = f32[2,1,32,4096]{3,2,1,0:T(8,128)} fusion(f32[1,1,32,4096]{3,2,1,0:T(8,128)S(1)} %stack_reshape.7, f32[1,1,32,4096]{3,2,1,0:T(8,128)S(1)} %stack_reshape.6), kind=kLoop, calls=%fused_computation.34 | loop fusion | flops 262144 | bytes 2097152 | tf_op jit(solution)/shard_map/stack | solution.py:175
  (72 shorter events, 8.6 us)
Async XLA Ops:
  0.0 10.6 %collective-permute-start.2 = (f32[2,32,512]{2,1,0:T(8,128)}, f32[2,32,512]{2,1,0:T(8,128)S(1)}, u32[]{:S(2)}, u32[]{:S(2)}) collective-permute-start(f32[2,32,512]{2,1,0:T(8,128)} %param.6), channel_id=1, source_target_pairs={{0,16},{4,20},{8,24},{12,28},{16,0},{20,4},{24,8},{28,12},{1,17},{... | collective-permute-start | bytes 393224 | tf_op jit(solution)/shard_map/ppermute | solution.py:107
  3.1 7.5 %collective-permute-start.1 = (f32[2,32,512]{2,1,0:T(8,128)}, f32[2,32,512]{2,1,0:T(8,128)S(1)}, u32[]{:S(2)}, u32[]{:S(2)}) collective-permute-start(f32[2,32,512]{2,1,0:T(8,128)} %param.6), channel_id=1, source_target_pairs={{0,8},{4,12},{8,0},{12,4},{16,24},{20,28},{24,16},{28,20},{1,9},{5... | collective-permute-start | bytes 393224 | tf_op jit(solution)/shard_map/ppermute | solution.py:107
  4.4 8.9 %collective-permute-start = (f32[2,32,512]{2,1,0:T(8,128)}, f32[2,32,512]{2,1,0:T(8,128)S(1)}, u32[]{:S(2)}, u32[]{:S(2)}) collective-permute-start(f32[2,32,512]{2,1,0:T(8,128)} %param.6), channel_id=1, source_target_pairs={{0,4},{4,0},{8,12},{12,8},{16,20},{20,16},{24,28},{28,24},{1,5},{5... | collective-permute-start | bytes 393224 | tf_op jit(solution)/shard_map/ppermute | solution.py:107
  10.7 7.8 %collective-permute-start.3 = (f32[2,2,32,512]{3,2,1,0:T(8,128)S(1)}, f32[2,2,32,512]{3,2,1,0:T(8,128)S(1)}, u32[]{:S(2)}, u32[]{:S(2)}) collective-permute-start(f32[2,2,32,512]{3,2,1,0:T(8,128)S(1)} %pad_maximum_fusion.3), channel_id=1, source_target_pairs={{0,4},{4,0},{8,12},{12,8},{16,20},{20,16},{24,28},{28,24},{1,5},{5... | collective-permute-start | bytes 786440 | tf_op jit(solution)/shard_map/ppermute | solution.py:107
  10.9 3.8 %collective-permute-start.4 = (f32[2,32,512]{2,1,0:T(8,128)S(1)}, f32[2,32,512]{2,1,0:T(8,128)S(1)}, u32[]{:S(2)}, u32[]{:S(2)}) collective-permute-start(f32[2,32,512]{2,1,0:T(8,128)S(1)} %collective-permute-done.2), channel_id=1, source_target_pairs={{0,8},{4,12},{8,0},{12,4},{16,24},{20,28},{24,16},{28,20},{1,9},{5... | collective-permute-start | bytes 393224 | tf_op jit(solution)/shard_map/ppermute | solution.py:107
  12.0 5.6 %collective-permute-start.5 = (f32[2,32,512]{2,1,0:T(8,128)S(1)}, f32[2,32,512]{2,1,0:T(8,128)S(1)}, u32[]{:S(2)}, u32[]{:S(2)}) collective-permute-start(f32[2,32,512]{2,1,0:T(8,128)S(1)} %collective-permute-done.2), channel_id=1, source_target_pairs={{0,12},{4,8},{8,4},{12,0},{16,28},{20,24},{24,20},{28,16},{1,13},{... | collective-permute-start | bytes 393224 | tf_op jit(solution)/shard_map/ppermute | solution.py:107
  21.8 15.0 %collective-permute-start.6 = (f32[16,4096]{1,0:T(8,128)}, f32[16,4096]{1,0:T(8,128)S(1)}, u32[]{:S(2)}, u32[]{:S(2)}) collective-permute-start(f32[16,4096]{1,0:T(8,128)} %bitcast.51), channel_id=1, source_target_pairs={{0,1},{2,3},{1,0},{3,2},{4,5},{6,7},{5,4},{7,6},{8,9},{10,11},{9,8... | collective-permute-start | bytes 786440 | tf_op jit(solution)/shard_map/ppermute | solution.py:22
  26.4 10.4 %collective-permute-start.7 = (f32[16,4096]{1,0:T(8,128)}, f32[16,4096]{1,0:T(8,128)S(1)}, u32[]{:S(2)}, u32[]{:S(2)}) collective-permute-start(f32[16,4096]{1,0:T(8,128)} %bitcast.53), channel_id=1, source_target_pairs={{1,2},{2,1},{5,6},{6,5},{9,10},{10,9},{13,14},{14,13},{17,18},{18,... | collective-permute-start | bytes 786440 | tf_op jit(solution)/shard_map/ppermute | solution.py:23
  29.4 3.3 %copy-start = (f32[2,33]{1,0:T(2,128)S(1)}, f32[2,33]{1,0:T(2,128)}, u32[]{:S(2)}) copy-start(f32[2,33]{1,0:T(2,128)} %param.5) | copy-start | bytes 796
  44.8 2.8 %collective-permute-start.8 = (f32[2,1,16,4096]{3,2,1,0:T(8,128)S(1)}, f32[2,1,16,4096]{3,2,1,0:T(8,128)S(1)}, u32[]{:S(2)}, u32[]{:S(2)}) collective-permute-start(f32[2,1,16,4096]{3,2,1,0:T(8,128)S(1)} %get-tuple-element.19), channel_id=1, source_target_pairs={{0,1},{2,3},{1,0},{3,2},{4,5},{6,7},{5,4},{7,6},{8,9},{10,11},{9,8... | collective-permute-start | bytes 1572872 | tf_op jit(solution)/shard_map/ppermute | solution.py:22
  44.9 10.5 %collective-permute-start.9 = (f32[2,1,16,4096]{3,2,1,0:T(8,128)S(1)}, f32[2,1,16,4096]{3,2,1,0:T(8,128)S(1)}, u32[]{:S(2)}, u32[]{:S(2)}) collective-permute-start(f32[2,1,16,4096]{3,2,1,0:T(8,128)S(1)} %get-tuple-element.20), channel_id=1, source_target_pairs={{1,2},{2,1},{5,6},{6,5},{9,10},{10,9},{13,14},{14,13},{17,18},{18,... | collective-permute-start | bytes 1572872 | tf_op jit(solution)/shard_map/ppermute | solution.py:23

commit v18 on v17

--- a/solution.py
+++ b/solution.py
@@ -166,12 +166,29 @@
     real = jnp.concatenate([piece[0] for piece in pieces], axis=1)
     imag = jnp.concatenate([piece[1] for piece in pieces], axis=1)
     real, imag = cross_pass(real, imag, taps)
+    count = lax.axis_size("tile")
+    odd = lax.axis_index("tile") % 2 == 1
+    across = [(i, i + 1) for i in range(1, count - 1, 2)] + [(i + 1, i) for i in range(1, count - 1, 2)]
+    within = [(i, i + 1) for i in range(0, count - 1, 2)] + [(i + 1, i) for i in range(0, count - 1, 2)]
+
+    def halves(x, axis):
+        head = lax.slice_in_dim(x, 0, HALF, axis=axis)
+        tail = lax.slice_in_dim(x, x.shape[axis] - HALF, x.shape[axis], axis=axis)
+        return jnp.where(odd, tail, head), jnp.where(odd, head, tail)
+
+    for plane in range(1, PLANES):
+        sent = []
+        for part, screen in zip(zip(*(halves(x, 1) for x in (real, imag))), halves(screens[plane], 0)):
+            part_real, part_imag = along_pass(part[0], part[1], taps)
+            sent.append(jnp.stack(transmit(part_real, part_imag, screen)))
+        got_across = lax.ppermute(sent[0], "tile", across)
+        got_within = lax.ppermute(sent[1], "tile", within)
+        own = jnp.where(odd, jnp.concatenate([sent[1], sent[0]], axis=2), jnp.concatenate(sent, axis=2))
+        before = jnp.where(odd, got_within, got_across)
+        after = jnp.where(odd, got_across, got_within)
+        packed = jnp.concatenate([before, own, after], axis=2)
+        real, imag = cross_pass(packed[0], packed[1], taps)
     real, imag = along_pass(real, imag, taps)
-    for plane in range(1, PLANES):
-        real, imag = transmit(real, imag, screens[plane])
-        packed = extended(jnp.stack([real, imag]), (("tile", 2),), HALF)
-        real, imag = cross_pass(packed[0], packed[1], taps)
-        real, imag = along_pass(real, imag, taps)
     return jnp.stack([real, imag])
 
 

time: 60.5 us -> 61 us (level)
  other arithmetic: 9.02 us -> 11.1 us
  local copies, waits for them, and re-layouts: 15.5 us -> 13.7 us
    ppermute x2 -> x1, waiting for transfers between devices: 7.75 us -> 0.01 us  [extended(): got_across = lax.ppermute(jnp.where(odd, tail, head), axis, across)]
    ppermute x0 -> x2, waiting for transfers between devices: none -> 7.45 us  [the longest x1 7.45 us: body(): got_across = lax.ppermute(sent[0], 'tile', across)]
    ppermute x0 -> x2, starting transfers between devices: none -> 2.84 us  [the longest x1 2.77 us: body(): got_across = lax.ppermute(sent[0], 'tile', across)]
    ppermute x2 -> x1, starting transfers between devices: 5.73 us -> 3.18 us  [extended(): got_across = lax.ppermute(jnp.where(odd, tail, head), axis, across)]
    sin x0 -> x1, other arithmetic: none -> 1.88 us  [transmit(): return rotate(real, imag, jnp.cos(screen), jnp.sin(screen))]
    sin x5 -> x6, local copies, waits for them, and re-layouts: 2.67 us -> 0.83 us  [transmit(): return rotate(real, imag, jnp.cos(screen), jnp.sin(screen))]
    dot_general x2 -> x3, matrix products: 2.27 us -> 2.47 us  [along_pass(): out = jnp.einsum('...nj,jc->...nc', win, kern, precision=lax.Precision.HIGH)]
    unnamed x21 -> x27, local copies, waits for them, and re-layouts: 3.12 us -> 3.29 us
where the time goes in v18:
time: 61 us; the launch traced here: 60.7 us
  starting transfers between devices  18.3 us (30%)
  local copies, waits for them, and re-layouts  13.7 us (22%)
  waiting for transfers between devices  11.4 us (19%)
  other arithmetic  11.1 us (18%)
  matrix products  3.83 us (6%)
  between operations  2.51 us (4%)
    ppermute x6, starting transfers between devices, exchange(): return lax.ppermute(x, axis, [(i, partner(i, k)) for i in range(count)])  8.39 us
    ppermute x1, waiting for transfers between devices, body(): got_across = lax.ppermute(sent[0], 'tile', across)  7.45 us
    ppermute x6, waiting for transfers between devices, exchange(): return lax.ppermute(x, axis, [(i, partner(i, k)) for i in range(count)])  3.91 us
    ppermute x1, starting transfers between devices, extended(): got_within = lax.ppermute(jnp.where(odd, head, tail), axis, within)  3.85 us
    unnamed x6, other arithmetic  3.49 us
    unnamed x27, local copies, waits for them, and re-layouts  3.29 us
    ppermute x1, starting transfers between devices, extended(): got_across = lax.ppermute(jnp.where(odd, tail, head), axis, across)  3.18 us
    ppermute x1, starting transfers between devices, body(): got_across = lax.ppermute(sent[0], 'tile', across)  2.77 us
  transfers between devices with their start and end apart: 10, of which 4 were waited for; matrix products, arithmetic and copies ran while one was open for 20% of the time, Pallas kernels for 0%

profile of v18, /device:TPU:1, one launch (start us, length us, event | category | flops | bytes accessed | tf_op | source)
XLA Modules:
  0.0 60.7 jit_solution(10297447739253572821)
XLA Ops:
  0.0 3.1 %collective-permute-start.2 = (f32[2,32,512]{2,1,0:T(8,128)}, f32[2,32,512]{2,1,0:T(8,128)S(1)}, u32[]{:S(2)}, u32[]{:S(2)}) collective-permute-start(f32[2,32,512]{2,1,0:T(8,128)} %param.6), channel_id=1, source_target_pairs={{0,16},{4,20},{8,24},{12,28},{16,0},{20,4},{24,8},{28,12},{1,17},{... | collective-permute-start | bytes 393224 | tf_op jit(solution)/shard_map/ppermute | solution.py:107
  3.1 1.3 %collective-permute-start.1 = (f32[2,32,512]{2,1,0:T(8,128)}, f32[2,32,512]{2,1,0:T(8,128)S(1)}, u32[]{:S(2)}, u32[]{:S(2)}) collective-permute-start(f32[2,32,512]{2,1,0:T(8,128)} %param.6), channel_id=1, source_target_pairs={{0,8},{4,12},{8,0},{12,4},{16,24},{20,28},{24,16},{28,20},{1,9},{5... | collective-permute-start | bytes 393224 | tf_op jit(solution)/shard_map/ppermute | solution.py:107
  4.4 1.2 %collective-permute-start = (f32[2,32,512]{2,1,0:T(8,128)}, f32[2,32,512]{2,1,0:T(8,128)S(1)}, u32[]{:S(2)}, u32[]{:S(2)}) collective-permute-start(f32[2,32,512]{2,1,0:T(8,128)} %param.6), channel_id=1, source_target_pairs={{0,4},{4,0},{8,12},{12,8},{16,20},{20,16},{24,28},{28,24},{1,5},{5... | collective-permute-start | bytes 393224 | tf_op jit(solution)/shard_map/ppermute | solution.py:107
  5.7 0.9 %bitcast_dynamic-update-slice_fusion.10 = f32[2,8,32,512]{3,2,0,1:T(8,128)S(1)} fusion(f32[2,32,512]{2,1,0:T(8,128)} %param.6), kind=kLoop, calls=%fused_computation.96 | loop fusion | bytes 262144
  6.6 1.4 %fusion.54 = (s32[1,1]{1,0:T(1,128)}, s32[1,1]{1,0:T(1,128)}) fusion(s32[1,2]{1,0:T(1,128)} %param.4), kind=kLoop, calls=%fused_computation.158 | loop fusion | bytes 16 | tf_op jit(solution)/shard_map/slice | solution.py:144
  8.0 0.7 %sine_select_fusion = (f32[1,64,1]{1,2,0:T(1,128)S(1)}, f32[1,64,1]{1,2,0:T(1,128)S(1)}) fusion(s32[]{:T(128)S(6)} %sub.175, s32[]{:T(128)} %bitcast), kind=kLoop, calls=%fused_computation.143 | loop fusion | flops 1280 | bytes 520 | tf_op jit(solution)/shard_map/jit(_where)/select_n | solution.py:148
  9.0 0.8 %fusion.38 = (f32[4096]{0:T(1024)S(1)}, f32[4096]{0:T(1024)S(1)}) fusion(s32[]{:T(128)} %bitcast.2), kind=kLoop, calls=%fused_computation.120 | loop fusion | flops 57344 | bytes 32772 | tf_op jit(solution)/shard_map/sin | solution.py:150
  9.8 0.8 %fusion.44 = (s32[8]{0:T(128)S(1)}, s32[8]{0:T(128)S(1)}) fusion(s32[2,8]{1,0:T(2,128)} %param.7, s32[]{:T(128)S(6)} %axis_index.33), kind=kLoop, calls=%fused_computation.134 | loop fusion | flops 64 | bytes 132 | tf_op jit(solution)/shard_map/select_n | solution.py:126
  10.9 1.1 %collective-permute-start.4 = (f32[2,32,512]{2,1,0:T(8,128)S(1)}, f32[2,32,512]{2,1,0:T(8,128)S(1)}, u32[]{:S(2)}, u32[]{:S(2)}) collective-permute-start(f32[2,32,512]{2,1,0:T(8,128)S(1)} %collective-permute-done.2), channel_id=1, source_target_pairs={{0,8},{4,12},{8,0},{12,4},{16,24},{20,28},{24,16},{28,20},{1,9},{5... | collective-permute-start | bytes 393224 | tf_op jit(solution)/shard_map/ppermute | solution.py:107
  12.0 1.4 %collective-permute-start.5 = (f32[2,32,512]{2,1,0:T(8,128)S(1)}, f32[2,32,512]{2,1,0:T(8,128)S(1)}, u32[]{:S(2)}, u32[]{:S(2)}) collective-permute-start(f32[2,32,512]{2,1,0:T(8,128)S(1)} %collective-permute-done.2), channel_id=1, source_target_pairs={{0,12},{4,8},{8,4},{12,0},{16,28},{20,24},{24,20},{28,16},{1,13},{... | collective-permute-start | bytes 393224 | tf_op jit(solution)/shard_map/ppermute | solution.py:107
  13.4 1.4 %collective-permute-done.4 = f32[2,32,512]{2,1,0:T(8,128)S(1)} collective-permute-done((f32[2,32,512]{2,1,0:T(8,128)S(1)}, f32[2,32,512]{2,1,0:T(8,128)S(1)}, u32[]{:S(2)}, u32[]{:S(2)}) %collective-permute-start.4) | collective-permute-done | bytes 131104 | tf_op jit(solution)/shard_map/ppermute | solution.py:107
  15.3 2.3 %collective-permute-done.5 = f32[2,32,512]{2,1,0:T(8,128)S(1)} collective-permute-done((f32[2,32,512]{2,1,0:T(8,128)S(1)}, f32[2,32,512]{2,1,0:T(8,128)S(1)}, u32[]{:S(2)}, u32[]{:S(2)}) %collective-permute-start.5) | collective-permute-done | bytes 131104 | tf_op jit(solution)/shard_map/ppermute | solution.py:107
  18.6 0.6 gather_fusion
  19.2 1.9 %bitcast_cosine_fusion = (f32[32,8,512]{2,0,1:T(8,128)S(1)}, f32[32,8,512]{2,0,1:T(8,128)S(1)}) fusion(f32[8,32,512]{2,1,0:T(8,128)S(1)} %gather_fusion), kind=kLoop, calls=%fused_computation.153 | loop fusion | bytes 1572864 | tf_op jit(solution)/shard_map/cos | solution.py:80
  21.1 0.7 %copy.21 = f32[8,2,8,512]{3,2,0,1:T(8,128)} copy(f32[8,2,8,512]{3,2,1,0:T(8,128)S(1)} %get-tuple-element.42) | data formatting | bytes 524288 | tf_op jit(solution)/shard_map/jit(_where)/select_n | solution.py:22
  21.8 3.8 %collective-permute-start.6 = (f32[16,4096]{1,0:T(8,128)}, f32[16,4096]{1,0:T(8,128)S(1)}, u32[]{:S(2)}, u32[]{:S(2)}) collective-permute-start(f32[16,4096]{1,0:T(8,128)} %bitcast.52), channel_id=1, source_target_pairs={{0,1},{2,3},{1,0},{3,2},{4,5},{6,7},{5,4},{7,6},{8,9},{10,11},{9,8... | collective-permute-start | bytes 786440 | tf_op jit(solution)/shard_map/ppermute | solution.py:22
  25.7 0.7 %copy.22 = f32[8,2,8,512]{3,2,0,1:T(8,128)} copy(f32[8,2,8,512]{3,2,1,0:T(8,128)S(1)} %get-tuple-element.41) | data formatting | bytes 524288 | tf_op jit(solution)/shard_map/jit(_where)/select_n | solution.py:23
  26.4 3.2 %collective-permute-start.7 = (f32[16,4096]{1,0:T(8,128)}, f32[16,4096]{1,0:T(8,128)S(1)}, u32[]{:S(2)}, u32[]{:S(2)}) collective-permute-start(f32[16,4096]{1,0:T(8,128)} %bitcast.54), channel_id=1, source_target_pairs={{1,2},{2,1},{5,6},{6,5},{9,10},{10,9},{13,14},{14,13},{17,18},{18,... | collective-permute-start | bytes 786440 | tf_op jit(solution)/shard_map/ppermute | solution.py:23
  33.6 0.6 gather_fusion.1
  34.2 1.9 %fusion.28 = (f32[16,8,512]{2,0,1:T(8,128)S(1)}, f32[16,8,512]{2,0,1:T(8,128)S(1)}, f32[16,8,512]{2,0,1:T(8,128)S(1)}, f32[16,8,512]{2,0,1:T(8,128)S(1)}) fusion(f32[32,8,512]{2,0,1:T(8,128)S(1)} %bitcast.190, pred[]{:T(512)S(6)} %eq.33), kind=kLoop, calls=%fused_computation.104 | loop fusion | flops 131072 | bytes 1572865 | tf_op jit(solution)/shard_map/sin | solution.py:80
  37.0 1.0 %bitcast_dynamic-update-slice_fusion.3 = f32[1,128,4096]{2,1,0:T(8,128)S(1)} fusion(f32[4096]{0:T(1024)S(1)} %get-tuple-element.61, f32[16]{0:T(128)S(1)} %get-tuple-element.58, f32[4096]{0:T(1024)S(1)} %get-tuple-element.62, f32[16]{0:T(128)S(1)} %get-tuple-element.56, f32[16,4096]{1,0:T(8,128)S(1)} %collective-permute-done.6, ...), kind=kLoop, calls=%fused_computation.61 | loop fusion | flops 655359 | bytes 819329
  38.2 1.0 %bitcast_dynamic-update-slice_fusion.2 = f32[1,128,4096]{2,1,0:T(8,128)S(1)} fusion(f32[1,128,4096]{2,1,0:T(8,128)S(1)} %subtract_dynamic-update-slice_fusion, f32[16]{0:T(128)S(1)} %get-tuple-element.57, f32[16]{0:T(128)S(1)} %get-tuple-element.55, f32[4096]{0:T(1024)S(1)} %get-tuple-element.61, f32[4096]{0:T(1024)S(1)} %get-tuple-element.62, ...), kind=kLoop, calls=%fused_computation.60 | loop fusion | flops 655360 | bytes 820225
  39.2 1.0 %bitcast_dynamic-update-slice_fusion.1 = f32[1,128,4096]{2,1,0:T(8,128)S(1)} fusion(f32[1,128,4096]{2,1,0:T(8,128)S(1)} %bitcast_dynamic-update-slice_fusion.2, f32[4096]{0:T(1024)S(1)} %get-tuple-element.61, f32[16]{0:T(128)S(1)} %get-tuple-element.58, f32[4096]{0:T(1024)S(1)} %get-tuple-element.62, f32[16]{0:T(128)S(1)} %get-tuple-element.56, ...), kind=kLoop, calls=%fused_computation.59 | loop fusion | flops 655360 | bytes 820225
  40.5 1.0 %bitcast_dynamic-update-slice_fusion = f32[1,128,4096]{2,1,0:T(8,128)S(1)} fusion(f32[1,128,4096]{2,1,0:T(8,128)S(1)} %add_dynamic-update-slice_fusion, f32[16]{0:T(128)S(1)} %get-tuple-element.57, f32[16]{0:T(128)S(1)} %get-tuple-element.55, f32[4096]{0:T(1024)S(1)} %get-tuple-element.61, f32[4096]{0:T(1024)S(1)} %get-tuple-element.62, ...), kind=kLoop, calls=%fused_computation.58 | loop fusion | flops 655360 | bytes 820225 | tf_op jit(solution)/shard_map/concatenate | solution.py:74
  41.5 0.7 %convolution_bitcast_fusion.1 = f32[1,64,4096]{2,1,0:T(8,128)S(1)} fusion(f32[1,128,4096]{2,1,0:T(8,128)S(1)} %bitcast_dynamic-update-slice_fusion, f32[32,64]{1,0:T(8,128)S(1)} %get-tuple-element.8, f32[32,64]{1,0:T(8,128)S(1)} %get-tuple-element.7, f32[32,64]{1,0:T(8,128)S(1)} %neg.4), kind=kOutput, calls=%fused_computation.3 | convolution fusion | flops 201351168 | bytes 3170304 | tf_op jit(solution)/shard_map/ij,ajy->aiy/dot_general | solution.py:75
  42.9 0.7 %convolution_bitcast_fusion.2 = f32[1,16,32,256]{3,2,1,0:T(8,128)S(1)} fusion(f32[1,16,32,32]{3,2,1,0:T(8,128)S(1)} %bitcast.197, f32[1,16,32,128]{3,2,1,0:T(8,128)S(1)} %bitcast.203, f32[1,16,32,32]{3,2,1,0:T(8,128)S(1)} %bitcast.199, f32[1,16,32,128]{3,2,1,0:T(8,128)S(1)} %bitcast.201, f32[160,128]{1,0:T(8,128)S(1)} %get-tuple-element.6, ...), kind=kOutput, calls=%fused_computation.21 | convolution fusion | flops 252395520 | bytes 1425408 | tf_op jit(solution)/shard_map/...nj,jc->...nc/dot_general | solution.py:67
  44.4 0.7 %convolution_bitcast_fusion.3 = f32[1,16,32,256]{3,2,1,0:T(8,128)S(1)} fusion(f32[1,16,32,32]{3,2,1,0:T(8,128)S(1)} %bitcast.198, f32[1,16,32,128]{3,2,1,0:T(8,128)S(1)} %bitcast.204, f32[1,16,32,32]{3,2,1,0:T(8,128)S(1)} %bitcast.200, f32[1,16,32,128]{3,2,1,0:T(8,128)S(1)} %bitcast.202, f32[160,128]{1,0:T(8,128)S(1)} %get-tuple-element.6, ...), kind=kOutput, calls=%fused_computation.22 | convolution fusion | flops 252395520 | bytes 1425408 | tf_op jit(solution)/shard_map/...nj,jc->...nc/dot_general | solution.py:67
  45.3 2.8 %collective-permute-start.9 = (f32[2,1,16,4096]{3,2,1,0:T(8,128)S(1)}, f32[2,1,16,4096]{3,2,1,0:T(8,128)S(1)}, u32[]{:S(2)}, u32[]{:S(2)}) collective-permute-start(f32[2,1,16,4096]{3,2,1,0:T(8,128)S(1)} %pad_maximum_fusion.3), channel_id=1, source_target_pairs={{1,2},{2,1},{5,6},{6,5},{9,10},{10,9},{13,14},{14,13},{17,18},{18,... | collective-permute-start | bytes 1572872 | tf_op jit(solution)/shard_map/ppermute | solution.py:184
  48.4 7.4 %collective-permute-done.9 = f32[2,1,16,4096]{3,2,1,0:T(8,128)S(1)} collective-permute-done((f32[2,1,16,4096]{3,2,1,0:T(8,128)S(1)}, f32[2,1,16,4096]{3,2,1,0:T(8,128)S(1)}, u32[]{:S(2)}, u32[]{:S(2)}) %collective-permute-start.9) | collective-permute-done | bytes 524320 | tf_op jit(solution)/shard_map/ppermute | solution.py:184
  56.3 0.7 %convolution_bitcast_fusion = f32[1,64,4096]{2,1,0:T(8,128)S(1)} fusion(f32[1,64,4096]{2,1,0:T(8,128)S(1)} %get-tuple-element.10, f32[1,64,4096]{2,1,0:T(8,128)S(1)} %get-tuple-element.9, f32[32,64]{1,0:T(8,128)S(1)} %get-tuple-element.8, f32[32,64]{1,0:T(8,128)S(1)} %get-tuple-element.7, f32[32,64]{1,0:T(8,128)S(1)} %neg.4), kind=kOutput, calls=%fused_computation.2 | convolution fusion | flops 201875456 | bytes 3170304 | tf_op jit(solution)/shard_map/ij,ajy->aiy/dot_general | solution.py:75
  58.2 1.1 %fusion.10 = f32[1,32,32,256]{3,2,1,0:T(8,128)S(1)} fusion(f32[1,32,32,32]{3,2,1,0:T(8,128)S(1)} %bitcast.192, f32[1,32,32,128]{3,2,1,0:T(8,128)S(1)} %bitcast.191, f32[1,32,32,32]{3,2,1,0:T(8,128)S(1)} %bitcast.193, f32[1,32,32,128]{3,2,1,0:T(8,128)S(1)} %bitcast.194, f32[160,128]{1,0:T(8,128)S(1)} %get-tuple-element.6, f32[160,128]{1,0:T(8,128)S(1)} %neg.5, ...), kind=kOutput, calls=%fused_computation.20 | convolution fusion | flops 504545280 | bytes 2605056 | tf_op jit(solution)/shard_map/...nj,jc->...nc/dot_general | solution.py:67
  59.7 1.0 %pad_maximum_fusion.1 = f32[2,1,32,4096]{3,2,1,0:T(8,128)} fusion(f32[1,1,32,4096]{3,2,1,0:T(8,128)S(1)} %stack_reshape.7, f32[1,1,32,4096]{3,2,1,0:T(8,128)S(1)} %stack_reshape.6), kind=kLoop, calls=%fused_computation.26 | loop fusion | flops 262144 | bytes 2097152 | tf_op jit(solution)/shard_map/stack | solution.py:192
  (89 shorter events, 9.5 us)
Async XLA Ops:
  0.0 10.6 %collective-permute-start.2 = (f32[2,32,512]{2,1,0:T(8,128)}, f32[2,32,512]{2,1,0:T(8,128)S(1)}, u32[]{:S(2)}, u32[]{:S(2)}) collective-permute-start(f32[2,32,512]{2,1,0:T(8,128)} %param.6), channel_id=1, source_target_pairs={{0,16},{4,20},{8,24},{12,28},{16,0},{20,4},{24,8},{28,12},{1,17},{... | collective-permute-start | bytes 393224 | tf_op jit(solution)/shard_map/ppermute | solution.py:107
  3.1 7.5 %collective-permute-start.1 = (f32[2,32,512]{2,1,0:T(8,128)}, f32[2,32,512]{2,1,0:T(8,128)S(1)}, u32[]{:S(2)}, u32[]{:S(2)}) collective-permute-start(f32[2,32,512]{2,1,0:T(8,128)} %param.6), channel_id=1, source_target_pairs={{0,8},{4,12},{8,0},{12,4},{16,24},{20,28},{24,16},{28,20},{1,9},{5... | collective-permute-start | bytes 393224 | tf_op jit(solution)/shard_map/ppermute | solution.py:107
  4.4 8.9 %collective-permute-start = (f32[2,32,512]{2,1,0:T(8,128)}, f32[2,32,512]{2,1,0:T(8,128)S(1)}, u32[]{:S(2)}, u32[]{:S(2)}) collective-permute-start(f32[2,32,512]{2,1,0:T(8,128)} %param.6), channel_id=1, source_target_pairs={{0,4},{4,0},{8,12},{12,8},{16,20},{20,16},{24,28},{28,24},{1,5},{5... | collective-permute-start | bytes 393224 | tf_op jit(solution)/shard_map/ppermute | solution.py:107
  10.6 7.8 %collective-permute-start.3 = (f32[2,2,32,512]{3,2,1,0:T(8,128)S(1)}, f32[2,2,32,512]{3,2,1,0:T(8,128)S(1)}, u32[]{:S(2)}, u32[]{:S(2)}) collective-permute-start(f32[2,2,32,512]{3,2,1,0:T(8,128)S(1)} %pad_maximum_fusion.4), channel_id=1, source_target_pairs={{0,4},{4,0},{8,12},{12,8},{16,20},{20,16},{24,28},{28,24},{1,5},{5... | collective-permute-start | bytes 786440 | tf_op jit(solution)/shard_map/ppermute | solution.py:107
  10.9 3.8 %collective-permute-start.4 = (f32[2,32,512]{2,1,0:T(8,128)S(1)}, f32[2,32,512]{2,1,0:T(8,128)S(1)}, u32[]{:S(2)}, u32[]{:S(2)}) collective-permute-start(f32[2,32,512]{2,1,0:T(8,128)S(1)} %collective-permute-done.2), channel_id=1, source_target_pairs={{0,8},{4,12},{8,0},{12,4},{16,24},{20,28},{24,16},{28,20},{1,9},{5... | collective-permute-start | bytes 393224 | tf_op jit(solution)/shard_map/ppermute | solution.py:107
  12.0 5.6 %collective-permute-start.5 = (f32[2,32,512]{2,1,0:T(8,128)S(1)}, f32[2,32,512]{2,1,0:T(8,128)S(1)}, u32[]{:S(2)}, u32[]{:S(2)}) collective-permute-start(f32[2,32,512]{2,1,0:T(8,128)S(1)} %collective-permute-done.2), channel_id=1, source_target_pairs={{0,12},{4,8},{8,4},{12,0},{16,28},{20,24},{24,20},{28,16},{1,13},{... | collective-permute-start | bytes 393224 | tf_op jit(solution)/shard_map/ppermute | solution.py:107
  19.2 12.8 %copy-start = (f32[2,33]{1,0:T(2,128)S(1)}, f32[2,33]{1,0:T(2,128)}, u32[]{:S(2)}) copy-start(f32[2,33]{1,0:T(2,128)} %param.5) | copy-start | bytes 796
  21.8 15.1 %collective-permute-start.6 = (f32[16,4096]{1,0:T(8,128)}, f32[16,4096]{1,0:T(8,128)S(1)}, u32[]{:S(2)}, u32[]{:S(2)}) collective-permute-start(f32[16,4096]{1,0:T(8,128)} %bitcast.52), channel_id=1, source_target_pairs={{0,1},{2,3},{1,0},{3,2},{4,5},{6,7},{5,4},{7,6},{8,9},{10,11},{9,8... | collective-permute-start | bytes 786440 | tf_op jit(solution)/shard_map/ppermute | solution.py:22
  26.4 10.6 %collective-permute-start.7 = (f32[16,4096]{1,0:T(8,128)}, f32[16,4096]{1,0:T(8,128)S(1)}, u32[]{:S(2)}, u32[]{:S(2)}) collective-permute-start(f32[16,4096]{1,0:T(8,128)} %bitcast.54), channel_id=1, source_target_pairs={{1,2},{2,1},{5,6},{6,5},{9,10},{10,9},{13,14},{14,13},{17,18},{18,... | collective-permute-start | bytes 786440 | tf_op jit(solution)/shard_map/ppermute | solution.py:23
  45.3 10.5 %collective-permute-start.9 = (f32[2,1,16,4096]{3,2,1,0:T(8,128)S(1)}, f32[2,1,16,4096]{3,2,1,0:T(8,128)S(1)}, u32[]{:S(2)}, u32[]{:S(2)}) collective-permute-start(f32[2,1,16,4096]{3,2,1,0:T(8,128)S(1)} %pad_maximum_fusion.3), channel_id=1, source_target_pairs={{1,2},{2,1},{5,6},{6,5},{9,10},{10,9},{13,14},{14,13},{17,18},{18,... | collective-permute-start | bytes 1572872 | tf_op jit(solution)/shard_map/ppermute | solution.py:184
  48.2 7.6 %collective-permute-start.8 = (f32[2,1,16,4096]{3,2,1,0:T(8,128)S(1)}, f32[2,1,16,4096]{3,2,1,0:T(8,128)S(1)}, u32[]{:S(2)}, u32[]{:S(2)}) collective-permute-start(f32[2,1,16,4096]{3,2,1,0:T(8,128)S(1)} %pad_maximum_fusion.2), channel_id=1, source_target_pairs={{0,1},{2,3},{1,0},{3,2},{4,5},{6,7},{5,4},{7,6},{8,9},{10,11},{9,8... | collective-permute-start | bytes 1572872 | tf_op jit(solution)/shard_map/ppermute | solution.py:185

commit v19 on v17

--- a/solution.py
+++ b/solution.py
@@ -108,8 +108,8 @@
 
     if count == 8:
         one, two, four = (exchange(stored_planes, k) for k in (1, 2, 4))
-        three, five = exchange(jnp.stack([two, four]), 1)
-        six = exchange(four, 2)
+        three, six = exchange(jnp.stack([one, four]), 2)
+        five = exchange(four, 1)
         seven = exchange(four, 3)
         parts = [stored_planes, one, two, three, four, five, six, seven]
         first = [three, six, seven]

time: 60.5 us -> 61.3 us (1.013)
  waiting for transfers between devices: 11.7 us -> 13.8 us
  starting transfers between devices: 18 us -> 16.9 us
    ppermute x6, waiting for transfers between devices: 3.95 us -> 6.06 us  [exchange(): return lax.ppermute(x, axis, [(i, partner(i, k)) for i in range(count)])]
    ppermute x2, starting transfers between devices: 3.92 us -> 2.81 us  [extended(): got_within = lax.ppermute(jnp.where(odd, head, tail), axis, within)]
  transfers between devices with their start and end apart: 10 -> 10, of which waited for: 4 -> 2; matrix products, arithmetic and copies ran while one was open for 20% -> 20% of each run, Pallas kernels for 0% -> 0%
where the time goes in v19:
time: 61.3 us; the launch traced here: 61.1 us
  starting transfers between devices  16.9 us (28%)
  local copies, waits for them, and re-layouts  15.4 us (25%)
  waiting for transfers between devices  13.8 us (23%)
  other arithmetic  8.91 us (15%)
  matrix products  3.64 us (6%)
  between operations  2.39 us (4%)
    ppermute x6, starting transfers between devices, exchange(): return lax.ppermute(x, axis, [(i, partner(i, k)) for i in range(count)])  8.39 us
    ppermute x2, waiting for transfers between devices, extended(): got_across = lax.ppermute(jnp.where(odd, tail, head), axis, across)  7.75 us
    ppermute x6, waiting for transfers between devices, exchange(): return lax.ppermute(x, axis, [(i, partner(i, k)) for i in range(count)])  6.06 us
    ppermute x2, starting transfers between devices, extended(): got_across = lax.ppermute(jnp.where(odd, tail, head), axis, across)  5.73 us
    unnamed x6, other arithmetic  3.49 us
    unnamed x21, local copies, waits for them, and re-layouts  3.12 us
    ppermute x2, starting transfers between devices, extended(): got_within = lax.ppermute(jnp.where(odd, head, tail), axis, within)  2.81 us
    cos x5, local copies, waits for them, and re-layouts, transmit(): return rotate(real, imag, jnp.cos(screen), jnp.sin(screen))  2.67 us
  transfers between devices with their start and end apart: 10, of which 2 were waited for; matrix products, arithmetic and copies ran while one was open for 20% of the time, Pallas kernels for 0%

profile of v19, /device:TPU:1, one launch (start us, length us, event | category | flops | bytes accessed | tf_op | source)
XLA Modules:
  0.0 61.1 jit_solution(3335274740529505576)
XLA Ops:
  0.0 3.1 %collective-permute-start.2 = (f32[2,32,512]{2,1,0:T(8,128)}, f32[2,32,512]{2,1,0:T(8,128)S(1)}, u32[]{:S(2)}, u32[]{:S(2)}) collective-permute-start(f32[2,32,512]{2,1,0:T(8,128)} %param.6), channel_id=1, source_target_pairs={{0,16},{4,20},{8,24},{12,28},{16,0},{20,4},{24,8},{28,12},{1,17},{... | collective-permute-start | bytes 393224 | tf_op jit(solution)/shard_map/ppermute | solution.py:107
  3.1 1.2 %collective-permute-start = (f32[2,32,512]{2,1,0:T(8,128)}, f32[2,32,512]{2,1,0:T(8,128)S(1)}, u32[]{:S(2)}, u32[]{:S(2)}) collective-permute-start(f32[2,32,512]{2,1,0:T(8,128)} %param.6), channel_id=1, source_target_pairs={{0,4},{4,0},{8,12},{12,8},{16,20},{20,16},{24,28},{28,24},{1,5},{5... | collective-permute-start | bytes 393224 | tf_op jit(solution)/shard_map/ppermute | solution.py:107
  4.4 1.3 %collective-permute-start.1 = (f32[2,32,512]{2,1,0:T(8,128)}, f32[2,32,512]{2,1,0:T(8,128)S(1)}, u32[]{:S(2)}, u32[]{:S(2)}) collective-permute-start(f32[2,32,512]{2,1,0:T(8,128)} %param.6), channel_id=1, source_target_pairs={{0,8},{4,12},{8,0},{12,4},{16,24},{20,28},{24,16},{28,20},{1,9},{5... | collective-permute-start | bytes 393224 | tf_op jit(solution)/shard_map/ppermute | solution.py:107
  5.7 0.9 %bitcast_dynamic-update-slice_fusion.11 = f32[2,8,32,512]{3,2,0,1:T(8,128)S(1)} fusion(f32[2,32,512]{2,1,0:T(8,128)} %param.6), kind=kLoop, calls=%fused_computation.81 | loop fusion | bytes 262144
  6.6 1.3 %fusion.45 = (s32[1,1]{1,0:T(1,128)}, s32[1,1]{1,0:T(1,128)}) fusion(s32[1,2]{1,0:T(1,128)} %param.4), kind=kLoop, calls=%fused_computation.139 | loop fusion | bytes 16 | tf_op jit(solution)/shard_map/slice | solution.py:144
  7.9 0.7 %sine_select_fusion = (f32[1,64,1]{1,2,0:T(1,128)S(1)}, f32[1,64,1]{1,2,0:T(1,128)S(1)}) fusion(s32[]{:T(128)S(6)} %sub.149, s32[]{:T(128)} %bitcast), kind=kLoop, calls=%fused_computation.125 | loop fusion | flops 1280 | bytes 520 | tf_op jit(solution)/shard_map/jit(_where)/select_n | solution.py:148
  8.9 0.7 %fusion.30 = (f32[4096]{0:T(1024)S(1)}, f32[4096]{0:T(1024)S(1)}) fusion(s32[]{:T(128)} %bitcast.2), kind=kLoop, calls=%fused_computation.102 | loop fusion | flops 57344 | bytes 32772 | tf_op jit(solution)/shard_map/sin | solution.py:150
  9.6 0.8 %fusion.36 = (s32[8]{0:T(128)S(1)}, s32[8]{0:T(128)S(1)}) fusion(s32[2,8]{1,0:T(2,128)} %param.7, s32[]{:T(128)S(6)} %axis_index.33), kind=kLoop, calls=%fused_computation.116 | loop fusion | flops 64 | bytes 132 | tf_op jit(solution)/shard_map/select_n | solution.py:126
  10.8 1.2 %collective-permute-start.4 = (f32[2,32,512]{2,1,0:T(8,128)S(1)}, f32[2,32,512]{2,1,0:T(8,128)S(1)}, u32[]{:S(2)}, u32[]{:S(2)}) collective-permute-start(f32[2,32,512]{2,1,0:T(8,128)S(1)} %collective-permute-done.2), channel_id=1, source_target_pairs={{0,4},{4,0},{8,12},{12,8},{16,20},{20,16},{24,28},{28,24},{1,5},{5... | collective-permute-start | bytes 393224 | tf_op jit(solution)/shard_map/ppermute | solution.py:107
  12.0 1.2 %collective-permute-start.5 = (f32[2,32,512]{2,1,0:T(8,128)S(1)}, f32[2,32,512]{2,1,0:T(8,128)S(1)}, u32[]{:S(2)}, u32[]{:S(2)}) collective-permute-start(f32[2,32,512]{2,1,0:T(8,128)S(1)} %collective-permute-done.2), channel_id=1, source_target_pairs={{0,12},{4,8},{8,4},{12,0},{16,28},{20,24},{24,20},{28,16},{1,13},{... | collective-permute-start | bytes 393224 | tf_op jit(solution)/shard_map/ppermute | solution.py:107
  13.2 6.0 %collective-permute-done.5 = f32[2,32,512]{2,1,0:T(8,128)S(1)} collective-permute-done((f32[2,32,512]{2,1,0:T(8,128)S(1)}, f32[2,32,512]{2,1,0:T(8,128)S(1)}, u32[]{:S(2)}, u32[]{:S(2)}) %collective-permute-start.5) | collective-permute-done | bytes 131104 | tf_op jit(solution)/shard_map/ppermute | solution.py:107
  20.0 0.6 gather_fusion
  20.6 1.9 %bitcast_cosine_fusion = (f32[32,8,512]{2,0,1:T(8,128)S(1)}, f32[32,8,512]{2,0,1:T(8,128)S(1)}) fusion(f32[8,32,512]{2,1,0:T(8,128)S(1)} %gather_fusion), kind=kLoop, calls=%fused_computation.134 | loop fusion | bytes 1572864 | tf_op jit(solution)/shard_map/cos | solution.py:80
  22.5 0.7 %copy.17 = f32[8,2,8,512]{3,2,0,1:T(8,128)} copy(f32[8,2,8,512]{3,2,1,0:T(8,128)S(1)} %get-tuple-element.40) | data formatting | bytes 524288 | tf_op jit(solution)/shard_map/jit(_where)/select_n | solution.py:22
  23.2 2.7 %collective-permute-start.6 = (f32[16,4096]{1,0:T(8,128)}, f32[16,4096]{1,0:T(8,128)S(1)}, u32[]{:S(2)}, u32[]{:S(2)}) collective-permute-start(f32[16,4096]{1,0:T(8,128)} %bitcast.52), channel_id=1, source_target_pairs={{0,1},{2,3},{1,0},{3,2},{4,5},{6,7},{5,4},{7,6},{8,9},{10,11},{9,8... | collective-permute-start | bytes 786440 | tf_op jit(solution)/shard_map/ppermute | solution.py:22
  25.9 0.7 %copy.18 = f32[8,2,8,512]{3,2,0,1:T(8,128)} copy(f32[8,2,8,512]{3,2,1,0:T(8,128)S(1)} %get-tuple-element.39) | data formatting | bytes 524288 | tf_op jit(solution)/shard_map/jit(_where)/select_n | solution.py:23
  26.7 3.0 %collective-permute-start.7 = (f32[16,4096]{1,0:T(8,128)}, f32[16,4096]{1,0:T(8,128)S(1)}, u32[]{:S(2)}, u32[]{:S(2)}) collective-permute-start(f32[16,4096]{1,0:T(8,128)} %bitcast.54), channel_id=1, source_target_pairs={{1,2},{2,1},{5,6},{6,5},{9,10},{10,9},{13,14},{14,13},{17,18},{18,... | collective-permute-start | bytes 786440 | tf_op jit(solution)/shard_map/ppermute | solution.py:23
  30.5 0.5 slice.193
  33.7 0.6 select_reduce_fusion
  34.3 0.6 gather_fusion.1
  34.9 1.9 %sine_bitcast_fusion = (f32[32,8,512]{2,0,1:T(8,128)S(1)}, f32[32,8,512]{2,0,1:T(8,128)S(1)}) fusion(f32[8,32,512]{2,1,0:T(8,128)S(1)} %gather_fusion.1), kind=kLoop, calls=%fused_computation.48 | loop fusion | bytes 1572864 | tf_op jit(solution)/shard_map/sin | solution.py:80
  37.6 1.0 %bitcast_dynamic-update-slice_fusion.3 = f32[1,128,4096]{2,1,0:T(8,128)S(1)} fusion(f32[4096]{0:T(1024)S(1)} %get-tuple-element.53, f32[16]{0:T(128)S(1)} %get-tuple-element.50, f32[4096]{0:T(1024)S(1)} %get-tuple-element.54, f32[16]{0:T(128)S(1)} %get-tuple-element.48, f32[16,4096]{1,0:T(8,128)S(1)} %collective-permute-done.6, ...), kind=kLoop, calls=%fused_computation.63 | loop fusion | flops 655359 | bytes 819329
  38.8 1.0 %bitcast_dynamic-update-slice_fusion.2 = f32[1,128,4096]{2,1,0:T(8,128)S(1)} fusion(f32[1,128,4096]{2,1,0:T(8,128)S(1)} %subtract_dynamic-update-slice_fusion, f32[16]{0:T(128)S(1)} %get-tuple-element.49, f32[16]{0:T(128)S(1)} %get-tuple-element.47, f32[4096]{0:T(1024)S(1)} %get-tuple-element.53, f32[4096]{0:T(1024)S(1)} %get-tuple-element.54, ...), kind=kLoop, calls=%fused_computation.62 | loop fusion | flops 655360 | bytes 820225
  39.8 1.0 %bitcast_dynamic-update-slice_fusion.1 = f32[1,128,4096]{2,1,0:T(8,128)S(1)} fusion(f32[1,128,4096]{2,1,0:T(8,128)S(1)} %bitcast_dynamic-update-slice_fusion.2, f32[4096]{0:T(1024)S(1)} %get-tuple-element.53, f32[16]{0:T(128)S(1)} %get-tuple-element.50, f32[4096]{0:T(1024)S(1)} %get-tuple-element.54, f32[16]{0:T(128)S(1)} %get-tuple-element.48, ...), kind=kLoop, calls=%fused_computation.61 | loop fusion | flops 655360 | bytes 820225
  41.1 1.0 %bitcast_dynamic-update-slice_fusion = f32[1,128,4096]{2,1,0:T(8,128)S(1)} fusion(f32[1,128,4096]{2,1,0:T(8,128)S(1)} %add_dynamic-update-slice_fusion, f32[16]{0:T(128)S(1)} %get-tuple-element.49, f32[16]{0:T(128)S(1)} %get-tuple-element.47, f32[4096]{0:T(1024)S(1)} %get-tuple-element.53, f32[4096]{0:T(1024)S(1)} %get-tuple-element.54, ...), kind=kLoop, calls=%fused_computation.60 | loop fusion | flops 655360 | bytes 820225 | tf_op jit(solution)/shard_map/concatenate | solution.py:74
  42.1 0.7 %convolution_bitcast_fusion.1 = f32[1,64,4096]{2,1,0:T(8,128)S(1)} fusion(f32[1,128,4096]{2,1,0:T(8,128)S(1)} %bitcast_dynamic-update-slice_fusion, f32[32,64]{1,0:T(8,128)S(1)} %get-tuple-element.8, f32[32,64]{1,0:T(8,128)S(1)} %get-tuple-element.7, f32[32,64]{1,0:T(8,128)S(1)} %neg.4), kind=kOutput, calls=%fused_computation.3 | convolution fusion | flops 201351168 | bytes 3170304 | tf_op jit(solution)/shard_map/ij,ajy->aiy/dot_general | solution.py:75
  43.9 1.1 %fusion.18 = f32[1,32,32,256]{3,2,1,0:T(8,128)S(1)} fusion(f32[1,32,32,32]{3,2,1,0:T(8,128)S(1)} %bitcast.164, f32[1,32,32,128]{3,2,1,0:T(8,128)S(1)} %bitcast.170, f32[1,32,32,32]{3,2,1,0:T(8,128)S(1)} %bitcast.166, f32[1,32,32,128]{3,2,1,0:T(8,128)S(1)} %bitcast.168, f32[160,128]{1,0:T(8,128)S(1)} %get-tuple-element.6, f32[160,128]{1,0:T(8,128)S(1)} %neg.5, ...), kind=kOutput, calls=%fused_computation.29 | convolution fusion | flops 504545280 | bytes 2605056 | tf_op jit(solution)/shard_map/...nj,jc->...nc/dot_general | solution.py:67
  45.7 2.7 %collective-permute-start.9 = (f32[2,1,16,4096]{3,2,1,0:T(8,128)S(1)}, f32[2,1,16,4096]{3,2,1,0:T(8,128)S(1)}, u32[]{:S(2)}, u32[]{:S(2)}) collective-permute-start(f32[2,1,16,4096]{3,2,1,0:T(8,128)S(1)} %get-tuple-element.20), channel_id=1, source_target_pairs={{1,2},{2,1},{5,6},{6,5},{9,10},{10,9},{13,14},{14,13},{17,18},{18,... | collective-permute-start | bytes 1572872 | tf_op jit(solution)/shard_map/ppermute | solution.py:23
  48.4 7.7 %collective-permute-done.9 = f32[2,1,16,4096]{3,2,1,0:T(8,128)S(1)} collective-permute-done((f32[2,1,16,4096]{3,2,1,0:T(8,128)S(1)}, f32[2,1,16,4096]{3,2,1,0:T(8,128)S(1)}, u32[]{:S(2)}, u32[]{:S(2)}) %collective-permute-start.9) | collective-permute-done | bytes 524320 | tf_op jit(solution)/shard_map/ppermute | solution.py:23
  56.6 0.7 %convolution_bitcast_fusion = f32[1,64,4096]{2,1,0:T(8,128)S(1)} fusion(f32[1,64,4096]{2,1,0:T(8,128)S(1)} %get-tuple-element.10, f32[1,64,4096]{2,1,0:T(8,128)S(1)} %get-tuple-element.9, f32[32,64]{1,0:T(8,128)S(1)} %get-tuple-element.8, f32[32,64]{1,0:T(8,128)S(1)} %get-tuple-element.7, f32[32,64]{1,0:T(8,128)S(1)} %neg.4), kind=kOutput, calls=%fused_computation.2 | convolution fusion | flops 201875456 | bytes 3170304 | tf_op jit(solution)/shard_map/ij,ajy->aiy/dot_general | solution.py:75
  58.5 1.1 %fusion.17 = f32[1,32,32,256]{3,2,1,0:T(8,128)S(1)} fusion(f32[1,32,32,32]{3,2,1,0:T(8,128)S(1)} %bitcast.163, f32[1,32,32,128]{3,2,1,0:T(8,128)S(1)} %bitcast.169, f32[1,32,32,32]{3,2,1,0:T(8,128)S(1)} %bitcast.165, f32[1,32,32,128]{3,2,1,0:T(8,128)S(1)} %bitcast.167, f32[160,128]{1,0:T(8,128)S(1)} %get-tuple-element.6, f32[160,128]{1,0:T(8,128)S(1)} %neg.5, ...), kind=kOutput, calls=%fused_computation.28 | convolution fusion | flops 504545280 | bytes 2605056 | tf_op jit(solution)/shard_map/...nj,jc->...nc/dot_general | solution.py:67
  60.0 1.0 %pad_maximum_fusion.1 = f32[2,1,32,4096]{3,2,1,0:T(8,128)} fusion(f32[1,1,32,4096]{3,2,1,0:T(8,128)S(1)} %stack_reshape.7, f32[1,1,32,4096]{3,2,1,0:T(8,128)S(1)} %stack_reshape.6), kind=kLoop, calls=%fused_computation.34 | loop fusion | flops 262144 | bytes 2097152 | tf_op jit(solution)/shard_map/stack | solution.py:175
  (72 shorter events, 7.9 us)
Async XLA Ops:
  0.0 10.4 %collective-permute-start.2 = (f32[2,32,512]{2,1,0:T(8,128)}, f32[2,32,512]{2,1,0:T(8,128)S(1)}, u32[]{:S(2)}, u32[]{:S(2)}) collective-permute-start(f32[2,32,512]{2,1,0:T(8,128)} %param.6), channel_id=1, source_target_pairs={{0,16},{4,20},{8,24},{12,28},{16,0},{20,4},{24,8},{28,12},{1,17},{... | collective-permute-start | bytes 393224 | tf_op jit(solution)/shard_map/ppermute | solution.py:107
  3.1 7.3 %collective-permute-start = (f32[2,32,512]{2,1,0:T(8,128)}, f32[2,32,512]{2,1,0:T(8,128)S(1)}, u32[]{:S(2)}, u32[]{:S(2)}) collective-permute-start(f32[2,32,512]{2,1,0:T(8,128)} %param.6), channel_id=1, source_target_pairs={{0,4},{4,0},{8,12},{12,8},{16,20},{20,16},{24,28},{28,24},{1,5},{5... | collective-permute-start | bytes 393224 | tf_op jit(solution)/shard_map/ppermute | solution.py:107
  4.4 8.8 %collective-permute-start.1 = (f32[2,32,512]{2,1,0:T(8,128)}, f32[2,32,512]{2,1,0:T(8,128)S(1)}, u32[]{:S(2)}, u32[]{:S(2)}) collective-permute-start(f32[2,32,512]{2,1,0:T(8,128)} %param.6), channel_id=1, source_target_pairs={{0,8},{4,12},{8,0},{12,4},{16,24},{20,28},{24,16},{28,20},{1,9},{5... | collective-permute-start | bytes 393224 | tf_op jit(solution)/shard_map/ppermute | solution.py:107
  10.4 9.3 %collective-permute-start.3 = (f32[2,2,32,512]{3,2,1,0:T(8,128)S(1)}, f32[2,2,32,512]{3,2,1,0:T(8,128)S(1)}, u32[]{:S(2)}, u32[]{:S(2)}) collective-permute-start(f32[2,2,32,512]{3,2,1,0:T(8,128)S(1)} %pad_maximum_fusion.3), channel_id=1, source_target_pairs={{0,8},{4,12},{8,0},{12,4},{16,24},{20,28},{24,16},{28,20},{1,9},{5... | collective-permute-start | bytes 786440 | tf_op jit(solution)/shard_map/ppermute | solution.py:107
  10.8 9.0 %collective-permute-start.4 = (f32[2,32,512]{2,1,0:T(8,128)S(1)}, f32[2,32,512]{2,1,0:T(8,128)S(1)}, u32[]{:S(2)}, u32[]{:S(2)}) collective-permute-start(f32[2,32,512]{2,1,0:T(8,128)S(1)} %collective-permute-done.2), channel_id=1, source_target_pairs={{0,4},{4,0},{8,12},{12,8},{16,20},{20,16},{24,28},{28,24},{1,5},{5... | collective-permute-start | bytes 393224 | tf_op jit(solution)/shard_map/ppermute | solution.py:107
  12.0 7.3 %collective-permute-start.5 = (f32[2,32,512]{2,1,0:T(8,128)S(1)}, f32[2,32,512]{2,1,0:T(8,128)S(1)}, u32[]{:S(2)}, u32[]{:S(2)}) collective-permute-start(f32[2,32,512]{2,1,0:T(8,128)S(1)} %collective-permute-done.2), channel_id=1, source_target_pairs={{0,12},{4,8},{8,4},{12,0},{16,28},{20,24},{24,20},{28,16},{1,13},{... | collective-permute-start | bytes 393224 | tf_op jit(solution)/shard_map/ppermute | solution.py:107
  23.2 14.4 %collective-permute-start.6 = (f32[16,4096]{1,0:T(8,128)}, f32[16,4096]{1,0:T(8,128)S(1)}, u32[]{:S(2)}, u32[]{:S(2)}) collective-permute-start(f32[16,4096]{1,0:T(8,128)} %bitcast.52), channel_id=1, source_target_pairs={{0,1},{2,3},{1,0},{3,2},{4,5},{6,7},{5,4},{7,6},{8,9},{10,11},{9,8... | collective-permute-start | bytes 786440 | tf_op jit(solution)/shard_map/ppermute | solution.py:22
  26.7 10.9 %collective-permute-start.7 = (f32[16,4096]{1,0:T(8,128)}, f32[16,4096]{1,0:T(8,128)S(1)}, u32[]{:S(2)}, u32[]{:S(2)}) collective-permute-start(f32[16,4096]{1,0:T(8,128)} %bitcast.54), channel_id=1, source_target_pairs={{1,2},{2,1},{5,6},{6,5},{9,10},{10,9},{13,14},{14,13},{17,18},{18,... | collective-permute-start | bytes 786440 | tf_op jit(solution)/shard_map/ppermute | solution.py:23
  30.0 3.5 %copy-start = (f32[2,33]{1,0:T(2,128)S(1)}, f32[2,33]{1,0:T(2,128)}, u32[]{:S(2)}) copy-start(f32[2,33]{1,0:T(2,128)} %param.5) | copy-start | bytes 796
  45.6 2.8 %collective-permute-start.8 = (f32[2,1,16,4096]{3,2,1,0:T(8,128)S(1)}, f32[2,1,16,4096]{3,2,1,0:T(8,128)S(1)}, u32[]{:S(2)}, u32[]{:S(2)}) collective-permute-start(f32[2,1,16,4096]{3,2,1,0:T(8,128)S(1)} %get-tuple-element.19), channel_id=1, source_target_pairs={{0,1},{2,3},{1,0},{3,2},{4,5},{6,7},{5,4},{7,6},{8,9},{10,11},{9,8... | collective-permute-start | bytes 1572872 | tf_op jit(solution)/shard_map/ppermute | solution.py:22
  45.7 10.5 %collective-permute-start.9 = (f32[2,1,16,4096]{3,2,1,0:T(8,128)S(1)}, f32[2,1,16,4096]{3,2,1,0:T(8,128)S(1)}, u32[]{:S(2)}, u32[]{:S(2)}) collective-permute-start(f32[2,1,16,4096]{3,2,1,0:T(8,128)S(1)} %get-tuple-element.20), channel_id=1, source_target_pairs={{1,2},{2,1},{5,6},{6,5},{9,10},{10,9},{13,14},{14,13},{17,18},{18,... | collective-permute-start | bytes 1572872 | tf_op jit(solution)/shard_map/ppermute | solution.py:23

commit v20 on v17

--- a/solution.py
+++ b/solution.py
@@ -21,9 +21,7 @@
         within = [(i, i + 1) for i in range(0, count - 1, 2)] + [(i + 1, i) for i in range(0, count - 1, 2)]
         got_within = lax.ppermute(jnp.where(odd, head, tail), axis, within)
         got_across = lax.ppermute(jnp.where(odd, tail, head), axis, across)
-        before = jnp.where(odd, got_within, got_across)
-        after = jnp.where(odd, got_across, got_within)
-        cells = jnp.concatenate([before, cells, after], axis=dim)
+        cells = jnp.concatenate([got_within, cells, got_across], axis=dim)
     return cells
 
 
@@ -68,9 +66,14 @@
     return out[..., :block].reshape(real.shape), out[..., block:].reshape(real.shape)
 
 
-def cross_pass(real, imag, taps):
+def cross_pass(real, imag, taps, odd):
     count = real.shape[1] - 2 * HALF
-    band = complex_stack(band_matrix(taps[0], count), band_matrix(taps[1], count))
+
+    def placed(band):
+        swapped = jnp.concatenate([band[:, HALF + count :], band[:, HALF : HALF + count], band[:, :HALF]], axis=1)
+        return jnp.where(odd, band, swapped)
+
+    band = complex_stack(placed(band_matrix(taps[0], count)), placed(band_matrix(taps[1], count)))
     field = jnp.concatenate([real, imag], axis=1)
     out = jnp.einsum("ij,ajy->aiy", band, field, precision=lax.Precision.HIGH)
     return out[:, :count], out[:, count:]
@@ -149,28 +152,34 @@
     along_cos = jnp.cos(two_pi * along)[:, None, :]
     along_sin = jnp.sin(two_pi * along)[:, None, :]
 
-    def incident(rows):
-        real = across_cos[:, rows] * along_cos - across_sin[:, rows] * along_sin
-        imag = across_sin[:, rows] * along_cos + across_cos[:, rows] * along_sin
+    odd = lax.axis_index("tile") % 2 == 1
+
+    def incident(rows, other=None):
+        a_cos, a_sin = across_cos[:, rows], across_sin[:, rows]
+        if other is not None:
+            a_cos = jnp.where(odd, a_cos, across_cos[:, other])
+            a_sin = jnp.where(odd, a_sin, across_sin[:, other])
+        real = a_cos * along_cos - a_sin * along_sin
+        imag = a_sin * along_cos + a_cos * along_sin
         return real, imag
 
     halo = extended(screens[0], (("tile", 0),), HALF)
     pieces = [
-        transmit(*incident(rows), screen)
+        transmit(*incident(*rows), screen)
         for rows, screen in (
-            (slice(0, HALF), halo[:HALF]),
-            (slice(HALF, HALF + local_rows), screens[0]),
-            (slice(HALF + local_rows, span), halo[HALF + local_rows :]),
+            ((slice(0, HALF), slice(HALF + local_rows, span)), halo[:HALF]),
+            ((slice(HALF, HALF + local_rows),), screens[0]),
+            ((slice(HALF + local_rows, span), slice(0, HALF)), halo[HALF + local_rows :]),
         )
     ]
     real = jnp.concatenate([piece[0] for piece in pieces], axis=1)
     imag = jnp.concatenate([piece[1] for piece in pieces], axis=1)
-    real, imag = cross_pass(real, imag, taps)
+    real, imag = cross_pass(real, imag, taps, odd)
     real, imag = along_pass(real, imag, taps)
     for plane in range(1, PLANES):
         real, imag = transmit(real, imag, screens[plane])
         packed = extended(jnp.stack([real, imag]), (("tile", 2),), HALF)
-        real, imag = cross_pass(packed[0], packed[1], taps)
+        real, imag = cross_pass(packed[0], packed[1], taps, odd)
         real, imag = along_pass(real, imag, taps)
     return jnp.stack([real, imag])
 

time: 60.5 us -> 63.6 us (1.051)
  local copies, waits for them, and re-layouts: 15.5 us -> 19.1 us
  other arithmetic: 9.02 us -> 8.32 us
    cos x5 -> x7, local copies, waits for them, and re-layouts: 2.67 us -> 4.61 us  [transmit(): return rotate(real, imag, jnp.cos(screen), jnp.sin(screen))]
    unnamed x6, other arithmetic: 3.49 us -> 1.66 us
    slice x0 -> x3, local copies, waits for them, and re-layouts: none -> 1.42 us  [the longest x2 0.74 us: placed(): band[:, HALF:HALF + count]]
    concatenate x1, other arithmetic: 1 us -> 0.15 us  [cross_pass(): field = jnp.concatenate([real, imag], axis=1)]
    select_n x1 -> x2, other arithmetic: 0.07 us -> 0.78 us  [the longest x1 0.7 us: body(): jnp.where(inside[None, :], jnp.cos(two_pi * across), 0.0)[:, :, None]]
    add x1, other arithmetic: 0.01 us -> 0.68 us  [body(): taps = taps + landed]
    mul x0 -> x1, other arithmetic: none -> 0.66 us  [incident(): real = a_cos * along_cos - a_sin * along_sin]
    unnamed x21 -> x37, local copies, waits for them, and re-layouts: 3.12 us -> 3.16 us
  transfers between devices with their start and end apart: 10 -> 10, of which waited for: 4 -> 4; matrix products, arithmetic and copies ran while one was open for 20% -> 24% of each run, Pallas kernels for 0% -> 0%
where the time goes in v20:
time: 63.6 us; the launch traced here: 63.3 us
  local copies, waits for them, and re-layouts  19.1 us (30%)
  starting transfers between devices  18 us (28%)
  waiting for transfers between devices  11.7 us (18%)
  other arithmetic  8.32 us (13%)
  matrix products  3.64 us (6%)
  between operations  2.55 us (4%)
    ppermute x6, starting transfers between devices, exchange(): return lax.ppermute(x, axis, [(i, partner(i, k)) for i in range(count)])  8.39 us
    ppermute x2, waiting for transfers between devices, extended(): got_across = lax.ppermute(jnp.where(odd, tail, head), axis, across)  7.75 us
    ppermute x2, starting transfers between devices, extended(): got_across = lax.ppermute(jnp.where(odd, tail, head), axis, across)  5.73 us
    cos x7, local copies, waits for them, and re-layouts, transmit(): return rotate(real, imag, jnp.cos(screen), jnp.sin(screen))  4.61 us
    ppermute x6, waiting for transfers between devices, exchange(): return lax.ppermute(x, axis, [(i, partner(i, k)) for i in range(count)])  3.92 us
    ppermute x2, starting transfers between devices, extended(): got_within = lax.ppermute(jnp.where(odd, head, tail), axis, within)  3.92 us
    unnamed x37, local copies, waits for them, and re-layouts  3.16 us
    sin x5, local copies, waits for them, and re-layouts, transmit(): return rotate(real, imag, jnp.cos(screen), jnp.sin(screen))  2.67 us
  transfers between devices with their start and end apart: 10, of which 4 were waited for; matrix products, arithmetic and copies ran while one was open for 24% of the time, Pallas kernels for 0%

profile of v20, /device:TPU:1, one launch (start us, length us, event | category | flops | bytes accessed | tf_op | source)
XLA Modules:
  0.0 63.3 jit_solution(16317816987011984892)
XLA Ops:
  0.0 3.1 %collective-permute-start.2 = (f32[2,32,512]{2,1,0:T(8,128)}, f32[2,32,512]{2,1,0:T(8,128)S(1)}, u32[]{:S(2)}, u32[]{:S(2)}) collective-permute-start(f32[2,32,512]{2,1,0:T(8,128)} %param.6), channel_id=1, source_target_pairs={{0,16},{4,20},{8,24},{12,28},{16,0},{20,4},{24,8},{28,12},{1,17},{... | collective-permute-start | bytes 393224 | tf_op jit(solution)/shard_map/ppermute | solution.py:110
  3.1 1.3 %collective-permute-start.1 = (f32[2,32,512]{2,1,0:T(8,128)}, f32[2,32,512]{2,1,0:T(8,128)S(1)}, u32[]{:S(2)}, u32[]{:S(2)}) collective-permute-start(f32[2,32,512]{2,1,0:T(8,128)} %param.6), channel_id=1, source_target_pairs={{0,8},{4,12},{8,0},{12,4},{16,24},{20,28},{24,16},{28,20},{1,9},{5... | collective-permute-start | bytes 393224 | tf_op jit(solution)/shard_map/ppermute | solution.py:110
  4.4 1.2 %collective-permute-start = (f32[2,32,512]{2,1,0:T(8,128)}, f32[2,32,512]{2,1,0:T(8,128)S(1)}, u32[]{:S(2)}, u32[]{:S(2)}) collective-permute-start(f32[2,32,512]{2,1,0:T(8,128)} %param.6), channel_id=1, source_target_pairs={{0,4},{4,0},{8,12},{12,8},{16,20},{20,16},{24,28},{28,24},{1,5},{5... | collective-permute-start | bytes 393224 | tf_op jit(solution)/shard_map/ppermute | solution.py:110
  5.7 0.9 %bitcast_dynamic-update-slice_fusion.10 = f32[2,8,32,512]{3,2,0,1:T(8,128)S(1)} fusion(f32[2,32,512]{2,1,0:T(8,128)} %param.6), kind=kLoop, calls=%fused_computation.80 | loop fusion | bytes 262144
  6.6 1.3 %fusion.51 = (s32[1,1]{1,0:T(1,128)}, s32[1,1]{1,0:T(1,128)}) fusion(s32[1,2]{1,0:T(1,128)} %param.4), kind=kLoop, calls=%fused_computation.142 | loop fusion | bytes 16 | tf_op jit(solution)/shard_map/slice | solution.py:147
  7.9 0.7 %cosine_select_fusion = f32[1,64,1]{1,2,0:T(1,128)S(1)} fusion(s32[]{:T(128)S(6)} %sub.149, s32[]{:T(128)} %bitcast), kind=kLoop, calls=%fused_computation.125 | loop fusion | flops 1216 | bytes 264 | tf_op jit(solution)/shard_map/jit(_where)/select_n | solution.py:150
  8.6 0.7 %sine_select_fusion = f32[1,64,1]{1,2,0:T(1,128)S(1)} fusion(s32[]{:T(128)S(6)} %sub.149, s32[]{:T(128)} %bitcast), kind=kLoop, calls=%fused_computation.124 | loop fusion | flops 1216 | bytes 264 | tf_op jit(solution)/shard_map/jit(_where)/select_n | solution.py:151
  9.4 0.6 %slice_bitcast_fusion.16 = (f32[32]{0:T(128)}, f32[32]{0:T(128)}) fusion(f32[1,64,1]{1,2,0:T(1,128)S(1)} %sine_select_fusion, f32[1,64,1]{1,2,0:T(1,128)S(1)} %cosine_select_fusion), kind=kLoop, calls=%fused_computation.122 | loop fusion | bytes 512 | tf_op jit(solution)/shard_map/mul | solution.py:162
  10.0 0.7 %fusion.31 = (f32[16]{0:T(128)}, f32[16]{0:T(128)}, f32[16]{0:T(128)}, f32[16]{0:T(128)}) fusion(pred[]{:T(512)S(6)} %eq.34, f32[1,64,1]{1,2,0:T(1,128)S(1)} %cosine_select_fusion, f32[1,64,1]{1,2,0:T(1,128)S(1)} %sine_select_fusion), kind=kLoop, calls=%fused_computation.112 | loop fusion | flops 64 | bytes 513 | tf_op jit(solution)/shard_map/mul | solution.py:162
  11.3 0.8 %fusion.37 = (s32[8]{0:T(128)S(1)}, s32[8]{0:T(128)S(1)}) fusion(s32[2,8]{1,0:T(2,128)} %param.7, s32[]{:T(128)S(6)} %axis_index.17), kind=kLoop, calls=%fused_computation.118 | loop fusion | flops 64 | bytes 132 | tf_op jit(solution)/shard_map/select_n | solution.py:129
  12.6 2.3 %collective-permute-start.5 = (f32[2,32,512]{2,1,0:T(8,128)S(1)}, f32[2,32,512]{2,1,0:T(8,128)S(1)}, u32[]{:S(2)}, u32[]{:S(2)}) collective-permute-start(f32[2,32,512]{2,1,0:T(8,128)S(1)} %collective-permute-done.2), channel_id=1, source_target_pairs={{0,12},{4,8},{8,4},{12,0},{16,28},{20,24},{24,20},{28,16},{1,13},{... | collective-permute-start | bytes 393224 | tf_op jit(solution)/shard_map/ppermute | solution.py:110
  14.9 1.4 %collective-permute-done.4 = f32[2,32,512]{2,1,0:T(8,128)S(1)} collective-permute-done((f32[2,32,512]{2,1,0:T(8,128)S(1)}, f32[2,32,512]{2,1,0:T(8,128)S(1)}, u32[]{:S(2)}, u32[]{:S(2)}) %collective-permute-start.4) | collective-permute-done | bytes 131104 | tf_op jit(solution)/shard_map/ppermute | solution.py:110
  16.8 2.3 %collective-permute-done.5 = f32[2,32,512]{2,1,0:T(8,128)S(1)} collective-permute-done((f32[2,32,512]{2,1,0:T(8,128)S(1)}, f32[2,32,512]{2,1,0:T(8,128)S(1)}, u32[]{:S(2)}, u32[]{:S(2)}) %collective-permute-start.5) | collective-permute-done | bytes 131104 | tf_op jit(solution)/shard_map/ppermute | solution.py:110
  22.3 0.7 %broadcast_add_fusion = f32[2,33]{1,0:T(2,128)S(1)} fusion(f32[2,33]{1,0:T(2,128)} %param.5, f32[]{:T(128)} %bitcast.28), kind=kLoop, calls=%fused_computation.121 | loop fusion | flops 66 | bytes 532 | tf_op jit(solution)/shard_map/add | solution.py:140
  23.2 0.7 %slice.228 = f32[32,32]{1,0:T(8,128)} slice(f32[32,64]{1,0:T(8,128)S(1)} %get-tuple-element.7), slice={[0:32], [16:48]} | slice | bytes 8192 | tf_op jit(solution)/shard_map/slice | solution.py:73
  23.9 0.7 %fusion.49 = (f32[32,16]{1,0:T(8,128)}, f32[32,16]{1,0:T(8,128)}, f32[32,16]{1,0:T(8,128)S(1)}, f32[32,16]{1,0:T(8,128)S(1)}) fusion(f32[32,64]{1,0:T(8,128)S(1)} %get-tuple-element.7, f32[32,64]{1,0:T(8,128)S(1)} %get-tuple-element.8), kind=kLoop, calls=%fused_computation.140 | loop fusion | bytes 16384 | tf_op jit(solution)/shard_map/slice | solution.py:73
  25.4 1.9 %bitcast_cosine_fusion = (f32[32,8,512]{2,0,1:T(8,128)S(1)}, f32[32,8,512]{2,0,1:T(8,128)S(1)}) fusion(f32[8,32,512]{2,1,0:T(8,128)S(1)} %gather_fusion), kind=kLoop, calls=%fused_computation.132 | loop fusion | bytes 1572864 | tf_op jit(solution)/shard_map/cos | solution.py:83
  27.3 0.7 %copy.17 = f32[8,2,8,512]{3,2,0,1:T(8,128)} copy(f32[8,2,8,512]{3,2,1,0:T(8,128)S(1)} %get-tuple-element.38) | data formatting | bytes 524288 | tf_op jit(solution)/shard_map/jit(_where)/select_n | solution.py:22
  28.0 3.8 %collective-permute-start.6 = (f32[16,4096]{1,0:T(8,128)}, f32[16,4096]{1,0:T(8,128)S(1)}, u32[]{:S(2)}, u32[]{:S(2)}) collective-permute-start(f32[16,4096]{1,0:T(8,128)} %bitcast.51), channel_id=1, source_target_pairs={{0,1},{2,3},{1,0},{3,2},{4,5},{6,7},{5,4},{7,6},{8,9},{10,11},{9,8... | collective-permute-start | bytes 786440 | tf_op jit(solution)/shard_map/ppermute | solution.py:22
  32.7 0.7 %copy.18 = f32[8,2,8,512]{3,2,0,1:T(8,128)} copy(f32[8,2,8,512]{3,2,1,0:T(8,128)S(1)} %get-tuple-element.37) | data formatting | bytes 524288 | tf_op jit(solution)/shard_map/jit(_where)/select_n | solution.py:23
  33.4 3.0 %collective-permute-start.7 = (f32[16,4096]{1,0:T(8,128)}, f32[16,4096]{1,0:T(8,128)S(1)}, u32[]{:S(2)}, u32[]{:S(2)}) collective-permute-start(f32[16,4096]{1,0:T(8,128)} %bitcast.53), channel_id=1, source_target_pairs={{1,2},{2,1},{5,6},{6,5},{9,10},{10,9},{13,14},{14,13},{17,18},{18,... | collective-permute-start | bytes 786440 | tf_op jit(solution)/shard_map/ppermute | solution.py:23
  37.0 1.9 %sine_bitcast_fusion = (f32[32,8,512]{2,0,1:T(8,128)S(1)}, f32[32,8,512]{2,0,1:T(8,128)S(1)}) fusion(f32[8,32,512]{2,1,0:T(8,128)S(1)} %gather_fusion.1), kind=kLoop, calls=%fused_computation.48 | loop fusion | bytes 1572864 | tf_op jit(solution)/shard_map/sin | solution.py:83
  40.6 1.0 %fusion.48 = (f32[16,4096]{1,0:T(8,128)S(1)}, f32[16,4096]{1,0:T(8,128)S(1)}) fusion(f32[16,4096]{1,0:T(8,128)S(1)} %collective-permute-done.6), kind=kLoop, calls=%fused_computation.139 | loop fusion | bytes 786432 | tf_op jit(solution)/shard_map/cos | solution.py:83
  41.8 0.9 %subtract_dynamic-update-slice_fusion = f32[1,128,4096]{2,1,0:T(8,128)S(1)} fusion(f32[1,128,4096]{2,1,0:T(8,128)S(1)} %bitcast_dynamic-update-slice_fusion.3, f32[1,32,4096]{2,1,0:T(8,128)S(1)} %sin.70, f32[1,32,4096]{2,1,0:T(8,128)S(1)} %cos.70, f32[4096]{0:T(1024)S(1)} %get-tuple-element.65, f32[32]{0:T(128)} %get-tuple-element.67, ...), kind=kLoop, calls=%fused_computation.55 | loop fusion | flops 1179648 | bytes 1605888
  42.7 1.0 %fusion.47 = (f32[16,4096]{1,0:T(8,128)S(1)}, f32[16,4096]{1,0:T(8,128)S(1)}) fusion(f32[16,4096]{1,0:T(8,128)S(1)} %collective-permute-done.7), kind=kLoop, calls=%fused_computation.138 | loop fusion | bytes 786432 | tf_op jit(solution)/shard_map/cos | solution.py:83
  44.4 0.7 %convolution_bitcast_fusion.1 = f32[1,64,4096]{2,1,0:T(8,128)S(1)} fusion(f32[1,128,4096]{2,1,0:T(8,128)S(1)} %bitcast_dynamic-update-slice_fusion, f32[32,64]{1,0:T(8,128)S(1)} %maximum_select_fusion, f32[32,64]{1,0:T(8,128)S(1)} %get-tuple-element.10, f32[32,64]{1,0:T(8,128)S(1)} %get-tuple-element.9), kind=kOutput, calls=%fused_computation.3 | convolution fusion | flops 201351168 | bytes 3170304 | tf_op jit(solution)/shard_map/ij,ajy->aiy/dot_general | solution.py:78
  46.3 1.1 %fusion.18 = f32[1,32,32,256]{3,2,1,0:T(8,128)S(1)} fusion(f32[1,32,32,32]{3,2,1,0:T(8,128)S(1)} %bitcast.164, f32[1,32,32,128]{3,2,1,0:T(8,128)S(1)} %bitcast.170, f32[1,32,32,32]{3,2,1,0:T(8,128)S(1)} %bitcast.166, f32[1,32,32,128]{3,2,1,0:T(8,128)S(1)} %bitcast.168, f32[160,128]{1,0:T(8,128)S(1)} %get-tuple-element.6, f32[160,128]{1,0:T(8,128)S(1)} %neg.5, ...), kind=kOutput, calls=%fused_computation.29 | convolution fusion | flops 504545280 | bytes 2605056 | tf_op jit(solution)/shard_map/...nj,jc->...nc/dot_general | solution.py:65
  48.0 2.7 %collective-permute-start.9 = (f32[2,1,16,4096]{3,2,1,0:T(8,128)S(1)}, f32[2,1,16,4096]{3,2,1,0:T(8,128)S(1)}, u32[]{:S(2)}, u32[]{:S(2)}) collective-permute-start(f32[2,1,16,4096]{3,2,1,0:T(8,128)S(1)} %get-tuple-element.20), channel_id=1, source_target_pairs={{1,2},{2,1},{5,6},{6,5},{9,10},{10,9},{13,14},{14,13},{17,18},{18,... | collective-permute-start | bytes 1572872 | tf_op jit(solution)/shard_map/ppermute | solution.py:23
  50.8 7.7 %collective-permute-done.9 = f32[2,1,16,4096]{3,2,1,0:T(8,128)S(1)} collective-permute-done((f32[2,1,16,4096]{3,2,1,0:T(8,128)S(1)}, f32[2,1,16,4096]{3,2,1,0:T(8,128)S(1)}, u32[]{:S(2)}, u32[]{:S(2)}) %collective-permute-start.9) | collective-permute-done | bytes 524320 | tf_op jit(solution)/shard_map/ppermute | solution.py:23
  58.9 0.7 %convolution_bitcast_fusion = f32[1,64,4096]{2,1,0:T(8,128)S(1)} fusion(f32[1,64,4096]{2,1,0:T(8,128)S(1)} %get-tuple-element.12, f32[1,64,4096]{2,1,0:T(8,128)S(1)} %get-tuple-element.11, f32[32,64]{1,0:T(8,128)S(1)} %maximum_select_fusion, f32[32,64]{1,0:T(8,128)S(1)} %get-tuple-element.10, f32[32,64]{1,0:T(8,128)S(1)} %get-tuple-element.9), kind=kOutput, calls=%fused_computation.2 | convolution fusion | flops 201875456 | bytes 3170304 | tf_op jit(solution)/shard_map/ij,ajy->aiy/dot_general | solution.py:78
  60.8 1.1 %fusion.17 = f32[1,32,32,256]{3,2,1,0:T(8,128)S(1)} fusion(f32[1,32,32,32]{3,2,1,0:T(8,128)S(1)} %bitcast.163, f32[1,32,32,128]{3,2,1,0:T(8,128)S(1)} %bitcast.169, f32[1,32,32,32]{3,2,1,0:T(8,128)S(1)} %bitcast.165, f32[1,32,32,128]{3,2,1,0:T(8,128)S(1)} %bitcast.167, f32[160,128]{1,0:T(8,128)S(1)} %get-tuple-element.6, f32[160,128]{1,0:T(8,128)S(1)} %neg.5, ...), kind=kOutput, calls=%fused_computation.28 | convolution fusion | flops 504545280 | bytes 2605056 | tf_op jit(solution)/shard_map/...nj,jc->...nc/dot_general | solution.py:65
  62.3 1.0 %pad_maximum_fusion.1 = f32[2,1,32,4096]{3,2,1,0:T(8,128)} fusion(f32[1,1,32,4096]{3,2,1,0:T(8,128)S(1)} %stack_reshape.7, f32[1,1,32,4096]{3,2,1,0:T(8,128)S(1)} %stack_reshape.6), kind=kLoop, calls=%fused_computation.34 | loop fusion | flops 262144 | bytes 2097152 | tf_op jit(solution)/shard_map/stack | solution.py:184
  (92 shorter events, 11.4 us)
Async XLA Ops:
  0.0 12.1 %collective-permute-start.2 = (f32[2,32,512]{2,1,0:T(8,128)}, f32[2,32,512]{2,1,0:T(8,128)S(1)}, u32[]{:S(2)}, u32[]{:S(2)}) collective-permute-start(f32[2,32,512]{2,1,0:T(8,128)} %param.6), channel_id=1, source_target_pairs={{0,16},{4,20},{8,24},{12,28},{16,0},{20,4},{24,8},{28,12},{1,17},{... | collective-permute-start | bytes 393224 | tf_op jit(solution)/shard_map/ppermute | solution.py:110
  3.1 9.0 %collective-permute-start.1 = (f32[2,32,512]{2,1,0:T(8,128)}, f32[2,32,512]{2,1,0:T(8,128)S(1)}, u32[]{:S(2)}, u32[]{:S(2)}) collective-permute-start(f32[2,32,512]{2,1,0:T(8,128)} %param.6), channel_id=1, source_target_pairs={{0,8},{4,12},{8,0},{12,4},{16,24},{20,28},{24,16},{28,20},{1,9},{5... | collective-permute-start | bytes 393224 | tf_op jit(solution)/shard_map/ppermute | solution.py:110
  4.4 10.4 %collective-permute-start = (f32[2,32,512]{2,1,0:T(8,128)}, f32[2,32,512]{2,1,0:T(8,128)S(1)}, u32[]{:S(2)}, u32[]{:S(2)}) collective-permute-start(f32[2,32,512]{2,1,0:T(8,128)} %param.6), channel_id=1, source_target_pairs={{0,4},{4,0},{8,12},{12,8},{16,20},{20,16},{24,28},{28,24},{1,5},{5... | collective-permute-start | bytes 393224 | tf_op jit(solution)/shard_map/ppermute | solution.py:110
  12.2 7.8 %collective-permute-start.3 = (f32[2,2,32,512]{3,2,1,0:T(8,128)S(1)}, f32[2,2,32,512]{3,2,1,0:T(8,128)S(1)}, u32[]{:S(2)}, u32[]{:S(2)}) collective-permute-start(f32[2,2,32,512]{3,2,1,0:T(8,128)S(1)} %pad_maximum_fusion.3), channel_id=1, source_target_pairs={{0,4},{4,0},{8,12},{12,8},{16,20},{20,16},{24,28},{28,24},{1,5},{5... | collective-permute-start | bytes 786440 | tf_op jit(solution)/shard_map/ppermute | solution.py:110
  12.4 3.8 %collective-permute-start.4 = (f32[2,32,512]{2,1,0:T(8,128)S(1)}, f32[2,32,512]{2,1,0:T(8,128)S(1)}, u32[]{:S(2)}, u32[]{:S(2)}) collective-permute-start(f32[2,32,512]{2,1,0:T(8,128)S(1)} %collective-permute-done.2), channel_id=1, source_target_pairs={{0,8},{4,12},{8,0},{12,4},{16,24},{20,28},{24,16},{28,20},{1,9},{5... | collective-permute-start | bytes 393224 | tf_op jit(solution)/shard_map/ppermute | solution.py:110
  12.6 6.5 %collective-permute-start.5 = (f32[2,32,512]{2,1,0:T(8,128)S(1)}, f32[2,32,512]{2,1,0:T(8,128)S(1)}, u32[]{:S(2)}, u32[]{:S(2)}) collective-permute-start(f32[2,32,512]{2,1,0:T(8,128)S(1)} %collective-permute-done.2), channel_id=1, source_target_pairs={{0,12},{4,8},{8,4},{12,0},{16,28},{20,24},{24,20},{28,16},{1,13},{... | collective-permute-start | bytes 393224 | tf_op jit(solution)/shard_map/ppermute | solution.py:110
  28.0 12.5 %collective-permute-start.6 = (f32[16,4096]{1,0:T(8,128)}, f32[16,4096]{1,0:T(8,128)S(1)}, u32[]{:S(2)}, u32[]{:S(2)}) collective-permute-start(f32[16,4096]{1,0:T(8,128)} %bitcast.51), channel_id=1, source_target_pairs={{0,1},{2,3},{1,0},{3,2},{4,5},{6,7},{5,4},{7,6},{8,9},{10,11},{9,8... | collective-permute-start | bytes 786440 | tf_op jit(solution)/shard_map/ppermute | solution.py:22
  33.4 9.3 %collective-permute-start.7 = (f32[16,4096]{1,0:T(8,128)}, f32[16,4096]{1,0:T(8,128)S(1)}, u32[]{:S(2)}, u32[]{:S(2)}) collective-permute-start(f32[16,4096]{1,0:T(8,128)} %bitcast.53), channel_id=1, source_target_pairs={{1,2},{2,1},{5,6},{6,5},{9,10},{10,9},{13,14},{14,13},{17,18},{18,... | collective-permute-start | bytes 786440 | tf_op jit(solution)/shard_map/ppermute | solution.py:23
  39.6 0.9 %copy-start = (f32[32,32]{1,0:T(8,128)S(1)}, f32[32,32]{1,0:T(8,128)}, u32[]{:S(2)}) copy-start(f32[32,32]{1,0:T(8,128)} %slice.228) | copy-start | bytes 12292
  39.6 0.9 %copy-start.1 = (f32[32,16]{1,0:T(8,128)S(1)}, f32[32,16]{1,0:T(8,128)}, u32[]{:S(2)}) copy-start(f32[32,16]{1,0:T(8,128)} %get-tuple-element.45) | copy-start | bytes 6148
  39.6 0.9 %copy-start.2 = (f32[32,16]{1,0:T(8,128)S(1)}, f32[32,16]{1,0:T(8,128)}, u32[]{:S(2)}) copy-start(f32[32,16]{1,0:T(8,128)} %get-tuple-element.46) | copy-start | bytes 6148
  39.9 1.7 %copy-start.5 = (f32[16]{0:T(128)S(1)}, f32[16]{0:T(128)}, u32[]{:S(2)}) copy-start(f32[16]{0:T(128)} %get-tuple-element.54) | copy-start | bytes 196
  39.9 1.7 %copy-start.6 = (f32[16]{0:T(128)S(1)}, f32[16]{0:T(128)}, u32[]{:S(2)}) copy-start(f32[16]{0:T(128)} %get-tuple-element.61) | copy-start | bytes 196
  40.5 3.2 %copy-start.3 = (f32[16]{0:T(128)S(1)}, f32[16]{0:T(128)}, u32[]{:S(2)}) copy-start(f32[16]{0:T(128)} %get-tuple-element.53) | copy-start | bytes 196
  40.5 3.2 %copy-start.4 = (f32[16]{0:T(128)S(1)}, f32[16]{0:T(128)}, u32[]{:S(2)}) copy-start(f32[16]{0:T(128)} %get-tuple-element.62) | copy-start | bytes 196
  41.7 2.3 %copy-start.7 = (f32[32]{0:T(128)S(1)}, f32[32]{0:T(128)}, u32[]{:S(2)}) copy-start(f32[32]{0:T(128)} %get-tuple-element.67) | copy-start | bytes 388
  41.7 2.3 %copy-start.8 = (f32[32]{0:T(128)S(1)}, f32[32]{0:T(128)}, u32[]{:S(2)}) copy-start(f32[32]{0:T(128)} %get-tuple-element.68) | copy-start | bytes 388
  48.0 2.8 %collective-permute-start.8 = (f32[2,1,16,4096]{3,2,1,0:T(8,128)S(1)}, f32[2,1,16,4096]{3,2,1,0:T(8,128)S(1)}, u32[]{:S(2)}, u32[]{:S(2)}) collective-permute-start(f32[2,1,16,4096]{3,2,1,0:T(8,128)S(1)} %get-tuple-element.19), channel_id=1, source_target_pairs={{0,1},{2,3},{1,0},{3,2},{4,5},{6,7},{5,4},{7,6},{8,9},{10,11},{9,8... | collective-permute-start | bytes 1572872 | tf_op jit(solution)/shard_map/ppermute | solution.py:22
  48.0 10.5 %collective-permute-start.9 = (f32[2,1,16,4096]{3,2,1,0:T(8,128)S(1)}, f32[2,1,16,4096]{3,2,1,0:T(8,128)S(1)}, u32[]{:S(2)}, u32[]{:S(2)}) collective-permute-start(f32[2,1,16,4096]{3,2,1,0:T(8,128)S(1)} %get-tuple-element.20), channel_id=1, source_target_pairs={{1,2},{2,1},{5,6},{6,5},{9,10},{10,9},{13,14},{14,13},{17,18},{18,... | collective-permute-start | bytes 1572872 | tf_op jit(solution)/shard_map/ppermute | solution.py:23
